TPU v7x, 32 devices: a whole 2x2x4 slice. The times are simulated.
32 devices in a mesh: dp: 4 (over y, x), tensor: 8 (over z, core).
Axes of the slice: x: 2, y: 2, z: 4, core: 2. Of those that a mesh axis runs over, the one named last changes fastest.
Arguments:
- tokens: bfloat16 [2688, 1024], P('dp', 'tensor'), may hold values from -6 to 6
- cotangent: bfloat16 [2688, 1024], P('dp', 'tensor'), may hold values from -6 to 6
- lengths: int32 [4, 4], replicated, may hold values from 24 to 192, as said below
- owners: int32 [4, 4], replicated, may hold values from 0 to 3, as said below
- proj_weight: bfloat16 [1024, 4, 1024], replicated, may hold values from -0.1875 to 0.1875
- norm_gain: float32 [1024], replicated, may hold values from 0.5 to 2
- out_weight: bfloat16 [1024, 1024], replicated, may hold values from -0.1875 to 0.1875
Outputs:
- mixed: bfloat16 [1728, 1024], P('dp', 'tensor')
- token_grad: bfloat16 [2688, 1024], P('dp', 'tensor')
- proj_grad: float32 [1024, 4, 1024], P('dp', None, 'tensor')
- out_grad: float32 [1024, 1024], P('tensor', 'dp')
Inputs may be any that keep to these rules, and one draw needn't show every extreme that they name: Sequence i of loader shard j has lengths[j, i] rows stored back to back from the shard's first row; the sequences sent to any one owner sum to exactly 432 rows. owners[j, i] is the owner of sequence i of loader shard j; each row names every owner once.
All inputs are finite; a program needn't handle non-finite values.
Results may differ from a plain program's by a relative error of at most 0.012.
Values may be sent and summed in bfloat16 or wider, within the bound.
No kernel may reach another device: no remote copies, remote signals or barrier semaphores. Data moves between devices by JAX's collectives and lax.ppermute only.
A program may use at most 128 MiB of HBM per device.

v0:
```python
import math

import jax
import jax.numpy as jnp
from jax import lax
from jax.sharding import PartitionSpec as P

D = 1024
H = 8
MAXLEN = 192


norm_eps = 1e-05
contract_rows = (((0,), (0,)), ((), ()))
contract_cols = (((1,), (1,)), ((), ()))


def silu_slope(argument):
    sigmoid_val = jax.nn.sigmoid(argument)
    return sigmoid_val * (1.0 + argument * (1.0 - sigmoid_val))


def exclusive_sum(counts):
    return jnp.cumsum(counts) - counts


def local(tokens, cotangent, lengths, owners, proj_weight, norm_gain, out_weight):
    dp_count = lax.axis_size("dp")
    tensor_count = lax.axis_size("tensor")
    dp_index = lax.axis_index("dp")
    tensor_index = lax.axis_index("tensor")
    col_width = tokens.shape[1]
    load_rows = tokens.shape[0]
    head_dim = D // H
    score_scale = 1.0 / math.sqrt(head_dim)
    padded_rows = dp_count * MAXLEN
    owned_rows = dp_count * (9 * MAXLEN // 16)
    places = jnp.arange(MAXLEN, dtype=jnp.int32)
    peer_ids = jnp.arange(dp_count, dtype=jnp.int32)
    seq_ids = jnp.arange(lengths.shape[1], dtype=jnp.int32)
    zero_bf = jnp.zeros((), jnp.bfloat16)
    my_lengths = lengths[dp_index]
    my_owners = owners[dp_index]
    my_starts = exclusive_sum(my_lengths)
    sent_to = my_owners[None, :] == peer_ids[:, None]
    send_len = jnp.sum(jnp.where(sent_to, my_lengths[None, :], 0), axis=1)
    send_start = jnp.sum(jnp.where(sent_to, my_starts[None, :], 0), axis=1)
    send_live = places[None, :] < send_len[:, None]
    send_ids = jnp.minimum(send_start[:, None] + places[None, :], load_rows - 1)
    send_tokens = jnp.where(send_live[..., None], tokens[send_ids], zero_bf)
    send_cotan = jnp.where(send_live[..., None], cotangent[send_ids], zero_bf)
    recv_tokens, recv_cotan = (
        lax.all_to_all(send_tokens, "dp", split_axis=0, concat_axis=0, tiled=True),
        lax.all_to_all(send_cotan, "dp", split_axis=0, concat_axis=0, tiled=True),
    )
    recv_len = jnp.sum(jnp.where(owners == dp_index, lengths, 0), axis=1)
    recv_start = exclusive_sum(recv_len)
    slot_live = (places[None, :] < recv_len[:, None]).reshape(padded_rows)
    compact_ids = jnp.arange(owned_rows, dtype=jnp.int32)
    compact_slot = (
        jnp.sum((compact_ids[:, None] >= recv_start[None, :]).astype(jnp.int32), axis=1) - 1
    )
    slot_pick = compact_slot[:, None] == peer_ids[None, :]
    compact_start = jnp.sum(jnp.where(slot_pick, recv_start[None, :], 0), axis=1)
    gather_ids = compact_slot * MAXLEN + compact_ids - compact_start
    flat_tokens = recv_tokens.reshape(padded_rows, col_width)
    flat_cotan = recv_cotan.reshape(padded_rows, col_width)
    full_tokens, full_cotan = (
        lax.all_gather(flat_tokens, "tensor", axis=1, tiled=True),
        lax.all_gather(flat_cotan, "tensor", axis=1, tiled=True),
    )
    head_start = tensor_index * H // tensor_count * head_dim
    own_start = tensor_index * col_width
    inner_start = own_start - head_start
    head_proj = lax.dynamic_slice_in_dim(proj_weight, head_start, head_dim, 2).reshape(
        D, 4 * head_dim
    )
    own_proj = lax.dynamic_slice_in_dim(proj_weight, own_start, col_width, 2).reshape(
        D, 4 * col_width
    )
    head_out = lax.dynamic_slice_in_dim(out_weight, head_start, head_dim, 0)
    own_out = lax.dynamic_slice_in_dim(out_weight, own_start, col_width, 0)
    head_gain = lax.dynamic_slice_in_dim(norm_gain, head_start, head_dim, 0)
    projected = jnp.dot(full_tokens, head_proj, preferred_element_type=jnp.float32)
    down_grad = lax.dot_general(
        full_cotan, head_out, contract_cols, preferred_element_type=jnp.float32
    )
    slot_proj = projected
    slot_down = down_grad
    slot_proj = slot_proj.reshape(dp_count, MAXLEN, 4, head_dim)
    slot_down = slot_down.reshape(dp_count, MAXLEN, head_dim)
    activated = jax.nn.silu(slot_proj).astype(jnp.bfloat16)
    gating = activated[:, :, 0]
    values = activated[:, :, 1]
    queries = activated[:, :, 2]
    keys_head = activated[:, :, 3]
    scores = jnp.einsum("smd,snd->smn", queries, keys_head, preferred_element_type=jnp.float32)
    live_slots = slot_live.reshape(dp_count, MAXLEN)
    allowed = (
        (places[:, None] >= places[None, :])[None] & live_slots[:, :, None] & live_slots[:, None, :]
    )
    weights = jnp.where(allowed, jax.nn.silu(scores * score_scale) / MAXLEN, 0.0).astype(
        jnp.bfloat16
    )
    attended = jnp.einsum("smn,snd->smd", weights, values, preferred_element_type=jnp.float32)
    inv_rms = lax.rsqrt(jnp.mean(attended * attended, axis=-1, keepdims=True) + norm_eps)
    normed = attended * inv_rms * head_gain
    gated_rows = (normed * gating).astype(jnp.bfloat16).reshape(padded_rows, head_dim)
    own_gated = lax.dynamic_slice_in_dim(gated_rows, inner_start, col_width, 1)
    out_part = jnp.dot(own_gated, own_out, preferred_element_type=jnp.float32)
    d_normed = slot_down * gating
    d_gating = slot_down * normed
    scaled = head_gain * d_normed
    d_attended = (
        inv_rms * scaled
        - attended * inv_rms**3 * jnp.mean(attended * scaled, axis=-1, keepdims=True)
    ).astype(jnp.bfloat16)
    d_weights = jnp.einsum("smd,snd->smn", d_attended, values, preferred_element_type=jnp.float32)
    d_values = jnp.einsum("smn,smd->snd", weights, d_attended, preferred_element_type=jnp.float32)
    d_scores = jnp.where(
        allowed, d_weights * silu_slope(scores * score_scale) * (score_scale / MAXLEN), 0.0
    ).astype(jnp.bfloat16)
    d_queries = jnp.einsum("smn,snd->smd", d_scores, keys_head, preferred_element_type=jnp.float32)
    d_keys = jnp.einsum("smn,smd->snd", d_scores, queries, preferred_element_type=jnp.float32)
    d_activated = jnp.stack([d_gating, d_values, d_queries, d_keys], axis=2)
    d_projected = (
        (d_activated * silu_slope(slot_proj)).astype(jnp.bfloat16).reshape(padded_rows, 4, head_dim)
    )
    own_grad = lax.dynamic_slice_in_dim(d_projected, inner_start, col_width, 2).reshape(
        -1, 4 * col_width
    )
    grad_part = lax.dot_general(
        own_grad, own_proj, contract_cols, preferred_element_type=jnp.float32
    )
    out_sum, grad_sum = (
        lax.psum_scatter(
            out_part.astype(jnp.bfloat16), "tensor", scatter_dimension=1, tiled=True
        ).astype(jnp.float32),
        lax.psum_scatter(
            grad_part.astype(jnp.bfloat16), "tensor", scatter_dimension=1, tiled=True
        ).astype(jnp.float32),
    )
    mixed_rows = (flat_tokens.astype(jnp.float32) + out_sum).astype(jnp.bfloat16)
    token_rows = (flat_cotan.astype(jnp.float32) + grad_sum).astype(jnp.bfloat16)
    mixed_out = mixed_rows[gather_ids]
    back_grads = lax.all_to_all(
        token_rows.reshape(dp_count, MAXLEN, col_width),
        "dp",
        split_axis=0,
        concat_axis=0,
        tiled=True,
    )
    back_grads = back_grads.reshape(padded_rows, col_width)
    proj_term = lax.dot_general(
        full_tokens, own_grad, contract_rows, preferred_element_type=jnp.float32
    )
    out_term = lax.dot_general(
        full_cotan, own_gated, contract_rows, preferred_element_type=jnp.float32
    )
    proj_part, out_piece = (
        lax.psum_scatter(
            proj_term.astype(jnp.bfloat16), "dp", scatter_dimension=0, tiled=True
        ).astype(jnp.float32),
        lax.psum_scatter(
            out_term.astype(jnp.bfloat16), "dp", scatter_dimension=0, tiled=True
        ).astype(jnp.float32),
    )
    proj_grad = proj_part.reshape(-1, 4, col_width)
    out_grad = out_piece.T
    load_ids = jnp.arange(load_rows, dtype=jnp.int32)
    seq_of = jnp.sum((load_ids[:, None] >= my_starts[None, :]).astype(jnp.int32), axis=1) - 1
    seq_pick = seq_of[:, None] == seq_ids[None, :]
    owner_of = jnp.sum(jnp.where(seq_pick, my_owners[None, :], 0), axis=1)
    start_of = jnp.sum(jnp.where(seq_pick, my_starts[None, :], 0), axis=1)
    back_ids = owner_of * MAXLEN + jnp.minimum(load_ids - start_of, MAXLEN - 1)
    row_used = load_ids < jnp.sum(my_lengths)
    token_grad = jnp.where(row_used[:, None], back_grads[back_ids], zero_bf)
    return (mixed_out, token_grad, proj_grad, out_grad)


def solution(mesh):
    in_specs = (P("dp", "tensor"), P("dp", "tensor"), P(), P(), P(), P(), P())
    out_specs = (P("dp", "tensor"), P("dp", "tensor"), P("dp", None, "tensor"), P("tensor", "dp"))
    return jax.shard_map(local, mesh=mesh, in_specs=in_specs, out_specs=out_specs, check_vma=False)
```

profile of v0, /device:TPU:0, one launch (start us, length us, event | category | flops | bytes accessed | tf_op | source)
XLA Modules:
  0.0 226.6 jit_solution(4375256259258220019)
XLA Ops:
  7.2 1.5 fusion.23
  10.6 2.5 %gather_fusion.2 = bf16[768,128]{1,0:T(8,128)(2,1)S(1)} fusion(bf16[672,128]{1,0:T(8,128)(2,1)} %param.8, s32[1024]{0:T(1024)S(1)} %pad_clamp_fusion.2), kind=kCustom, calls=%fused_computation.2 | custom fusion | bytes 396288 | tf_op jit(solution)/shard_map/gather | solution.py:51
  13.2 1.9 gather_fusion
  15.3 10.6 %all_to_all.15 = bf16[4,192,128]{2,1,0:T(8,128)(2,1)} all-to-all(bf16[4,192,128]{2,1,0:T(8,128)(2,1)S(1)} %get-tuple-element.41), channel_id=1, replica_groups=mesh['dp'=4,'tensor'=8] {'dp'}, dimensions={0} | all-to-all | bytes 393216 | tf_op jit(solution)/shard_map/all_to_all | solution.py:53
  26.0 8.6 %all_to_all.16 = bf16[4,192,128]{2,1,0:T(8,128)(2,1)} all-to-all(bf16[4,192,128]{2,1,0:T(8,128)(2,1)S(1)} %get-tuple-element.40), channel_id=1, replica_groups=mesh['dp'=4,'tensor'=8] {'dp'}, dimensions={0} | all-to-all | bytes 393216 | tf_op jit(solution)/shard_map/all_to_all | solution.py:54
  34.7 3.4 %constant_dynamic-slice_fusion = (bf16[1024,4,128]{2,1,0:T(4,128)(2,1)}, bf16[1024,4,128]{2,1,0:T(4,128)(2,1)S(1)}) fusion(bf16[1024,4,1024]{2,1,0:T(4,128)(2,1)} %param.11, s32[]{:T(128)S(6)} %select_n.100, s32[]{:T(128)S(6)} %select_n.98), kind=kLoop, calls=%fused_computation.87 | loop fusion | bytes 4194312 | tf_op jit(solution)/shard_map/dynamic_slice | solution.py:78
  38.1 1.5 copy.56
  40.5 12.3 %all-gather.3.cloned.1.call-done = bf16[768,1024]{1,0:T(8,128)(2,1)} async-done(((bf16[768,128]{1,0:T(8,128)(2,1)}), bf16[768,1024]{1,0:T(8,128)(2,1)}) %all-gather.3.cloned.1.call-update) | async-done | bytes 1572880 | tf_op jit(solution)/shard_map/all_gather | solution.py:69
  52.8 2.7 %fusion.7 = f32[4,192,4,128]{3,1,2,0:T(8,128)S(1)} fusion(bf16[4,192,1024,1]{2,1,3,0:T(8,128)(2,1)} %bitcast.122, bf16[1024,4,128]{0,2,1:T(8,128)(2,1)} %copy.56), kind=kOutput, calls=%fused_computation.25 | convolution fusion | flops 805306368 | bytes 4194304 | tf_op jit(solution)/shard_map/dot_general | solution.py:84
  55.5 2.2 broadcast_subtract_fusion
  57.8 1.5 select_convert_fusion
  59.3 21.5 %all-gather.5.cloned.1.call-done = bf16[768,1024]{1,0:T(8,128)(2,1)} async-done(((bf16[768,128]{1,0:T(8,128)(2,1)}), bf16[768,1024]{1,0:T(8,128)(2,1)}) %all-gather.5.cloned.1.call-update) | async-done | bytes 1572880 | tf_op jit(solution)/shard_map/all_gather | solution.py:70
  80.8 2.0 fusion.15
  83.3 1.1 subtract_convert_fusion
  86.3 1.2 convolution_bitcast_fusion
  87.5 1.3 convolution_convert_fusion.3
  88.9 3.0 %fusion = bf16[4,192,4,128]{3,1,2,0:T(8,128)(2,1)S(1)} fusion(f32[4,192,1,128]{3,1,2,0:T(8,128)S(1)} %copy-done.7, f32[4,192,1,128]{3,1,2,0:T(8,128)S(1)} %copy-done.6, f32[4,192,1,128]{3,1,2,0:T(8,128)S(1)} %convolution_bitcast_fusion.2, f32[4,192,1,128]{3,1,2,0:T(8,128)} %get-tuple-element.35, f32[4,192,4,128]{3,1,0,2:T(8,128)} %get-tuple-element.31, ...), kind=kLoop, calls=%fused_computation.7 | loop fusion | flops 3145728 | bytes 7077888 | tf_op jit(solution)/shard_map/convert_element_type | solution.py:127
  93.3 2.1 convolution_convert_fusion.2
  95.4 3.4 %convolution_convert_fusion = bf16[768,1024]{1,0:T(8,128)(2,1)} fusion(bf16[128,8,4,128]{3,2,1,0:T(4,128)(2,1)} %bitcast.110, bf16[96,8,4,128]{3,2,1,0:T(4,128)(2,1)S(1)} %bitcast.112), kind=kOutput, calls=%fused_computation.4 | convolution fusion | flops 806092800 | bytes 3407872 | tf_op jit(solution)/shard_map/dot_general | solution.py:132
  98.8 2.6 %copy.54 = bf16[768,1024]{0,1:T(8,128)(2,1)} copy(bf16[768,1024]{1,0:T(8,128)(2,1)} %convolution_convert_fusion) | data formatting | bytes 3145728
  101.7 1.7 convolution_convert_fusion.1
  103.4 2.6 %copy.52 = bf16[768,1024]{0,1:T(8,128)(2,1)} copy(bf16[768,1024]{1,0:T(8,128)(2,1)} %convolution_convert_fusion.1) | data formatting | bytes 3145728
  107.3 5.0 %reduce-scatter.11.cloned.1.call-done = bf16[256,128]{1,0:T(8,128)(2,1)} async-done(((bf16[1024,128]{1,0:T(8,128)(2,1)}), bf16[256,128]{1,0:T(8,128)(2,1)}) %reduce-scatter.11.cloned.1.call-update) | async-done | bytes 65552 | tf_op jit(solution)/shard_map/reduce_scatter | solution.py:164
  113.9 29.1 %reduce-scatter.9.cloned.1.call-done = bf16[256,512]{1,0:T(8,128)(2,1)} async-done(((bf16[1024,512]{1,0:T(8,128)(2,1)}), bf16[256,512]{1,0:T(8,128)(2,1)}) %reduce-scatter.9.cloned.1.call-update) | async-done | bytes 262160 | tf_op jit(solution)/shard_map/reduce_scatter | solution.py:161
  143.0 1.9 reshape.310
  144.9 34.5 %reduce-scatter.15.cloned.1.call-done = bf16[128,768]{1,0:T(8,128)(2,1)} async-done(((bf16[1024,768]{1,0:T(8,128)(2,1)}), bf16[128,768]{1,0:T(8,128)(2,1)}) %reduce-scatter.15.cloned.1.call-update) | async-done | bytes 196624
  179.4 1.1 copy.55
  181.3 3.4 %all-to-all-start.2 = ((bf16[4,192,128]{2,1,0:T(8,128)(2,1)}), bf16[4,192,128]{2,1,0:T(8,128)(2,1)S(1)}, u32[]{:S(2)}, u32[]{:S(2)}) async-start(bf16[4,192,128]{2,1,0:T(8,128)(2,1)} %bitcast.30), calls=%async_computation.2 | async-start | bytes 393216 | tf_op jit(solution)/shard_map/all_to_all | solution.py:146
  184.7 29.1 %reduce-scatter.13.cloned.1.call-done = bf16[128,768]{1,0:T(8,128)(2,1)} async-done(((bf16[1024,768]{1,0:T(8,128)(2,1)}), bf16[128,768]{1,0:T(8,128)(2,1)}) %reduce-scatter.13.cloned.1.call-update) | async-done | bytes 196624
  213.8 1.1 copy.53
  215.0 1.9 gather_fusion.1
  216.9 2.0 gather_fusion.3
  (75 shorter events, 11.8 us)
Async XLA Ops:
  7.2 73.6 %copy-start = (bf16[1024,1024]{1,0:T(8,128)(2,1)S(1)}, bf16[1024,1024]{1,0:T(8,128)(2,1)}, u32[]{:S(2)}) copy-start(bf16[1024,1024]{1,0:T(8,128)(2,1)} %param.13) | copy-start | bytes 6291460
  7.2 6.0 %copy-start.1 = (bf16[672,128]{1,0:T(8,128)(2,1)S(1)}, bf16[672,128]{1,0:T(8,128)(2,1)}, u32[]{:S(2)}) copy-start(bf16[672,128]{1,0:T(8,128)(2,1)} %param.7) | copy-start | bytes 516100
  7.2 45.6 %all-gather.3.cloned.1.call-start = ((), (), s32[]{:S(2)}) async-start(), calls=%async_computation.7 | async-start | bytes 1769472 | tf_op jit(solution)/shard_map/all_gather | solution.py:69
  25.9 54.8 %all-gather.5.cloned.1.call-start = ((), (), s32[]{:S(2)}) async-start(), calls=%async_computation.8 | async-start | bytes 1769472 | tf_op jit(solution)/shard_map/all_gather | solution.py:70
  34.6 77.6 %reduce-scatter.11.cloned.1.call-start = ((), (), s32[]{:S(2)}) async-start(), calls=%async_computation.10 | async-start | bytes 327680 | tf_op jit(solution)/shard_map/reduce_scatter | solution.py:164
  55.5 2.2 copy-start.2
  59.3 24.0 %copy-start.8 = (bf16[4,192,192]{2,1,0:T(8,128)(2,1)}, bf16[4,192,192]{2,1,0:T(8,128)(2,1)S(1)}, u32[]{:S(2)}) copy-start(bf16[4,192,192]{2,1,0:T(8,128)(2,1)S(1)} %get-tuple-element.42) | copy-start | bytes 884740
  83.3 1.5 copy-start.11
  83.3 1.1 copy-start.9
  85.3 2.2 copy-start.3
  87.5 1.4 copy-start.6
  87.5 1.4 copy-start.7
  88.9 54.1 %reduce-scatter.9.cloned.1.call-start = ((), (), s32[]{:S(2)}) async-start(), calls=%async_computation.9 | async-start | bytes 1310720 | tf_op jit(solution)/shard_map/reduce_scatter | solution.py:161
  91.9 1.4 copy-start.10
  95.4 84.1 %reduce-scatter.15.cloned.1.call-start = ((), (), s32[]{:S(2)}) async-start(), calls=%async_computation.12 | async-start | bytes 1769472
  101.4 112.3 %reduce-scatter.13.cloned.1.call-start = ((), (), s32[]{:S(2)}) async-start(), calls=%async_computation.11 | async-start | bytes 1769472
  106.0 74.5 %copy-start.5 = (bf16[4,192,128]{2,1,0:T(8,128)(2,1)S(1)}, bf16[4,192,128]{2,1,0:T(8,128)(2,1)}, u32[]{:S(2)}) copy-start(bf16[4,192,128]{2,1,0:T(8,128)(2,1)} %all_to_all.16) | copy-start | bytes 589828
  106.0 108.9 %copy-start.4 = (bf16[4,192,128]{2,1,0:T(8,128)(2,1)S(1)}, bf16[4,192,128]{2,1,0:T(8,128)(2,1)}, u32[]{:S(2)}) copy-start(bf16[4,192,128]{2,1,0:T(8,128)(2,1)} %all_to_all.15) | copy-start | bytes 589828
  181.3 35.6 %all-to-all-start.2 = ((bf16[4,192,128]{2,1,0:T(8,128)(2,1)}), bf16[4,192,128]{2,1,0:T(8,128)(2,1)S(1)}, u32[]{:S(2)}, u32[]{:S(2)}) async-start(bf16[4,192,128]{2,1,0:T(8,128)(2,1)} %bitcast.30), calls=%async_computation.2 | async-start | bytes 393216 | tf_op jit(solution)/shard_map/all_to_all | solution.py:146
Sparse Core Ops, SparseCore 0:
  26.1 26.6 all-gather.2
  54.4 26.3 all-gather.4
  89.0 23.2 reduce-scatter.10
  115.3 27.6 reduce-scatter.8
  145.2 34.2 reduce-scatter.14
  181.6 32.1 reduce-scatter.12
where the time goes:
time: 227 us
  waiting for transfers between devices  132 us (58%)
  local copies, waits for them, and re-layouts  26.3 us (12%)
  blocking collectives  19.2 us (8%)
  matrix products  18.2 us (8%)
  between operations  14.4 us (6%)
  other arithmetic  13 us (6%)
  starting transfers between devices  3.85 us (2%)
    unnamed x8, waiting for transfers between devices  63.7 us
    reduce_scatter x1, waiting for transfers between devices, local(): lax.psum_scatter(proj_term.astype(jnp.bfloat16), 'dp', scatter_dimension=...  29.1 us
    all_gather x1, waiting for transfers between devices, local(): lax.all_gather(flat_cotan, 'tensor', axis=1, tiled=True)  21.5 us
    all_gather x1, waiting for transfers between devices, local(): lax.all_gather(flat_tokens, 'tensor', axis=1, tiled=True)  12.3 us
    all_to_all x1, blocking collectives, local(): lax.all_to_all(send_tokens, 'dp', split_axis=0, concat_axis=0, tiled=True)  10.6 us
    unnamed x30, local copies, waits for them, and re-layouts  10.5 us
    all_to_all x1, blocking collectives, local(): lax.all_to_all(send_cotan, 'dp', split_axis=0, concat_axis=0, tiled=True)  8.61 us
    reduce_scatter x1, waiting for transfers between devices, local(): lax.psum_scatter(out_term.astype(jnp.bfloat16), 'dp', scatter_dimension=0...  4.95 us
  transfers between devices with their start and end apart: 7, of which 6 were waited for; matrix products, arithmetic and copies ran while one was open for 17% of the time, Pallas kernels for 0%

commit v1 on v0

v1 whole, which is shorter than its diff:
```python
import math

import jax
import jax.numpy as jnp
from jax import lax
from jax.sharding import PartitionSpec as P

D = 1024
H = 8
MAXLEN = 192


norm_eps = 1e-05


def silu_slope(argument):
    sigmoid_val = jax.nn.sigmoid(argument)
    return sigmoid_val * (1.0 + argument * (1.0 - sigmoid_val))


def exclusive_sum(counts):
    return jnp.cumsum(counts) - counts


def local(tokens, cotangent, lengths, owners, proj_weight, norm_gain, out_weight):
    f32 = jnp.float32
    bf16 = jnp.bfloat16
    dp_count = lax.axis_size("dp")
    tensor_count = lax.axis_size("tensor")
    dp_index = lax.axis_index("dp")
    tensor_index = lax.axis_index("tensor")
    col_width = tokens.shape[1]
    load_rows = tokens.shape[0]
    head_dim = D // H
    score_scale = 1.0 / math.sqrt(head_dim)
    owned_rows = dp_count * (9 * MAXLEN // 16)
    places = jnp.arange(MAXLEN, dtype=jnp.int32)
    peer_ids = jnp.arange(dp_count, dtype=jnp.int32)
    seq_ids = jnp.arange(lengths.shape[1], dtype=jnp.int32)
    zero_bf = jnp.zeros((), bf16)

    my_lengths = lengths[dp_index]
    my_owners = owners[dp_index]
    my_starts = exclusive_sum(my_lengths)
    sent_to = my_owners[None, :] == peer_ids[:, None]
    send_start = jnp.sum(jnp.where(sent_to, my_starts[None, :], 0), axis=1)
    send_ids = jnp.minimum(send_start[:, None] + places[None, :], load_rows - 1)
    both = jnp.concatenate([tokens, cotangent], axis=1)
    send_both = both[send_ids]
    recv_both = lax.all_to_all(send_both, "dp", split_axis=0, concat_axis=0, tiled=True)

    recv_len = jnp.sum(jnp.where(owners == dp_index, lengths, 0), axis=1)
    recv_start = exclusive_sum(recv_len)
    compact_ids = jnp.arange(owned_rows, dtype=jnp.int32)
    compact_slot = (
        jnp.sum((compact_ids[:, None] >= recv_start[None, :]).astype(jnp.int32), axis=1) - 1
    )
    slot_pick = compact_slot[:, None] == peer_ids[None, :]
    compact_start = jnp.sum(jnp.where(slot_pick, recv_start[None, :], 0), axis=1)
    gather_ids = compact_slot * MAXLEN + compact_ids - compact_start
    own_both = recv_both.reshape(dp_count * MAXLEN, 2 * col_width)[gather_ids]
    own_tokens = own_both[:, :col_width]
    own_cotan = own_both[:, col_width:]

    gathered = lax.all_gather(own_both, "tensor", axis=0, tiled=False)
    g_tok = gathered[..., :col_width]
    g_cot = gathered[..., col_width:]

    head_start = tensor_index * H // tensor_count * head_dim
    own_start = tensor_index * col_width
    inner_start = own_start - head_start
    head_proj = lax.dynamic_slice_in_dim(proj_weight, head_start, head_dim, 2).reshape(
        tensor_count, col_width, 4 * head_dim
    )
    own_proj = lax.dynamic_slice_in_dim(proj_weight, own_start, col_width, 2).reshape(
        tensor_count, col_width, 4 * col_width
    )
    head_out = lax.dynamic_slice_in_dim(out_weight, head_start, head_dim, 0).reshape(
        head_dim, tensor_count, col_width
    )
    own_out = lax.dynamic_slice_in_dim(out_weight, own_start, col_width, 0).reshape(
        col_width, tensor_count, col_width
    )
    head_gain = lax.dynamic_slice_in_dim(norm_gain, head_start, head_dim, 0)

    projected = jnp.einsum("trc,tcn->rn", g_tok, head_proj, preferred_element_type=f32)
    down_grad = jnp.einsum("trc,dtc->rd", g_cot, head_out, preferred_element_type=f32)
    proj4 = projected.reshape(owned_rows, 4, head_dim)
    activated = jax.nn.silu(proj4).astype(bf16)
    gating = activated[:, 0]
    values = activated[:, 1]
    queries = activated[:, 2]
    keys_head = activated[:, 3]
    scores = jnp.einsum("md,nd->mn", queries, keys_head, preferred_element_type=f32)
    allowed = (compact_slot[:, None] == compact_slot[None, :]) & (
        compact_ids[:, None] >= compact_ids[None, :]
    )
    weights = jnp.where(allowed, jax.nn.silu(scores * score_scale) / MAXLEN, 0.0).astype(bf16)
    attended = jnp.einsum("mn,nd->md", weights, values, preferred_element_type=f32)
    inv_rms = lax.rsqrt(jnp.mean(attended * attended, axis=-1, keepdims=True) + norm_eps)
    normed = attended * inv_rms * head_gain
    gated = (normed * gating).astype(bf16)
    own_gated = lax.dynamic_slice_in_dim(gated, inner_start, col_width, 1)
    out_part = jnp.einsum("rc,ctk->trk", own_gated, own_out, preferred_element_type=f32)
    out_sum = lax.psum_scatter(
        out_part.astype(bf16), "tensor", scatter_dimension=0, tiled=True
    ).reshape(owned_rows, col_width)
    mixed_out = (own_tokens.astype(f32) + out_sum.astype(f32)).astype(bf16)

    d_normed = down_grad * gating
    d_gating = down_grad * normed
    scaled = head_gain * d_normed
    d_attended = (
        inv_rms * scaled
        - attended * inv_rms**3 * jnp.mean(attended * scaled, axis=-1, keepdims=True)
    ).astype(bf16)
    d_weights = jnp.einsum("md,nd->mn", d_attended, values, preferred_element_type=f32)
    d_values = jnp.einsum("mn,md->nd", weights, d_attended, preferred_element_type=f32)
    d_scores = jnp.where(
        allowed, d_weights * silu_slope(scores * score_scale) * (score_scale / MAXLEN), 0.0
    ).astype(bf16)
    d_queries = jnp.einsum("mn,nd->md", d_scores, keys_head, preferred_element_type=f32)
    d_keys = jnp.einsum("mn,md->nd", d_scores, queries, preferred_element_type=f32)
    d_activated = jnp.stack([d_gating, d_values, d_queries, d_keys], axis=1)
    d_projected = (d_activated * silu_slope(proj4)).astype(bf16)
    own_grad = lax.dynamic_slice_in_dim(d_projected, inner_start, col_width, 2).reshape(
        owned_rows, 4 * col_width
    )
    grad_part = jnp.einsum("rn,tkn->trk", own_grad, own_proj, preferred_element_type=f32)
    grad_sum = lax.psum_scatter(
        grad_part.astype(bf16), "tensor", scatter_dimension=0, tiled=True
    ).reshape(owned_rows, col_width)
    token_rows = (own_cotan.astype(f32) + grad_sum.astype(f32)).astype(bf16)

    proj_term = jnp.einsum("trc,rn->tcn", g_tok, own_grad, preferred_element_type=f32)
    out_term = jnp.einsum("trc,rd->tcd", g_cot, own_gated, preferred_element_type=f32)
    terms = jnp.concatenate(
        [proj_term.reshape(D, 4 * col_width), out_term.reshape(D, col_width)], axis=1
    ).astype(bf16)
    term_sum = lax.psum_scatter(terms, "dp", scatter_dimension=0, tiled=True).astype(f32)
    proj_grad = term_sum[:, : 4 * col_width].reshape(-1, 4, col_width)
    out_grad = term_sum[:, 4 * col_width :].T

    back_src = jnp.minimum(recv_start[:, None] + places[None, :], owned_rows - 1)
    back_send = token_rows[back_src]
    back_grads = lax.all_to_all(back_send, "dp", split_axis=0, concat_axis=0, tiled=True)
    back_grads = back_grads.reshape(dp_count * MAXLEN, col_width)
    load_ids = jnp.arange(load_rows, dtype=jnp.int32)
    seq_of = jnp.sum((load_ids[:, None] >= my_starts[None, :]).astype(jnp.int32), axis=1) - 1
    seq_pick = seq_of[:, None] == seq_ids[None, :]
    owner_of = jnp.sum(jnp.where(seq_pick, my_owners[None, :], 0), axis=1)
    start_of = jnp.sum(jnp.where(seq_pick, my_starts[None, :], 0), axis=1)
    back_ids = owner_of * MAXLEN + jnp.minimum(load_ids - start_of, MAXLEN - 1)
    row_used = load_ids < jnp.sum(my_lengths)
    token_grad = jnp.where(row_used[:, None], back_grads[back_ids], zero_bf)
    return (mixed_out, token_grad, proj_grad, out_grad)


def solution(mesh):
    in_specs = (P("dp", "tensor"), P("dp", "tensor"), P(), P(), P(), P(), P())
    out_specs = (P("dp", "tensor"), P("dp", "tensor"), P("dp", None, "tensor"), P("tensor", "dp"))
    return jax.shard_map(local, mesh=mesh, in_specs=in_specs, out_specs=out_specs, check_vma=False)
```

time: 227 us -> 169 us (0.74)
  waiting for transfers between devices: 132 us -> 102 us
  blocking collectives: 19.2 us -> 0 us
  matrix products: 18.2 us -> 11.1 us
  starting transfers between devices: 3.85 us -> 8.96 us
  other arithmetic: 13 us -> 9.11 us
  local copies, waits for them, and re-layouts: 26.3 us -> 23.5 us
    unnamed x8 -> x4, waiting for transfers between devices: 63.7 us -> 0.07 us
    reduce_scatter x2 -> x3, waiting for transfers between devices: 34.1 us -> 69.9 us  [the longest x1 32.4 us: local(): lax.psum_scatter(out_part.astype(bf16), 'tensor', scatter_dimension=0, ti...]
    all_to_all x2 -> x0, blocking collectives: 19.2 us -> none  [the longest x1 10.6 us: local(): lax.all_to_all(send_tokens, 'dp', split_axis=0, concat_axis=0, tiled=True)]
    all_gather x2 -> x1, waiting for transfers between devices: 33.8 us -> 19.3 us  [local(): gathered = lax.all_gather(own_both, 'tensor', axis=0, tiled=False)]
    all_to_all x1 -> x2, waiting for transfers between devices: 0.01 us -> 12.4 us  [the longest x1 6.21 us: local(): lax.all_to_all(send_both, 'dp', split_axis=0, concat_axis=0, tiled=True)]
    dot_general x12, matrix products: 18.2 us -> 11.1 us  [the longest x1 2.01 us: local(): jnp.einsum('trc,rn->tcn', g_tok, own_grad, preferred_element_type=f32)]
    unnamed x30 -> x17, local copies, waits for them, and re-layouts: 10.5 us -> 3.45 us
    all_to_all x1 -> x2, starting transfers between devices: 3.42 us -> 8.84 us  [the longest x1 5.16 us: local(): lax.all_to_all(send_both, 'dp', split_axis=0, concat_axis=0, tiled=True)]
  transfers between devices with their start and end apart: 7 -> 6, of which waited for: 6 -> 6; matrix products, arithmetic and copies ran while one was open for 17% -> 13% of each run, Pallas kernels for 0% -> 0%
where the time goes in v1:
time: 169 us; the launch traced here: 168 us
  waiting for transfers between devices  102 us (60%)
  local copies, waits for them, and re-layouts  23.5 us (14%)
  between operations  14.1 us (8%)
  matrix products  11.1 us (7%)
  other arithmetic  9.11 us (5%)
  starting transfers between devices  8.96 us (5%)
    reduce_scatter x1, waiting for transfers between devices, local(): lax.psum_scatter(out_part.astype(bf16), 'tensor', scatter_dimension=0, ti...  32.4 us
    reduce_scatter x1, waiting for transfers between devices, local(): lax.psum_scatter(grad_part.astype(bf16), 'tensor', scatter_dimension=0, t...  24.5 us
    all_gather x1, waiting for transfers between devices, local(): gathered = lax.all_gather(own_both, 'tensor', axis=0, tiled=False)  19.3 us
    reduce_scatter x1, waiting for transfers between devices, local(): lax.psum_scatter(terms, 'dp', scatter_dimension=0, tiled=True).astype(f32)  13 us
    all_to_all x1, waiting for transfers between devices, local(): lax.all_to_all(send_both, 'dp', split_axis=0, concat_axis=0, tiled=True)  6.21 us
    all_to_all x1, waiting for transfers between devices, local(): lax.all_to_all(back_send, 'dp', split_axis=0, concat_axis=0, tiled=True)  6.19 us
    all_to_all x1, starting transfers between devices, local(): lax.all_to_all(send_both, 'dp', split_axis=0, concat_axis=0, tiled=True)  5.16 us
    all_to_all x1, starting transfers between devices, local(): lax.all_to_all(back_send, 'dp', split_axis=0, concat_axis=0, tiled=True)  3.67 us
  transfers between devices with their start and end apart: 6, of which 6 were waited for; matrix products, arithmetic and copies ran while one was open for 13% of the time, Pallas kernels for 0%

profile of v1, /device:TPU:0, one launch (start us, length us, event | category | flops | bytes accessed | tf_op | source)
XLA Modules:
  0.0 168.4 jit_solution(6129958076720182823)
XLA Ops:
  7.2 1.3 fusion.24
  9.4 0.8 select_reduce_fusion.3
  10.4 1.0 pad_maximum_fusion.1
  11.4 3.3 %gather_fusion = bf16[768,256]{1,0:T(8,128)(2,1)} fusion(bf16[672,256]{1,0:T(8,128)(2,1)S(1)} %pad_maximum_fusion.1, s32[1024]{0:T(1024)S(1)} %pad_clamp_fusion.3), kind=kCustom, calls=%fused_computation | custom fusion | bytes 789504 | tf_op jit(solution)/shard_map/gather | solution.py:49
  14.7 5.2 %all-to-all-start = ((bf16[4,192,256]{2,1,0:T(8,128)(2,1)}), bf16[4,192,256]{2,1,0:T(8,128)(2,1)S(1)}, u32[]{:S(2)}, u32[]{:S(2)}) async-start(bf16[4,192,256]{2,1,0:T(8,128)(2,1)} %bitcast.2), calls=%async_computation | async-start | bytes 786432 | tf_op jit(solution)/shard_map/all_to_all | solution.py:50
  20.3 6.2 %all-to-all-done = bf16[4,192,256]{2,1,0:T(8,128)(2,1)S(1)} async-done(((bf16[4,192,256]{2,1,0:T(8,128)(2,1)}), bf16[4,192,256]{2,1,0:T(8,128)(2,1)S(1)}, u32[]{:S(2)}, u32[]{:S(2)}) %all-to-all-start) | async-done | bytes 393248 | tf_op jit(solution)/shard_map/all_to_all | solution.py:50
  26.5 2.6 %gather_fusion.1 = bf16[432,256]{1,0:T(8,128)(2,1)} fusion(bf16[768,256]{1,0:T(8,128)(2,1)S(1)} %bitcast.113, s32[1024]{0:T(1024)S(1)} %pad_clamp_fusion.2), kind=kCustom, calls=%fused_computation.1 | custom fusion | bytes 444096 | tf_op jit(solution)/shard_map/gather | solution.py:61
  29.1 2.4 %constant_dynamic-slice_fusion.1 = (bf16[1024,4,128]{2,1,0:T(4,128)(2,1)S(1)}, bf16[1024,4,128]{2,1,0:T(4,128)(2,1)S(1)}) fusion(bf16[1024,4,1024]{2,1,0:T(4,128)(2,1)} %param.11, s32[]{:T(128)S(6)} %select_n.96, s32[]{:T(128)S(6)} %select_n.98), kind=kLoop, calls=%fused_computation.88 | loop fusion | bytes 4194312 | tf_op jit(solution)/shard_map/dynamic_slice | solution.py:75
  32.0 1.5 copy.36
  33.4 1.2 constant_dynamic-slice_fusion
  34.6 0.8 copy.39
  35.4 0.8 dynamic_slice.27
  36.6 19.3 %all-gather.3.cloned.1.call-done = bf16[3456,256]{1,0:T(8,128)(2,1)} async-done(((bf16[432,256]{1,0:T(8,128)(2,1)}), bf16[3456,256]{1,0:T(8,128)(2,1)}) %all-gather.3.cloned.1.call-update) | async-done | bytes 1769488 | tf_op jit(solution)/shard_map/all_gather | solution.py:65
  55.9 1.9 %multiply_convert_fusion = (bf16[432,4,128]{2,0,1:T(8,128)(2,1)S(1)}, f32[432,4,128]{2,0,1:T(8,128)S(1)}) fusion(bf16[4,128,128,8]{2,3,1,0:T(8,128)(2,1)S(1)} %bitcast.116, bf16[8,432,256]{2,1,0:T(8,128)(2,1)} %bitcast.123), kind=kOutput, calls=%fused_computation.29 | convolution fusion | flops 454090752 | bytes 3260416 | tf_op jit(solution)/shard_map/trc,tcn->rn/dot_general | solution.py:86
  58.3 0.7 copy-done.5
  59.0 0.7 copy-done.6
  62.9 1.6 fusion.3
  64.7 1.3 fusion
  66.1 1.7 %convolution_convert_fusion.3 = bf16[8,128,128]{2,1,0:T(8,128)(2,1)S(1)} fusion(bf16[432,128,1]{1,0,2:T(8,128)(2,1)S(1)} %get-tuple-element.27, bf16[8,432,256]{2,1,0:T(8,128)(2,1)} %bitcast.124), kind=kOutput, calls=%fused_computation.16 | convolution fusion | flops 113377280 | bytes 1257472 | tf_op jit(solution)/shard_map/trc,rd->tcd/dot_general | solution.py:136
  68.0 2.0 %convolution_convert_fusion = bf16[1024,512]{0,1:T(8,128)(2,1)S(1)} fusion(bf16[8,432,256]{2,1,0:T(8,128)(2,1)} %bitcast.125, f32[432,4,128]{2,0,1:T(8,128)S(1)} %copy-done.4, f32[432,1,128]{2,0,1:T(8,128)S(1)} %convolution_bitcast_fusion.1, f32[432,1,128]{2,0,1:T(8,128)S(1)} %convolution_bitcast_fusion.2, f32[432,1,128]{2,0,1:T(8,128)S(1)} %convolution_bitcast_fusion.3, ...), kind=kOutput, calls=%fused_computation.4 | convolution fusion | flops 456163328 | bytes 3702784 | tf_op jit(solution)/shard_map/trc,rn->tcn/dot_general | solution.py:135
  70.0 1.2 pad_maximum_fusion
  71.6 24.5 %reduce-scatter.6.cloned.1.call-done = bf16[1,432,128]{2,1,0:T(8,128)(2,1)} async-done(((bf16[8,432,128]{2,1,0:T(8,128)(2,1)}), bf16[1,432,128]{2,1,0:T(8,128)(2,1)}) %reduce-scatter.6.cloned.1.call-update) | async-done | bytes 110608 | tf_op jit(solution)/shard_map/reduce_scatter | solution.py:130
  96.0 32.4 %reduce-scatter.4.cloned.1.call-done = bf16[1,432,128]{2,1,0:T(8,128)(2,1)} async-done(((bf16[8,432,128]{2,1,0:T(8,128)(2,1)}), bf16[1,432,128]{2,1,0:T(8,128)(2,1)}) %reduce-scatter.4.cloned.1.call-update) | async-done | bytes 110608 | tf_op jit(solution)/shard_map/reduce_scatter | solution.py:105
  128.5 1.7 fusion.18
  130.1 2.5 %gather_fusion.2 = bf16[768,128]{1,0:T(8,128)(2,1)} fusion(bf16[432,128]{1,0:T(8,128)(2,1)S(1)} %get-tuple-element.29, s32[1024]{0:T(1024)S(1)} %pad_clamp_fusion.1), kind=kCustom, calls=%fused_computation.2 | custom fusion | bytes 396288 | tf_op jit(solution)/shard_map/gather | solution.py:145
  132.7 3.7 %all-to-all-start.1 = ((bf16[4,192,128]{2,1,0:T(8,128)(2,1)}), bf16[4,192,128]{2,1,0:T(8,128)(2,1)S(1)}, u32[]{:S(2)}, u32[]{:S(2)}) async-start(bf16[4,192,128]{2,1,0:T(8,128)(2,1)} %bitcast.32), calls=%async_computation.3 | async-start | bytes 393216 | tf_op jit(solution)/shard_map/all_to_all | solution.py:146
  137.0 6.2 %all-to-all-done.1 = bf16[4,192,128]{2,1,0:T(8,128)(2,1)S(1)} async-done(((bf16[4,192,128]{2,1,0:T(8,128)(2,1)}), bf16[4,192,128]{2,1,0:T(8,128)(2,1)S(1)}, u32[]{:S(2)}, u32[]{:S(2)}) %all-to-all-start.1) | async-done | bytes 196640 | tf_op jit(solution)/shard_map/all_to_all | solution.py:146
  143.2 2.0 %gather_fusion.3 = bf16[672,128]{1,0:T(8,128)(2,1)S(1)} fusion(bf16[768,128]{1,0:T(8,128)(2,1)S(1)} %bitcast.112, s32[1024]{0:T(1024)S(1)} %pad_clamp_fusion), kind=kCustom, calls=%fused_computation.3 | custom fusion | bytes 346752 | tf_op jit(solution)/shard_map/gather | solution.py:155
  145.2 0.8 broadcast_select_fusion
  146.1 13.0 %reduce-scatter.8.cloned.1.call-done = bf16[256,640]{0,1:T(8,128)(2,1)} async-done(((bf16[1024,640]{0,1:T(8,128)(2,1)}), bf16[256,640]{0,1:T(8,128)(2,1)}) %reduce-scatter.8.cloned.1.call-update) | async-done | bytes 327696 | tf_op jit(solution)/shard_map/reduce_scatter | solution.py:140
  159.1 1.1 slice.56
  160.1 1.0 copy.32
  (62 shorter events, 8.0 us)
Async XLA Ops:
  14.7 11.8 %all-to-all-start = ((bf16[4,192,256]{2,1,0:T(8,128)(2,1)}), bf16[4,192,256]{2,1,0:T(8,128)(2,1)S(1)}, u32[]{:S(2)}, u32[]{:S(2)}) async-start(bf16[4,192,256]{2,1,0:T(8,128)(2,1)} %bitcast.2), calls=%async_computation | async-start | bytes 786432 | tf_op jit(solution)/shard_map/all_to_all | solution.py:50
  19.9 36.0 %all-gather.3.cloned.1.call-start = ((), (), s32[]{:S(2)}) async-start(), calls=%async_computation.8 | async-start | bytes 1990656 | tf_op jit(solution)/shard_map/all_gather | solution.py:65
  29.1 67.0 %reduce-scatter.6.cloned.1.call-start = ((), (), s32[]{:S(2)}) async-start(), calls=%async_computation.6 | async-start | bytes 995328 | tf_op jit(solution)/shard_map/reduce_scatter | solution.py:130
  33.4 22.4 %copy-start.2 = (bf16[8,128,512]{1,0,2:T(8,128)(2,1)S(1)}, bf16[8,128,512]{1,0,2:T(8,128)(2,1)}, u32[]{:S(2)}) copy-start(bf16[8,128,512]{1,0,2:T(8,128)(2,1)} %copy.36) | copy-start | bytes 3145732
  57.8 4.3 %copy-start.3 = (f32[432,4,128]{2,0,1:T(8,128)}, f32[432,4,128]{2,0,1:T(8,128)S(1)}, u32[]{:S(2)}) copy-start(f32[432,4,128]{2,0,1:T(8,128)S(1)} %get-tuple-element.36) | copy-start | bytes 2654212
  57.8 1.1 copy-start.5
  57.8 1.9 %copy-start.6 = (bf16[3456,256]{1,0:T(8,128)(2,1)S(1)}, bf16[3456,256]{1,0:T(8,128)(2,1)}, u32[]{:S(2)}) copy-start(bf16[3456,256]{1,0:T(8,128)(2,1)} %all-gather.3.cloned.1.call-done) | copy-start | bytes 5308420
  64.5 64.0 %reduce-scatter.4.cloned.1.call-start = ((), (), s32[]{:S(2)}) async-start(), calls=%async_computation.5 | async-start | bytes 995328 | tf_op jit(solution)/shard_map/reduce_scatter | solution.py:105
  66.0 2.0 %copy-start.4 = (f32[432,4,128]{2,0,1:T(8,128)S(1)}, f32[432,4,128]{2,0,1:T(8,128)}, u32[]{:S(2)}) copy-start(f32[432,4,128]{2,0,1:T(8,128)} %copy-done.3) | copy-start | bytes 2654212
  66.1 93.0 %reduce-scatter.8.cloned.1.call-start = ((), (), s32[]{:S(2)}) async-start(), calls=%async_computation.7 | async-start | bytes 1638400 | tf_op jit(solution)/shard_map/reduce_scatter | solution.py:140
  70.0 58.5 %copy-start.1 = (bf16[432,256]{1,0:T(8,128)(2,1)S(1)}, bf16[432,256]{1,0:T(8,128)(2,1)}, u32[]{:S(2)}) copy-start(bf16[432,256]{1,0:T(8,128)(2,1)} %gather_fusion.1) | copy-start | bytes 663556
  132.7 10.6 %all-to-all-start.1 = ((bf16[4,192,128]{2,1,0:T(8,128)(2,1)}), bf16[4,192,128]{2,1,0:T(8,128)(2,1)S(1)}, u32[]{:S(2)}, u32[]{:S(2)}) async-start(bf16[4,192,128]{2,1,0:T(8,128)(2,1)} %bitcast.32), calls=%async_computation.3 | async-start | bytes 393216 | tf_op jit(solution)/shard_map/all_to_all | solution.py:146
  159.1 2.1 %copy-start = (bf16[256,640]{0,1:T(8,128)(2,1)S(1)}, bf16[256,640]{0,1:T(8,128)(2,1)}, u32[]{:S(2)}) copy-start(bf16[256,640]{0,1:T(8,128)(2,1)} %reduce-scatter.8.cloned.1.call-done) | copy-start | bytes 983044
Sparse Core Ops, SparseCore 0:
  29.2 26.6 all-gather.2
  64.6 31.4 reduce-scatter.5
  98.4 29.9 reduce-scatter.3
  131.3 27.7 reduce-scatter.7

commit v2 on v1

--- a/solution.py
+++ b/solution.py
@@ -78,9 +78,6 @@
     head_out = lax.dynamic_slice_in_dim(out_weight, head_start, head_dim, 0).reshape(
         head_dim, tensor_count, col_width
     )
-    own_out = lax.dynamic_slice_in_dim(out_weight, own_start, col_width, 0).reshape(
-        col_width, tensor_count, col_width
-    )
     head_gain = lax.dynamic_slice_in_dim(norm_gain, head_start, head_dim, 0)
 
     projected = jnp.einsum("trc,tcn->rn", g_tok, head_proj, preferred_element_type=f32)
@@ -101,11 +98,12 @@
     normed = attended * inv_rms * head_gain
     gated = (normed * gating).astype(bf16)
     own_gated = lax.dynamic_slice_in_dim(gated, inner_start, col_width, 1)
-    out_part = jnp.einsum("rc,ctk->trk", own_gated, own_out, preferred_element_type=f32)
-    out_sum = lax.psum_scatter(
-        out_part.astype(bf16), "tensor", scatter_dimension=0, tiled=True
-    ).reshape(owned_rows, col_width)
-    mixed_out = (own_tokens.astype(f32) + out_sum.astype(f32)).astype(bf16)
+    g_gated = lax.all_gather(own_gated, "tensor", axis=0, tiled=False)
+    out_cols = lax.dynamic_slice_in_dim(out_weight, own_start, col_width, 1).reshape(
+        tensor_count, col_width, col_width
+    )
+    out_sum = jnp.einsum("trc,tck->rk", g_gated, out_cols, preferred_element_type=f32)
+    mixed_out = (own_tokens.astype(f32) + out_sum).astype(bf16)
 
     d_normed = down_grad * gating
     d_gating = down_grad * normed
@@ -127,17 +125,21 @@
         owned_rows, 4 * col_width
     )
     grad_part = jnp.einsum("rn,tkn->trk", own_grad, own_proj, preferred_element_type=f32)
-    grad_sum = lax.psum_scatter(
-        grad_part.astype(bf16), "tensor", scatter_dimension=0, tiled=True
-    ).reshape(owned_rows, col_width)
-    token_rows = (own_cotan.astype(f32) + grad_sum.astype(f32)).astype(bf16)
+    grad_pieces = lax.all_to_all(
+        grad_part.astype(bf16), "tensor", split_axis=0, concat_axis=0, tiled=True
+    )
+    grad_sum = jnp.sum(grad_pieces.astype(f32), axis=0)
+    token_rows = (own_cotan.astype(f32) + grad_sum).astype(bf16)
 
     proj_term = jnp.einsum("trc,rn->tcn", g_tok, own_grad, preferred_element_type=f32)
     out_term = jnp.einsum("trc,rd->tcd", g_cot, own_gated, preferred_element_type=f32)
     terms = jnp.concatenate(
         [proj_term.reshape(D, 4 * col_width), out_term.reshape(D, col_width)], axis=1
     ).astype(bf16)
-    term_sum = lax.psum_scatter(terms, "dp", scatter_dimension=0, tiled=True).astype(f32)
+    term_pieces = lax.all_to_all(
+        terms.reshape(dp_count, D // dp_count, 5 * col_width), "dp", 0, 0, tiled=True
+    )
+    term_sum = jnp.sum(term_pieces.astype(f32), axis=0)
     proj_grad = term_sum[:, : 4 * col_width].reshape(-1, 4, col_width)
     out_grad = term_sum[:, 4 * col_width :].T
 

time: 169 us -> 156 us (0.923)
  waiting for transfers between devices: 102 us -> 40.6 us
  blocking collectives: 0 us -> 31.7 us
  starting transfers between devices: 8.96 us -> 16.4 us
  local copies, waits for them, and re-layouts: 23.5 us -> 30.8 us
    reduce_scatter x3 -> x0, waiting for transfers between devices: 69.9 us -> none  [the longest x1 32.4 us: local(): lax.psum_scatter(out_part.astype(bf16), 'tensor', scatter_dimension=0, ti...]
    all_gather x0 -> x1, blocking collectives: none -> 31.7 us  [local(): g_gated = lax.all_gather(own_gated, 'tensor', axis=0, tiled=False)]
    all_to_all x0 -> x2, waiting for transfers between devices: none -> 11.6 us  [the longest x1 11.6 us: local(): lax.all_to_all(terms.reshape(dp_count, D // dp_count, 5 * col_width), 'dp...]
    all_to_all x0 -> x2, starting transfers between devices: none -> 7.86 us  [the longest x1 4.22 us: local(): lax.all_to_all(grad_part.astype(bf16), 'tensor', split_axis=0, concat_axi...]
    dot_general x0 -> x3, local copies, waits for them, and re-layouts: none -> 3.41 us  [local(): jnp.einsum('trc,rn->tcn', g_tok, own_grad, preferred_element_type=f32)]
    all_to_all x1, waiting for transfers between devices: 6.19 us -> 3.92 us  [local(): lax.all_to_all(back_send, 'dp', split_axis=0, concat_axis=0, tiled=True)]
    reshape x1, local copies, waits for them, and re-layouts: 0.42 us -> 2.27 us  [local(): lax.dynamic_slice_in_dim(proj_weight, own_start, col_width, 2)]
    unnamed x17 -> x15, local copies, waits for them, and re-layouts: 3.45 us -> 4.49 us
  transfers between devices with their start and end apart: 6 -> 5, of which waited for: 6 -> 4; matrix products, arithmetic and copies ran while one was open for 13% -> 13% of each run, Pallas kernels for 0% -> 0%
where the time goes in v2:
time: 156 us; the launch traced here: 155 us
  waiting for transfers between devices  40.6 us (26%)
  blocking collectives  31.7 us (20%)
  local copies, waits for them, and re-layouts  30.8 us (20%)
  starting transfers between devices  16.4 us (11%)
  between operations  14.4 us (9%)
  matrix products  11.8 us (8%)
  other arithmetic  9.08 us (6%)
    all_gather x1, blocking collectives, local(): g_gated = lax.all_gather(own_gated, 'tensor', axis=0, tiled=False)  31.7 us
    all_gather x1, waiting for transfers between devices, local(): gathered = lax.all_gather(own_both, 'tensor', axis=0, tiled=False)  18.8 us
    all_to_all x1, waiting for transfers between devices, local(): lax.all_to_all(terms.reshape(dp_count, D // dp_count, 5 * col_width), 'dp...  11.6 us
    all_to_all x1, waiting for transfers between devices, local(): lax.all_to_all(send_both, 'dp', split_axis=0, concat_axis=0, tiled=True)  6.21 us
    all_to_all x1, starting transfers between devices, local(): lax.all_to_all(send_both, 'dp', split_axis=0, concat_axis=0, tiled=True)  5.16 us
    unnamed x15, local copies, waits for them, and re-layouts  4.49 us
    all_to_all x1, starting transfers between devices, local(): lax.all_to_all(grad_part.astype(bf16), 'tensor', split_axis=0, concat_axi...  4.22 us
    all_to_all x1, waiting for transfers between devices, local(): lax.all_to_all(back_send, 'dp', split_axis=0, concat_axis=0, tiled=True)  3.92 us
  transfers between devices with their start and end apart: 5, of which 4 were waited for; matrix products, arithmetic and copies ran while one was open for 13% of the time, Pallas kernels for 0%

profile of v2, /device:TPU:0, one launch (start us, length us, event | category | flops | bytes accessed | tf_op | source)
XLA Modules:
  0.0 154.7 jit_solution(16595497244159766899)
XLA Ops:
  7.2 1.5 fusion.20
  10.5 1.0 pad_maximum_fusion.1
  11.6 3.3 %gather_fusion = bf16[768,256]{1,0:T(8,128)(2,1)} fusion(bf16[672,256]{1,0:T(8,128)(2,1)S(1)} %pad_maximum_fusion.1, s32[1024]{0:T(1024)S(1)} %pad_clamp_fusion.3), kind=kCustom, calls=%fused_computation | custom fusion | bytes 789504 | tf_op jit(solution)/shard_map/gather | solution.py:49
  14.9 5.2 %all-to-all-start = ((bf16[4,192,256]{2,1,0:T(8,128)(2,1)}), bf16[4,192,256]{2,1,0:T(8,128)(2,1)S(1)}, u32[]{:S(2)}, u32[]{:S(2)}) async-start(bf16[4,192,256]{2,1,0:T(8,128)(2,1)} %bitcast.2), calls=%async_computation | async-start | bytes 786432 | tf_op jit(solution)/shard_map/all_to_all | solution.py:50
  20.4 6.2 %all-to-all-done = bf16[4,192,256]{2,1,0:T(8,128)(2,1)S(1)} async-done(((bf16[4,192,256]{2,1,0:T(8,128)(2,1)}), bf16[4,192,256]{2,1,0:T(8,128)(2,1)S(1)}, u32[]{:S(2)}, u32[]{:S(2)}) %all-to-all-start) | async-done | bytes 393248 | tf_op jit(solution)/shard_map/all_to_all | solution.py:50
  26.6 2.6 %gather_fusion.1 = bf16[432,256]{1,0:T(8,128)(2,1)} fusion(bf16[768,256]{1,0:T(8,128)(2,1)S(1)} %bitcast.102, s32[1024]{0:T(1024)S(1)} %pad_clamp_fusion.2), kind=kCustom, calls=%fused_computation.1 | custom fusion | bytes 444096 | tf_op jit(solution)/shard_map/gather | solution.py:61
  29.2 3.4 %constant_dynamic-slice_fusion.1 = (bf16[1024,4,128]{2,1,0:T(4,128)(2,1)}, bf16[1024,4,128]{2,1,0:T(4,128)(2,1)S(1)}) fusion(bf16[1024,4,1024]{2,1,0:T(4,128)(2,1)} %param.11, s32[]{:T(128)S(6)} %select_n.99, s32[]{:T(128)S(6)} %select_n.97), kind=kLoop, calls=%fused_computation.85 | loop fusion | bytes 4194312 | tf_op jit(solution)/shard_map/dynamic_slice | solution.py:75
  32.6 1.2 reshape.321
  33.9 1.7 %copy.41 = bf16[8,128,512]{1,0,2:T(8,128)(2,1)S(1)} copy(bf16[8,128,512]{2,1,0:T(8,128)(2,1)} %reshape.321) | data formatting | bytes 2097152 | tf_op jit(solution)/shard_map/reshape | solution.py:72
  37.2 18.8 %all-gather.4.cloned.1.call-done = bf16[3456,256]{1,0:T(8,128)(2,1)} async-done(((bf16[432,256]{1,0:T(8,128)(2,1)}), bf16[3456,256]{1,0:T(8,128)(2,1)}) %all-gather.4.cloned.1.call-update) | async-done | bytes 1769488 | tf_op jit(solution)/shard_map/all_gather | solution.py:65
  56.0 1.9 %multiply_convert_fusion = (bf16[432,4,128]{2,0,1:T(8,128)(2,1)S(1)}, f32[432,4,128]{2,0,1:T(8,128)S(1)}) fusion(bf16[4,128,128,8]{2,3,1,0:T(8,128)(2,1)S(1)} %bitcast.105, bf16[8,432,256]{2,1,0:T(8,128)(2,1)} %bitcast.107), kind=kOutput, calls=%fused_computation.31 | convolution fusion | flops 454090752 | bytes 3260416 | tf_op jit(solution)/shard_map/trc,tcn->rn/dot_general | solution.py:83
  58.4 1.0 copy-done.3
  62.6 0.9 reshape.319
  63.5 1.2 copy.34
  64.7 2.1 %dot_general.57 = bf16[4,256,432]{1,0,2:T(4,128)(2,1)S(1)} reshape(bf16[8,128,432]{1,0,2:T(8,128)(2,1)} %copy.34) | data formatting | bytes 1769472 | tf_op jit(solution)/shard_map/trc,rn->tcn/dot_general | solution.py:134
  66.8 1.7 %convolution_convert_fusion.2 = bf16[8,128,128]{2,1,0:T(8,128)(2,1)S(1)} fusion(bf16[8,432,256]{2,1,0:T(8,128)(2,1)} %bitcast.108, bf16[432,128]{1,0:T(8,128)(2,1)S(1)} %get-tuple-element.25), kind=kOutput, calls=%fused_computation.16 | convolution fusion | flops 113377280 | bytes 1257472 | tf_op jit(solution)/shard_map/trc,rd->tcd/dot_general | solution.py:135
  69.2 1.2 pad_maximum_fusion
  70.4 3.6 %all-to-all-start.3 = ((bf16[4,256,640]{2,1,0:T(8,128)(2,1)}), bf16[4,256,640]{2,1,0:T(8,128)(2,1)S(1)}, u32[]{:S(2)}, u32[]{:S(2)}) async-start(bf16[4,256,640]{2,1,0:T(8,128)(2,1)} %pad_maximum_fusion), calls=%async_computation.3 | async-start | bytes 2621440 | tf_op jit(solution)/shard_map/all_to_all | solution.py:139
  74.1 2.3 %reshape.273 = bf16[8,128,512]{2,1,0:T(8,128)(2,1)} reshape(bf16[1024,4,128]{2,1,0:T(4,128)(2,1)} %get-tuple-element.22) | data formatting | bytes 2097152 | tf_op jit(solution)/shard_map/reshape | solution.py:75
  76.5 2.9 %fusion.2 = bf16[8,432,128]{2,1,0:T(8,128)(2,1)} fusion(bf16[8,128,512]{2,1,0:T(8,128)(2,1)} %reshape.273, bf16[432,512,1]{1,0,2:T(8,128)(2,1)} %reshape.319), kind=kOutput, calls=%fused_computation.13 | convolution fusion | flops 453427200 | bytes 2375680 | tf_op jit(solution)/shard_map/rn,tkn->trk/dot_general | solution.py:127
  79.4 11.6 %all-to-all-done.3 = bf16[4,256,640]{2,1,0:T(8,128)(2,1)S(1)} async-done(((bf16[4,256,640]{2,1,0:T(8,128)(2,1)}), bf16[4,256,640]{2,1,0:T(8,128)(2,1)S(1)}, u32[]{:S(2)}, u32[]{:S(2)}) %all-to-all-start.3) | async-done | bytes 1310752 | tf_op jit(solution)/shard_map/all_to_all | solution.py:139
  91.0 4.2 %all-to-all-start.1 = ((bf16[8,432,128]{2,1,0:T(8,128)(2,1)}), bf16[8,432,128]{2,1,0:T(8,128)(2,1)}, u32[]{:S(2)}, u32[]{:S(2)}) async-start(bf16[8,432,128]{2,1,0:T(8,128)(2,1)} %fusion.2), calls=%async_computation.1 | async-start | bytes 1769472 | tf_op jit(solution)/shard_map/all_to_all | solution.py:128
  96.2 31.7 %all-gather.1 = bf16[3456,128]{1,0:T(8,128)(2,1)S(1)} all-gather(bf16[432,128]{1,0:T(8,128)(2,1)S(1)} %get-tuple-element.25), channel_id=3, replica_groups=mesh['dp'=4,'tensor'=8] {'tensor'}, dimensions={0}, use_global_device_ids=true | all-gather | bytes 995328 | tf_op jit(solution)/shard_map/all_gather | solution.py:101
  127.9 1.9 %fusion.5 = bf16[432,128]{1,0:T(8,128)(2,1)} fusion(bf16[8,432,128]{2,1,0:T(8,128)(2,1)S(1)} %bitcast.103, bf16[8,128,128]{2,1,0:T(8,128)(2,1)S(1)} %bitcast.106, bf16[432,256]{1,0:T(8,128)(2,1)} %gather_fusion.1), kind=kOutput, calls=%fused_computation.23 | convolution fusion | flops 113412096 | bytes 1368064 | tf_op jit(solution)/shard_map/trc,tck->rk/dot_general | solution.py:105
  130.0 0.8 copy-done.1
  131.1 1.0 copy.37
  132.1 1.3 convert_reduce_fusion.1
  133.5 2.5 %gather_fusion.2 = bf16[768,128]{1,0:T(8,128)(2,1)} fusion(bf16[432,128]{1,0:T(8,128)(2,1)S(1)} %add_convert_fusion, s32[1024]{0:T(1024)S(1)} %pad_clamp_fusion.1), kind=kCustom, calls=%fused_computation.2 | custom fusion | bytes 396288 | tf_op jit(solution)/shard_map/gather | solution.py:147
  136.0 3.4 %all-to-all-start.2 = ((bf16[4,192,128]{2,1,0:T(8,128)(2,1)}), bf16[4,192,128]{2,1,0:T(8,128)(2,1)S(1)}, u32[]{:S(2)}, u32[]{:S(2)}) async-start(bf16[4,192,128]{2,1,0:T(8,128)(2,1)} %bitcast.30), calls=%async_computation.2 | async-start | bytes 393216 | tf_op jit(solution)/shard_map/all_to_all | solution.py:148
  139.4 0.9 slice_bitcast_fusion.1
  141.1 3.9 %all-to-all-done.2 = bf16[4,192,128]{2,1,0:T(8,128)(2,1)S(1)} async-done(((bf16[4,192,128]{2,1,0:T(8,128)(2,1)}), bf16[4,192,128]{2,1,0:T(8,128)(2,1)S(1)}, u32[]{:S(2)}, u32[]{:S(2)}) %all-to-all-start.2) | async-done | bytes 196640 | tf_op jit(solution)/shard_map/all_to_all | solution.py:148
  145.0 2.0 %gather_fusion.3 = bf16[672,128]{1,0:T(8,128)(2,1)S(1)} fusion(bf16[768,128]{1,0:T(8,128)(2,1)S(1)} %bitcast.101, s32[1024]{0:T(1024)S(1)} %pad_clamp_fusion), kind=kCustom, calls=%fused_computation.3 | custom fusion | bytes 346752 | tf_op jit(solution)/shard_map/gather | solution.py:157
  (61 shorter events, 11.3 us)
Async XLA Ops:
  7.2 28.4 %copy-start = (bf16[1024,1024]{1,0:T(8,128)(2,1)S(1)}, bf16[1024,1024]{1,0:T(8,128)(2,1)}, u32[]{:S(2)}) copy-start(bf16[1024,1024]{1,0:T(8,128)(2,1)} %param.13) | copy-start | bytes 6291460
  14.9 11.8 %all-to-all-start = ((bf16[4,192,256]{2,1,0:T(8,128)(2,1)}), bf16[4,192,256]{2,1,0:T(8,128)(2,1)S(1)}, u32[]{:S(2)}, u32[]{:S(2)}) async-start(bf16[4,192,256]{2,1,0:T(8,128)(2,1)} %bitcast.2), calls=%async_computation | async-start | bytes 786432 | tf_op jit(solution)/shard_map/all_to_all | solution.py:50
  20.0 36.0 %all-gather.4.cloned.1.call-start = ((), (), s32[]{:S(2)}) async-start(), calls=%async_computation.4 | async-start | bytes 1990656 | tf_op jit(solution)/shard_map/all_gather | solution.py:65
  58.0 1.5 copy-start.3
  58.0 1.5 copy-start.5
  64.7 3.8 %copy-start.4 = (bf16[432,512,1]{1,0,2:T(8,128)(2,1)S(1)}, bf16[432,512,1]{1,0,2:T(8,128)(2,1)}, u32[]{:S(2)}) copy-start(bf16[432,512,1]{1,0,2:T(8,128)(2,1)} %reshape.319) | copy-start | bytes 1327108
  70.4 20.6 %all-to-all-start.3 = ((bf16[4,256,640]{2,1,0:T(8,128)(2,1)}), bf16[4,256,640]{2,1,0:T(8,128)(2,1)S(1)}, u32[]{:S(2)}, u32[]{:S(2)}) async-start(bf16[4,256,640]{2,1,0:T(8,128)(2,1)} %pad_maximum_fusion), calls=%async_computation.3 | async-start | bytes 2621440 | tf_op jit(solution)/shard_map/all_to_all | solution.py:139
  91.0 41.1 %all-to-all-start.1 = ((bf16[8,432,128]{2,1,0:T(8,128)(2,1)}), bf16[8,432,128]{2,1,0:T(8,128)(2,1)}, u32[]{:S(2)}, u32[]{:S(2)}) async-start(bf16[8,432,128]{2,1,0:T(8,128)(2,1)} %fusion.2), calls=%async_computation.1 | async-start | bytes 1769472 | tf_op jit(solution)/shard_map/all_to_all | solution.py:128
  130.0 0.9 copy-start.1
  130.9 2.5 %copy-start.2 = (bf16[432,256]{1,0:T(8,128)(2,1)S(1)}, bf16[432,256]{1,0:T(8,128)(2,1)}, u32[]{:S(2)}) copy-start(bf16[432,256]{1,0:T(8,128)(2,1)} %gather_fusion.1) | copy-start | bytes 663556
  136.0 9.0 %all-to-all-start.2 = ((bf16[4,192,128]{2,1,0:T(8,128)(2,1)}), bf16[4,192,128]{2,1,0:T(8,128)(2,1)S(1)}, u32[]{:S(2)}, u32[]{:S(2)}) async-start(bf16[4,192,128]{2,1,0:T(8,128)(2,1)} %bitcast.30), calls=%async_computation.2 | async-start | bytes 393216 | tf_op jit(solution)/shard_map/all_to_all | solution.py:148
Sparse Core Ops, SparseCore 0:
  29.3 26.6 all-gather.3

commit v3 on v1

--- a/solution.py
+++ b/solution.py
@@ -36,7 +36,6 @@
     owned_rows = dp_count * (9 * MAXLEN // 16)
     places = jnp.arange(MAXLEN, dtype=jnp.int32)
     peer_ids = jnp.arange(dp_count, dtype=jnp.int32)
-    seq_ids = jnp.arange(lengths.shape[1], dtype=jnp.int32)
     zero_bf = jnp.zeros((), bf16)
 
     my_lengths = lengths[dp_index]
@@ -44,9 +43,11 @@
     my_starts = exclusive_sum(my_lengths)
     sent_to = my_owners[None, :] == peer_ids[:, None]
     send_start = jnp.sum(jnp.where(sent_to, my_starts[None, :], 0), axis=1)
-    send_ids = jnp.minimum(send_start[:, None] + places[None, :], load_rows - 1)
     both = jnp.concatenate([tokens, cotangent], axis=1)
-    send_both = both[send_ids]
+    both_pad = jnp.concatenate([both, jnp.zeros((MAXLEN, 2 * col_width), bf16)], axis=0)
+    send_both = jnp.stack(
+        [lax.dynamic_slice_in_dim(both_pad, send_start[p], MAXLEN, 0) for p in range(dp_count)]
+    )
     recv_both = lax.all_to_all(send_both, "dp", split_axis=0, concat_axis=0, tiled=True)
 
     recv_len = jnp.sum(jnp.where(owners == dp_index, lengths, 0), axis=1)
@@ -55,10 +56,10 @@
     compact_slot = (
         jnp.sum((compact_ids[:, None] >= recv_start[None, :]).astype(jnp.int32), axis=1) - 1
     )
-    slot_pick = compact_slot[:, None] == peer_ids[None, :]
-    compact_start = jnp.sum(jnp.where(slot_pick, recv_start[None, :], 0), axis=1)
-    gather_ids = compact_slot * MAXLEN + compact_ids - compact_start
-    own_both = recv_both.reshape(dp_count * MAXLEN, 2 * col_width)[gather_ids]
+    own_buf = jnp.zeros((owned_rows + MAXLEN, 2 * col_width), bf16)
+    for j in range(dp_count):
+        own_buf = lax.dynamic_update_slice_in_dim(own_buf, recv_both[j], recv_start[j], 0)
+    own_both = own_buf[:owned_rows]
     own_tokens = own_both[:, :col_width]
     own_cotan = own_both[:, col_width:]
 
@@ -77,9 +78,6 @@
     )
     head_out = lax.dynamic_slice_in_dim(out_weight, head_start, head_dim, 0).reshape(
         head_dim, tensor_count, col_width
-    )
-    own_out = lax.dynamic_slice_in_dim(out_weight, own_start, col_width, 0).reshape(
-        col_width, tensor_count, col_width
     )
     head_gain = lax.dynamic_slice_in_dim(norm_gain, head_start, head_dim, 0)
 
@@ -101,6 +99,9 @@
     normed = attended * inv_rms * head_gain
     gated = (normed * gating).astype(bf16)
     own_gated = lax.dynamic_slice_in_dim(gated, inner_start, col_width, 1)
+    own_out = lax.dynamic_slice_in_dim(out_weight, own_start, col_width, 0).reshape(
+        col_width, tensor_count, col_width
+    )
     out_part = jnp.einsum("rc,ctk->trk", own_gated, own_out, preferred_element_type=f32)
     out_sum = lax.psum_scatter(
         out_part.astype(bf16), "tensor", scatter_dimension=0, tiled=True
@@ -127,10 +128,11 @@
         owned_rows, 4 * col_width
     )
     grad_part = jnp.einsum("rn,tkn->trk", own_grad, own_proj, preferred_element_type=f32)
-    grad_sum = lax.psum_scatter(
-        grad_part.astype(bf16), "tensor", scatter_dimension=0, tiled=True
-    ).reshape(owned_rows, col_width)
-    token_rows = (own_cotan.astype(f32) + grad_sum.astype(f32)).astype(bf16)
+    grad_pieces = lax.all_to_all(
+        grad_part.astype(bf16), "tensor", split_axis=0, concat_axis=0, tiled=True
+    )
+    grad_sum = jnp.sum(grad_pieces.astype(f32), axis=0)
+    token_rows = (own_cotan.astype(f32) + grad_sum).astype(bf16)
 
     proj_term = jnp.einsum("trc,rn->tcn", g_tok, own_grad, preferred_element_type=f32)
     out_term = jnp.einsum("trc,rd->tcd", g_cot, own_gated, preferred_element_type=f32)
@@ -141,18 +143,18 @@
     proj_grad = term_sum[:, : 4 * col_width].reshape(-1, 4, col_width)
     out_grad = term_sum[:, 4 * col_width :].T
 
-    back_src = jnp.minimum(recv_start[:, None] + places[None, :], owned_rows - 1)
-    back_send = token_rows[back_src]
+    rows_pad = jnp.concatenate([token_rows, jnp.zeros((MAXLEN, col_width), bf16)], axis=0)
+    back_send = jnp.stack(
+        [lax.dynamic_slice_in_dim(rows_pad, recv_start[j], MAXLEN, 0) for j in range(dp_count)]
+    )
     back_grads = lax.all_to_all(back_send, "dp", split_axis=0, concat_axis=0, tiled=True)
-    back_grads = back_grads.reshape(dp_count * MAXLEN, col_width)
+    grad_buf = jnp.zeros((load_rows + MAXLEN, col_width), bf16)
+    for i in range(lengths.shape[1]):
+        slab = lax.dynamic_index_in_dim(back_grads, my_owners[i], 0, keepdims=False)
+        grad_buf = lax.dynamic_update_slice_in_dim(grad_buf, slab, my_starts[i], 0)
     load_ids = jnp.arange(load_rows, dtype=jnp.int32)
-    seq_of = jnp.sum((load_ids[:, None] >= my_starts[None, :]).astype(jnp.int32), axis=1) - 1
-    seq_pick = seq_of[:, None] == seq_ids[None, :]
-    owner_of = jnp.sum(jnp.where(seq_pick, my_owners[None, :], 0), axis=1)
-    start_of = jnp.sum(jnp.where(seq_pick, my_starts[None, :], 0), axis=1)
-    back_ids = owner_of * MAXLEN + jnp.minimum(load_ids - start_of, MAXLEN - 1)
     row_used = load_ids < jnp.sum(my_lengths)
-    token_grad = jnp.where(row_used[:, None], back_grads[back_ids], zero_bf)
+    token_grad = jnp.where(row_used[:, None], grad_buf[:load_rows], zero_bf)
     return (mixed_out, token_grad, proj_grad, out_grad)
 
 

time: 169 us -> 156 us (0.923)
  waiting for transfers between devices: 102 us -> 49.5 us
  between operations: 14.1 us -> 44.7 us
  matrix products: 11.1 us -> 15.3 us
  starting transfers between devices: 8.96 us -> 12.5 us
  other arithmetic: 9.11 us -> 10.9 us
    reduce_scatter x1, waiting for transfers between devices: 32.4 us -> 0.02 us  [local(): lax.psum_scatter(out_part.astype(bf16), 'tensor', scatter_dimension=0, ti...]
    reduce_scatter x1 -> x0, waiting for transfers between devices: 24.5 us -> none  [local(): lax.psum_scatter(grad_part.astype(bf16), 'tensor', scatter_dimension=0, t...]
    all_to_all x0 -> x1, waiting for transfers between devices: none -> 23.9 us  [local(): lax.all_to_all(grad_part.astype(bf16), 'tensor', split_axis=0, concat_axi...]
    gather x4 -> x0, local copies, waits for them, and re-layouts: 10.4 us -> none  [the longest x1 3.28 us: local(): send_both = both[send_ids]]
    reduce_scatter x1, waiting for transfers between devices: 13 us -> 4.42 us  [local(): lax.psum_scatter(terms, 'dp', scatter_dimension=0, tiled=True).astype(f32)]
    all_to_all x1, waiting for transfers between devices: 6.21 us -> 0.01 us  [local(): lax.all_to_all(send_both, 'dp', split_axis=0, concat_axis=0, tiled=True)]
    all_to_all x1, waiting for transfers between devices: 6.19 us -> 0.01 us  [local(): lax.all_to_all(back_send, 'dp', split_axis=0, concat_axis=0, tiled=True)]
    dynamic_update_slice x0 -> x8, local copies, waits for them, and re-layouts: none -> 4.72 us  [the longest x4 3.51 us: local(): lax.dynamic_update_slice_in_dim(own_buf, recv_both[j], recv_start[j], 0)]
  transfers between devices with their start and end apart: 6 -> 6, of which waited for: 6 -> 3; matrix products, arithmetic and copies ran while one was open for 13% -> 17% of each run, Pallas kernels for 0% -> 0%
where the time goes in v3:
time: 156 us; the launch traced here: 155 us
  waiting for transfers between devices  49.5 us (32%)
  between operations  44.7 us (29%)
  local copies, waits for them, and re-layouts  22.3 us (14%)
  matrix products  15.3 us (10%)
  starting transfers between devices  12.5 us (8%)
  other arithmetic  10.9 us (7%)
    all_to_all x1, waiting for transfers between devices, local(): lax.all_to_all(grad_part.astype(bf16), 'tensor', split_axis=0, concat_axi...  23.9 us
    all_gather x1, waiting for transfers between devices, local(): gathered = lax.all_gather(own_both, 'tensor', axis=0, tiled=False)  21.1 us
    all_to_all x1, starting transfers between devices, local(): lax.all_to_all(send_both, 'dp', split_axis=0, concat_axis=0, tiled=True)  5.16 us
    reduce_scatter x1, waiting for transfers between devices, local(): lax.psum_scatter(terms, 'dp', scatter_dimension=0, tiled=True).astype(f32)  4.42 us
    all_to_all x1, starting transfers between devices, local(): lax.all_to_all(back_send, 'dp', split_axis=0, concat_axis=0, tiled=True)  3.67 us
    all_to_all x1, starting transfers between devices, local(): lax.all_to_all(grad_part.astype(bf16), 'tensor', split_axis=0, concat_axi...  3.55 us
    dynamic_update_slice x4, local copies, waits for them, and re-layouts, local(): lax.dynamic_update_slice_in_dim(own_buf, recv_both[j], recv_start[j], 0)  3.51 us
  transfers between devices with their start and end apart: 6, of which 3 were waited for; matrix products, arithmetic and copies ran while one was open for 17% of the time, Pallas kernels for 0%

profile of v3, /device:TPU:0, one launch (start us, length us, event | category | flops | bytes accessed | tf_op | source)
XLA Modules:
  0.0 155.1 jit_solution(7791116095609686713)
XLA Ops:
  7.2 1.3 fusion.29
  9.9 0.8 select_reduce_fusion
  19.1 1.0 fusion.16
  21.0 5.2 %all-to-all-start = ((bf16[4,192,256]{2,1,0:T(8,128)(2,1)}), bf16[4,192,256]{2,1,0:T(8,128)(2,1)S(1)}, u32[]{:S(2)}, u32[]{:S(2)}) async-start(bf16[4,192,256]{2,1,0:T(8,128)(2,1)} %pad_maximum_fusion.1), calls=%async_computation | async-start | bytes 786432 | tf_op jit(solution)/shard_map/all_to_all | solution.py:51
  34.6 0.9 dynamic_update_slice.24
  35.5 0.9 dynamic_update_slice.25
  36.4 0.9 dynamic_update_slice.26
  37.3 0.8 dynamic_update_slice.27
  38.9 2.4 %constant_dynamic-slice_fusion.1 = (bf16[1024,4,128]{2,1,0:T(4,128)(2,1)S(1)}, bf16[1024,4,128]{2,1,0:T(4,128)(2,1)S(1)}) fusion(bf16[1024,4,1024]{2,1,0:T(4,128)(2,1)} %param.11, s32[]{:T(128)S(6)} %select_n.103, s32[]{:T(128)S(6)} %select_n.105), kind=kLoop, calls=%fused_computation.85 | loop fusion | bytes 4194312 | tf_op jit(solution)/shard_map/dynamic_slice | solution.py:76
  41.7 1.5 copy.36
  43.2 1.1 constant_dynamic-slice_fusion
  45.9 21.1 %all-gather.3.cloned.1.call-done = bf16[3456,256]{1,0:T(8,128)(2,1)} async-done(((bf16[432,256]{1,0:T(8,128)(2,1)}), bf16[3456,256]{1,0:T(8,128)(2,1)}) %all-gather.3.cloned.1.call-update) | async-done | bytes 1769488 | tf_op jit(solution)/shard_map/all_gather | solution.py:66
  67.0 2.4 %multiply_convert_fusion = (bf16[432,4,128]{2,0,1:T(8,128)(2,1)S(1)}, f32[432,4,128]{2,0,1:T(8,128)S(1)}) fusion(bf16[4,128,128,8]{2,3,1,0:T(8,128)(2,1)} %bitcast.157, bf16[8,432,256]{2,1,0:T(8,128)(2,1)} %bitcast.162), kind=kOutput, calls=%fused_computation.29 | convolution fusion | flops 454090752 | bytes 3260416 | tf_op jit(solution)/shard_map/trc,tcn->rn/dot_general | solution.py:84
  69.9 1.3 select_convert_fusion
  71.7 0.9 subtract_convert_fusion
  72.6 1.2 convolution_convert_fusion.3
  73.8 1.1 copy.37
  74.9 1.3 fusion
  76.2 1.2 convolution_bitcast_fusion.3
  77.5 1.7 %fusion.4 = bf16[432,432]{1,0:T(8,128)(2,1)S(1)} fusion(bf16[432,128]{1,0:T(8,128)(2,1)} %get-tuple-element.24, f32[432,432]{1,0:T(8,128)} %get-tuple-element.66, s32[432]{0:T(512)S(1)} %copy-done.6, bf16[432,4,128]{2,0,1:T(8,128)(2,1)} %copy-done.3), kind=kOutput, calls=%fused_computation.12 | convolution fusion | flops 50388480 | bytes 1483264 | tf_op jit(solution)/shard_map/md,nd->mn/dot_general | solution.py:118
  80.4 0.9 reshape.128
  81.3 2.7 %fusion.3 = bf16[8,432,128]{2,1,0:T(8,128)(2,1)} fusion(bf16[8,128,512]{2,1,0:T(8,128)(2,1)S(1)} %reshape.115, bf16[432,512,1]{1,0,2:T(8,128)(2,1)} %reshape.128), kind=kOutput, calls=%fused_computation.10 | convolution fusion | flops 453427200 | bytes 2375680 | tf_op jit(solution)/shard_map/rn,tkn->trk/dot_general | solution.py:130
  84.0 3.5 %all-to-all-start.1 = ((bf16[8,432,128]{2,1,0:T(8,128)(2,1)}), bf16[8,432,128]{2,1,0:T(8,128)(2,1)S(1)}, u32[]{:S(2)}, u32[]{:S(2)}) async-start(bf16[8,432,128]{2,1,0:T(8,128)(2,1)} %fusion.3), calls=%async_computation.2 | async-start | bytes 1769472 | tf_op jit(solution)/shard_map/all_to_all | solution.py:131
  87.6 2.0 %convolution_convert_fusion = bf16[1024,512]{0,1:T(8,128)(2,1)S(1)} fusion(bf16[8,432,256]{2,1,0:T(8,128)(2,1)} %bitcast.163, f32[432,4,128]{2,0,1:T(8,128)S(1)} %copy-done.2, f32[432,1,128]{2,0,1:T(8,128)S(1)} %convolution_bitcast_fusion.1, f32[432,1,128]{2,0,1:T(8,128)S(1)} %convolution_bitcast_fusion.2, f32[432,1,128]{2,0,1:T(8,128)S(1)} %convolution_bitcast_fusion.3, ...), kind=kOutput, calls=%fused_computation.1 | convolution fusion | flops 456163328 | bytes 3702784 | tf_op jit(solution)/shard_map/trc,rn->tcn/dot_general | solution.py:137
  89.6 1.2 pad_maximum_fusion
  92.2 23.9 %all-to-all-done.1 = bf16[8,432,128]{2,1,0:T(8,128)(2,1)S(1)} async-done(((bf16[8,432,128]{2,1,0:T(8,128)(2,1)}), bf16[8,432,128]{2,1,0:T(8,128)(2,1)S(1)}, u32[]{:S(2)}, u32[]{:S(2)}) %all-to-all-start.1) | async-done | bytes 884768 | tf_op jit(solution)/shard_map/all_to_all | solution.py:131
  116.2 1.6 %add_convert_fusion = (bf16[432,128]{1,0:T(8,128)(2,1)S(1)}, bf16[432,128]{1,0:T(8,128)(2,1)}) fusion(f32[432,128]{1,0:T(8,128)S(1)} %convert_reduce_fusion, bf16[624,256]{1,0:T(8,128)(2,1)S(1)} %dynamic_update_slice.27, bf16[1,432,128]{2,1,0:T(8,128)(2,1)} %reduce-scatter.3.cloned.1.call-done), kind=kLoop, calls=%fused_computation.47 | loop fusion | flops 387072 | bytes 774144 | tf_op jit(solution)/shard_map/convert_element_type | solution.py:135
  118.9 3.7 %all-to-all-start.2 = ((bf16[4,192,128]{2,1,0:T(8,128)(2,1)}), bf16[4,192,128]{2,1,0:T(8,128)(2,1)S(1)}, u32[]{:S(2)}, u32[]{:S(2)}) async-start(bf16[4,192,128]{2,1,0:T(8,128)(2,1)} %pad_maximum_fusion.2), calls=%async_computation.3 | async-start | bytes 393216 | tf_op jit(solution)/shard_map/all_to_all | solution.py:150
  140.6 0.8 slice_select_fusion
  141.4 4.4 %reduce-scatter.5.cloned.1.call-done = bf16[256,640]{0,1:T(8,128)(2,1)} async-done(((bf16[1024,640]{0,1:T(8,128)(2,1)}), bf16[256,640]{0,1:T(8,128)(2,1)}) %reduce-scatter.5.cloned.1.call-update) | async-done | bytes 327696 | tf_op jit(solution)/shard_map/reduce_scatter | solution.py:142
  145.8 1.1 slice.152
  146.9 1.0 copy.32
  (76 shorter events, 14.5 us)
Async XLA Ops:
  8.5 12.5 %copy-start.7 = (s32[1,4]{1,0:T(1,128)}, s32[1,4]{1,0:T(1,128)S(1)}, u32[]{:S(2)}) copy-start(s32[1,4]{1,0:T(1,128)S(1)} %get-tuple-element.19) | copy-start | bytes 52
  8.7 0.5 copy-start.10
  21.0 13.4 %all-to-all-start = ((bf16[4,192,256]{2,1,0:T(8,128)(2,1)}), bf16[4,192,256]{2,1,0:T(8,128)(2,1)S(1)}, u32[]{:S(2)}, u32[]{:S(2)}) async-start(bf16[4,192,256]{2,1,0:T(8,128)(2,1)} %pad_maximum_fusion.1), calls=%async_computation | async-start | bytes 786432 | tf_op jit(solution)/shard_map/all_to_all | solution.py:51
  26.2 40.8 %all-gather.3.cloned.1.call-start = ((), (), s32[]{:S(2)}) async-start(), calls=%async_computation.7 | async-start | bytes 1990656 | tf_op jit(solution)/shard_map/all_gather | solution.py:66
  38.8 77.4 %reduce-scatter.3.cloned.1.call-start = ((), (), s32[]{:S(2)}) async-start(), calls=%async_computation.5 | async-start | bytes 995328 | tf_op jit(solution)/shard_map/reduce_scatter | solution.py:106
  45.9 24.0 %copy-start.5 = (s32[432]{0:T(512)}, s32[432]{0:T(512)S(1)}, u32[]{:S(2)}) copy-start(s32[432]{0:T(512)S(1)} %broadcast_add_fusion) | copy-start | bytes 5188
  67.0 2.4 %copy-start.9 = (bf16[3456,256]{1,0:T(8,128)(2,1)S(1)}, bf16[3456,256]{1,0:T(8,128)(2,1)}, u32[]{:S(2)}) copy-start(bf16[3456,256]{1,0:T(8,128)(2,1)} %all-gather.3.cloned.1.call-done) | copy-start | bytes 5308420
  69.5 2.2 %copy-start.3 = (bf16[432,4,128]{2,0,1:T(8,128)(2,1)}, bf16[432,4,128]{2,0,1:T(8,128)(2,1)S(1)}, u32[]{:S(2)}) copy-start(bf16[432,4,128]{2,0,1:T(8,128)(2,1)S(1)} %get-tuple-element.63) | copy-start | bytes 1327108
  69.5 10.4 %copy-start.1 = (f32[432,4,128]{2,0,1:T(8,128)}, f32[432,4,128]{2,0,1:T(8,128)S(1)}, u32[]{:S(2)}) copy-start(f32[432,4,128]{2,0,1:T(8,128)S(1)} %get-tuple-element.64) | copy-start | bytes 2654212
  73.8 3.7 %copy-start.6 = (s32[432]{0:T(512)S(1)}, s32[432]{0:T(512)}, u32[]{:S(2)}) copy-start(s32[432]{0:T(512)} %copy-done.5) | copy-start | bytes 5188
  77.5 1.7 %copy-start.4 = (bf16[432,4,128]{2,0,1:T(8,128)(2,1)S(1)}, bf16[432,4,128]{2,0,1:T(8,128)(2,1)}, u32[]{:S(2)}) copy-start(bf16[432,4,128]{2,0,1:T(8,128)(2,1)} %copy-done.3) | copy-start | bytes 1327108
  81.3 6.3 %copy-start.2 = (f32[432,4,128]{2,0,1:T(8,128)S(1)}, f32[432,4,128]{2,0,1:T(8,128)}, u32[]{:S(2)}) copy-start(f32[432,4,128]{2,0,1:T(8,128)} %copy-done.1) | copy-start | bytes 2654212
  84.0 32.1 %all-to-all-start.1 = ((bf16[8,432,128]{2,1,0:T(8,128)(2,1)}), bf16[8,432,128]{2,1,0:T(8,128)(2,1)S(1)}, u32[]{:S(2)}, u32[]{:S(2)}) async-start(bf16[8,432,128]{2,1,0:T(8,128)(2,1)} %fusion.3), calls=%async_computation.2 | async-start | bytes 1769472 | tf_op jit(solution)/shard_map/all_to_all | solution.py:131
  87.5 58.3 %reduce-scatter.5.cloned.1.call-start = ((), (), s32[]{:S(2)}) async-start(), calls=%async_computation.6 | async-start | bytes 1638400 | tf_op jit(solution)/shard_map/reduce_scatter | solution.py:142
  89.6 2.6 %copy-start.8 = (s32[1,4]{1,0:T(1,128)S(1)}, s32[1,4]{1,0:T(1,128)}, u32[]{:S(2)}) copy-start(s32[1,4]{1,0:T(1,128)} %copy-done.7) | copy-start | bytes 52
  89.6 2.6 %copy-start.11 = (s32[4,1]{0,1:T(1,128)S(1)}, s32[4,1]{0,1:T(1,128)}, u32[]{:S(2)}) copy-start(s32[4,1]{0,1:T(1,128)} %copy-done.10) | copy-start | bytes 52
  118.9 20.4 %all-to-all-start.2 = ((bf16[4,192,128]{2,1,0:T(8,128)(2,1)}), bf16[4,192,128]{2,1,0:T(8,128)(2,1)S(1)}, u32[]{:S(2)}, u32[]{:S(2)}) async-start(bf16[4,192,128]{2,1,0:T(8,128)(2,1)} %pad_maximum_fusion.2), calls=%async_computation.3 | async-start | bytes 393216 | tf_op jit(solution)/shard_map/all_to_all | solution.py:150
  145.8 2.1 %copy-start = (bf16[256,640]{0,1:T(8,128)(2,1)S(1)}, bf16[256,640]{0,1:T(8,128)(2,1)}, u32[]{:S(2)}) copy-start(bf16[256,640]{0,1:T(8,128)(2,1)} %reduce-scatter.5.cloned.1.call-done) | copy-start | bytes 983044
Sparse Core Ops, SparseCore 0:
  38.9 28.0 all-gather.2
  76.4 34.5 reduce-scatter.2
  114.1 31.6 reduce-scatter.4

commit v4 on v2

--- a/solution.py
+++ b/solution.py
@@ -62,9 +62,27 @@
     own_tokens = own_both[:, :col_width]
     own_cotan = own_both[:, col_width:]
 
-    gathered = lax.all_gather(own_both, "tensor", axis=0, tiled=False)
-    g_tok = gathered[..., :col_width]
-    g_cot = gathered[..., col_width:]
+    half_count = tensor_count // 2
+    core = tensor_index % 2
+    same_core = [[2 * z + c for z in range(half_count)] for c in range(2)]
+    sibling = [(t, t ^ 1) for t in range(tensor_count)]
+    mine = lax.all_gather(own_both, "tensor", axis=0, tiled=False, axis_index_groups=same_core)
+    other = lax.ppermute(mine, "tensor", sibling)
+    mine_tok, mine_cot = mine[..., :col_width], mine[..., col_width:]
+    other_tok, other_cot = other[..., :col_width], other[..., col_width:]
+
+    def by_core(weight, axis):
+        split = weight.reshape(weight.shape[:axis] + (half_count, 2) + weight.shape[axis + 1 :])
+        return (
+            lax.dynamic_index_in_dim(split, core, axis + 1, keepdims=False),
+            lax.dynamic_index_in_dim(split, 1 - core, axis + 1, keepdims=False),
+        )
+
+    def reduce_blocks(part):
+        keep, send = by_core(part, 0)
+        pair_sum = (keep.astype(f32) + lax.ppermute(send, "tensor", sibling).astype(f32)).astype(bf16)
+        pieces = lax.all_to_all(pair_sum, "tensor", 0, 0, tiled=True, axis_index_groups=same_core)
+        return jnp.sum(pieces.astype(f32), axis=0)
 
     head_start = tensor_index * H // tensor_count * head_dim
     own_start = tensor_index * col_width
@@ -80,8 +98,14 @@
     )
     head_gain = lax.dynamic_slice_in_dim(norm_gain, head_start, head_dim, 0)
 
-    projected = jnp.einsum("trc,tcn->rn", g_tok, head_proj, preferred_element_type=f32)
-    down_grad = jnp.einsum("trc,dtc->rd", g_cot, head_out, preferred_element_type=f32)
+    proj_mine, proj_other = by_core(head_proj, 0)
+    projected = jnp.einsum(
+        "trc,tcn->rn", mine_tok, proj_mine, preferred_element_type=f32
+    ) + jnp.einsum("trc,tcn->rn", other_tok, proj_other, preferred_element_type=f32)
+    out_mine, out_other = by_core(head_out, 1)
+    down_grad = jnp.einsum(
+        "trc,dtc->rd", mine_cot, out_mine, preferred_element_type=f32
+    ) + jnp.einsum("trc,dtc->rd", other_cot, out_other, preferred_element_type=f32)
     proj4 = projected.reshape(owned_rows, 4, head_dim)
     activated = jax.nn.silu(proj4).astype(bf16)
     gating = activated[:, 0]
@@ -98,11 +122,11 @@
     normed = attended * inv_rms * head_gain
     gated = (normed * gating).astype(bf16)
     own_gated = lax.dynamic_slice_in_dim(gated, inner_start, col_width, 1)
-    g_gated = lax.all_gather(own_gated, "tensor", axis=0, tiled=False)
-    out_cols = lax.dynamic_slice_in_dim(out_weight, own_start, col_width, 1).reshape(
-        tensor_count, col_width, col_width
+    own_out = lax.dynamic_slice_in_dim(out_weight, own_start, col_width, 0).reshape(
+        col_width, tensor_count, col_width
     )
-    out_sum = jnp.einsum("trc,tck->rk", g_gated, out_cols, preferred_element_type=f32)
+    out_part = jnp.einsum("rc,ctk->trk", own_gated, own_out, preferred_element_type=f32)
+    out_sum = reduce_blocks(out_part.astype(bf16))
     mixed_out = (own_tokens.astype(f32) + out_sum).astype(bf16)
 
     d_normed = down_grad * gating
@@ -125,21 +149,24 @@
         owned_rows, 4 * col_width
     )
     grad_part = jnp.einsum("rn,tkn->trk", own_grad, own_proj, preferred_element_type=f32)
-    grad_pieces = lax.all_to_all(
-        grad_part.astype(bf16), "tensor", split_axis=0, concat_axis=0, tiled=True
-    )
-    grad_sum = jnp.sum(grad_pieces.astype(f32), axis=0)
+    grad_sum = reduce_blocks(grad_part.astype(bf16))
     token_rows = (own_cotan.astype(f32) + grad_sum).astype(bf16)
 
-    proj_term = jnp.einsum("trc,rn->tcn", g_tok, own_grad, preferred_element_type=f32)
-    out_term = jnp.einsum("trc,rd->tcd", g_cot, own_gated, preferred_element_type=f32)
-    terms = jnp.concatenate(
-        [proj_term.reshape(D, 4 * col_width), out_term.reshape(D, col_width)], axis=1
-    ).astype(bf16)
-    term_pieces = lax.all_to_all(
-        terms.reshape(dp_count, D // dp_count, 5 * col_width), "dp", 0, 0, tiled=True
+    def by_rows(term_mine, term_other):
+        pair = jnp.stack([term_mine, term_other], axis=1)
+        pair = jnp.where(core == 0, pair, pair[:, ::-1])
+        return pair.reshape((D,) + term_mine.shape[2:])
+
+    proj_term = by_rows(
+        jnp.einsum("trc,rn->tcn", mine_tok, own_grad, preferred_element_type=f32),
+        jnp.einsum("trc,rn->tcn", other_tok, own_grad, preferred_element_type=f32),
     )
-    term_sum = jnp.sum(term_pieces.astype(f32), axis=0)
+    out_term = by_rows(
+        jnp.einsum("trc,rd->tcd", mine_cot, own_gated, preferred_element_type=f32),
+        jnp.einsum("trc,rd->tcd", other_cot, own_gated, preferred_element_type=f32),
+    )
+    terms = jnp.concatenate([proj_term, out_term], axis=1).astype(bf16)
+    term_sum = lax.psum_scatter(terms, "dp", scatter_dimension=0, tiled=True).astype(f32)
     proj_grad = term_sum[:, : 4 * col_width].reshape(-1, 4, col_width)
     out_grad = term_sum[:, 4 * col_width :].T
 

time: 156 us -> 136 us (0.87)
  blocking collectives: 31.7 us -> 21 us
  waiting for transfers between devices: 40.6 us -> 35.6 us
  local copies, waits for them, and re-layouts: 30.8 us -> 26.4 us
  other arithmetic: 9.08 us -> 10.7 us
    all_gather x1 -> x0, waiting for transfers between devices: 18.8 us -> none  [local(): gathered = lax.all_gather(own_both, 'tensor', axis=0, tiled=False)]
    all_to_all x2, waiting for transfers between devices: 11.6 us -> 24.7 us  [reduce_blocks(): lax.all_to_all(pair_sum, 'tensor', 0, 0, tiled=True, axis_index_groups=sa...]
    all_gather x1, blocking collectives: 31.7 us -> 21 us  [local(): lax.all_gather(own_both, 'tensor', axis=0, tiled=False, axis_index_groups...]
    reshape x3 -> x0, local copies, waits for them, and re-layouts: 3.87 us -> none  [the longest x2 2.94 us: local(): lax.dynamic_slice_in_dim(proj_weight, head_start, head_dim, 2)]
    dot_general x3 -> x0, local copies, waits for them, and re-layouts: 3.41 us -> none  [local(): jnp.einsum('trc,rn->tcn', g_tok, own_grad, preferred_element_type=f32)]
    dot_general x1, matrix products: 2.94 us -> 0.65 us  [local(): jnp.einsum('rn,tkn->trk', own_grad, own_proj, preferred_element_type=f32)]
    convert_element_type x0 -> x4, other arithmetic: none -> 2.06 us  [the longest x2 1.77 us: reduce_blocks(): (keep.astype(f32) + lax.ppermute(send, 'tensor', sibling).astype(f32)).as...]
    dynamic_slice x1, local copies, waits for them, and re-layouts: 0.03 us -> 1.82 us  [local(): lax.dynamic_slice_in_dim(out_weight, head_start, head_dim, 0)]
  transfers between devices with their start and end apart: 5 -> 8, of which waited for: 4 -> 4; matrix products, arithmetic and copies ran while one was open for 13% -> 17% of each run, Pallas kernels for 0% -> 0%
where the time goes in v4:
time: 136 us; the launch traced here: 135 us
  waiting for transfers between devices  35.6 us (26%)
  local copies, waits for them, and re-layouts  26.4 us (19%)
  blocking collectives  21 us (15%)
  starting transfers between devices  16.2 us (12%)
  between operations  14.4 us (11%)
  matrix products  11.1 us (8%)
  other arithmetic  10.7 us (8%)
    all_to_all x2, waiting for transfers between devices, reduce_blocks(): lax.all_to_all(pair_sum, 'tensor', 0, 0, tiled=True, axis_index_groups=sa...  24.7 us
    all_gather x1, blocking collectives, local(): lax.all_gather(own_both, 'tensor', axis=0, tiled=False, axis_index_groups...  21 us
    all_to_all x2, starting transfers between devices, reduce_blocks(): lax.all_to_all(pair_sum, 'tensor', 0, 0, tiled=True, axis_index_groups=sa...  6.93 us
    all_to_all x1, waiting for transfers between devices, local(): lax.all_to_all(send_both, 'dp', split_axis=0, concat_axis=0, tiled=True)  6.4 us
    unnamed x16, local copies, waits for them, and re-layouts  5.2 us
    all_to_all x1, starting transfers between devices, local(): lax.all_to_all(send_both, 'dp', split_axis=0, concat_axis=0, tiled=True)  5.16 us
    all_to_all x1, waiting for transfers between devices, local(): lax.all_to_all(back_send, 'dp', split_axis=0, concat_axis=0, tiled=True)  4.46 us
    all_to_all x1, starting transfers between devices, local(): lax.all_to_all(back_send, 'dp', split_axis=0, concat_axis=0, tiled=True)  3.37 us
  transfers between devices with their start and end apart: 8, of which 4 were waited for; matrix products, arithmetic and copies ran while one was open for 17% of the time, Pallas kernels for 0%

profile of v4, /device:TPU:0, one launch (start us, length us, event | category | flops | bytes accessed | tf_op | source)
XLA Modules:
  0.0 135.3 jit_solution(2191103385196442071)
XLA Ops:
  7.2 1.3 fusion.44
  10.6 1.0 pad_maximum_fusion.3
  11.7 3.3 %gather_fusion = bf16[768,256]{1,0:T(8,128)(2,1)} fusion(bf16[672,256]{1,0:T(8,128)(2,1)S(1)} %pad_maximum_fusion.3, s32[1024]{0:T(1024)S(1)} %pad_clamp_fusion.3), kind=kCustom, calls=%fused_computation | custom fusion | bytes 789504 | tf_op jit(solution)/shard_map/gather | solution.py:49
  15.0 5.2 %all-to-all-start = ((bf16[4,192,256]{2,1,0:T(8,128)(2,1)}), bf16[4,192,256]{2,1,0:T(8,128)(2,1)S(1)}, u32[]{:S(2)}, u32[]{:S(2)}) async-start(bf16[4,192,256]{2,1,0:T(8,128)(2,1)} %bitcast.2), calls=%async_computation | async-start | bytes 786432 | tf_op jit(solution)/shard_map/all_to_all | solution.py:50
  20.3 6.4 %all-to-all-done = bf16[4,192,256]{2,1,0:T(8,128)(2,1)S(1)} async-done(((bf16[4,192,256]{2,1,0:T(8,128)(2,1)}), bf16[4,192,256]{2,1,0:T(8,128)(2,1)S(1)}, u32[]{:S(2)}, u32[]{:S(2)}) %all-to-all-start) | async-done | bytes 393248 | tf_op jit(solution)/shard_map/all_to_all | solution.py:50
  26.7 2.1 %gather_fusion.1 = bf16[432,256]{1,0:T(8,128)(2,1)S(1)} fusion(bf16[768,256]{1,0:T(8,128)(2,1)S(1)} %bitcast.155, s32[1024]{0:T(1024)S(1)} %pad_clamp_fusion.2), kind=kCustom, calls=%fused_computation.1 | custom fusion | bytes 444096 | tf_op jit(solution)/shard_map/gather | solution.py:61
  28.8 21.0 %all-gather = bf16[1728,256]{1,0:T(8,128)(2,1)S(1)} all-gather(bf16[432,256]{1,0:T(8,128)(2,1)S(1)} %gather_fusion.1), channel_id=2, replica_groups={{0,2,4,6},{1,3,5,7},{8,10,12,14},{9,11,13,15},{16,18,20,22},{17,19,21,2..., dimensions={0}, use_global_device_ids=true | all-gather | bytes 1105920 | tf_op jit(solution)/shard_map/all_gather | solution.py:69
  49.8 2.4 %constant_dynamic-slice_fusion.1 = (bf16[1024,4,128]{2,1,0:T(4,128)(2,1)S(1)}, bf16[1024,4,128]{2,1,0:T(4,128)(2,1)S(1)}) fusion(bf16[1024,4,1024]{2,1,0:T(4,128)(2,1)} %param.11, s32[]{:T(128)S(6)} %select_n.133, s32[]{:T(128)S(6)} %select_n.135), kind=kLoop, calls=%fused_computation.112 | loop fusion | bytes 4194312 | tf_op jit(solution)/shard_map/dynamic_slice | solution.py:93
  52.2 1.2 reshape_reshape.6
  53.5 1.8 %constant_dynamic-slice_fusion = (bf16[128,1024]{1,0:T(8,128)(2,1)S(1)}, bf16[128,1024]{1,0:T(8,128)(2,1)}) fusion(bf16[1024,1024]{1,0:T(8,128)(2,1)} %param.13, s32[]{:T(128)S(6)} %select_n.135, s32[]{:T(128)S(6)} %select_n.133), kind=kLoop, calls=%fused_computation.111 | loop fusion | bytes 1048584 | tf_op jit(solution)/shard_map/dynamic_slice | solution.py:96
  55.3 0.9 copy.42
  56.9 1.1 copy.41
  58.1 1.2 reshape.276
  59.3 1.2 convolution_bitcast_fusion.10
  60.9 1.4 %fusion.3 = f32[432,512]{1,0:T(8,128)S(1)} fusion(f32[432,512]{1,0:T(8,128)S(1)} %convolution_bitcast_fusion.3, bf16[4,2,128,512]{3,2,1,0:T(8,128)(2,1)S(1)} %copy-done, s32[]{:T(128)S(6)} %select_n.138, bf16[4,432,256]{2,1,0:T(8,128)(2,1)} %collective-permute-done), kind=kOutput, calls=%fused_computation.18 | convolution fusion | flops 226713600 | bytes 2736132 | tf_op jit(solution)/shard_map/trc,tcn->rn/dot_general | solution.py:104
  63.5 1.3 fusion.5
  67.7 1.5 %convolution_bitcast_fusion = bf16[4,1,128,512]{3,2,0,1:T(8,128)(2,1)S(1)} fusion(bf16[432,512]{1,0:T(8,128)(2,1)S(1)} %fusion.6, bf16[4,432,256]{2,1,0:T(8,128)(2,1)} %collective-permute-done), kind=kOutput, calls=%fused_computation.9 | convolution fusion | flops 226492416 | bytes 1409024 | tf_op jit(solution)/shard_map/trc,rn->tcn/dot_general | solution.py:162
  69.9 1.4 %convolution_bitcast_fusion.4 = bf16[4,1,128,128]{3,2,0,1:T(8,128)(2,1)S(1)} fusion(bf16[432,128,1]{1,0,2:T(8,128)(2,1)S(1)} %get-tuple-element.23, bf16[4,432,256]{2,1,0:T(8,128)(2,1)} %collective-permute-done), kind=kOutput, calls=%fused_computation.20 | convolution fusion | flops 56623104 | bytes 684032 | tf_op jit(solution)/shard_map/trc,rd->tcd/dot_general | solution.py:166
  73.0 1.2 pad_maximum_fusion.1
  74.9 0.9 copy-done.4
  76.9 0.9 fusion.12
  77.8 3.5 %all-to-all-start.1 = ((bf16[4,432,128]{2,1,0:T(8,128)(2,1)}), bf16[4,432,128]{2,1,0:T(8,128)(2,1)S(1)}, u32[]{:S(2)}, u32[]{:S(2)}) async-start(bf16[4,432,128]{2,1,0:T(8,128)(2,1)} %fusion.12), calls=%async_computation.1 | async-start | bytes 884736 | tf_op jit(solution)/shard_map/all_to_all | solution.py:84
  81.5 0.9 fusion.11
  82.4 12.3 %all-to-all-done.1 = bf16[4,432,128]{2,1,0:T(8,128)(2,1)S(1)} async-done(((bf16[4,432,128]{2,1,0:T(8,128)(2,1)}), bf16[4,432,128]{2,1,0:T(8,128)(2,1)S(1)}, u32[]{:S(2)}, u32[]{:S(2)}) %all-to-all-start.1) | async-done | bytes 442400 | tf_op jit(solution)/shard_map/all_to_all | solution.py:84
  94.7 3.5 %all-to-all-start.2 = ((bf16[4,432,128]{2,1,0:T(8,128)(2,1)}), bf16[4,432,128]{2,1,0:T(8,128)(2,1)S(1)}, u32[]{:S(2)}, u32[]{:S(2)}) async-start(bf16[4,432,128]{2,1,0:T(8,128)(2,1)} %fusion.11), calls=%async_computation.2 | async-start | bytes 884736 | tf_op jit(solution)/shard_map/all_to_all | solution.py:84
  98.3 12.4 %all-to-all-done.2 = bf16[4,432,128]{2,1,0:T(8,128)(2,1)S(1)} async-done(((bf16[4,432,128]{2,1,0:T(8,128)(2,1)}), bf16[4,432,128]{2,1,0:T(8,128)(2,1)S(1)}, u32[]{:S(2)}, u32[]{:S(2)}) %all-to-all-start.2) | async-done | bytes 442400 | tf_op jit(solution)/shard_map/all_to_all | solution.py:84
  111.5 2.5 %gather_fusion.2 = bf16[768,128]{1,0:T(8,128)(2,1)} fusion(bf16[432,128]{1,0:T(8,128)(2,1)S(1)} %get-tuple-element.25, s32[1024]{0:T(1024)S(1)} %pad_clamp_fusion.1), kind=kCustom, calls=%fused_computation.2 | custom fusion | bytes 396288 | tf_op jit(solution)/shard_map/gather | solution.py:174
  114.0 3.4 %all-to-all-start.3 = ((bf16[4,192,128]{2,1,0:T(8,128)(2,1)}), bf16[4,192,128]{2,1,0:T(8,128)(2,1)S(1)}, u32[]{:S(2)}, u32[]{:S(2)}) async-start(bf16[4,192,128]{2,1,0:T(8,128)(2,1)} %bitcast.41), calls=%async_computation.3 | async-start | bytes 393216 | tf_op jit(solution)/shard_map/all_to_all | solution.py:175
  118.1 4.5 %all-to-all-done.3 = bf16[4,192,128]{2,1,0:T(8,128)(2,1)S(1)} async-done(((bf16[4,192,128]{2,1,0:T(8,128)(2,1)}), bf16[4,192,128]{2,1,0:T(8,128)(2,1)S(1)}, u32[]{:S(2)}, u32[]{:S(2)}) %all-to-all-start.3) | async-done | bytes 196640 | tf_op jit(solution)/shard_map/all_to_all | solution.py:175
  122.5 2.0 %gather_fusion.3 = bf16[672,128]{1,0:T(8,128)(2,1)S(1)} fusion(bf16[768,128]{1,0:T(8,128)(2,1)S(1)} %bitcast.154, s32[1024]{0:T(1024)S(1)} %pad_clamp_fusion), kind=kCustom, calls=%fused_computation.3 | custom fusion | bytes 346752 | tf_op jit(solution)/shard_map/gather | solution.py:184
  125.4 1.1 slice.66
  126.7 1.0 copy.38
  (77 shorter events, 15.3 us)
Async XLA Ops:
  15.0 11.8 %all-to-all-start = ((bf16[4,192,256]{2,1,0:T(8,128)(2,1)}), bf16[4,192,256]{2,1,0:T(8,128)(2,1)S(1)}, u32[]{:S(2)}, u32[]{:S(2)}) async-start(bf16[4,192,256]{2,1,0:T(8,128)(2,1)} %bitcast.2), calls=%async_computation | async-start | bytes 786432 | tf_op jit(solution)/shard_map/all_to_all | solution.py:50
  20.1 105.2 %reduce-scatter.2.cloned.1.call-start = ((), (), s32[]{:S(2)}) async-start(), calls=%async_computation.5 | async-start | bytes 1638400 | tf_op jit(solution)/shard_map/reduce_scatter | solution.py:169
  49.8 11.1 %collective-permute-start = (bf16[4,432,256]{2,1,0:T(8,128)(2,1)S(1)}, bf16[4,432,256]{2,1,0:T(8,128)(2,1)}, u32[]{:S(2)}, u32[]{:S(2)}) collective-permute-start(bf16[4,432,256]{2,1,0:T(8,128)(2,1)S(1)} %bitcast.156), channel_id=1, source_target_pairs={{0,1},{1,0},{2,3},{3,2},{4,5},{5,4},{6,7},{7,6},{8,9},{9,8},{10,11... | collective-permute-start | bytes 2654216 | tf_op jit(solution)/shard_map/ppermute | solution.py:70
  55.3 5.2 %copy-start = (bf16[4,2,128,512]{3,2,1,0:T(8,128)(2,1)S(1)}, bf16[4,2,128,512]{3,2,1,0:T(8,128)(2,1)}, u32[]{:S(2)}) copy-start(bf16[4,2,128,512]{3,2,1,0:T(8,128)(2,1)} %reshape_reshape.6) | copy-start | bytes 3145732
  62.6 1.0 copy-start.3
  72.6 1.6 %copy-start.2 = (bf16[8,128,512]{2,1,0:T(8,128)(2,1)S(1)}, bf16[8,128,512]{2,1,0:T(8,128)(2,1)}, u32[]{:S(2)}) copy-start(bf16[8,128,512]{2,1,0:T(8,128)(2,1)} %reshape.276) | copy-start | bytes 3145732
  72.6 4.3 %collective-permute-start.1 = (bf16[4,432,128]{2,1,0:T(8,128)(2,1)}, bf16[4,432,128]{2,1,0:T(8,128)(2,1)S(1)}, u32[]{:S(2)}, u32[]{:S(2)}) collective-permute-start(bf16[4,432,128]{2,1,0:T(8,128)(2,1)} %dynamic-slice_bitcast_fusion.1), channel_id=1, source_target_pairs={{0,1},{1,0},{2,3},{3,2},{4,5},{5,4},{6,7},{7,6},{8,9},{9,8},{10,11... | collective-permute-start | bytes 1327112 | tf_op jit(solution)/shard_map/ppermute | solution.py:83
  74.9 1.0 copy-start.4
  76.6 4.8 %copy-start.5 = (bf16[8,128,432]{1,2,0:T(8,128)(2,1)S(1)}, bf16[8,128,432]{1,2,0:T(8,128)(2,1)}, u32[]{:S(2)}) copy-start(bf16[8,128,432]{1,2,0:T(8,128)(2,1)} %copy-done.4) | copy-start | bytes 2654212
  76.6 4.8 %collective-permute-start.2 = (bf16[4,432,128]{2,1,0:T(8,128)(2,1)}, bf16[4,432,128]{2,1,0:T(8,128)(2,1)S(1)}, u32[]{:S(2)}, u32[]{:S(2)}) collective-permute-start(bf16[4,432,128]{2,1,0:T(8,128)(2,1)} %dynamic-slice_bitcast_fusion), channel_id=1, source_target_pairs={{0,1},{1,0},{2,3},{3,2},{4,5},{5,4},{6,7},{7,6},{8,9},{9,8},{10,11... | collective-permute-start | bytes 1327112 | tf_op jit(solution)/shard_map/ppermute | solution.py:83
  77.8 16.9 %all-to-all-start.1 = ((bf16[4,432,128]{2,1,0:T(8,128)(2,1)}), bf16[4,432,128]{2,1,0:T(8,128)(2,1)S(1)}, u32[]{:S(2)}, u32[]{:S(2)}) async-start(bf16[4,432,128]{2,1,0:T(8,128)(2,1)} %fusion.12), calls=%async_computation.1 | async-start | bytes 884736 | tf_op jit(solution)/shard_map/all_to_all | solution.py:84
  94.7 16.0 %all-to-all-start.2 = ((bf16[4,432,128]{2,1,0:T(8,128)(2,1)}), bf16[4,432,128]{2,1,0:T(8,128)(2,1)S(1)}, u32[]{:S(2)}, u32[]{:S(2)}) async-start(bf16[4,432,128]{2,1,0:T(8,128)(2,1)} %fusion.11), calls=%async_computation.2 | async-start | bytes 884736 | tf_op jit(solution)/shard_map/all_to_all | solution.py:84
  114.0 8.5 %all-to-all-start.3 = ((bf16[4,192,128]{2,1,0:T(8,128)(2,1)}), bf16[4,192,128]{2,1,0:T(8,128)(2,1)S(1)}, u32[]{:S(2)}, u32[]{:S(2)}) async-start(bf16[4,192,128]{2,1,0:T(8,128)(2,1)} %bitcast.41), calls=%async_computation.3 | async-start | bytes 393216 | tf_op jit(solution)/shard_map/all_to_all | solution.py:175
  125.4 2.3 %copy-start.1 = (bf16[256,640]{1,0:T(8,128)(2,1)S(1)}, bf16[256,640]{1,0:T(8,128)(2,1)}, u32[]{:S(2)}) copy-start(bf16[256,640]{1,0:T(8,128)(2,1)} %reduce-scatter.2.cloned.1.call-done) | copy-start | bytes 983044
Sparse Core Ops, SparseCore 0:
  74.3 27.3 reduce-scatter.1

commit v5 on v4

--- a/solution.py
+++ b/solution.py
@@ -126,8 +126,6 @@
         col_width, tensor_count, col_width
     )
     out_part = jnp.einsum("rc,ctk->trk", own_gated, own_out, preferred_element_type=f32)
-    out_sum = reduce_blocks(out_part.astype(bf16))
-    mixed_out = (own_tokens.astype(f32) + out_sum).astype(bf16)
 
     d_normed = down_grad * gating
     d_gating = down_grad * normed
@@ -149,7 +147,10 @@
         owned_rows, 4 * col_width
     )
     grad_part = jnp.einsum("rn,tkn->trk", own_grad, own_proj, preferred_element_type=f32)
-    grad_sum = reduce_blocks(grad_part.astype(bf16))
+    both_sum = reduce_blocks(jnp.concatenate([out_part, grad_part], axis=2).astype(bf16))
+    out_sum = both_sum[:, :col_width]
+    grad_sum = both_sum[:, col_width:]
+    mixed_out = (own_tokens.astype(f32) + out_sum).astype(bf16)
     token_rows = (own_cotan.astype(f32) + grad_sum).astype(bf16)
 
     def by_rows(term_mine, term_other):

time: 136 us -> 128 us (0.941)
  local copies, waits for them, and re-layouts: 26.4 us -> 22.6 us
  starting transfers between devices: 16.2 us -> 12.5 us
  waiting for transfers between devices: 35.6 us -> 33.4 us
  other arithmetic: 10.7 us -> 12.3 us
    all_to_all x2 -> x1, starting transfers between devices: 6.93 us -> 3.53 us  [reduce_blocks(): lax.all_to_all(pair_sum, 'tensor', 0, 0, tiled=True, axis_index_groups=sa...]
    all_to_all x2 -> x1, waiting for transfers between devices: 24.7 us -> 22.5 us  [reduce_blocks(): lax.all_to_all(pair_sum, 'tensor', 0, 0, tiled=True, axis_index_groups=sa...]
    squeeze x2 -> x0, local copies, waits for them, and re-layouts: 1.59 us -> none  [by_core(): lax.dynamic_index_in_dim(split, 1 - core, axis + 1, keepdims=False)]
    unnamed x16 -> x12, local copies, waits for them, and re-layouts: 5.2 us -> 3.68 us
  transfers between devices with their start and end apart: 8 -> 6, of which waited for: 4 -> 3; matrix products, arithmetic and copies ran while one was open for 17% -> 19% of each run, Pallas kernels for 0% -> 0%
where the time goes in v5:
time: 128 us; the launch traced here: 127 us
  waiting for transfers between devices  33.4 us (26%)
  local copies, waits for them, and re-layouts  22.6 us (18%)
  blocking collectives  21 us (16%)
  between operations  14.4 us (11%)
  starting transfers between devices  12.5 us (10%)
  other arithmetic  12.3 us (10%)
  matrix products  11.1 us (9%)
    all_to_all x1, waiting for transfers between devices, reduce_blocks(): lax.all_to_all(pair_sum, 'tensor', 0, 0, tiled=True, axis_index_groups=sa...  22.5 us
    all_gather x1, blocking collectives, local(): lax.all_gather(own_both, 'tensor', axis=0, tiled=False, axis_index_groups...  21 us
    all_to_all x1, waiting for transfers between devices, local(): lax.all_to_all(send_both, 'dp', split_axis=0, concat_axis=0, tiled=True)  6.4 us
    all_to_all x1, starting transfers between devices, local(): lax.all_to_all(send_both, 'dp', split_axis=0, concat_axis=0, tiled=True)  5.16 us
    all_to_all x1, waiting for transfers between devices, local(): lax.all_to_all(back_send, 'dp', split_axis=0, concat_axis=0, tiled=True)  4.46 us
    unnamed x12, local copies, waits for them, and re-layouts  3.68 us
    all_to_all x1, starting transfers between devices, reduce_blocks(): lax.all_to_all(pair_sum, 'tensor', 0, 0, tiled=True, axis_index_groups=sa...  3.53 us
    all_to_all x1, starting transfers between devices, local(): lax.all_to_all(back_send, 'dp', split_axis=0, concat_axis=0, tiled=True)  3.37 us
  transfers between devices with their start and end apart: 6, of which 3 were waited for; matrix products, arithmetic and copies ran while one was open for 19% of the time, Pallas kernels for 0%

profile of v5, /device:TPU:0, one launch (start us, length us, event | category | flops | bytes accessed | tf_op | source)
XLA Modules:
  0.0 127.2 jit_solution(14894498969159557934)
XLA Ops:
  7.2 1.3 %fusion.49 = (s32[]{:T(128)}, s32[1,4]{1,0:T(1,128)S(1)}) fusion(s32[4,4]{1,0:T(4,128)} %param.9, s32[]{:T(128)S(6)} %select_n.125), kind=kLoop, calls=%fused_computation.138 | loop fusion | flops 3 | bytes 40 | tf_op jit(solution)/shard_map/reduce_sum | solution.py:184
  9.2 0.8 select_reduce_fusion.3
  10.6 1.0 pad_maximum_fusion.3
  11.7 3.3 %gather_fusion = bf16[768,256]{1,0:T(8,128)(2,1)} fusion(bf16[672,256]{1,0:T(8,128)(2,1)S(1)} %pad_maximum_fusion.3, s32[1024]{0:T(1024)S(1)} %pad_clamp_fusion.3), kind=kCustom, calls=%fused_computation | custom fusion | bytes 789504 | tf_op jit(solution)/shard_map/gather | solution.py:49
  15.0 5.2 %all-to-all-start = ((bf16[4,192,256]{2,1,0:T(8,128)(2,1)}), bf16[4,192,256]{2,1,0:T(8,128)(2,1)S(1)}, u32[]{:S(2)}, u32[]{:S(2)}) async-start(bf16[4,192,256]{2,1,0:T(8,128)(2,1)} %bitcast.2), calls=%async_computation | async-start | bytes 786432 | tf_op jit(solution)/shard_map/all_to_all | solution.py:50
  20.3 6.4 %all-to-all-done = bf16[4,192,256]{2,1,0:T(8,128)(2,1)S(1)} async-done(((bf16[4,192,256]{2,1,0:T(8,128)(2,1)}), bf16[4,192,256]{2,1,0:T(8,128)(2,1)S(1)}, u32[]{:S(2)}, u32[]{:S(2)}) %all-to-all-start) | async-done | bytes 393248 | tf_op jit(solution)/shard_map/all_to_all | solution.py:50
  26.7 2.1 %gather_fusion.1 = bf16[432,256]{1,0:T(8,128)(2,1)S(1)} fusion(bf16[768,256]{1,0:T(8,128)(2,1)S(1)} %bitcast.152, s32[1024]{0:T(1024)S(1)} %pad_clamp_fusion.2), kind=kCustom, calls=%fused_computation.1 | custom fusion | bytes 444096 | tf_op jit(solution)/shard_map/gather | solution.py:61
  28.8 21.0 %all-gather = bf16[1728,256]{1,0:T(8,128)(2,1)S(1)} all-gather(bf16[432,256]{1,0:T(8,128)(2,1)S(1)} %gather_fusion.1), channel_id=2, replica_groups={{0,2,4,6},{1,3,5,7},{8,10,12,14},{9,11,13,15},{16,18,20,22},{17,19,21,2..., dimensions={0}, use_global_device_ids=true | all-gather | bytes 1105920 | tf_op jit(solution)/shard_map/all_gather | solution.py:69
  49.8 2.4 %constant_dynamic-slice_fusion.1 = (bf16[1024,4,128]{2,1,0:T(4,128)(2,1)S(1)}, bf16[1024,4,128]{2,1,0:T(4,128)(2,1)S(1)}) fusion(bf16[1024,4,1024]{2,1,0:T(4,128)(2,1)} %param.11, s32[]{:T(128)S(6)} %select_n.131, s32[]{:T(128)S(6)} %select_n.133), kind=kLoop, calls=%fused_computation.117 | loop fusion | bytes 4194312 | tf_op jit(solution)/shard_map/dynamic_slice | solution.py:93
  52.2 1.2 reshape_reshape.6
  53.5 1.1 constant_dynamic-slice_fusion
  54.6 0.8 copy.42
  55.4 0.8 dynamic_slice.50
  56.3 1.2 reshape.272
  57.7 1.2 convolution_bitcast_fusion.10
  59.3 1.4 %fusion.4 = f32[432,512]{1,0:T(8,128)S(1)} fusion(f32[432,512]{1,0:T(8,128)S(1)} %convolution_bitcast_fusion.3, bf16[4,2,128,512]{3,2,1,0:T(8,128)(2,1)S(1)} %copy-done, s32[]{:T(128)S(6)} %select_n.136, bf16[4,432,256]{2,1,0:T(8,128)(2,1)} %collective-permute-done), kind=kOutput, calls=%fused_computation.25 | convolution fusion | flops 226713600 | bytes 2736132 | tf_op jit(solution)/shard_map/trc,tcn->rn/dot_general | solution.py:104
  61.9 1.3 %fusion.6 = f32[432,128]{1,0:T(8,128)S(1)} fusion(f32[432,128]{1,0:T(8,128)S(1)} %convolution_bitcast_fusion.10, bf16[4,432,256]{2,1,0:T(8,128)(2,1)} %collective-permute-done, bf16[128,4,2,128]{0,3,2,1:T(8,128)(2,1)S(1)} %bitcast.167, s32[]{:T(128)S(6)} %select_n.136), kind=kOutput, calls=%fused_computation.34 | convolution fusion | flops 56678400 | bytes 1015812 | tf_op jit(solution)/shard_map/trc,dtc->rd/dot_general | solution.py:108
  67.5 1.0 fusion.8
  68.9 1.5 %convolution_bitcast_fusion = bf16[4,1,128,512]{3,2,0,1:T(8,128)(2,1)S(1)} fusion(bf16[432,512]{1,0:T(8,128)(2,1)S(1)} %fusion.11, bf16[4,432,256]{2,1,0:T(8,128)(2,1)} %collective-permute-done), kind=kOutput, calls=%fused_computation.16 | convolution fusion | flops 226492416 | bytes 1409024 | tf_op jit(solution)/shard_map/trc,rn->tcn/dot_general | solution.py:163
  71.2 1.4 %convolution_bitcast_fusion.4 = bf16[4,1,128,128]{3,2,0,1:T(8,128)(2,1)S(1)} fusion(bf16[432,128,1]{1,0,2:T(8,128)(2,1)S(1)} %get-tuple-element.23, bf16[4,432,256]{2,1,0:T(8,128)(2,1)} %collective-permute-done), kind=kOutput, calls=%fused_computation.27 | convolution fusion | flops 56623104 | bytes 684032 | tf_op jit(solution)/shard_map/trc,rd->tcd/dot_general | solution.py:167
  72.7 1.2 pad_maximum_fusion.1
  73.9 2.3 %fusion.1 = bf16[4,432,256]{2,1,0:T(8,128)(2,1)} fusion(bf16[4,432,256]{2,1,0:T(8,128)(2,1)} %collective-permute-done.1, s32[]{:T(128)S(6)} %select_n.135, bf16[4,2,432,128]{3,2,1,0:T(8,128)(2,1)S(1)} %bitcast.154, bf16[4,2,432,128]{3,2,1,0:T(8,128)(2,1)S(1)} %bitcast.162), kind=kLoop, calls=%fused_computation.12 | loop fusion | flops 3538944 | bytes 3538948 | tf_op jit(solution)/shard_map/convert_element_type | solution.py:83
  76.2 3.5 %all-to-all-start.1 = ((bf16[4,432,256]{2,1,0:T(8,128)(2,1)}), bf16[4,432,256]{2,1,0:T(8,128)(2,1)S(1)}, u32[]{:S(2)}, u32[]{:S(2)}) async-start(bf16[4,432,256]{2,1,0:T(8,128)(2,1)} %fusion.1), calls=%async_computation.1 | async-start | bytes 1769472 | tf_op jit(solution)/shard_map/all_to_all | solution.py:84
  80.1 22.5 %all-to-all-done.1 = bf16[4,432,256]{2,1,0:T(8,128)(2,1)S(1)} async-done(((bf16[4,432,256]{2,1,0:T(8,128)(2,1)}), bf16[4,432,256]{2,1,0:T(8,128)(2,1)S(1)}, u32[]{:S(2)}, u32[]{:S(2)}) %all-to-all-start.1) | async-done | bytes 884768 | tf_op jit(solution)/shard_map/all_to_all | solution.py:84
  103.4 2.5 %gather_fusion.2 = bf16[768,128]{1,0:T(8,128)(2,1)} fusion(bf16[432,128]{1,0:T(8,128)(2,1)S(1)} %get-tuple-element.24, s32[1024]{0:T(1024)S(1)} %pad_clamp_fusion.1), kind=kCustom, calls=%fused_computation.2 | custom fusion | bytes 396288 | tf_op jit(solution)/shard_map/gather | solution.py:175
  105.9 3.4 %all-to-all-start.2 = ((bf16[4,192,128]{2,1,0:T(8,128)(2,1)}), bf16[4,192,128]{2,1,0:T(8,128)(2,1)S(1)}, u32[]{:S(2)}, u32[]{:S(2)}) async-start(bf16[4,192,128]{2,1,0:T(8,128)(2,1)} %bitcast.37), calls=%async_computation.2 | async-start | bytes 393216 | tf_op jit(solution)/shard_map/all_to_all | solution.py:176
  110.0 4.5 %all-to-all-done.2 = bf16[4,192,128]{2,1,0:T(8,128)(2,1)S(1)} async-done(((bf16[4,192,128]{2,1,0:T(8,128)(2,1)}), bf16[4,192,128]{2,1,0:T(8,128)(2,1)S(1)}, u32[]{:S(2)}, u32[]{:S(2)}) %all-to-all-start.2) | async-done | bytes 196640 | tf_op jit(solution)/shard_map/all_to_all | solution.py:176
  114.5 2.0 %gather_fusion.3 = bf16[672,128]{1,0:T(8,128)(2,1)S(1)} fusion(bf16[768,128]{1,0:T(8,128)(2,1)S(1)} %bitcast.151, s32[1024]{0:T(1024)S(1)} %pad_clamp_fusion), kind=kCustom, calls=%fused_computation.3 | custom fusion | bytes 346752 | tf_op jit(solution)/shard_map/gather | solution.py:185
  116.5 0.8 broadcast_select_fusion
  117.3 1.1 slice.76
  118.6 1.0 copy.38
  119.6 0.8 copy.39
  (66 shorter events, 10.8 us)
Async XLA Ops:
  15.0 11.8 %all-to-all-start = ((bf16[4,192,256]{2,1,0:T(8,128)(2,1)}), bf16[4,192,256]{2,1,0:T(8,128)(2,1)S(1)}, u32[]{:S(2)}, u32[]{:S(2)}) async-start(bf16[4,192,256]{2,1,0:T(8,128)(2,1)} %bitcast.2), calls=%async_computation | async-start | bytes 786432 | tf_op jit(solution)/shard_map/all_to_all | solution.py:50
  20.1 97.2 %reduce-scatter.2.cloned.1.call-start = ((), (), s32[]{:S(2)}) async-start(), calls=%async_computation.4 | async-start | bytes 1638400 | tf_op jit(solution)/shard_map/reduce_scatter | solution.py:170
  49.8 9.4 %collective-permute-start = (bf16[4,432,256]{2,1,0:T(8,128)(2,1)S(1)}, bf16[4,432,256]{2,1,0:T(8,128)(2,1)}, u32[]{:S(2)}, u32[]{:S(2)}) collective-permute-start(bf16[4,432,256]{2,1,0:T(8,128)(2,1)S(1)} %bitcast.155), channel_id=1, source_target_pairs={{0,1},{1,0},{2,3},{3,2},{4,5},{5,4},{6,7},{7,6},{8,9},{9,8},{10,11... | collective-permute-start | bytes 2654216 | tf_op jit(solution)/shard_map/ppermute | solution.py:70
  55.4 3.4 %copy-start = (bf16[4,2,128,512]{3,2,1,0:T(8,128)(2,1)S(1)}, bf16[4,2,128,512]{3,2,1,0:T(8,128)(2,1)}, u32[]{:S(2)}) copy-start(bf16[4,2,128,512]{3,2,1,0:T(8,128)(2,1)} %reshape_reshape.6) | copy-start | bytes 3145732
  60.9 1.0 copy-start.3
  65.2 1.2 copy-start.2
  68.5 5.4 %collective-permute-start.1 = (bf16[4,432,256]{2,1,0:T(8,128)(2,1)}, bf16[4,432,256]{2,1,0:T(8,128)(2,1)}, u32[]{:S(2)}, u32[]{:S(2)}) collective-permute-start(bf16[4,432,256]{2,1,0:T(8,128)(2,1)} %fusion.8), channel_id=1, source_target_pairs={{0,1},{1,0},{2,3},{3,2},{4,5},{5,4},{6,7},{7,6},{8,9},{9,8},{10,11... | collective-permute-start | bytes 2654216 | tf_op jit(solution)/shard_map/ppermute | solution.py:83
  76.2 26.3 %all-to-all-start.1 = ((bf16[4,432,256]{2,1,0:T(8,128)(2,1)}), bf16[4,432,256]{2,1,0:T(8,128)(2,1)S(1)}, u32[]{:S(2)}, u32[]{:S(2)}) async-start(bf16[4,432,256]{2,1,0:T(8,128)(2,1)} %fusion.1), calls=%async_computation.1 | async-start | bytes 1769472 | tf_op jit(solution)/shard_map/all_to_all | solution.py:84
  105.9 8.5 %all-to-all-start.2 = ((bf16[4,192,128]{2,1,0:T(8,128)(2,1)}), bf16[4,192,128]{2,1,0:T(8,128)(2,1)S(1)}, u32[]{:S(2)}, u32[]{:S(2)}) async-start(bf16[4,192,128]{2,1,0:T(8,128)(2,1)} %bitcast.37), calls=%async_computation.2 | async-start | bytes 393216 | tf_op jit(solution)/shard_map/all_to_all | solution.py:176
  117.3 2.3 %copy-start.1 = (bf16[256,640]{1,0:T(8,128)(2,1)S(1)}, bf16[256,640]{1,0:T(8,128)(2,1)}, u32[]{:S(2)}) copy-start(bf16[256,640]{1,0:T(8,128)(2,1)} %reduce-scatter.2.cloned.1.call-done) | copy-start | bytes 983044
Sparse Core Ops, SparseCore 0:
  74.0 27.4 reduce-scatter.1

commit v6 on v5

--- a/solution.py
+++ b/solution.py
@@ -167,7 +167,14 @@
         jnp.einsum("trc,rd->tcd", other_cot, own_gated, preferred_element_type=f32),
     )
     terms = jnp.concatenate([proj_term, out_term], axis=1).astype(bf16)
-    term_sum = lax.psum_scatter(terms, "dp", scatter_dimension=0, tiled=True).astype(f32)
+    bit_count = dp_count.bit_length() - 1
+    term_sum = terms.reshape((2,) * bit_count + (D // dp_count,) + terms.shape[1:]).astype(f32)
+    for level in range(bit_count - 1, -1, -1):
+        my_bit = (dp_index >> level) & 1
+        keep = lax.dynamic_index_in_dim(term_sum, my_bit, 0, keepdims=False)
+        send = lax.dynamic_index_in_dim(term_sum, 1 - my_bit, 0, keepdims=False)
+        partners = [(d, d ^ (1 << level)) for d in range(dp_count)]
+        term_sum = keep + lax.ppermute(send.astype(bf16), "dp", partners).astype(f32)
     proj_grad = term_sum[:, : 4 * col_width].reshape(-1, 4, col_width)
     out_grad = term_sum[:, 4 * col_width :].T
 

time: 128 us -> 109 us (0.85)
  between operations: 14.4 us -> 1.08 us
  waiting for transfers between devices: 33.4 us -> 28.5 us
  starting transfers between devices: 12.5 us -> 15.2 us
  other arithmetic: 12.3 us -> 10.4 us
    all_to_all x1, waiting for transfers between devices: 22.5 us -> 0.08 us  [reduce_blocks(): lax.all_to_all(pair_sum, 'tensor', 0, 0, tiled=True, axis_index_groups=sa...]
    ppermute x0 -> x2, waiting for transfers between devices: none -> 17.7 us  [local(): lax.ppermute(send.astype(bf16), 'dp', partners).astype(f32)]
    ppermute x0 -> x2, starting transfers between devices: none -> 2.68 us  [local(): lax.ppermute(send.astype(bf16), 'dp', partners).astype(f32)]
  transfers between devices with their start and end apart: 6 -> 7, of which waited for: 3 -> 5; matrix products, arithmetic and copies ran while one was open for 19% -> 15% of each run, Pallas kernels for 0% -> 0%
where the time goes in v6:
time: 109 us; the launch traced here: 108 us
  waiting for transfers between devices  28.5 us (26%)
  local copies, waits for them, and re-layouts  21.9 us (20%)
  blocking collectives  21 us (19%)
  starting transfers between devices  15.2 us (14%)
  other arithmetic  10.4 us (10%)
  matrix products  10.2 us (9%)
    all_gather x1, blocking collectives, local(): lax.all_gather(own_both, 'tensor', axis=0, tiled=False, axis_index_groups...  21 us
    ppermute x2, waiting for transfers between devices, local(): lax.ppermute(send.astype(bf16), 'dp', partners).astype(f32)  17.7 us
    all_to_all x1, waiting for transfers between devices, local(): lax.all_to_all(send_both, 'dp', split_axis=0, concat_axis=0, tiled=True)  6.4 us
    all_to_all x1, starting transfers between devices, local(): lax.all_to_all(send_both, 'dp', split_axis=0, concat_axis=0, tiled=True)  5.16 us
    all_to_all x1, waiting for transfers between devices, local(): lax.all_to_all(back_send, 'dp', split_axis=0, concat_axis=0, tiled=True)  4.39 us
    all_to_all x1, starting transfers between devices, reduce_blocks(): lax.all_to_all(pair_sum, 'tensor', 0, 0, tiled=True, axis_index_groups=sa...  3.5 us
    all_to_all x1, starting transfers between devices, local(): lax.all_to_all(back_send, 'dp', split_axis=0, concat_axis=0, tiled=True)  3.36 us
    gather x1, local copies, waits for them, and re-layouts, local(): send_both = both[send_ids]  3.28 us
  transfers between devices with their start and end apart: 7, of which 5 were waited for; matrix products, arithmetic and copies ran while one was open for 15% of the time, Pallas kernels for 0%

profile of v6, /device:TPU:0, one launch (start us, length us, event | category | flops | bytes accessed | tf_op | source)
XLA Modules:
  0.0 108.4 jit_solution(6748734448942149151)
XLA Ops:
  0.6 1.3 %fusion.51 = (s32[]{:T(128)}, s32[1,4]{1,0:T(1,128)S(1)}) fusion(s32[4,4]{1,0:T(4,128)} %param.9, s32[]{:T(128)S(6)} %select_n.139), kind=kLoop, calls=%fused_computation.144 | loop fusion | flops 3 | bytes 40 | tf_op jit(solution)/shard_map/reduce_sum | solution.py:191
  2.6 0.8 select_reduce_fusion.3
  4.1 1.0 pad_maximum_fusion.2
  5.2 3.3 %gather_fusion = bf16[768,256]{1,0:T(8,128)(2,1)} fusion(bf16[672,256]{1,0:T(8,128)(2,1)S(1)} %pad_maximum_fusion.2, s32[1024]{0:T(1024)S(1)} %pad_clamp_fusion.3), kind=kCustom, calls=%fused_computation | custom fusion | bytes 789504 | tf_op jit(solution)/shard_map/gather | solution.py:49
  8.4 5.2 %all-to-all-start = ((bf16[4,192,256]{2,1,0:T(8,128)(2,1)}), bf16[4,192,256]{2,1,0:T(8,128)(2,1)S(1)}, u32[]{:S(2)}, u32[]{:S(2)}) async-start(bf16[4,192,256]{2,1,0:T(8,128)(2,1)} %bitcast.2), calls=%async_computation | async-start | bytes 786432 | tf_op jit(solution)/shard_map/all_to_all | solution.py:50
  13.8 6.4 %all-to-all-done = bf16[4,192,256]{2,1,0:T(8,128)(2,1)S(1)} async-done(((bf16[4,192,256]{2,1,0:T(8,128)(2,1)}), bf16[4,192,256]{2,1,0:T(8,128)(2,1)S(1)}, u32[]{:S(2)}, u32[]{:S(2)}) %all-to-all-start) | async-done | bytes 393248 | tf_op jit(solution)/shard_map/all_to_all | solution.py:50
  20.2 2.1 %gather_fusion.1 = bf16[432,256]{1,0:T(8,128)(2,1)S(1)} fusion(bf16[768,256]{1,0:T(8,128)(2,1)S(1)} %bitcast.160, s32[1024]{0:T(1024)S(1)} %pad_clamp_fusion.2), kind=kCustom, calls=%fused_computation.1 | custom fusion | bytes 444096 | tf_op jit(solution)/shard_map/gather | solution.py:61
  22.3 21.0 %all-gather = bf16[1728,256]{1,0:T(8,128)(2,1)S(1)} all-gather(bf16[432,256]{1,0:T(8,128)(2,1)S(1)} %gather_fusion.1), channel_id=2, replica_groups={{0,2,4,6},{1,3,5,7},{8,10,12,14},{9,11,13,15},{16,18,20,22},{17,19,21,2..., dimensions={0}, use_global_device_ids=true | all-gather | bytes 1105920 | tf_op jit(solution)/shard_map/all_gather | solution.py:69
  43.3 2.4 %constant_dynamic-slice_fusion.1 = (bf16[1024,4,128]{2,1,0:T(4,128)(2,1)S(1)}, bf16[1024,4,128]{2,1,0:T(4,128)(2,1)S(1)}) fusion(bf16[1024,4,1024]{2,1,0:T(4,128)(2,1)} %param.11, s32[]{:T(128)S(6)} %select_n.145, s32[]{:T(128)S(6)} %select_n.147), kind=kLoop, calls=%fused_computation.118 | loop fusion | bytes 4194312 | tf_op jit(solution)/shard_map/dynamic_slice | solution.py:93
  45.7 1.2 %reshape_reshape.6 = bf16[4,2,128,512]{3,2,1,0:T(8,128)(2,1)} reshape(bf16[1024,4,128]{2,1,0:T(4,128)(2,1)S(1)} %get-tuple-element.19) | data formatting | bytes 2097152 | tf_op jit(solution)/shard_map/reshape;reshape | solution.py:75
  47.0 1.1 %constant_dynamic-slice_fusion = (bf16[128,1024]{1,0:T(8,128)(2,1)S(1)}, bf16[128,1024]{1,0:T(8,128)(2,1)S(1)}) fusion(bf16[1024,1024]{1,0:T(8,128)(2,1)} %param.13, s32[]{:T(128)S(6)} %select_n.147, s32[]{:T(128)S(6)} %select_n.145), kind=kLoop, calls=%fused_computation.117 | loop fusion | bytes 1048584 | tf_op jit(solution)/shard_map/dynamic_slice | solution.py:96
  48.3 0.9 dynamic_slice.64
  49.1 1.2 %reshape.275 = bf16[8,128,512]{2,1,0:T(8,128)(2,1)} reshape(bf16[1024,4,128]{2,1,0:T(4,128)(2,1)S(1)} %get-tuple-element.18) | data formatting | bytes 2097152 | tf_op jit(solution)/shard_map/reshape | solution.py:93
  51.3 1.4 %fusion.4 = f32[432,512]{1,0:T(8,128)S(1)} fusion(f32[432,512]{1,0:T(8,128)S(1)} %convolution_bitcast_fusion.3, bf16[4,2,128,512]{3,2,1,0:T(8,128)(2,1)S(1)} %copy-done, s32[]{:T(128)S(6)} %select_n.150, bf16[4,432,256]{2,1,0:T(8,128)(2,1)} %collective-permute-done), kind=kOutput, calls=%fused_computation.27 | convolution fusion | flops 226713600 | bytes 2736132 | tf_op jit(solution)/shard_map/trc,tcn->rn/dot_general | solution.py:104
  53.4 1.3 %fusion.6 = f32[432,128]{1,0:T(8,128)S(1)} fusion(f32[432,128]{1,0:T(8,128)S(1)} %convolution_bitcast_fusion.10, bf16[4,432,256]{2,1,0:T(8,128)(2,1)} %collective-permute-done, bf16[128,4,2,128]{0,3,2,1:T(8,128)(2,1)S(1)} %bitcast.174, s32[]{:T(128)S(6)} %select_n.150), kind=kOutput, calls=%fused_computation.36 | convolution fusion | flops 56678400 | bytes 1015812 | tf_op jit(solution)/shard_map/trc,dtc->rd/dot_general | solution.py:108
  57.6 1.5 %convolution_bitcast_fusion = bf16[4,1,128,512]{3,2,0,1:T(8,128)(2,1)S(1)} fusion(bf16[432,512]{1,0:T(8,128)(2,1)S(1)} %fusion.11, bf16[4,432,256]{2,1,0:T(8,128)(2,1)} %collective-permute-done), kind=kOutput, calls=%fused_computation.16 | convolution fusion | flops 226492416 | bytes 1409024 | tf_op jit(solution)/shard_map/trc,rn->tcn/dot_general | solution.py:163
  59.5 0.9 copy-done.3
  62.4 1.4 %convolution_bitcast_fusion.4 = bf16[4,1,128,128]{3,2,0,1:T(8,128)(2,1)S(1)} fusion(bf16[432,128,1]{1,0,2:T(8,128)(2,1)S(1)} %get-tuple-element.23, bf16[4,432,256]{2,1,0:T(8,128)(2,1)} %collective-permute-done), kind=kOutput, calls=%fused_computation.29 | convolution fusion | flops 56623104 | bytes 684032 | tf_op jit(solution)/shard_map/trc,rd->tcd/dot_general | solution.py:167
  64.1 0.9 fusion.17
  65.0 1.5 %collective-permute-start.2 = (bf16[2,256,640]{2,1,0:T(8,128)(2,1)}, bf16[2,256,640]{2,1,0:T(8,128)(2,1)}, u32[]{:S(2)}, u32[]{:S(2)}) collective-permute-start(bf16[2,256,640]{2,1,0:T(8,128)(2,1)} %fusion.17), channel_id=1, source_target_pairs={{0,16},{8,24},{16,0},{24,8},{1,17},{9,25},{17,1},{25,9},{2,18},{10... | collective-permute-start | bytes 1966088 | tf_op jit(solution)/shard_map/ppermute | solution.py:177
  66.5 1.2 %fusion.1 = bf16[4,432,256]{2,1,0:T(8,128)(2,1)} fusion(bf16[4,432,256]{2,1,0:T(8,128)(2,1)S(1)} %collective-permute-done.1, s32[]{:T(128)S(6)} %select_n.149, bf16[4,2,432,128]{3,2,1,0:T(8,128)(2,1)S(1)} %bitcast.162, bf16[4,2,432,128]{3,2,1,0:T(8,128)(2,1)S(1)} %bitcast.170), kind=kLoop, calls=%fused_computation.12 | loop fusion | flops 3538944 | bytes 3538948 | tf_op jit(solution)/shard_map/convert_element_type | solution.py:83
  67.7 3.5 %all-to-all-start.1 = ((bf16[4,432,256]{2,1,0:T(8,128)(2,1)}), bf16[4,432,256]{2,1,0:T(8,128)(2,1)S(1)}, u32[]{:S(2)}, u32[]{:S(2)}) async-start(bf16[4,432,256]{2,1,0:T(8,128)(2,1)} %fusion.1), calls=%async_computation.1 | async-start | bytes 1769472 | tf_op jit(solution)/shard_map/all_to_all | solution.py:84
  71.5 10.6 %collective-permute-done.2 = bf16[2,256,640]{2,1,0:T(8,128)(2,1)} collective-permute-done((bf16[2,256,640]{2,1,0:T(8,128)(2,1)}, bf16[2,256,640]{2,1,0:T(8,128)(2,1)}, u32[]{:S(2)}, u32[]{:S(2)}) %collective-permute-start.2) | collective-permute-done | bytes 655392 | tf_op jit(solution)/shard_map/ppermute | solution.py:177
  82.1 1.2 %bitcast_add_fusion = f32[2,256,640]{2,1,0:T(8,128)S(1)} fusion(bf16[2,256,640]{2,1,0:T(8,128)(2,1)} %collective-permute-done.2, f32[2,2,256,640]{3,2,1,0:T(8,128)S(1)} %maximum_convert_fusion, s32[]{:T(128)S(6)} %select_n.162), kind=kLoop, calls=%fused_computation.25 | loop fusion | flops 655360 | bytes 3276804 | tf_op jit(solution)/shard_map/add | solution.py:177
  83.3 1.2 %collective-permute-start.3 = (bf16[256,640]{1,0:T(8,128)(2,1)S(1)}, bf16[256,640]{1,0:T(8,128)(2,1)S(1)}, u32[]{:S(2)}, u32[]{:S(2)}) collective-permute-start(bf16[256,640]{1,0:T(8,128)(2,1)S(1)} %fusion.34), channel_id=1, source_target_pairs={{0,8},{8,0},{16,24},{24,16},{1,9},{9,1},{17,25},{25,17},{2,10},{10... | collective-permute-start | bytes 983048 | tf_op jit(solution)/shard_map/ppermute | solution.py:177
  85.2 7.0 %collective-permute-done.3 = bf16[256,640]{1,0:T(8,128)(2,1)S(1)} collective-permute-done((bf16[256,640]{1,0:T(8,128)(2,1)S(1)}, bf16[256,640]{1,0:T(8,128)(2,1)S(1)}, u32[]{:S(2)}, u32[]{:S(2)}) %collective-permute-start.3) | collective-permute-done | bytes 327712 | tf_op jit(solution)/shard_map/ppermute | solution.py:177
  92.6 1.0 copy.38
  94.5 2.5 %gather_fusion.2 = bf16[768,128]{1,0:T(8,128)(2,1)} fusion(bf16[432,128]{1,0:T(8,128)(2,1)S(1)} %get-tuple-element.24, s32[1024]{0:T(1024)S(1)} %pad_clamp_fusion.1), kind=kCustom, calls=%fused_computation.2 | custom fusion | bytes 396288 | tf_op jit(solution)/shard_map/gather | solution.py:182
  97.0 3.4 %all-to-all-start.2 = ((bf16[4,192,128]{2,1,0:T(8,128)(2,1)}), bf16[4,192,128]{2,1,0:T(8,128)(2,1)S(1)}, u32[]{:S(2)}, u32[]{:S(2)}) async-start(bf16[4,192,128]{2,1,0:T(8,128)(2,1)} %bitcast.37), calls=%async_computation.2 | async-start | bytes 393216 | tf_op jit(solution)/shard_map/all_to_all | solution.py:183
  101.2 4.4 %all-to-all-done.2 = bf16[4,192,128]{2,1,0:T(8,128)(2,1)S(1)} async-done(((bf16[4,192,128]{2,1,0:T(8,128)(2,1)}), bf16[4,192,128]{2,1,0:T(8,128)(2,1)S(1)}, u32[]{:S(2)}, u32[]{:S(2)}) %all-to-all-start.2) | async-done | bytes 196640 | tf_op jit(solution)/shard_map/all_to_all | solution.py:183
  105.6 2.0 %gather_fusion.3 = bf16[672,128]{1,0:T(8,128)(2,1)S(1)} fusion(bf16[768,128]{1,0:T(8,128)(2,1)S(1)} %bitcast.159, s32[1024]{0:T(1024)S(1)} %pad_clamp_fusion), kind=kCustom, calls=%fused_computation.3 | custom fusion | bytes 346752 | tf_op jit(solution)/shard_map/gather | solution.py:192
  107.6 0.8 broadcast_select_fusion
  (70 shorter events, 11.6 us)
Async XLA Ops:
  8.4 11.8 %all-to-all-start = ((bf16[4,192,256]{2,1,0:T(8,128)(2,1)}), bf16[4,192,256]{2,1,0:T(8,128)(2,1)S(1)}, u32[]{:S(2)}, u32[]{:S(2)}) async-start(bf16[4,192,256]{2,1,0:T(8,128)(2,1)} %bitcast.2), calls=%async_computation | async-start | bytes 786432 | tf_op jit(solution)/shard_map/all_to_all | solution.py:50
  22.3 21.0 %copy-start.1 = (bf16[432,256]{1,0:T(8,128)(2,1)}, bf16[432,256]{1,0:T(8,128)(2,1)S(1)}, u32[]{:S(2)}) copy-start(bf16[432,256]{1,0:T(8,128)(2,1)S(1)} %gather_fusion.1) | copy-start | bytes 663556
  43.3 8.0 %collective-permute-start = (bf16[4,432,256]{2,1,0:T(8,128)(2,1)S(1)}, bf16[4,432,256]{2,1,0:T(8,128)(2,1)}, u32[]{:S(2)}, u32[]{:S(2)}) collective-permute-start(bf16[4,432,256]{2,1,0:T(8,128)(2,1)S(1)} %bitcast.163), channel_id=1, source_target_pairs={{0,1},{1,0},{2,3},{3,2},{4,5},{5,4},{6,7},{7,6},{8,9},{9,8},{10,11... | collective-permute-start | bytes 2654216 | tf_op jit(solution)/shard_map/ppermute | solution.py:70
  48.3 2.7 %copy-start = (bf16[4,2,128,512]{3,2,1,0:T(8,128)(2,1)S(1)}, bf16[4,2,128,512]{3,2,1,0:T(8,128)(2,1)}, u32[]{:S(2)}) copy-start(bf16[4,2,128,512]{3,2,1,0:T(8,128)(2,1)} %reshape_reshape.6) | copy-start | bytes 3145732
  59.2 1.2 %copy-start.3 = (bf16[8,128,512]{2,1,0:T(8,128)(2,1)S(1)}, bf16[8,128,512]{2,1,0:T(8,128)(2,1)}, u32[]{:S(2)}) copy-start(bf16[8,128,512]{2,1,0:T(8,128)(2,1)} %reshape.275) | copy-start | bytes 3145732
  61.6 4.9 %collective-permute-start.1 = (bf16[4,432,256]{2,1,0:T(8,128)(2,1)S(1)}, bf16[4,432,256]{2,1,0:T(8,128)(2,1)S(1)}, u32[]{:S(2)}, u32[]{:S(2)}) collective-permute-start(bf16[4,432,256]{2,1,0:T(8,128)(2,1)S(1)} %fusion.8), channel_id=1, source_target_pairs={{0,1},{1,0},{2,3},{3,2},{4,5},{5,4},{6,7},{7,6},{8,9},{9,8},{10,11... | collective-permute-start | bytes 2654216 | tf_op jit(solution)/shard_map/ppermute | solution.py:83
  65.0 17.0 %collective-permute-start.2 = (bf16[2,256,640]{2,1,0:T(8,128)(2,1)}, bf16[2,256,640]{2,1,0:T(8,128)(2,1)}, u32[]{:S(2)}, u32[]{:S(2)}) collective-permute-start(bf16[2,256,640]{2,1,0:T(8,128)(2,1)} %fusion.17), channel_id=1, source_target_pairs={{0,16},{8,24},{16,0},{24,8},{1,17},{9,25},{17,1},{25,9},{2,18},{10... | collective-permute-start | bytes 1966088 | tf_op jit(solution)/shard_map/ppermute | solution.py:177
  67.7 26.0 %all-to-all-start.1 = ((bf16[4,432,256]{2,1,0:T(8,128)(2,1)}), bf16[4,432,256]{2,1,0:T(8,128)(2,1)S(1)}, u32[]{:S(2)}, u32[]{:S(2)}) async-start(bf16[4,432,256]{2,1,0:T(8,128)(2,1)} %fusion.1), calls=%async_computation.1 | async-start | bytes 1769472 | tf_op jit(solution)/shard_map/all_to_all | solution.py:84
  83.3 8.9 %collective-permute-start.3 = (bf16[256,640]{1,0:T(8,128)(2,1)S(1)}, bf16[256,640]{1,0:T(8,128)(2,1)S(1)}, u32[]{:S(2)}, u32[]{:S(2)}) collective-permute-start(bf16[256,640]{1,0:T(8,128)(2,1)S(1)} %fusion.34), channel_id=1, source_target_pairs={{0,8},{8,0},{16,24},{24,16},{1,9},{9,1},{17,25},{25,17},{2,10},{10... | collective-permute-start | bytes 983048 | tf_op jit(solution)/shard_map/ppermute | solution.py:177
  92.4 1.4 %copy-start.2 = (bf16[432,256]{1,0:T(8,128)(2,1)S(1)}, bf16[432,256]{1,0:T(8,128)(2,1)}, u32[]{:S(2)}) copy-start(bf16[432,256]{1,0:T(8,128)(2,1)} %copy-done.1) | copy-start | bytes 663556
  97.0 8.5 %all-to-all-start.2 = ((bf16[4,192,128]{2,1,0:T(8,128)(2,1)}), bf16[4,192,128]{2,1,0:T(8,128)(2,1)S(1)}, u32[]{:S(2)}, u32[]{:S(2)}) async-start(bf16[4,192,128]{2,1,0:T(8,128)(2,1)} %bitcast.37), calls=%async_computation.2 | async-start | bytes 393216 | tf_op jit(solution)/shard_map/all_to_all | solution.py:183

commit v7 on v6

--- a/solution.py
+++ b/solution.py
@@ -37,7 +37,6 @@
     places = jnp.arange(MAXLEN, dtype=jnp.int32)
     peer_ids = jnp.arange(dp_count, dtype=jnp.int32)
     seq_ids = jnp.arange(lengths.shape[1], dtype=jnp.int32)
-    zero_bf = jnp.zeros((), bf16)
 
     my_lengths = lengths[dp_index]
     my_owners = owners[dp_index]
@@ -45,8 +44,14 @@
     sent_to = my_owners[None, :] == peer_ids[:, None]
     send_start = jnp.sum(jnp.where(sent_to, my_starts[None, :], 0), axis=1)
     send_ids = jnp.minimum(send_start[:, None] + places[None, :], load_rows - 1)
-    both = jnp.concatenate([tokens, cotangent], axis=1)
-    send_both = both[send_ids]
+    def pick_rows(row_ids, source):
+        one_hot = (row_ids[:, None] == jnp.arange(source.shape[0], dtype=jnp.int32)[None, :]).astype(bf16)
+        return jnp.dot(one_hot, source, preferred_element_type=f32).astype(bf16)
+
+    flat_send = send_ids.reshape(-1)
+    send_both = jnp.concatenate(
+        [pick_rows(flat_send, tokens), pick_rows(flat_send, cotangent)], axis=1
+    ).reshape(dp_count, MAXLEN, 2 * col_width)
     recv_both = lax.all_to_all(send_both, "dp", split_axis=0, concat_axis=0, tiled=True)
 
     recv_len = jnp.sum(jnp.where(owners == dp_index, lengths, 0), axis=1)
@@ -58,7 +63,7 @@
     slot_pick = compact_slot[:, None] == peer_ids[None, :]
     compact_start = jnp.sum(jnp.where(slot_pick, recv_start[None, :], 0), axis=1)
     gather_ids = compact_slot * MAXLEN + compact_ids - compact_start
-    own_both = recv_both.reshape(dp_count * MAXLEN, 2 * col_width)[gather_ids]
+    own_both = pick_rows(gather_ids, recv_both.reshape(dp_count * MAXLEN, 2 * col_width))
     own_tokens = own_both[:, :col_width]
     own_cotan = own_both[:, col_width:]
 
@@ -179,7 +184,7 @@
     out_grad = term_sum[:, 4 * col_width :].T
 
     back_src = jnp.minimum(recv_start[:, None] + places[None, :], owned_rows - 1)
-    back_send = token_rows[back_src]
+    back_send = pick_rows(back_src.reshape(-1), token_rows).reshape(dp_count, MAXLEN, col_width)
     back_grads = lax.all_to_all(back_send, "dp", split_axis=0, concat_axis=0, tiled=True)
     back_grads = back_grads.reshape(dp_count * MAXLEN, col_width)
     load_ids = jnp.arange(load_rows, dtype=jnp.int32)
@@ -189,7 +194,7 @@
     start_of = jnp.sum(jnp.where(seq_pick, my_starts[None, :], 0), axis=1)
     back_ids = owner_of * MAXLEN + jnp.minimum(load_ids - start_of, MAXLEN - 1)
     row_used = load_ids < jnp.sum(my_lengths)
-    token_grad = jnp.where(row_used[:, None], back_grads[back_ids], zero_bf)
+    token_grad = pick_rows(jnp.where(row_used, back_ids, -1), back_grads)
     return (mixed_out, token_grad, proj_grad, out_grad)
 
 

time: 109 us -> 107 us (0.982)
  local copies, waits for them, and re-layouts: 21.9 us -> 12.4 us
  matrix products: 10.2 us -> 16.2 us
  other arithmetic: 10.4 us -> 12.2 us
    gather x4 -> x0, local copies, waits for them, and re-layouts: 9.86 us -> none  [the longest x1 3.28 us: local(): send_both = both[send_ids]]
    dot_general x0 -> x5, matrix products: none -> 5.04 us  [pick_rows(): return jnp.dot(one_hot, source, preferred_element_type=f32).astype(bf16)]
    ppermute x2, waiting for transfers between devices: 17.7 us -> 15.3 us  [local(): lax.ppermute(send.astype(bf16), 'dp', partners).astype(f32)]
    all_to_all x1, waiting for transfers between devices: 0.08 us -> 1.86 us  [reduce_blocks(): lax.all_to_all(pair_sum, 'tensor', 0, 0, tiled=True, axis_index_groups=sa...]
    convert_element_type x1, other arithmetic: 1.22 us -> 2.56 us  [reduce_blocks(): (keep.astype(f32) + lax.ppermute(send, 'tensor', sibling).astype(f32)).as...]
    reduce_sum x1, other arithmetic: 0.12 us -> 1.33 us  [reduce_blocks(): return jnp.sum(pieces.astype(f32), axis=0)]
    unnamed x12 -> x20, local copies, waits for them, and re-layouts: 3.05 us -> 3.35 us
  transfers between devices with their start and end apart: 7 -> 7, of which waited for: 5 -> 5; matrix products, arithmetic and copies ran while one was open for 15% -> 20% of each run, Pallas kernels for 0% -> 0%
where the time goes in v7:
time: 107 us
  waiting for transfers between devices  27.9 us (26%)
  blocking collectives  21 us (20%)
  matrix products  16.2 us (15%)
  starting transfers between devices  15.9 us (15%)
  local copies, waits for them, and re-layouts  12.4 us (12%)
  other arithmetic  12.2 us (11%)
    all_gather x1, blocking collectives, local(): lax.all_gather(own_both, 'tensor', axis=0, tiled=False, axis_index_groups...  21 us
    ppermute x2, waiting for transfers between devices, local(): lax.ppermute(send.astype(bf16), 'dp', partners).astype(f32)  15.3 us
    all_to_all x1, waiting for transfers between devices, local(): lax.all_to_all(send_both, 'dp', split_axis=0, concat_axis=0, tiled=True)  6.23 us
    all_to_all x1, starting transfers between devices, local(): lax.all_to_all(send_both, 'dp', split_axis=0, concat_axis=0, tiled=True)  5.16 us
    dot_general x5, matrix products, pick_rows(): return jnp.dot(one_hot, source, preferred_element_type=f32).astype(bf16)  5.04 us
    all_to_all x1, waiting for transfers between devices, local(): lax.all_to_all(back_send, 'dp', split_axis=0, concat_axis=0, tiled=True)  4.49 us
    all_to_all x1, starting transfers between devices, reduce_blocks(): lax.all_to_all(pair_sum, 'tensor', 0, 0, tiled=True, axis_index_groups=sa...  4.21 us
    all_to_all x1, starting transfers between devices, local(): lax.all_to_all(back_send, 'dp', split_axis=0, concat_axis=0, tiled=True)  3.36 us
  transfers between devices with their start and end apart: 7, of which 5 were waited for; matrix products, arithmetic and copies ran while one was open for 20% of the time, Pallas kernels for 0%

profile of v7, /device:TPU:0, one launch (start us, length us, event | category | flops | bytes accessed | tf_op | source)
XLA Modules:
  0.0 106.6 jit_solution(14652110559936377090)
XLA Ops:
  0.7 1.4 %fusion.67 = (s32[]{:T(128)}, s32[1,4]{1,0:T(1,128)S(1)}) fusion(s32[4,4]{1,0:T(4,128)} %param.9, s32[]{:T(128)S(6)} %select_n.105), kind=kLoop, calls=%fused_computation.152 | loop fusion | flops 3 | bytes 40 | tf_op jit(solution)/shard_map/reduce_sum | solution.py:196
  4.6 1.6 %fusion.16 = bf16[768,128]{0,1:T(8,128)(2,1)S(1)} fusion(bf16[672,128]{1,0:T(8,128)(2,1)} %param.8, s32[768]{0:T(1024)S(1)} %min.38), kind=kOutput, calls=%fused_computation.39 | convolution fusion | flops 132734976 | bytes 371712 | tf_op jit(solution)/shard_map/dot_general | solution.py:49
  6.3 0.9 copy.28
  7.2 5.2 %all-to-all-start = ((bf16[4,192,256]{2,1,0:T(8,128)(2,1)}), bf16[4,192,256]{2,1,0:T(8,128)(2,1)S(1)}, u32[]{:S(2)}, u32[]{:S(2)}) async-start(bf16[4,192,256]{2,1,0:T(8,128)(2,1)} %bitcast.4), calls=%async_computation | async-start | bytes 786432 | tf_op jit(solution)/shard_map/all_to_all | solution.py:55
  12.7 6.2 %all-to-all-done = bf16[4,192,256]{2,1,0:T(8,128)(2,1)S(1)} async-done(((bf16[4,192,256]{2,1,0:T(8,128)(2,1)}), bf16[4,192,256]{2,1,0:T(8,128)(2,1)S(1)}, u32[]{:S(2)}, u32[]{:S(2)}) %all-to-all-start) | async-done | bytes 393248 | tf_op jit(solution)/shard_map/all_to_all | solution.py:55
  19.4 21.0 %all-gather = bf16[1728,256]{1,0:T(8,128)(2,1)S(1)} all-gather(bf16[432,256]{1,0:T(8,128)(2,1)S(1)} %fusion.11), channel_id=2, replica_groups={{0,2,4,6},{1,3,5,7},{8,10,12,14},{9,11,13,15},{16,18,20,22},{17,19,21,2..., dimensions={0}, use_global_device_ids=true | all-gather | bytes 1105920 | tf_op jit(solution)/shard_map/all_gather | solution.py:74
  40.4 2.4 %constant_dynamic-slice_fusion.1 = (bf16[1024,4,128]{2,1,0:T(4,128)(2,1)S(1)}, bf16[1024,4,128]{2,1,0:T(4,128)(2,1)S(1)}) fusion(bf16[1024,4,1024]{2,1,0:T(4,128)(2,1)} %param.11, s32[]{:T(128)S(6)} %select_n.107, s32[]{:T(128)S(6)} %select_n.109), kind=kLoop, calls=%fused_computation.129 | loop fusion | bytes 4194312 | tf_op jit(solution)/shard_map/dynamic_slice | solution.py:98
  42.8 1.2 %reshape_reshape.6 = bf16[4,2,128,512]{3,2,1,0:T(8,128)(2,1)} reshape(bf16[1024,4,128]{2,1,0:T(4,128)(2,1)S(1)} %get-tuple-element.19) | data formatting | bytes 2097152 | tf_op jit(solution)/shard_map/reshape;reshape | solution.py:80
  44.0 1.1 %constant_dynamic-slice_fusion = (bf16[128,1024]{1,0:T(8,128)(2,1)S(1)}, bf16[128,1024]{1,0:T(8,128)(2,1)S(1)}) fusion(bf16[1024,1024]{1,0:T(8,128)(2,1)} %param.13, s32[]{:T(128)S(6)} %select_n.109, s32[]{:T(128)S(6)} %select_n.107), kind=kLoop, calls=%fused_computation.128 | loop fusion | bytes 1048584 | tf_op jit(solution)/shard_map/dynamic_slice | solution.py:101
  45.1 0.8 copy.44
  46.0 0.8 dynamic_slice.64
  46.8 1.2 %reshape.181 = bf16[8,128,512]{2,1,0:T(8,128)(2,1)} reshape(bf16[1024,4,128]{2,1,0:T(4,128)(2,1)S(1)} %get-tuple-element.18) | data formatting | bytes 2097152 | tf_op jit(solution)/shard_map/reshape | solution.py:98
  48.2 1.2 %convolution_bitcast_fusion.10 = f32[432,128]{1,0:T(8,128)S(1)} fusion(bf16[4,432,256]{2,1,0:T(8,128)(2,1)S(1)} %bitcast.159, bf16[128,4,2,128]{0,3,2,1:T(8,128)(2,1)} %bitcast.168, s32[]{:T(128)S(6)} %select_n.111), kind=kOutput, calls=%fused_computation.47 | convolution fusion | flops 56623104 | bytes 794628 | tf_op jit(solution)/shard_map/trc,dtc->rd/dot_general | solution.py:111
  49.9 1.4 %fusion.9 = f32[432,512]{1,0:T(8,128)S(1)} fusion(f32[432,512]{1,0:T(8,128)S(1)} %convolution_bitcast_fusion.3, bf16[4,2,128,512]{3,2,1,0:T(8,128)(2,1)S(1)} %copy-done.2, s32[]{:T(128)S(6)} %select_n.112, bf16[4,432,256]{2,1,0:T(8,128)(2,1)} %collective-permute-done), kind=kOutput, calls=%fused_computation.32 | convolution fusion | flops 226713600 | bytes 2736132 | tf_op jit(solution)/shard_map/trc,tcn->rn/dot_general | solution.py:109
  52.5 1.3 %fusion.18 = f32[432,128]{1,0:T(8,128)S(1)} fusion(f32[432,128]{1,0:T(8,128)S(1)} %convolution_bitcast_fusion.10, bf16[4,432,256]{2,1,0:T(8,128)(2,1)} %collective-permute-done, bf16[128,4,2,128]{0,3,2,1:T(8,128)(2,1)S(1)} %bitcast.169, s32[]{:T(128)S(6)} %select_n.112), kind=kOutput, calls=%fused_computation.48 | convolution fusion | flops 56678400 | bytes 1015812 | tf_op jit(solution)/shard_map/trc,dtc->rd/dot_general | solution.py:113
  58.1 1.1 %fusion.21 = bf16[4,432,256]{2,1,0:T(8,128)(2,1)} fusion(s32[]{:T(128)S(6)} %select_n.112, bf16[4,2,432,128]{3,2,1,0:T(8,128)(2,1)S(1)} %bitcast.156, bf16[4,2,432,128]{3,2,1,0:T(8,128)(2,1)S(1)} %bitcast.164), kind=kLoop, calls=%fused_computation.51 | loop fusion | flops 1769472 | bytes 2654212 | tf_op jit(solution)/shard_map/jit(dynamic_index_in_dim)/squeeze | solution.py:83
  59.7 1.5 %convolution_bitcast_fusion = bf16[4,1,128,512]{3,2,0,1:T(8,128)(2,1)S(1)} fusion(bf16[432,512]{1,0:T(8,128)(2,1)S(1)} %fusion.24, bf16[4,432,256]{2,1,0:T(8,128)(2,1)} %collective-permute-done), kind=kOutput, calls=%fused_computation.19 | convolution fusion | flops 226492416 | bytes 1409024 | tf_op jit(solution)/shard_map/trc,rn->tcn/dot_general | solution.py:168
  61.5 1.4 %convolution_bitcast_fusion.4 = bf16[4,1,128,128]{3,2,0,1:T(8,128)(2,1)S(1)} fusion(bf16[432,128,1]{1,0,2:T(8,128)(2,1)S(1)} %get-tuple-element.23, bf16[4,432,256]{2,1,0:T(8,128)(2,1)} %collective-permute-done), kind=kOutput, calls=%fused_computation.40 | convolution fusion | flops 56623104 | bytes 684032 | tf_op jit(solution)/shard_map/trc,rd->tcd/dot_general | solution.py:172
  63.3 1.5 %collective-permute-start.2 = (bf16[2,256,640]{2,1,0:T(8,128)(2,1)S(1)}, bf16[2,256,640]{2,1,0:T(8,128)(2,1)}, u32[]{:S(2)}, u32[]{:S(2)}) collective-permute-start(bf16[2,256,640]{2,1,0:T(8,128)(2,1)S(1)} %fusion.32), channel_id=1, source_target_pairs={{0,16},{8,24},{16,0},{24,8},{1,17},{9,25},{17,1},{25,9},{2,18},{10... | collective-permute-start | bytes 1966088 | tf_op jit(solution)/shard_map/ppermute | solution.py:182
  65.1 2.6 %fusion.4 = bf16[4,432,256]{2,1,0:T(8,128)(2,1)} fusion(bf16[4,432,256]{2,1,0:T(8,128)(2,1)} %collective-permute-done.1, s32[]{:T(128)S(6)} %select_n.111, bf16[4,2,432,128]{3,2,1,0:T(8,128)(2,1)} %bitcast.157, bf16[4,2,432,128]{3,2,1,0:T(8,128)(2,1)} %bitcast.165), kind=kLoop, calls=%fused_computation.13 | loop fusion | flops 3538944 | bytes 3538948 | tf_op jit(solution)/shard_map/convert_element_type | solution.py:88
  67.7 4.2 %all-to-all-start.1 = ((bf16[4,432,256]{2,1,0:T(8,128)(2,1)}), bf16[4,432,256]{2,1,0:T(8,128)(2,1)}, u32[]{:S(2)}, u32[]{:S(2)}) async-start(bf16[4,432,256]{2,1,0:T(8,128)(2,1)} %fusion.4), calls=%async_computation.1 | async-start | bytes 1769472 | tf_op jit(solution)/shard_map/all_to_all | solution.py:89
  71.9 8.3 %collective-permute-done.2 = bf16[2,256,640]{2,1,0:T(8,128)(2,1)} collective-permute-done((bf16[2,256,640]{2,1,0:T(8,128)(2,1)S(1)}, bf16[2,256,640]{2,1,0:T(8,128)(2,1)}, u32[]{:S(2)}, u32[]{:S(2)}) %collective-permute-start.2) | collective-permute-done | bytes 655392 | tf_op jit(solution)/shard_map/ppermute | solution.py:182
  80.2 1.2 %bitcast_add_fusion = f32[2,256,640]{2,1,0:T(8,128)S(1)} fusion(bf16[2,256,640]{2,1,0:T(8,128)(2,1)} %collective-permute-done.2, f32[2,2,256,640]{3,2,1,0:T(8,128)S(1)} %maximum_convert_fusion, s32[]{:T(128)S(6)} %select_n.122), kind=kLoop, calls=%fused_computation.30 | loop fusion | flops 655360 | bytes 3276804 | tf_op jit(solution)/shard_map/add | solution.py:182
  81.5 1.2 %collective-permute-start.3 = (bf16[256,640]{1,0:T(8,128)(2,1)S(1)}, bf16[256,640]{1,0:T(8,128)(2,1)S(1)}, u32[]{:S(2)}, u32[]{:S(2)}) collective-permute-start(bf16[256,640]{1,0:T(8,128)(2,1)S(1)} %fusion.49), channel_id=1, source_target_pairs={{0,8},{8,0},{16,24},{24,16},{1,9},{9,1},{17,25},{25,17},{2,10},{10... | collective-permute-start | bytes 983048 | tf_op jit(solution)/shard_map/ppermute | solution.py:182
  83.4 7.0 %collective-permute-done.3 = bf16[256,640]{1,0:T(8,128)(2,1)S(1)} collective-permute-done((bf16[256,640]{1,0:T(8,128)(2,1)S(1)}, bf16[256,640]{1,0:T(8,128)(2,1)S(1)}, u32[]{:S(2)}, u32[]{:S(2)}) %collective-permute-start.3) | collective-permute-done | bytes 327712 | tf_op jit(solution)/shard_map/ppermute | solution.py:182
  90.8 1.0 copy.40
  92.5 1.9 %all-to-all-done.1 = bf16[4,432,256]{2,1,0:T(8,128)(2,1)} async-done(((bf16[4,432,256]{2,1,0:T(8,128)(2,1)}), bf16[4,432,256]{2,1,0:T(8,128)(2,1)}, u32[]{:S(2)}, u32[]{:S(2)}) %all-to-all-start.1) | async-done | bytes 884768 | tf_op jit(solution)/shard_map/all_to_all | solution.py:89
  94.4 1.3 %convert_reduce_fusion = f32[432,256]{1,0:T(8,128)S(1)} fusion(bf16[4,432,256]{2,1,0:T(8,128)(2,1)} %all-to-all-done.1), kind=kLoop, calls=%fused_computation.14 | loop fusion | flops 774144 | bytes 1327104 | tf_op jit(solution)/shard_map/reduce_sum | solution.py:90
  95.7 1.1 %fusion.14 = bf16[768,128]{1,0:T(8,128)(2,1)} fusion(s32[768]{0:T(1024)S(1)} %min.43, f32[432,256]{1,0:T(8,128)S(1)} %convert_reduce_fusion, bf16[432,256]{1,0:T(8,128)(2,1)S(1)} %copy-done.7), kind=kOutput, calls=%fused_computation.37 | convolution fusion | flops 85530624 | bytes 532480 | tf_op jit(solution)/shard_map/dot_general | solution.py:49
  96.8 3.4 %all-to-all-start.2 = ((bf16[4,192,128]{2,1,0:T(8,128)(2,1)}), bf16[4,192,128]{2,1,0:T(8,128)(2,1)S(1)}, u32[]{:S(2)}, u32[]{:S(2)}) async-start(bf16[4,192,128]{2,1,0:T(8,128)(2,1)} %bitcast.34), calls=%async_computation.2 | async-start | bytes 393216 | tf_op jit(solution)/shard_map/all_to_all | solution.py:188
  100.9 4.5 %all-to-all-done.2 = bf16[4,192,128]{2,1,0:T(8,128)(2,1)S(1)} async-done(((bf16[4,192,128]{2,1,0:T(8,128)(2,1)}), bf16[4,192,128]{2,1,0:T(8,128)(2,1)S(1)}, u32[]{:S(2)}, u32[]{:S(2)}) %all-to-all-start.2) | async-done | bytes 196640 | tf_op jit(solution)/shard_map/all_to_all | solution.py:188
  105.4 1.2 %fusion.17 = bf16[672,128]{1,0:T(8,128)(2,1)} fusion(bf16[768,128]{1,0:T(8,128)(2,1)S(1)} %bitcast.172, s32[672]{0:T(1024)S(1)} %add_select_fusion), kind=kOutput, calls=%fused_computation.42 | convolution fusion | flops 132722688 | bytes 371328 | tf_op jit(solution)/shard_map/dot_general | solution.py:49
  (73 shorter events, 13.3 us)
Async XLA Ops:
  0.6 3.3 %copy-start = (bf16[672,128]{1,0:T(8,128)(2,1)S(1)}, bf16[672,128]{1,0:T(8,128)(2,1)}, u32[]{:S(2)}) copy-start(bf16[672,128]{1,0:T(8,128)(2,1)} %param.7) | copy-start | bytes 516100
  7.2 11.8 %all-to-all-start = ((bf16[4,192,256]{2,1,0:T(8,128)(2,1)}), bf16[4,192,256]{2,1,0:T(8,128)(2,1)S(1)}, u32[]{:S(2)}, u32[]{:S(2)}) async-start(bf16[4,192,256]{2,1,0:T(8,128)(2,1)} %bitcast.4), calls=%async_computation | async-start | bytes 786432 | tf_op jit(solution)/shard_map/all_to_all | solution.py:55
  19.4 21.0 %copy-start.6 = (bf16[432,256]{1,0:T(8,128)(2,1)}, bf16[432,256]{1,0:T(8,128)(2,1)S(1)}, u32[]{:S(2)}) copy-start(bf16[432,256]{1,0:T(8,128)(2,1)S(1)} %fusion.11) | copy-start | bytes 663556
  40.4 9.5 %collective-permute-start = (bf16[4,432,256]{2,1,0:T(8,128)(2,1)S(1)}, bf16[4,432,256]{2,1,0:T(8,128)(2,1)}, u32[]{:S(2)}, u32[]{:S(2)}) collective-permute-start(bf16[4,432,256]{2,1,0:T(8,128)(2,1)S(1)} %bitcast.158), channel_id=1, source_target_pairs={{0,1},{1,0},{2,3},{3,2},{4,5},{5,4},{6,7},{7,6},{8,9},{9,8},{10,11... | collective-permute-start | bytes 2654216 | tf_op jit(solution)/shard_map/ppermute | solution.py:75
  46.0 3.5 %copy-start.2 = (bf16[4,2,128,512]{3,2,1,0:T(8,128)(2,1)S(1)}, bf16[4,2,128,512]{3,2,1,0:T(8,128)(2,1)}, u32[]{:S(2)}) copy-start(bf16[4,2,128,512]{3,2,1,0:T(8,128)(2,1)} %reshape_reshape.6) | copy-start | bytes 3145732
  51.5 1.0 copy-start.5
  55.8 1.2 %copy-start.4 = (bf16[8,128,512]{2,1,0:T(8,128)(2,1)S(1)}, bf16[8,128,512]{2,1,0:T(8,128)(2,1)}, u32[]{:S(2)}) copy-start(bf16[8,128,512]{2,1,0:T(8,128)(2,1)} %reshape.181) | copy-start | bytes 3145732
  57.7 1.6 %copy-start.3 = (bf16[8,128,432]{1,2,0:T(8,128)(2,1)}, bf16[8,128,432]{1,2,0:T(8,128)(2,1)S(1)}, u32[]{:S(2)}) copy-start(bf16[8,128,432]{1,2,0:T(8,128)(2,1)S(1)} %convolution_convert_fusion) | copy-start | bytes 2654212
  58.1 3.0 %copy-start.1 = (bf16[8,128,432]{1,2,0:T(8,128)(2,1)}, bf16[8,128,432]{1,2,0:T(8,128)(2,1)S(1)}, u32[]{:S(2)}) copy-start(bf16[8,128,432]{1,2,0:T(8,128)(2,1)S(1)} %convolution_convert_fusion.1) | copy-start | bytes 2654212
  59.2 5.9 %collective-permute-start.1 = (bf16[4,432,256]{2,1,0:T(8,128)(2,1)}, bf16[4,432,256]{2,1,0:T(8,128)(2,1)}, u32[]{:S(2)}, u32[]{:S(2)}) collective-permute-start(bf16[4,432,256]{2,1,0:T(8,128)(2,1)} %fusion.21), channel_id=1, source_target_pairs={{0,1},{1,0},{2,3},{3,2},{4,5},{5,4},{6,7},{7,6},{8,9},{9,8},{10,11... | collective-permute-start | bytes 2654216 | tf_op jit(solution)/shard_map/ppermute | solution.py:88
  63.3 16.9 %collective-permute-start.2 = (bf16[2,256,640]{2,1,0:T(8,128)(2,1)S(1)}, bf16[2,256,640]{2,1,0:T(8,128)(2,1)}, u32[]{:S(2)}, u32[]{:S(2)}) collective-permute-start(bf16[2,256,640]{2,1,0:T(8,128)(2,1)S(1)} %fusion.32), channel_id=1, source_target_pairs={{0,16},{8,24},{16,0},{24,8},{1,17},{9,25},{17,1},{25,9},{2,18},{10... | collective-permute-start | bytes 1966088 | tf_op jit(solution)/shard_map/ppermute | solution.py:182
  67.7 26.7 %all-to-all-start.1 = ((bf16[4,432,256]{2,1,0:T(8,128)(2,1)}), bf16[4,432,256]{2,1,0:T(8,128)(2,1)}, u32[]{:S(2)}, u32[]{:S(2)}) async-start(bf16[4,432,256]{2,1,0:T(8,128)(2,1)} %fusion.4), calls=%async_computation.1 | async-start | bytes 1769472 | tf_op jit(solution)/shard_map/all_to_all | solution.py:89
  81.5 8.9 %collective-permute-start.3 = (bf16[256,640]{1,0:T(8,128)(2,1)S(1)}, bf16[256,640]{1,0:T(8,128)(2,1)S(1)}, u32[]{:S(2)}, u32[]{:S(2)}) collective-permute-start(bf16[256,640]{1,0:T(8,128)(2,1)S(1)} %fusion.49), channel_id=1, source_target_pairs={{0,8},{8,0},{16,24},{24,16},{1,9},{9,1},{17,25},{25,17},{2,10},{10... | collective-permute-start | bytes 983048 | tf_op jit(solution)/shard_map/ppermute | solution.py:182
  90.6 5.2 %copy-start.7 = (bf16[432,256]{1,0:T(8,128)(2,1)S(1)}, bf16[432,256]{1,0:T(8,128)(2,1)}, u32[]{:S(2)}) copy-start(bf16[432,256]{1,0:T(8,128)(2,1)} %copy-done.6) | copy-start | bytes 663556
  96.8 8.5 %all-to-all-start.2 = ((bf16[4,192,128]{2,1,0:T(8,128)(2,1)}), bf16[4,192,128]{2,1,0:T(8,128)(2,1)S(1)}, u32[]{:S(2)}, u32[]{:S(2)}) async-start(bf16[4,192,128]{2,1,0:T(8,128)(2,1)} %bitcast.34), calls=%async_computation.2 | async-start | bytes 393216 | tf_op jit(solution)/shard_map/all_to_all | solution.py:188

commit v8 on v7

--- a/solution.py
+++ b/solution.py
@@ -54,6 +54,39 @@
     ).reshape(dp_count, MAXLEN, 2 * col_width)
     recv_both = lax.all_to_all(send_both, "dp", split_axis=0, concat_axis=0, tiled=True)
 
+    half_count = tensor_count // 2
+    core = tensor_index % 2
+
+    def by_core(weight, axis):
+        split = weight.reshape(weight.shape[:axis] + (half_count, 2) + weight.shape[axis + 1 :])
+        return (
+            lax.dynamic_index_in_dim(split, core, axis + 1, keepdims=False),
+            lax.dynamic_index_in_dim(split, 1 - core, axis + 1, keepdims=False),
+        )
+
+    head_start = tensor_index * H // tensor_count * head_dim
+    own_start = tensor_index * col_width
+    inner_start = own_start - head_start
+    head_proj = lax.dynamic_slice_in_dim(proj_weight, head_start, head_dim, 2).reshape(
+        tensor_count, col_width, 4 * head_dim
+    )
+    own_proj = lax.dynamic_slice_in_dim(proj_weight, own_start, col_width, 2).reshape(
+        tensor_count, col_width, 4 * col_width
+    )
+    head_out = lax.dynamic_slice_in_dim(out_weight, head_start, head_dim, 0).reshape(
+        head_dim, tensor_count, col_width
+    )
+    head_gain = lax.dynamic_slice_in_dim(norm_gain, head_start, head_dim, 0)
+
+    proj_mine, proj_other = by_core(head_proj, 0)
+    out_mine, out_other = by_core(head_out, 1)
+    own_out = lax.dynamic_slice_in_dim(out_weight, own_start, col_width, 0).reshape(
+        col_width, tensor_count, col_width
+    )
+    weight_pack = (proj_mine, proj_other, out_mine, out_other, own_proj, own_out, head_gain)
+    recv_both, weight_pack = lax.optimization_barrier((recv_both, weight_pack))
+    proj_mine, proj_other, out_mine, out_other, own_proj, own_out, head_gain = weight_pack
+
     recv_len = jnp.sum(jnp.where(owners == dp_index, lengths, 0), axis=1)
     recv_start = exclusive_sum(recv_len)
     compact_ids = jnp.arange(owned_rows, dtype=jnp.int32)
@@ -67,8 +100,6 @@
     own_tokens = own_both[:, :col_width]
     own_cotan = own_both[:, col_width:]
 
-    half_count = tensor_count // 2
-    core = tensor_index % 2
     same_core = [[2 * z + c for z in range(half_count)] for c in range(2)]
     sibling = [(t, t ^ 1) for t in range(tensor_count)]
     mine = lax.all_gather(own_both, "tensor", axis=0, tiled=False, axis_index_groups=same_core)
@@ -76,38 +107,15 @@
     mine_tok, mine_cot = mine[..., :col_width], mine[..., col_width:]
     other_tok, other_cot = other[..., :col_width], other[..., col_width:]
 
-    def by_core(weight, axis):
-        split = weight.reshape(weight.shape[:axis] + (half_count, 2) + weight.shape[axis + 1 :])
-        return (
-            lax.dynamic_index_in_dim(split, core, axis + 1, keepdims=False),
-            lax.dynamic_index_in_dim(split, 1 - core, axis + 1, keepdims=False),
-        )
-
     def reduce_blocks(part):
         keep, send = by_core(part, 0)
         pair_sum = (keep.astype(f32) + lax.ppermute(send, "tensor", sibling).astype(f32)).astype(bf16)
         pieces = lax.all_to_all(pair_sum, "tensor", 0, 0, tiled=True, axis_index_groups=same_core)
         return jnp.sum(pieces.astype(f32), axis=0)
 
-    head_start = tensor_index * H // tensor_count * head_dim
-    own_start = tensor_index * col_width
-    inner_start = own_start - head_start
-    head_proj = lax.dynamic_slice_in_dim(proj_weight, head_start, head_dim, 2).reshape(
-        tensor_count, col_width, 4 * head_dim
-    )
-    own_proj = lax.dynamic_slice_in_dim(proj_weight, own_start, col_width, 2).reshape(
-        tensor_count, col_width, 4 * col_width
-    )
-    head_out = lax.dynamic_slice_in_dim(out_weight, head_start, head_dim, 0).reshape(
-        head_dim, tensor_count, col_width
-    )
-    head_gain = lax.dynamic_slice_in_dim(norm_gain, head_start, head_dim, 0)
-
-    proj_mine, proj_other = by_core(head_proj, 0)
     projected = jnp.einsum(
         "trc,tcn->rn", mine_tok, proj_mine, preferred_element_type=f32
     ) + jnp.einsum("trc,tcn->rn", other_tok, proj_other, preferred_element_type=f32)
-    out_mine, out_other = by_core(head_out, 1)
     down_grad = jnp.einsum(
         "trc,dtc->rd", mine_cot, out_mine, preferred_element_type=f32
     ) + jnp.einsum("trc,dtc->rd", other_cot, out_other, preferred_element_type=f32)
@@ -127,9 +135,6 @@
     normed = attended * inv_rms * head_gain
     gated = (normed * gating).astype(bf16)
     own_gated = lax.dynamic_slice_in_dim(gated, inner_start, col_width, 1)
-    own_out = lax.dynamic_slice_in_dim(out_weight, own_start, col_width, 0).reshape(
-        col_width, tensor_count, col_width
-    )
     out_part = jnp.einsum("rc,ctk->trk", own_gated, own_out, preferred_element_type=f32)
 
     d_normed = down_grad * gating

time: 107 us -> 98.6 us (0.921)
  waiting for transfers between devices: 27.9 us -> 23.1 us
  matrix products: 16.2 us -> 12.1 us
  local copies, waits for them, and re-layouts: 12.4 us -> 11.3 us
    all_to_all x1, waiting for transfers between devices: 6.23 us -> 0.01 us  [local(): lax.all_to_all(send_both, 'dp', split_axis=0, concat_axis=0, tiled=True)]
    ppermute x1, waiting for transfers between devices: 0.01 us -> 1.75 us  [local(): other = lax.ppermute(mine, 'tensor', sibling)]
    unnamed x20 -> x26, local copies, waits for them, and re-layouts: 3.35 us -> 2.19 us
    ppermute x2, starting transfers between devices: 2.73 us -> 3.84 us  [local(): lax.ppermute(send.astype(bf16), 'dp', partners).astype(f32)]
  transfers between devices with their start and end apart: 7 -> 7, of which waited for: 5 -> 5; matrix products, arithmetic and copies ran while one was open for 20% -> 18% of each run, Pallas kernels for 0% -> 0%
where the time goes in v8:
time: 98.6 us; the launch traced here: 97.8 us
  waiting for transfers between devices  23.1 us (23%)
  blocking collectives  21.3 us (22%)
  starting transfers between devices  16.7 us (17%)
  other arithmetic  12.2 us (12%)
  matrix products  12.1 us (12%)
  local copies, waits for them, and re-layouts  11.3 us (11%)
  between operations  1.14 us (1%)
    all_gather x1, blocking collectives, local(): lax.all_gather(own_both, 'tensor', axis=0, tiled=False, axis_index_groups...  21.3 us
    ppermute x2, waiting for transfers between devices, local(): lax.ppermute(send.astype(bf16), 'dp', partners).astype(f32)  15.3 us
    dot_general x5, matrix products, pick_rows(): return jnp.dot(one_hot, source, preferred_element_type=f32).astype(bf16)  6.02 us
    all_to_all x1, starting transfers between devices, local(): lax.all_to_all(send_both, 'dp', split_axis=0, concat_axis=0, tiled=True)  5.16 us
    all_to_all x1, waiting for transfers between devices, local(): lax.all_to_all(back_send, 'dp', split_axis=0, concat_axis=0, tiled=True)  4.49 us
    all_to_all x1, starting transfers between devices, reduce_blocks(): lax.all_to_all(pair_sum, 'tensor', 0, 0, tiled=True, axis_index_groups=sa...  4.2 us
    ppermute x2, starting transfers between devices, local(): lax.ppermute(send.astype(bf16), 'dp', partners).astype(f32)  3.84 us
    all_to_all x1, starting transfers between devices, local(): lax.all_to_all(back_send, 'dp', split_axis=0, concat_axis=0, tiled=True)  3.36 us
  transfers between devices with their start and end apart: 7, of which 5 were waited for; matrix products, arithmetic and copies ran while one was open for 18% of the time, Pallas kernels for 0%

profile of v8, /device:TPU:0, one launch (start us, length us, event | category | flops | bytes accessed | tf_op | source)
XLA Modules:
  0.0 97.8 jit_solution(7458660259193118711)
XLA Ops:
  0.7 1.4 %fusion.55 = (s32[]{:T(128)}, s32[1,4]{1,0:T(1,128)S(1)}) fusion(s32[4,4]{1,0:T(4,128)} %param.9, s32[]{:T(128)S(6)} %select_n.105), kind=kLoop, calls=%fused_computation.144 | loop fusion | flops 3 | bytes 40 | tf_op jit(solution)/shard_map/reduce_sum | solution.py:201
  2.2 0.7 fusion.54
  2.9 0.8 select_reduce_fusion.3
  3.9 0.7 fusion.15
  4.6 1.6 %fusion.16 = bf16[768,128]{0,1:T(8,128)(2,1)S(1)} fusion(bf16[672,128]{1,0:T(8,128)(2,1)} %param.8, s32[768]{0:T(1024)S(1)} %min.38), kind=kOutput, calls=%fused_computation.39 | convolution fusion | flops 132734976 | bytes 371712 | tf_op jit(solution)/shard_map/dot_general | solution.py:49
  6.3 0.9 copy.40
  7.2 5.2 %all-to-all-start = ((bf16[4,192,256]{2,1,0:T(8,128)(2,1)}), bf16[4,192,256]{2,1,0:T(8,128)(2,1)}, u32[]{:S(2)}, u32[]{:S(2)}) async-start(bf16[4,192,256]{2,1,0:T(8,128)(2,1)} %bitcast.4), calls=%async_computation | async-start | bytes 786432 | tf_op jit(solution)/shard_map/all_to_all | solution.py:55
  12.4 2.4 %constant_dynamic-slice_fusion.1 = (bf16[1024,4,128]{2,1,0:T(4,128)(2,1)S(1)}, bf16[1024,4,128]{2,1,0:T(4,128)(2,1)S(1)}) fusion(bf16[1024,4,1024]{2,1,0:T(4,128)(2,1)} %param.11, s32[]{:T(128)S(6)} %select_n.112, s32[]{:T(128)S(6)} %select_n.108), kind=kLoop, calls=%fused_computation.121 | loop fusion | bytes 4194312 | tf_op jit(solution)/shard_map/dynamic_slice | solution.py:73
  15.2 1.2 %reshape.178 = bf16[8,128,512]{2,1,0:T(8,128)(2,1)} reshape(bf16[1024,4,128]{2,1,0:T(4,128)(2,1)S(1)} %get-tuple-element.38) | data formatting | bytes 2097152 | tf_op jit(solution)/shard_map/reshape | solution.py:73
  16.5 1.1 %constant_dynamic-slice_fusion = (bf16[128,1024]{1,0:T(8,128)(2,1)S(1)}, bf16[128,1024]{1,0:T(8,128)(2,1)S(1)}) fusion(bf16[1024,1024]{1,0:T(8,128)(2,1)} %param.13, s32[]{:T(128)S(6)} %select_n.112, s32[]{:T(128)S(6)} %select_n.108), kind=kLoop, calls=%fused_computation.120 | loop fusion | bytes 1048584 | tf_op jit(solution)/shard_map/dynamic_slice | solution.py:83
  18.4 1.3 %dynamic_slice.68 = f32[128]{0:T(128)} dynamic-slice(f32[1024]{0:T(1024)} %param.12, s32[]{:T(128)S(6)} %select_n.108), dynamic_slice_sizes={128} | dynamic-slice | bytes 1028 | tf_op jit(solution)/shard_map/dynamic_slice | solution.py:79
  20.0 1.4 %fusion.11 = bf16[432,256]{1,0:T(8,128)(2,1)S(1)} fusion(bf16[768,256]{1,0:T(8,128)(2,1)} %bitcast.11, s32[432]{0:T(512)S(1)} %add_subtract_fusion), kind=kOutput, calls=%fused_computation.34 | convolution fusion | flops 170311680 | bytes 616128 | tf_op jit(solution)/shard_map/dot_general | solution.py:49
  21.4 21.3 %all-gather = bf16[1728,256]{1,0:T(8,128)(2,1)S(1)} all-gather(bf16[432,256]{1,0:T(8,128)(2,1)S(1)} %fusion.11), channel_id=2, replica_groups={{0,2,4,6},{1,3,5,7},{8,10,12,14},{9,11,13,15},{16,18,20,22},{17,19,21,2..., dimensions={0}, use_global_device_ids=true | all-gather | bytes 1105920 | tf_op jit(solution)/shard_map/all_gather | solution.py:105
  43.4 1.7 %collective-permute-done = bf16[4,432,256]{2,1,0:T(8,128)(2,1)S(1)} collective-permute-done((bf16[4,432,256]{2,1,0:T(8,128)(2,1)S(1)}, bf16[4,432,256]{2,1,0:T(8,128)(2,1)S(1)}, u32[]{:S(2)}, u32[]{:S(2)}) %collective-permute-start) | collective-permute-done | bytes 884768 | tf_op jit(solution)/shard_map/ppermute | solution.py:106
  50.8 1.1 %fusion.21 = bf16[4,432,256]{2,1,0:T(8,128)(2,1)} fusion(s32[]{:T(128)S(6)} %select_n.111, bf16[4,2,432,128]{3,2,1,0:T(8,128)(2,1)S(1)} %bitcast.152, bf16[4,2,432,128]{3,2,1,0:T(8,128)(2,1)S(1)} %bitcast.160), kind=kLoop, calls=%fused_computation.51 | loop fusion | flops 1769472 | bytes 2654212 | tf_op jit(solution)/shard_map/jit(dynamic_index_in_dim)/squeeze | solution.py:64
  53.8 2.1 %collective-permute-start.2 = (bf16[2,256,640]{2,1,0:T(8,128)(2,1)S(1)}, bf16[2,256,640]{2,1,0:T(8,128)(2,1)}, u32[]{:S(2)}, u32[]{:S(2)}) collective-permute-start(bf16[2,256,640]{2,1,0:T(8,128)(2,1)S(1)} %fusion.32), channel_id=1, source_target_pairs={{0,16},{8,24},{16,0},{24,8},{1,17},{9,25},{17,1},{25,9},{2,18},{10... | collective-permute-start | bytes 1966088 | tf_op jit(solution)/shard_map/ppermute | solution.py:187
  56.1 2.6 %fusion.4 = bf16[4,432,256]{2,1,0:T(8,128)(2,1)} fusion(bf16[4,432,256]{2,1,0:T(8,128)(2,1)} %collective-permute-done.1, s32[]{:T(128)S(6)} %select_n.110, bf16[4,2,432,128]{3,2,1,0:T(8,128)(2,1)} %bitcast.153, bf16[4,2,432,128]{3,2,1,0:T(8,128)(2,1)} %bitcast.161), kind=kLoop, calls=%fused_computation.13 | loop fusion | flops 3538944 | bytes 3538948 | tf_op jit(solution)/shard_map/convert_element_type | solution.py:112
  58.7 4.2 %all-to-all-start.1 = ((bf16[4,432,256]{2,1,0:T(8,128)(2,1)}), bf16[4,432,256]{2,1,0:T(8,128)(2,1)}, u32[]{:S(2)}, u32[]{:S(2)}) async-start(bf16[4,432,256]{2,1,0:T(8,128)(2,1)} %fusion.4), calls=%async_computation.1 | async-start | bytes 1769472 | tf_op jit(solution)/shard_map/all_to_all | solution.py:113
  62.9 8.3 %collective-permute-done.2 = bf16[2,256,640]{2,1,0:T(8,128)(2,1)} collective-permute-done((bf16[2,256,640]{2,1,0:T(8,128)(2,1)S(1)}, bf16[2,256,640]{2,1,0:T(8,128)(2,1)}, u32[]{:S(2)}, u32[]{:S(2)}) %collective-permute-start.2) | collective-permute-done | bytes 655392 | tf_op jit(solution)/shard_map/ppermute | solution.py:187
  71.2 1.2 %bitcast_add_fusion = f32[2,256,640]{2,1,0:T(8,128)S(1)} fusion(bf16[2,256,640]{2,1,0:T(8,128)(2,1)} %collective-permute-done.2, f32[2,2,256,640]{3,2,1,0:T(8,128)S(1)} %maximum_convert_fusion, s32[]{:T(128)S(6)} %select_n.122), kind=kLoop, calls=%fused_computation.30 | loop fusion | flops 655360 | bytes 3276804 | tf_op jit(solution)/shard_map/add | solution.py:187
  72.5 1.8 %collective-permute-start.3 = (bf16[256,640]{1,0:T(8,128)(2,1)S(1)}, bf16[256,640]{1,0:T(8,128)(2,1)S(1)}, u32[]{:S(2)}, u32[]{:S(2)}) collective-permute-start(bf16[256,640]{1,0:T(8,128)(2,1)S(1)} %fusion.45), channel_id=1, source_target_pairs={{0,8},{8,0},{16,24},{24,16},{1,9},{9,1},{17,25},{25,17},{2,10},{10... | collective-permute-start | bytes 983048 | tf_op jit(solution)/shard_map/ppermute | solution.py:187
  74.3 0.7 add_select_fusion
  75.0 7.0 %collective-permute-done.3 = bf16[256,640]{1,0:T(8,128)(2,1)S(1)} collective-permute-done((bf16[256,640]{1,0:T(8,128)(2,1)S(1)}, bf16[256,640]{1,0:T(8,128)(2,1)S(1)}, u32[]{:S(2)}, u32[]{:S(2)}) %collective-permute-start.3) | collective-permute-done | bytes 327712 | tf_op jit(solution)/shard_map/ppermute | solution.py:187
  82.3 1.0 %copy.52 = f32[256,4,128]{2,1,0:T(4,128)} copy(f32[256,4,128]{0,2,1:T(8,128)S(1)} %bitcast.162) | data formatting | bytes 1048576
  83.3 0.8 copy.53
  84.1 1.6 %all-to-all-done.1 = bf16[4,432,256]{2,1,0:T(8,128)(2,1)} async-done(((bf16[4,432,256]{2,1,0:T(8,128)(2,1)}), bf16[4,432,256]{2,1,0:T(8,128)(2,1)}, u32[]{:S(2)}, u32[]{:S(2)}) %all-to-all-start.1) | async-done | bytes 884768 | tf_op jit(solution)/shard_map/all_to_all | solution.py:113
  85.7 1.3 %convert_reduce_fusion = f32[432,256]{1,0:T(8,128)S(1)} fusion(bf16[4,432,256]{2,1,0:T(8,128)(2,1)} %all-to-all-done.1), kind=kLoop, calls=%fused_computation.14 | loop fusion | flops 774144 | bytes 1327104 | tf_op jit(solution)/shard_map/reduce_sum | solution.py:114
  87.0 1.1 %fusion.14 = bf16[768,128]{1,0:T(8,128)(2,1)} fusion(s32[768]{0:T(1024)S(1)} %min.43, f32[432,256]{1,0:T(8,128)S(1)} %convert_reduce_fusion, bf16[432,256]{1,0:T(8,128)(2,1)S(1)} %copy-done.5), kind=kOutput, calls=%fused_computation.37 | convolution fusion | flops 85530624 | bytes 532480 | tf_op jit(solution)/shard_map/dot_general | solution.py:49
  88.1 3.4 %all-to-all-start.2 = ((bf16[4,192,128]{2,1,0:T(8,128)(2,1)}), bf16[4,192,128]{2,1,0:T(8,128)(2,1)S(1)}, u32[]{:S(2)}, u32[]{:S(2)}) async-start(bf16[4,192,128]{2,1,0:T(8,128)(2,1)} %bitcast.34), calls=%async_computation.2 | async-start | bytes 393216 | tf_op jit(solution)/shard_map/all_to_all | solution.py:193
  91.5 0.7 fusion.49
  92.2 4.5 %all-to-all-done.2 = bf16[4,192,128]{2,1,0:T(8,128)(2,1)S(1)} async-done(((bf16[4,192,128]{2,1,0:T(8,128)(2,1)}), bf16[4,192,128]{2,1,0:T(8,128)(2,1)S(1)}, u32[]{:S(2)}, u32[]{:S(2)}) %all-to-all-start.2) | async-done | bytes 196640 | tf_op jit(solution)/shard_map/all_to_all | solution.py:193
  96.7 1.2 %fusion.17 = bf16[672,128]{1,0:T(8,128)(2,1)} fusion(bf16[768,128]{1,0:T(8,128)(2,1)S(1)} %bitcast.168, s32[672]{0:T(1024)S(1)} %add_select_fusion), kind=kOutput, calls=%fused_computation.42 | convolution fusion | flops 132722688 | bytes 371328 | tf_op jit(solution)/shard_map/dot_general | solution.py:49
  (83 shorter events, 10.5 us)
Async XLA Ops:
  0.6 3.3 %copy-start = (bf16[672,128]{1,0:T(8,128)(2,1)S(1)}, bf16[672,128]{1,0:T(8,128)(2,1)}, u32[]{:S(2)}) copy-start(bf16[672,128]{1,0:T(8,128)(2,1)} %param.7) | copy-start | bytes 516100
  2.2 1.5 %copy-start.6 = (s32[4]{0:T(128)}, s32[4]{0:T(128)S(1)}, u32[]{:S(2)}) copy-start(s32[4]{0:T(128)S(1)} %subtract_bitcast_fusion) | copy-start | bytes 52
  2.9 0.9 copy-start.9
  7.2 12.8 %all-to-all-start = ((bf16[4,192,256]{2,1,0:T(8,128)(2,1)}), bf16[4,192,256]{2,1,0:T(8,128)(2,1)}, u32[]{:S(2)}, u32[]{:S(2)}) async-start(bf16[4,192,256]{2,1,0:T(8,128)(2,1)} %bitcast.4), calls=%async_computation | async-start | bytes 786432 | tf_op jit(solution)/shard_map/all_to_all | solution.py:55
  21.4 21.3 %copy-start.4 = (bf16[432,256]{1,0:T(8,128)(2,1)}, bf16[432,256]{1,0:T(8,128)(2,1)S(1)}, u32[]{:S(2)}) copy-start(bf16[432,256]{1,0:T(8,128)(2,1)S(1)} %fusion.11) | copy-start | bytes 663556
  42.7 2.4 %collective-permute-start = (bf16[4,432,256]{2,1,0:T(8,128)(2,1)S(1)}, bf16[4,432,256]{2,1,0:T(8,128)(2,1)S(1)}, u32[]{:S(2)}, u32[]{:S(2)}) collective-permute-start(bf16[4,432,256]{2,1,0:T(8,128)(2,1)S(1)} %bitcast.154), channel_id=1, source_target_pairs={{0,1},{1,0},{2,3},{3,2},{4,5},{5,4},{6,7},{7,6},{8,9},{9,8},{10,11... | collective-permute-start | bytes 2654216 | tf_op jit(solution)/shard_map/ppermute | solution.py:106
  45.8 0.7 copy-start.8
  48.5 1.2 %copy-start.3 = (bf16[8,128,512]{2,1,0:T(8,128)(2,1)S(1)}, bf16[8,128,512]{2,1,0:T(8,128)(2,1)}, u32[]{:S(2)}) copy-start(bf16[8,128,512]{2,1,0:T(8,128)(2,1)} %reshape.178) | copy-start | bytes 3145732
  50.4 1.6 %copy-start.2 = (bf16[8,128,432]{1,2,0:T(8,128)(2,1)}, bf16[8,128,432]{1,2,0:T(8,128)(2,1)S(1)}, u32[]{:S(2)}) copy-start(bf16[8,128,432]{1,2,0:T(8,128)(2,1)S(1)} %convolution_convert_fusion) | copy-start | bytes 2654212
  50.8 1.8 %copy-start.1 = (bf16[8,128,432]{1,2,0:T(8,128)(2,1)}, bf16[8,128,432]{1,2,0:T(8,128)(2,1)S(1)}, u32[]{:S(2)}) copy-start(bf16[8,128,432]{1,2,0:T(8,128)(2,1)S(1)} %convolution_convert_fusion.1) | copy-start | bytes 2654212
  52.0 4.1 %collective-permute-start.1 = (bf16[4,432,256]{2,1,0:T(8,128)(2,1)}, bf16[4,432,256]{2,1,0:T(8,128)(2,1)}, u32[]{:S(2)}, u32[]{:S(2)}) collective-permute-start(bf16[4,432,256]{2,1,0:T(8,128)(2,1)} %fusion.21), channel_id=1, source_target_pairs={{0,1},{1,0},{2,3},{3,2},{4,5},{5,4},{6,7},{7,6},{8,9},{9,8},{10,11... | collective-permute-start | bytes 2654216 | tf_op jit(solution)/shard_map/ppermute | solution.py:112
  53.5 2.5 %copy-start.7 = (s32[4]{0:T(128)S(1)}, s32[4]{0:T(128)}, u32[]{:S(2)}) copy-start(s32[4]{0:T(128)} %copy-done.6) | copy-start | bytes 52
  53.8 17.4 %collective-permute-start.2 = (bf16[2,256,640]{2,1,0:T(8,128)(2,1)S(1)}, bf16[2,256,640]{2,1,0:T(8,128)(2,1)}, u32[]{:S(2)}, u32[]{:S(2)}) collective-permute-start(bf16[2,256,640]{2,1,0:T(8,128)(2,1)S(1)} %fusion.32), channel_id=1, source_target_pairs={{0,16},{8,24},{16,0},{24,8},{1,17},{9,25},{17,1},{25,9},{2,18},{10... | collective-permute-start | bytes 1966088 | tf_op jit(solution)/shard_map/ppermute | solution.py:187
  58.7 27.0 %all-to-all-start.1 = ((bf16[4,432,256]{2,1,0:T(8,128)(2,1)}), bf16[4,432,256]{2,1,0:T(8,128)(2,1)}, u32[]{:S(2)}, u32[]{:S(2)}) async-start(bf16[4,432,256]{2,1,0:T(8,128)(2,1)} %fusion.4), calls=%async_computation.1 | async-start | bytes 1769472 | tf_op jit(solution)/shard_map/all_to_all | solution.py:113
  62.9 11.4 %copy-start.10 = (s32[4]{0:T(128)S(1)}, s32[4]{0:T(128)}, u32[]{:S(2)}) copy-start(s32[4]{0:T(128)} %copy-done.9) | copy-start | bytes 52
  72.5 9.5 %collective-permute-start.3 = (bf16[256,640]{1,0:T(8,128)(2,1)S(1)}, bf16[256,640]{1,0:T(8,128)(2,1)S(1)}, u32[]{:S(2)}, u32[]{:S(2)}) collective-permute-start(bf16[256,640]{1,0:T(8,128)(2,1)S(1)} %fusion.45), channel_id=1, source_target_pairs={{0,8},{8,0},{16,24},{24,16},{1,9},{9,1},{17,25},{25,17},{2,10},{10... | collective-permute-start | bytes 983048 | tf_op jit(solution)/shard_map/ppermute | solution.py:187
  82.1 4.9 %copy-start.5 = (bf16[432,256]{1,0:T(8,128)(2,1)S(1)}, bf16[432,256]{1,0:T(8,128)(2,1)}, u32[]{:S(2)}) copy-start(bf16[432,256]{1,0:T(8,128)(2,1)} %copy-done.4) | copy-start | bytes 663556
  88.1 8.5 %all-to-all-start.2 = ((bf16[4,192,128]{2,1,0:T(8,128)(2,1)}), bf16[4,192,128]{2,1,0:T(8,128)(2,1)S(1)}, u32[]{:S(2)}, u32[]{:S(2)}) async-start(bf16[4,192,128]{2,1,0:T(8,128)(2,1)} %bitcast.34), calls=%async_computation.2 | async-start | bytes 393216 | tf_op jit(solution)/shard_map/all_to_all | solution.py:193

commit v9 on v8

--- a/solution.py
+++ b/solution.py
@@ -70,8 +70,15 @@
     head_proj = lax.dynamic_slice_in_dim(proj_weight, head_start, head_dim, 2).reshape(
         tensor_count, col_width, 4 * head_dim
     )
-    own_proj = lax.dynamic_slice_in_dim(proj_weight, own_start, col_width, 2).reshape(
-        tensor_count, col_width, 4 * col_width
+    sib_start = (tensor_index ^ 1) * col_width
+    dest_proj = by_core(proj_weight.reshape(tensor_count, col_width, 4, D), 0)[0]
+    pair_proj = jnp.stack(
+        [
+            lax.dynamic_slice_in_dim(dest_proj, start, col_width, 3).reshape(
+                half_count, col_width, 4 * col_width
+            )
+            for start in (own_start, sib_start)
+        ]
     )
     head_out = lax.dynamic_slice_in_dim(out_weight, head_start, head_dim, 0).reshape(
         head_dim, tensor_count, col_width
@@ -80,12 +87,13 @@
 
     proj_mine, proj_other = by_core(head_proj, 0)
     out_mine, out_other = by_core(head_out, 1)
-    own_out = lax.dynamic_slice_in_dim(out_weight, own_start, col_width, 0).reshape(
-        col_width, tensor_count, col_width
-    )
-    weight_pack = (proj_mine, proj_other, out_mine, out_other, own_proj, own_out, head_gain)
+    dest_out = by_core(out_weight.reshape(D, tensor_count, col_width), 1)[0]
+    pair_out = jnp.stack(
+        [lax.dynamic_slice_in_dim(dest_out, start, col_width, 0) for start in (own_start, sib_start)]
+    )
+    weight_pack = (proj_mine, proj_other, out_mine, out_other, pair_proj, pair_out, head_gain)
     recv_both, weight_pack = lax.optimization_barrier((recv_both, weight_pack))
-    proj_mine, proj_other, out_mine, out_other, own_proj, own_out, head_gain = weight_pack
+    proj_mine, proj_other, out_mine, out_other, pair_proj, pair_out, head_gain = weight_pack
 
     recv_len = jnp.sum(jnp.where(owners == dp_index, lengths, 0), axis=1)
     recv_start = exclusive_sum(recv_len)
@@ -108,9 +116,7 @@
     other_tok, other_cot = other[..., :col_width], other[..., col_width:]
 
     def reduce_blocks(part):
-        keep, send = by_core(part, 0)
-        pair_sum = (keep.astype(f32) + lax.ppermute(send, "tensor", sibling).astype(f32)).astype(bf16)
-        pieces = lax.all_to_all(pair_sum, "tensor", 0, 0, tiled=True, axis_index_groups=same_core)
+        pieces = lax.all_to_all(part, "tensor", 0, 0, tiled=True, axis_index_groups=same_core)
         return jnp.sum(pieces.astype(f32), axis=0)
 
     projected = jnp.einsum(
@@ -135,7 +141,8 @@
     normed = attended * inv_rms * head_gain
     gated = (normed * gating).astype(bf16)
     own_gated = lax.dynamic_slice_in_dim(gated, inner_start, col_width, 1)
-    out_part = jnp.einsum("rc,ctk->trk", own_gated, own_out, preferred_element_type=f32)
+    pair_gated = jnp.stack([own_gated, lax.ppermute(own_gated, "tensor", sibling)])
+    out_part = jnp.einsum("src,sczk->zrk", pair_gated, pair_out, preferred_element_type=f32)
 
     d_normed = down_grad * gating
     d_gating = down_grad * normed
@@ -156,7 +163,8 @@
     own_grad = lax.dynamic_slice_in_dim(d_projected, inner_start, col_width, 2).reshape(
         owned_rows, 4 * col_width
     )
-    grad_part = jnp.einsum("rn,tkn->trk", own_grad, own_proj, preferred_element_type=f32)
+    pair_grad = jnp.stack([own_grad, lax.ppermute(own_grad, "tensor", sibling)])
+    grad_part = jnp.einsum("srn,szkn->zrk", pair_grad, pair_proj, preferred_element_type=f32)
     both_sum = reduce_blocks(jnp.concatenate([out_part, grad_part], axis=2).astype(bf16))
     out_sum = both_sum[:, :col_width]
     grad_sum = both_sum[:, col_width:]

time: 98.6 us -> 110 us (1.12)
  local copies, waits for them, and re-layouts: 11.3 us -> 18.8 us
  matrix products: 12.1 us -> 16.1 us
    dynamic_slice x2 -> x4, local copies, waits for them, and re-layouts: 3.54 us -> 6.96 us  [the longest x1 2.36 us: local(): lax.dynamic_slice_in_dim(dest_proj, start, col_width, 3)]
    another operation x1 -> x2, local copies, waits for them, and re-layouts: 0.44 us -> 3.65 us  [by_core(): weight.reshape(weight.shape[:axis] + (half_count, 2) + weight.shape[axis...]
    convert_element_type x2 -> x1, other arithmetic: 2.83 us -> 0.25 us  [local(): gated = (normed * gating).astype(bf16)]
    another operation x4 -> x6, other arithmetic: 0.62 us -> 2.4 us  [the longest x1 1.08 us: local(): jnp.stack([lax.dynamic_slice_in_dim(dest_proj, start, col_width, 3).resha...]
    another operation x2 -> x5, local copies, waits for them, and re-layouts: 0.09 us -> 1.33 us  [the longest x2 1.19 us: local(): jnp.stack([lax.dynamic_slice_in_dim(dest_proj, start, col_width, 3).resha...]
    reshape x1 -> x0, local copies, waits for them, and re-layouts: 1.24 us -> none  [local(): lax.dynamic_slice_in_dim(proj_weight, own_start, col_width, 2)]
    squeeze x1 -> x0, other arithmetic: 1.14 us -> none  [by_core(): lax.dynamic_index_in_dim(split, 1 - core, axis + 1, keepdims=False)]
    unnamed x26 -> x25, local copies, waits for them, and re-layouts: 2.19 us -> 2.67 us
  transfers between devices with their start and end apart: 7 -> 8, of which waited for: 5 -> 5; matrix products, arithmetic and copies ran while one was open for 18% -> 27% of each run, Pallas kernels for 0% -> 0%
where the time goes in v9:
time: 110 us; the launch traced here: 109 us
  waiting for transfers between devices  22.8 us (21%)
  blocking collectives  21.5 us (20%)
  local copies, waits for them, and re-layouts  18.8 us (17%)
  starting transfers between devices  17.2 us (16%)
  matrix products  16.1 us (15%)
  other arithmetic  11.3 us (10%)
  between operations  1.14 us (1%)
    all_gather x1, blocking collectives, local(): lax.all_gather(own_both, 'tensor', axis=0, tiled=False, axis_index_groups...  21.5 us
    ppermute x2, waiting for transfers between devices, local(): lax.ppermute(send.astype(bf16), 'dp', partners).astype(f32)  15.6 us
    dot_general x5, matrix products, pick_rows(): return jnp.dot(one_hot, source, preferred_element_type=f32).astype(bf16)  6.03 us
    all_to_all x1, starting transfers between devices, local(): lax.all_to_all(send_both, 'dp', split_axis=0, concat_axis=0, tiled=True)  5.16 us
    all_to_all x1, waiting for transfers between devices, local(): lax.all_to_all(back_send, 'dp', split_axis=0, concat_axis=0, tiled=True)  4.49 us
    all_to_all x1, starting transfers between devices, reduce_blocks(): lax.all_to_all(part, 'tensor', 0, 0, tiled=True, axis_index_groups=same_c...  4.2 us
    ppermute x2, starting transfers between devices, local(): lax.ppermute(send.astype(bf16), 'dp', partners).astype(f32)  3.82 us
    another operation x2, local copies, waits for them, and re-layouts, by_core(): weight.reshape(weight.shape[:axis] + (half_count, 2) + weight.shape[axis...  3.65 us
  transfers between devices with their start and end apart: 8, of which 5 were waited for; matrix products, arithmetic and copies ran while one was open for 27% of the time, Pallas kernels for 0%

profile of v9, /device:TPU:0, one launch (start us, length us, event | category | flops | bytes accessed | tf_op | source)
XLA Modules:
  0.0 108.8 jit_solution(9941890813266725241)
XLA Ops:
  0.7 1.4 %fusion.60 = (s32[]{:T(128)}, s32[1,4]{1,0:T(1,128)S(1)}) fusion(s32[4,4]{1,0:T(4,128)} %param.9, s32[]{:T(128)S(6)} %select_n.116), kind=kLoop, calls=%fused_computation.153 | loop fusion | flops 3 | bytes 40 | tf_op jit(solution)/shard_map/reduce_sum | solution.py:209
  4.6 1.6 %fusion.19 = bf16[768,128]{0,1:T(8,128)(2,1)S(1)} fusion(bf16[672,128]{1,0:T(8,128)(2,1)} %param.8, s32[768]{0:T(1024)S(1)} %min.38), kind=kOutput, calls=%fused_computation.37 | convolution fusion | flops 132734976 | bytes 371712 | tf_op jit(solution)/shard_map/dot_general | solution.py:49
  6.3 0.9 copy.42
  7.2 5.2 %all-to-all-start = ((bf16[4,192,256]{2,1,0:T(8,128)(2,1)}), bf16[4,192,256]{2,1,0:T(8,128)(2,1)}, u32[]{:S(2)}, u32[]{:S(2)}) async-start(bf16[4,192,256]{2,1,0:T(8,128)(2,1)} %bitcast.4), calls=%async_computation | async-start | bytes 786432 | tf_op jit(solution)/shard_map/all_to_all | solution.py:55
  12.4 3.2 %reshape_reshape.15 = bf16[1024,4,2,128]{3,2,1,0:T(2,128)(2,1)S(1)} reshape(bf16[1024,1024]{1,0:T(8,128)(2,1)} %param.13) | data formatting | bytes 4194304 | tf_op jit(solution)/shard_map/reshape;reshape | solution.py:61
  15.6 1.7 %constant_dynamic-slice_fusion.6 = bf16[128,1024]{1,0:T(8,128)(2,1)} fusion(bf16[1024,1024]{1,0:T(8,128)(2,1)} %param.13, s32[]{:T(128)S(6)} %select_n.119), kind=kLoop, calls=%fused_computation.135 | loop fusion | bytes 524292 | tf_op jit(solution)/shard_map/dynamic_slice | solution.py:83
  17.3 1.6 %constant_dynamic-slice_fusion.7 = bf16[1024,4,128]{2,1,0:T(4,128)(2,1)S(1)} fusion(bf16[1024,4,1024]{2,1,0:T(4,128)(2,1)} %param.11, s32[]{:T(128)S(6)} %select_n.119), kind=kLoop, calls=%fused_computation.136 | loop fusion | bytes 2097156 | tf_op jit(solution)/shard_map/dynamic_slice | solution.py:70
  18.9 1.3 %constant_dynamic-slice_fusion.1 = (bf16[128,4,1,128]{3,2,1,0:T(2,128)(2,1)}, bf16[128,4,1,128]{3,2,1,0:T(2,128)(2,1)}) fusion(bf16[1024,4,2,128]{3,2,1,0:T(2,128)(2,1)S(1)} %reshape_reshape.15, s32[]{:T(128)S(6)} %select_n.125, s32[]{:T(128)S(6)} %select_n.123, s32[]{:T(128)S(6)} %select_n.127), kind=kLoop, calls=%fused_computation.130 | loop fusion | bytes 524300 | tf_op jit(solution)/shard_map/dynamic_slice | solution.py:92
  20.2 2.4 %constant_dynamic-slice_fusion.3 = (bf16[4,1,128,4,128]{4,3,2,1,0:T(4,128)(2,1)S(1)}, bf16[4,1,128,4,128]{4,3,2,1,0:T(4,128)(2,1)S(1)}) fusion(bf16[4,2,128,4,1024]{4,3,2,1,0:T(4,128)(2,1)} %bitcast.180, s32[]{:T(128)S(6)} %select_n.123, s32[]{:T(128)S(6)} %select_n.125, s32[]{:T(128)S(6)} %select_n.127), kind=kLoop, calls=%fused_computation.132 | loop fusion | bytes 2097164 | tf_op jit(solution)/shard_map/dynamic_slice | solution.py:77
  22.8 1.0 stack_reshape.8
  28.2 1.1 pad_maximum_fusion.1
  29.4 1.4 %fusion.14 = bf16[432,256]{1,0:T(8,128)(2,1)S(1)} fusion(bf16[768,256]{1,0:T(8,128)(2,1)} %bitcast.13, s32[432]{0:T(512)S(1)} %add_subtract_fusion), kind=kOutput, calls=%fused_computation.32 | convolution fusion | flops 170311680 | bytes 616128 | tf_op jit(solution)/shard_map/dot_general | solution.py:49
  30.8 21.5 %all-gather = bf16[1728,256]{1,0:T(8,128)(2,1)S(1)} all-gather(bf16[432,256]{1,0:T(8,128)(2,1)S(1)} %fusion.14), channel_id=2, replica_groups={{0,2,4,6},{1,3,5,7},{8,10,12,14},{9,11,13,15},{16,18,20,22},{17,19,21,2..., dimensions={0}, use_global_device_ids=true | all-gather | bytes 1105920 | tf_op jit(solution)/shard_map/all_gather | solution.py:113
  53.3 1.6 %collective-permute-done = bf16[4,432,256]{2,1,0:T(8,128)(2,1)} collective-permute-done((bf16[4,432,256]{2,1,0:T(8,128)(2,1)S(1)}, bf16[4,432,256]{2,1,0:T(8,128)(2,1)}, u32[]{:S(2)}, u32[]{:S(2)}) %collective-permute-start) | collective-permute-done | bytes 884768 | tf_op jit(solution)/shard_map/ppermute | solution.py:114
  54.9 1.4 %fusion.8 = f32[432,512]{1,0:T(8,128)S(1)} fusion(f32[432,512]{1,0:T(8,128)S(1)} %convolution_bitcast_fusion.5, bf16[4,128,512]{2,1,0:T(8,128)(2,1)S(1)} %copy-done.2, bf16[4,432,256]{2,1,0:T(8,128)(2,1)} %collective-permute-done), kind=kOutput, calls=%fused_computation.26 | convolution fusion | flops 226713600 | bytes 2736128 | tf_op jit(solution)/shard_map/trc,tcn->rn/dot_general | solution.py:124
  57.0 1.3 %fusion.21 = f32[432,128]{1,0:T(8,128)S(1)} fusion(f32[432,128]{1,0:T(8,128)S(1)} %convolution_bitcast_fusion.12, bf16[128,4,128]{2,0,1:T(8,128)(2,1)S(1)} %bitcast.181, bf16[4,432,256]{2,1,0:T(8,128)(2,1)} %collective-permute-done), kind=kOutput, calls=%fused_computation.46 | convolution fusion | flops 56678400 | bytes 1015808 | tf_op jit(solution)/shard_map/trc,dtc->rd/dot_general | solution.py:127
  62.1 1.5 %convolution_bitcast_fusion = bf16[4,1,128,512]{3,2,0,1:T(8,128)(2,1)S(1)} fusion(bf16[432,512]{1,0:T(8,128)(2,1)S(1)} %fusion.23, bf16[4,432,256]{2,1,0:T(8,128)(2,1)} %collective-permute-done), kind=kOutput, calls=%fused_computation.11 | convolution fusion | flops 226492416 | bytes 1409024 | tf_op jit(solution)/shard_map/trc,rn->tcn/dot_general | solution.py:181
  64.0 1.4 %convolution_bitcast_fusion.6 = bf16[4,1,128,128]{3,2,0,1:T(8,128)(2,1)S(1)} fusion(bf16[4,432,256]{2,1,0:T(8,128)(2,1)} %collective-permute-done, bf16[432,128]{1,0:T(8,128)(2,1)S(1)} %get-tuple-element.44), kind=kOutput, calls=%fused_computation.38 | convolution fusion | flops 56623104 | bytes 684032 | tf_op jit(solution)/shard_map/trc,rd->tcd/dot_general | solution.py:185
  65.8 2.0 %collective-permute-start.3 = (bf16[2,256,640]{2,1,0:T(8,128)(2,1)S(1)}, bf16[2,256,640]{2,1,0:T(8,128)(2,1)}, u32[]{:S(2)}, u32[]{:S(2)}) collective-permute-start(bf16[2,256,640]{2,1,0:T(8,128)(2,1)S(1)} %fusion.33), channel_id=1, source_target_pairs={{0,16},{8,24},{16,0},{24,8},{1,17},{9,25},{17,1},{25,9},{2,18},{10... | collective-permute-start | bytes 1966088 | tf_op jit(solution)/shard_map/ppermute | solution.py:195
  68.8 1.0 pad_maximum_fusion.2
  69.8 4.2 %all-to-all-start.1 = ((bf16[4,432,256]{2,1,0:T(8,128)(2,1)}), bf16[4,432,256]{2,1,0:T(8,128)(2,1)}, u32[]{:S(2)}, u32[]{:S(2)}) async-start(bf16[4,432,256]{2,1,0:T(8,128)(2,1)} %pad_maximum_fusion.2), calls=%async_computation.1 | async-start | bytes 1769472 | tf_op jit(solution)/shard_map/all_to_all | solution.py:119
  74.0 8.9 %collective-permute-done.3 = bf16[2,256,640]{2,1,0:T(8,128)(2,1)} collective-permute-done((bf16[2,256,640]{2,1,0:T(8,128)(2,1)S(1)}, bf16[2,256,640]{2,1,0:T(8,128)(2,1)}, u32[]{:S(2)}, u32[]{:S(2)}) %collective-permute-start.3) | collective-permute-done | bytes 655392 | tf_op jit(solution)/shard_map/ppermute | solution.py:195
  83.0 1.2 %bitcast_add_fusion = f32[2,256,640]{2,1,0:T(8,128)S(1)} fusion(bf16[2,256,640]{2,1,0:T(8,128)(2,1)} %collective-permute-done.3, f32[2,2,256,640]{3,2,1,0:T(8,128)S(1)} %maximum_convert_fusion, s32[]{:T(128)S(6)} %select_n.137), kind=kLoop, calls=%fused_computation.24 | loop fusion | flops 655360 | bytes 3276804 | tf_op jit(solution)/shard_map/add | solution.py:195
  84.2 1.8 %collective-permute-start.4 = (bf16[256,640]{1,0:T(8,128)(2,1)S(1)}, bf16[256,640]{1,0:T(8,128)(2,1)S(1)}, u32[]{:S(2)}, u32[]{:S(2)}) collective-permute-start(bf16[256,640]{1,0:T(8,128)(2,1)S(1)} %fusion.45), channel_id=1, source_target_pairs={{0,8},{8,0},{16,24},{24,16},{1,9},{9,1},{17,25},{25,17},{2,10},{10... | collective-permute-start | bytes 983048 | tf_op jit(solution)/shard_map/ppermute | solution.py:195
  86.8 6.7 %collective-permute-done.4 = bf16[256,640]{1,0:T(8,128)(2,1)S(1)} collective-permute-done((bf16[256,640]{1,0:T(8,128)(2,1)S(1)}, bf16[256,640]{1,0:T(8,128)(2,1)S(1)}, u32[]{:S(2)}, u32[]{:S(2)}) %collective-permute-start.4) | collective-permute-done | bytes 327712 | tf_op jit(solution)/shard_map/ppermute | solution.py:195
  93.8 1.0 copy.54
  95.6 1.0 all-to-all-done.1
  96.6 1.3 %convert_reduce_fusion = f32[432,256]{1,0:T(8,128)S(1)} fusion(bf16[4,432,256]{2,1,0:T(8,128)(2,1)} %all-to-all-done.1), kind=kLoop, calls=%fused_computation.8 | loop fusion | flops 774144 | bytes 1327104 | tf_op jit(solution)/shard_map/reduce_sum | solution.py:120
  98.0 1.1 %fusion.17 = bf16[768,128]{1,0:T(8,128)(2,1)} fusion(s32[768]{0:T(1024)S(1)} %min.43, f32[432,256]{1,0:T(8,128)S(1)} %convert_reduce_fusion, bf16[432,256]{1,0:T(8,128)(2,1)S(1)} %copy-done.10), kind=kOutput, calls=%fused_computation.35 | convolution fusion | flops 85530624 | bytes 532480 | tf_op jit(solution)/shard_map/dot_general | solution.py:49
  99.1 3.4 %all-to-all-start.2 = ((bf16[4,192,128]{2,1,0:T(8,128)(2,1)}), bf16[4,192,128]{2,1,0:T(8,128)(2,1)S(1)}, u32[]{:S(2)}, u32[]{:S(2)}) async-start(bf16[4,192,128]{2,1,0:T(8,128)(2,1)} %bitcast.40), calls=%async_computation.2 | async-start | bytes 393216 | tf_op jit(solution)/shard_map/all_to_all | solution.py:201
  103.1 4.5 %all-to-all-done.2 = bf16[4,192,128]{2,1,0:T(8,128)(2,1)S(1)} async-done(((bf16[4,192,128]{2,1,0:T(8,128)(2,1)}), bf16[4,192,128]{2,1,0:T(8,128)(2,1)S(1)}, u32[]{:S(2)}, u32[]{:S(2)}) %all-to-all-start.2) | async-done | bytes 196640 | tf_op jit(solution)/shard_map/all_to_all | solution.py:201
  107.6 1.2 %fusion.20 = bf16[672,128]{1,0:T(8,128)(2,1)} fusion(bf16[768,128]{1,0:T(8,128)(2,1)S(1)} %bitcast.183, s32[672]{0:T(1024)S(1)} %add_select_fusion), kind=kOutput, calls=%fused_computation.40 | convolution fusion | flops 132722688 | bytes 371328 | tf_op jit(solution)/shard_map/dot_general | solution.py:49
  (90 shorter events, 16.8 us)
Async XLA Ops:
  0.6 3.3 %copy-start = (bf16[672,128]{1,0:T(8,128)(2,1)S(1)}, bf16[672,128]{1,0:T(8,128)(2,1)}, u32[]{:S(2)}) copy-start(bf16[672,128]{1,0:T(8,128)(2,1)} %param.7) | copy-start | bytes 516100
  7.2 22.2 %all-to-all-start = ((bf16[4,192,256]{2,1,0:T(8,128)(2,1)}), bf16[4,192,256]{2,1,0:T(8,128)(2,1)}, u32[]{:S(2)}, u32[]{:S(2)}) async-start(bf16[4,192,256]{2,1,0:T(8,128)(2,1)} %bitcast.4), calls=%async_computation | async-start | bytes 786432 | tf_op jit(solution)/shard_map/all_to_all | solution.py:55
  22.6 1.7 %copy-start.6 = (bf16[128,1024]{1,0:T(8,128)(2,1)S(1)}, bf16[128,1024]{1,0:T(8,128)(2,1)}, u32[]{:S(2)}) copy-start(bf16[128,1024]{1,0:T(8,128)(2,1)} %constant_dynamic-slice_fusion.6) | copy-start | bytes 786436
  24.2 3.2 %copy-start.3 = (bf16[128,4,1,128]{3,2,1,0:T(2,128)(2,1)S(1)}, bf16[128,4,1,128]{3,2,1,0:T(2,128)(2,1)}, u32[]{:S(2)}) copy-start(bf16[128,4,1,128]{3,2,1,0:T(2,128)(2,1)} %get-tuple-element.40) | copy-start | bytes 393220
  24.2 3.2 %copy-start.4 = (bf16[128,4,1,128]{3,2,1,0:T(2,128)(2,1)S(1)}, bf16[128,4,1,128]{3,2,1,0:T(2,128)(2,1)}, u32[]{:S(2)}) copy-start(bf16[128,4,1,128]{3,2,1,0:T(2,128)(2,1)} %get-tuple-element.41) | copy-start | bytes 393220
  25.1 0.9 copy-start.8
  25.1 3.1 %copy-start.1 = (bf16[1,4,128,512]{3,2,0,1:T(8,128)(2,1)S(1)}, bf16[1,4,128,512]{3,2,0,1:T(8,128)(2,1)}, u32[]{:S(2)}) copy-start(bf16[1,4,128,512]{3,2,0,1:T(8,128)(2,1)} %stack_reshape.8) | copy-start | bytes 1572868
  30.8 21.7 %copy-start.9 = (bf16[432,256]{1,0:T(8,128)(2,1)}, bf16[432,256]{1,0:T(8,128)(2,1)S(1)}, u32[]{:S(2)}) copy-start(bf16[432,256]{1,0:T(8,128)(2,1)S(1)} %fusion.14) | copy-start | bytes 663556
  30.8 24.1 %copy-start.2 = (bf16[4,128,512]{2,1,0:T(8,128)(2,1)S(1)}, bf16[4,128,512]{2,1,0:T(8,128)(2,1)}, u32[]{:S(2)}) copy-start(bf16[4,128,512]{2,1,0:T(8,128)(2,1)} %get-tuple-element.15) | copy-start | bytes 1572868
  52.3 2.6 %collective-permute-start = (bf16[4,432,256]{2,1,0:T(8,128)(2,1)S(1)}, bf16[4,432,256]{2,1,0:T(8,128)(2,1)}, u32[]{:S(2)}, u32[]{:S(2)}) collective-permute-start(bf16[4,432,256]{2,1,0:T(8,128)(2,1)S(1)} %bitcast.169), channel_id=1, source_target_pairs={{0,1},{1,0},{2,3},{3,2},{4,5},{5,4},{6,7},{7,6},{8,9},{9,8},{10,11... | collective-permute-start | bytes 2654216 | tf_op jit(solution)/shard_map/ppermute | solution.py:114
  60.7 7.1 %collective-permute-start.1 = (bf16[432,128]{1,0:T(8,128)(2,1)S(1)}, bf16[432,128]{1,0:T(8,128)(2,1)S(1)}, u32[]{:S(2)}, u32[]{:S(2)}) collective-permute-start(bf16[432,128]{1,0:T(8,128)(2,1)S(1)} %get-tuple-element.44), channel_id=1, source_target_pairs={{0,1},{1,0},{2,3},{3,2},{4,5},{5,4},{6,7},{7,6},{8,9},{9,8},{10,11... | collective-permute-start | bytes 331784 | tf_op jit(solution)/shard_map/ppermute | solution.py:144
  61.7 6.4 %collective-permute-start.2 = (bf16[432,512]{1,0:T(8,128)(2,1)S(1)}, bf16[432,512]{1,0:T(8,128)(2,1)S(1)}, u32[]{:S(2)}, u32[]{:S(2)}) collective-permute-start(bf16[432,512]{1,0:T(8,128)(2,1)S(1)} %fusion.23), channel_id=1, source_target_pairs={{0,1},{1,0},{2,3},{3,2},{4,5},{5,4},{6,7},{7,6},{8,9},{9,8},{10,11... | collective-permute-start | bytes 1327112 | tf_op jit(solution)/shard_map/ppermute | solution.py:166
  65.5 2.3 %copy-start.5 = (bf16[2,128,4,128]{3,1,0,2:T(8,128)(2,1)S(1)}, bf16[2,128,4,128]{3,1,0,2:T(8,128)(2,1)}, u32[]{:S(2)}) copy-start(bf16[2,128,4,128]{3,1,0,2:T(8,128)(2,1)} %pad_maximum_fusion.5) | copy-start | bytes 786436
  65.7 2.4 %copy-start.7 = (bf16[2,4,128,512]{3,2,0,1:T(8,128)(2,1)S(1)}, bf16[2,4,128,512]{3,2,0,1:T(8,128)(2,1)}, u32[]{:S(2)}) copy-start(bf16[2,4,128,512]{3,2,0,1:T(8,128)(2,1)} %pad_maximum_fusion.1) | copy-start | bytes 3145732
  65.8 17.2 %collective-permute-start.3 = (bf16[2,256,640]{2,1,0:T(8,128)(2,1)S(1)}, bf16[2,256,640]{2,1,0:T(8,128)(2,1)}, u32[]{:S(2)}, u32[]{:S(2)}) collective-permute-start(bf16[2,256,640]{2,1,0:T(8,128)(2,1)S(1)} %fusion.33), channel_id=1, source_target_pairs={{0,16},{8,24},{16,0},{24,8},{1,17},{9,25},{17,1},{25,9},{2,18},{10... | collective-permute-start | bytes 1966088 | tf_op jit(solution)/shard_map/ppermute | solution.py:195
  69.8 26.8 %all-to-all-start.1 = ((bf16[4,432,256]{2,1,0:T(8,128)(2,1)}), bf16[4,432,256]{2,1,0:T(8,128)(2,1)}, u32[]{:S(2)}, u32[]{:S(2)}) async-start(bf16[4,432,256]{2,1,0:T(8,128)(2,1)} %pad_maximum_fusion.2), calls=%async_computation.1 | async-start | bytes 1769472 | tf_op jit(solution)/shard_map/all_to_all | solution.py:119
  84.2 9.2 %collective-permute-start.4 = (bf16[256,640]{1,0:T(8,128)(2,1)S(1)}, bf16[256,640]{1,0:T(8,128)(2,1)S(1)}, u32[]{:S(2)}, u32[]{:S(2)}) collective-permute-start(bf16[256,640]{1,0:T(8,128)(2,1)S(1)} %fusion.45), channel_id=1, source_target_pairs={{0,8},{8,0},{16,24},{24,16},{1,9},{9,1},{17,25},{25,17},{2,10},{10... | collective-permute-start | bytes 983048 | tf_op jit(solution)/shard_map/ppermute | solution.py:195
  93.6 4.3 %copy-start.10 = (bf16[432,256]{1,0:T(8,128)(2,1)S(1)}, bf16[432,256]{1,0:T(8,128)(2,1)}, u32[]{:S(2)}) copy-start(bf16[432,256]{1,0:T(8,128)(2,1)} %copy-done.9) | copy-start | bytes 663556
  99.1 8.5 %all-to-all-start.2 = ((bf16[4,192,128]{2,1,0:T(8,128)(2,1)}), bf16[4,192,128]{2,1,0:T(8,128)(2,1)S(1)}, u32[]{:S(2)}, u32[]{:S(2)}) async-start(bf16[4,192,128]{2,1,0:T(8,128)(2,1)} %bitcast.40), calls=%async_computation.2 | async-start | bytes 393216 | tf_op jit(solution)/shard_map/all_to_all | solution.py:201

commit v10 on v8

--- a/solution.py
+++ b/solution.py
@@ -44,6 +44,13 @@
     sent_to = my_owners[None, :] == peer_ids[:, None]
     send_start = jnp.sum(jnp.where(sent_to, my_starts[None, :], 0), axis=1)
     send_ids = jnp.minimum(send_start[:, None] + places[None, :], load_rows - 1)
+    def exchange(blocks):
+        pieces = [lax.dynamic_index_in_dim(blocks, dp_index, 0, keepdims=False)]
+        for k in range(1, dp_count):
+            outgoing = lax.dynamic_index_in_dim(blocks, dp_index ^ k, 0, keepdims=False)
+            pieces.append(lax.ppermute(outgoing, "dp", [(d, d ^ k) for d in range(dp_count)]))
+        return jnp.stack(pieces)
+
     def pick_rows(row_ids, source):
         one_hot = (row_ids[:, None] == jnp.arange(source.shape[0], dtype=jnp.int32)[None, :]).astype(bf16)
         return jnp.dot(one_hot, source, preferred_element_type=f32).astype(bf16)
@@ -52,7 +59,7 @@
     send_both = jnp.concatenate(
         [pick_rows(flat_send, tokens), pick_rows(flat_send, cotangent)], axis=1
     ).reshape(dp_count, MAXLEN, 2 * col_width)
-    recv_both = lax.all_to_all(send_both, "dp", split_axis=0, concat_axis=0, tiled=True)
+    recv_both = exchange(send_both)
 
     half_count = tensor_count // 2
     core = tensor_index % 2
@@ -95,7 +102,7 @@
     )
     slot_pick = compact_slot[:, None] == peer_ids[None, :]
     compact_start = jnp.sum(jnp.where(slot_pick, recv_start[None, :], 0), axis=1)
-    gather_ids = compact_slot * MAXLEN + compact_ids - compact_start
+    gather_ids = (compact_slot ^ dp_index) * MAXLEN + compact_ids - compact_start
     own_both = pick_rows(gather_ids, recv_both.reshape(dp_count * MAXLEN, 2 * col_width))
     own_tokens = own_both[:, :col_width]
     own_cotan = own_both[:, col_width:]
@@ -190,14 +197,14 @@
 
     back_src = jnp.minimum(recv_start[:, None] + places[None, :], owned_rows - 1)
     back_send = pick_rows(back_src.reshape(-1), token_rows).reshape(dp_count, MAXLEN, col_width)
-    back_grads = lax.all_to_all(back_send, "dp", split_axis=0, concat_axis=0, tiled=True)
+    back_grads = exchange(back_send)
     back_grads = back_grads.reshape(dp_count * MAXLEN, col_width)
     load_ids = jnp.arange(load_rows, dtype=jnp.int32)
     seq_of = jnp.sum((load_ids[:, None] >= my_starts[None, :]).astype(jnp.int32), axis=1) - 1
     seq_pick = seq_of[:, None] == seq_ids[None, :]
     owner_of = jnp.sum(jnp.where(seq_pick, my_owners[None, :], 0), axis=1)
     start_of = jnp.sum(jnp.where(seq_pick, my_starts[None, :], 0), axis=1)
-    back_ids = owner_of * MAXLEN + jnp.minimum(load_ids - start_of, MAXLEN - 1)
+    back_ids = (owner_of ^ dp_index) * MAXLEN + jnp.minimum(load_ids - start_of, MAXLEN - 1)
     row_used = load_ids < jnp.sum(my_lengths)
     token_grad = pick_rows(jnp.where(row_used, back_ids, -1), back_grads)
     return (mixed_out, token_grad, proj_grad, out_grad)

time: 98.6 us -> 96.7 us (0.981)
  matrix products: 12.1 us -> 10.5 us
  waiting for transfers between devices: 23.1 us -> 21.8 us
  starting transfers between devices: 16.7 us -> 15.5 us
  other arithmetic: 12.2 us -> 13.3 us
  local copies, waits for them, and re-layouts: 11.3 us -> 12.4 us
    all_to_all x2 -> x0, starting transfers between devices: 8.53 us -> none  [the longest x1 5.16 us: local(): lax.all_to_all(send_both, 'dp', split_axis=0, concat_axis=0, tiled=True)]
    ppermute x0 -> x6, starting transfers between devices: none -> 8.01 us  [exchange(): lax.ppermute(outgoing, 'dp', [(d, d ^ k) for d in range(dp_count)])]
    all_to_all x2 -> x0, waiting for transfers between devices: 4.49 us -> none  [the longest x1 4.49 us: local(): lax.all_to_all(back_send, 'dp', split_axis=0, concat_axis=0, tiled=True)]
    ppermute x0 -> x6, waiting for transfers between devices: none -> 3.03 us  [exchange(): lax.ppermute(outgoing, 'dp', [(d, d ^ k) for d in range(dp_count)])]
    dot_general x5, matrix products: 6.02 us -> 4.36 us  [pick_rows(): return jnp.dot(one_hot, source, preferred_element_type=f32).astype(bf16)]
    another operation x4 -> x6, other arithmetic: 0.62 us -> 1.69 us  [the longest x2 1.07 us: exchange(): return jnp.stack(pieces)]
    unnamed x26 -> x30, local copies, waits for them, and re-layouts: 2.19 us -> 2.64 us
  transfers between devices with their start and end apart: 7 -> 11, of which waited for: 5 -> 6; matrix products, arithmetic and copies ran while one was open for 18% -> 19% of each run, Pallas kernels for 0% -> 0%
where the time goes in v10:
time: 96.7 us; the launch traced here: 96.2 us
  waiting for transfers between devices  21.8 us (23%)
  blocking collectives  21.3 us (22%)
  starting transfers between devices  15.5 us (16%)
  other arithmetic  13.3 us (14%)
  local copies, waits for them, and re-layouts  12.4 us (13%)
  matrix products  10.5 us (11%)
  between operations  1.22 us (1%)
    all_gather x1, blocking collectives, local(): lax.all_gather(own_both, 'tensor', axis=0, tiled=False, axis_index_groups...  21.3 us
    ppermute x2, waiting for transfers between devices, local(): lax.ppermute(send.astype(bf16), 'dp', partners).astype(f32)  15.4 us
    ppermute x6, starting transfers between devices, exchange(): lax.ppermute(outgoing, 'dp', [(d, d ^ k) for d in range(dp_count)])  8.01 us
    dot_general x5, matrix products, pick_rows(): return jnp.dot(one_hot, source, preferred_element_type=f32).astype(bf16)  4.36 us
    all_to_all x1, starting transfers between devices, reduce_blocks(): lax.all_to_all(pair_sum, 'tensor', 0, 0, tiled=True, axis_index_groups=sa...  4.2 us
    ppermute x2, starting transfers between devices, local(): lax.ppermute(send.astype(bf16), 'dp', partners).astype(f32)  3.15 us
    ppermute x6, waiting for transfers between devices, exchange(): lax.ppermute(outgoing, 'dp', [(d, d ^ k) for d in range(dp_count)])  3.03 us
    unnamed x30, local copies, waits for them, and re-layouts  2.64 us
  transfers between devices with their start and end apart: 11, of which 6 were waited for; matrix products, arithmetic and copies ran while one was open for 19% of the time, Pallas kernels for 0%

profile of v10, /device:TPU:0, one launch (start us, length us, event | category | flops | bytes accessed | tf_op | source)
XLA Modules:
  0.0 96.2 jit_solution(3616856923539547478)
XLA Ops:
  0.7 1.4 %fusion.55 = (s32[]{:T(128)}, s32[1,4]{1,0:T(1,128)S(1)}) fusion(s32[4,4]{1,0:T(4,128)} %param.9, s32[]{:T(128)S(6)} %select_n.121), kind=kLoop, calls=%fused_computation.154 | loop fusion | flops 3 | bytes 40 | tf_op jit(solution)/shard_map/reduce_sum | solution.py:208
  3.0 0.8 select_reduce_fusion.3
  4.0 0.7 fusion.15
  4.7 1.6 %fusion.16 = bf16[768,128]{0,1:T(8,128)(2,1)S(1)} fusion(bf16[672,128]{1,0:T(8,128)(2,1)} %param.8, s32[768]{0:T(1024)S(1)} %min.38), kind=kOutput, calls=%fused_computation.39 | convolution fusion | flops 132734976 | bytes 371712 | tf_op jit(solution)/shard_map/dot_general | solution.py:56
  6.6 0.8 constant_dynamic-slice_fusion.7
  7.3 3.9 %collective-permute-start.2 = (bf16[192,256]{1,0:T(8,128)(2,1)}, bf16[192,256]{1,0:T(8,128)(2,1)}, u32[]{:S(2)}, u32[]{:S(2)}) collective-permute-start(bf16[192,256]{1,0:T(8,128)(2,1)} %get-tuple-element.48), channel_id=1, source_target_pairs={{0,24},{8,16},{16,8},{24,0},{1,25},{9,17},{17,9},{25,1},{2,26},{10... | collective-permute-start | bytes 294920 | tf_op jit(solution)/shard_map/ppermute | solution.py:51
  11.8 2.4 %constant_dynamic-slice_fusion.2 = (bf16[1024,4,128]{2,1,0:T(4,128)(2,1)S(1)}, bf16[1024,4,128]{2,1,0:T(4,128)(2,1)S(1)}) fusion(bf16[1024,4,1024]{2,1,0:T(4,128)(2,1)} %param.11, s32[]{:T(128)S(6)} %select_n.131, s32[]{:T(128)S(6)} %select_n.127), kind=kLoop, calls=%fused_computation.130 | loop fusion | bytes 4194312 | tf_op jit(solution)/shard_map/dynamic_slice | solution.py:80
  14.7 1.2 %reshape.180 = bf16[8,128,512]{2,1,0:T(8,128)(2,1)} reshape(bf16[1024,4,128]{2,1,0:T(4,128)(2,1)S(1)} %get-tuple-element.38) | data formatting | bytes 2097152 | tf_op jit(solution)/shard_map/reshape | solution.py:80
  15.9 1.1 %constant_dynamic-slice_fusion.1 = (bf16[128,1024]{1,0:T(8,128)(2,1)S(1)}, bf16[128,1024]{1,0:T(8,128)(2,1)S(1)}) fusion(bf16[1024,1024]{1,0:T(8,128)(2,1)} %param.13, s32[]{:T(128)S(6)} %select_n.131, s32[]{:T(128)S(6)} %select_n.127), kind=kLoop, calls=%fused_computation.129 | loop fusion | bytes 1048584 | tf_op jit(solution)/shard_map/dynamic_slice | solution.py:90
  17.4 0.8 copy.43
  18.4 1.3 %dynamic_slice.98 = f32[128]{0:T(128)} dynamic-slice(f32[1024]{0:T(1024)} %param.12, s32[]{:T(128)S(6)} %select_n.127), dynamic_slice_sizes={128} | dynamic-slice | bytes 1028 | tf_op jit(solution)/shard_map/dynamic_slice | solution.py:86
  20.2 1.0 %pad_maximum_fusion.3 = bf16[4,192,256]{2,1,0:T(8,128)(2,1)S(1)} fusion(bf16[1,192,256]{2,1,0:T(8,128)(2,1)} %bitcast.10, bf16[1,192,256]{2,1,0:T(8,128)(2,1)} %bitcast.8, bf16[1,192,256]{2,1,0:T(8,128)(2,1)} %bitcast.6, bf16[1,192,256]{2,1,0:T(8,128)(2,1)S(1)} %copy-done.7), kind=kLoop, calls=%fused_computation.81 | loop fusion | flops 589824 | bytes 786432 | tf_op jit(solution)/shard_map/stack | solution.py:52
  21.6 21.3 %all-gather = bf16[1728,256]{1,0:T(8,128)(2,1)S(1)} all-gather(bf16[432,256]{1,0:T(8,128)(2,1)S(1)} %fusion.11), channel_id=2, replica_groups={{0,2,4,6},{1,3,5,7},{8,10,12,14},{9,11,13,15},{16,18,20,22},{17,19,21,2..., dimensions={0}, use_global_device_ids=true | all-gather | bytes 1105920 | tf_op jit(solution)/shard_map/all_gather | solution.py:112
  43.6 1.7 %collective-permute-done.3 = bf16[4,432,256]{2,1,0:T(8,128)(2,1)S(1)} collective-permute-done((bf16[4,432,256]{2,1,0:T(8,128)(2,1)S(1)}, bf16[4,432,256]{2,1,0:T(8,128)(2,1)S(1)}, u32[]{:S(2)}, u32[]{:S(2)}) %collective-permute-start.3) | collective-permute-done | bytes 884768 | tf_op jit(solution)/shard_map/ppermute | solution.py:113
  51.5 1.1 %fusion.21 = bf16[4,432,256]{2,1,0:T(8,128)(2,1)} fusion(s32[]{:T(128)S(6)} %select_n.130, bf16[4,2,432,128]{3,2,1,0:T(8,128)(2,1)S(1)} %bitcast.170, bf16[4,2,432,128]{3,2,1,0:T(8,128)(2,1)S(1)} %bitcast.178), kind=kLoop, calls=%fused_computation.51 | loop fusion | flops 1769472 | bytes 2654212 | tf_op jit(solution)/shard_map/jit(dynamic_index_in_dim)/squeeze | solution.py:71
  54.5 1.6 %collective-permute-start.8 = (bf16[2,256,640]{2,1,0:T(8,128)(2,1)S(1)}, bf16[2,256,640]{2,1,0:T(8,128)(2,1)}, u32[]{:S(2)}, u32[]{:S(2)}) collective-permute-start(bf16[2,256,640]{2,1,0:T(8,128)(2,1)S(1)} %fusion.32), channel_id=1, source_target_pairs={{0,16},{8,24},{16,0},{24,8},{1,17},{9,25},{17,1},{25,9},{2,18},{10... | collective-permute-start | bytes 1966088 | tf_op jit(solution)/shard_map/ppermute | solution.py:194
  56.3 2.6 %fusion.4 = bf16[4,432,256]{2,1,0:T(8,128)(2,1)} fusion(bf16[4,432,256]{2,1,0:T(8,128)(2,1)} %collective-permute-done.4, s32[]{:T(128)S(6)} %select_n.129, bf16[4,2,432,128]{3,2,1,0:T(8,128)(2,1)} %bitcast.171, bf16[4,2,432,128]{3,2,1,0:T(8,128)(2,1)} %bitcast.179), kind=kLoop, calls=%fused_computation.13 | loop fusion | flops 3538944 | bytes 3538948 | tf_op jit(solution)/shard_map/convert_element_type | solution.py:119
  58.9 4.2 %all-to-all-start = ((bf16[4,432,256]{2,1,0:T(8,128)(2,1)}), bf16[4,432,256]{2,1,0:T(8,128)(2,1)}, u32[]{:S(2)}, u32[]{:S(2)}) async-start(bf16[4,432,256]{2,1,0:T(8,128)(2,1)} %fusion.4), calls=%async_computation | async-start | bytes 1769472 | tf_op jit(solution)/shard_map/all_to_all | solution.py:120
  63.1 8.5 %collective-permute-done.8 = bf16[2,256,640]{2,1,0:T(8,128)(2,1)} collective-permute-done((bf16[2,256,640]{2,1,0:T(8,128)(2,1)S(1)}, bf16[2,256,640]{2,1,0:T(8,128)(2,1)}, u32[]{:S(2)}, u32[]{:S(2)}) %collective-permute-start.8) | collective-permute-done | bytes 655392 | tf_op jit(solution)/shard_map/ppermute | solution.py:194
  71.6 1.2 %bitcast_add_fusion = f32[2,256,640]{2,1,0:T(8,128)S(1)} fusion(bf16[2,256,640]{2,1,0:T(8,128)(2,1)} %collective-permute-done.8, f32[2,2,256,640]{3,2,1,0:T(8,128)S(1)} %maximum_convert_fusion, s32[]{:T(128)S(6)} %select_n.141), kind=kLoop, calls=%fused_computation.30 | loop fusion | flops 655360 | bytes 3276804 | tf_op jit(solution)/shard_map/add | solution.py:194
  72.9 1.6 %collective-permute-start.9 = (bf16[256,640]{1,0:T(8,128)(2,1)S(1)}, bf16[256,640]{1,0:T(8,128)(2,1)S(1)}, u32[]{:S(2)}, u32[]{:S(2)}) collective-permute-start(bf16[256,640]{1,0:T(8,128)(2,1)S(1)} %fusion.45), channel_id=1, source_target_pairs={{0,8},{8,0},{16,24},{24,16},{1,9},{9,1},{17,25},{25,17},{2,10},{10... | collective-permute-start | bytes 983048 | tf_op jit(solution)/shard_map/ppermute | solution.py:194
  75.2 6.9 %collective-permute-done.9 = bf16[256,640]{1,0:T(8,128)(2,1)S(1)} collective-permute-done((bf16[256,640]{1,0:T(8,128)(2,1)S(1)}, bf16[256,640]{1,0:T(8,128)(2,1)S(1)}, u32[]{:S(2)}, u32[]{:S(2)}) %collective-permute-start.9) | collective-permute-done | bytes 327712 | tf_op jit(solution)/shard_map/ppermute | solution.py:194
  82.5 1.0 %copy.52 = f32[256,4,128]{2,1,0:T(4,128)} copy(f32[256,4,128]{0,2,1:T(8,128)S(1)} %bitcast.180) | data formatting | bytes 1048576
  83.5 0.8 copy.53
  84.2 1.6 %all-to-all-done = bf16[4,432,256]{2,1,0:T(8,128)(2,1)} async-done(((bf16[4,432,256]{2,1,0:T(8,128)(2,1)}), bf16[4,432,256]{2,1,0:T(8,128)(2,1)}, u32[]{:S(2)}, u32[]{:S(2)}) %all-to-all-start) | async-done | bytes 884768 | tf_op jit(solution)/shard_map/all_to_all | solution.py:120
  85.9 1.3 %convert_reduce_fusion = f32[432,256]{1,0:T(8,128)S(1)} fusion(bf16[4,432,256]{2,1,0:T(8,128)(2,1)} %all-to-all-done), kind=kLoop, calls=%fused_computation.14 | loop fusion | flops 774144 | bytes 1327104 | tf_op jit(solution)/shard_map/reduce_sum | solution.py:121
  87.7 1.6 %collective-permute-start.5 = (bf16[192,128]{1,0:T(8,128)(2,1)S(1)}, bf16[192,128]{1,0:T(8,128)(2,1)S(1)}, u32[]{:S(2)}, u32[]{:S(2)}) collective-permute-start(bf16[192,128]{1,0:T(8,128)(2,1)S(1)} %get-tuple-element.56), channel_id=1, source_target_pairs={{0,8},{8,0},{16,24},{24,16},{1,9},{9,1},{17,25},{25,17},{2,10},{10... | collective-permute-start | bytes 147464 | tf_op jit(solution)/shard_map/ppermute | solution.py:51
  89.2 0.7 collective-permute-start.6
  90.0 1.3 %collective-permute-start.7 = (bf16[192,128]{1,0:T(8,128)(2,1)S(1)}, bf16[192,128]{1,0:T(8,128)(2,1)S(1)}, u32[]{:S(2)}, u32[]{:S(2)}) collective-permute-start(bf16[192,128]{1,0:T(8,128)(2,1)S(1)} %get-tuple-element.54), channel_id=1, source_target_pairs={{0,24},{8,16},{16,8},{24,0},{1,25},{9,17},{17,9},{25,1},{2,26},{10... | collective-permute-start | bytes 147464 | tf_op jit(solution)/shard_map/ppermute | solution.py:51
  91.9 1.4 %collective-permute-done.6 = bf16[192,128]{1,0:T(8,128)(2,1)S(1)} collective-permute-done((bf16[192,128]{1,0:T(8,128)(2,1)S(1)}, bf16[192,128]{1,0:T(8,128)(2,1)S(1)}, u32[]{:S(2)}, u32[]{:S(2)}) %collective-permute-start.6) | collective-permute-done | bytes 49184 | tf_op jit(solution)/shard_map/ppermute | solution.py:51
  93.3 1.6 %collective-permute-done.7 = bf16[192,128]{1,0:T(8,128)(2,1)S(1)} collective-permute-done((bf16[192,128]{1,0:T(8,128)(2,1)S(1)}, bf16[192,128]{1,0:T(8,128)(2,1)S(1)}, u32[]{:S(2)}, u32[]{:S(2)}) %collective-permute-start.7) | collective-permute-done | bytes 49184 | tf_op jit(solution)/shard_map/ppermute | solution.py:51
  95.0 1.2 %fusion.17 = bf16[672,128]{1,0:T(8,128)(2,1)} fusion(bf16[768,128]{1,0:T(8,128)(2,1)S(1)} %bitcast.189, s32[672]{0:T(1024)S(1)} %add_select_fusion), kind=kOutput, calls=%fused_computation.42 | convolution fusion | flops 132722688 | bytes 371328 | tf_op jit(solution)/shard_map/dot_general | solution.py:56
  (99 shorter events, 14.5 us)
Async XLA Ops:
  0.6 3.4 %copy-start = (bf16[672,128]{1,0:T(8,128)(2,1)S(1)}, bf16[672,128]{1,0:T(8,128)(2,1)}, u32[]{:S(2)}) copy-start(bf16[672,128]{1,0:T(8,128)(2,1)} %param.7) | copy-start | bytes 516100
  2.3 1.5 %copy-start.8 = (s32[4]{0:T(128)}, s32[4]{0:T(128)S(1)}, u32[]{:S(2)}) copy-start(s32[4]{0:T(128)S(1)} %subtract_bitcast_fusion) | copy-start | bytes 52
  3.0 0.9 copy-start.11
  7.3 12.8 %collective-permute-start.2 = (bf16[192,256]{1,0:T(8,128)(2,1)}, bf16[192,256]{1,0:T(8,128)(2,1)}, u32[]{:S(2)}, u32[]{:S(2)}) collective-permute-start(bf16[192,256]{1,0:T(8,128)(2,1)} %get-tuple-element.48), channel_id=1, source_target_pairs={{0,24},{8,16},{16,8},{24,0},{1,25},{9,17},{17,9},{25,1},{2,26},{10... | collective-permute-start | bytes 294920 | tf_op jit(solution)/shard_map/ppermute | solution.py:51
  11.2 8.9 %collective-permute-start = (bf16[192,256]{1,0:T(8,128)(2,1)}, bf16[192,256]{1,0:T(8,128)(2,1)}, u32[]{:S(2)}, u32[]{:S(2)}) collective-permute-start(bf16[192,256]{1,0:T(8,128)(2,1)} %get-tuple-element.50), channel_id=1, source_target_pairs={{0,8},{8,0},{16,24},{24,16},{1,9},{9,1},{17,25},{25,17},{2,10},{10... | collective-permute-start | bytes 294920 | tf_op jit(solution)/shard_map/ppermute | solution.py:51
  11.8 8.4 %collective-permute-start.1 = (bf16[192,256]{1,0:T(8,128)(2,1)}, bf16[192,256]{1,0:T(8,128)(2,1)}, u32[]{:S(2)}, u32[]{:S(2)}) collective-permute-start(bf16[192,256]{1,0:T(8,128)(2,1)} %get-tuple-element.49), channel_id=1, source_target_pairs={{0,16},{8,24},{16,0},{24,8},{1,17},{9,25},{17,1},{25,9},{2,18},{10... | collective-permute-start | bytes 294920 | tf_op jit(solution)/shard_map/ppermute | solution.py:51
  17.2 2.9 %copy-start.7 = (bf16[1,192,256]{2,1,0:T(8,128)(2,1)S(1)}, bf16[1,192,256]{2,1,0:T(8,128)(2,1)}, u32[]{:S(2)}) copy-start(bf16[1,192,256]{2,1,0:T(8,128)(2,1)} %get-tuple-element.47) | copy-start | bytes 294916
  21.6 21.3 %copy-start.5 = (bf16[432,256]{1,0:T(8,128)(2,1)}, bf16[432,256]{1,0:T(8,128)(2,1)S(1)}, u32[]{:S(2)}) copy-start(bf16[432,256]{1,0:T(8,128)(2,1)S(1)} %fusion.11) | copy-start | bytes 663556
  42.9 2.4 %collective-permute-start.3 = (bf16[4,432,256]{2,1,0:T(8,128)(2,1)S(1)}, bf16[4,432,256]{2,1,0:T(8,128)(2,1)S(1)}, u32[]{:S(2)}, u32[]{:S(2)}) collective-permute-start(bf16[4,432,256]{2,1,0:T(8,128)(2,1)S(1)} %bitcast.172), channel_id=1, source_target_pairs={{0,1},{1,0},{2,3},{3,2},{4,5},{5,4},{6,7},{7,6},{8,9},{9,8},{10,11... | collective-permute-start | bytes 2654216 | tf_op jit(solution)/shard_map/ppermute | solution.py:113
  46.0 0.9 copy-start.4
  46.0 1.2 %copy-start.10 = (f32[128]{0:T(128)S(1)}, f32[128]{0:T(128)}, u32[]{:S(2)}) copy-start(f32[128]{0:T(128)} %dynamic_slice.98) | copy-start | bytes 1540
  49.2 1.2 %copy-start.3 = (bf16[8,128,512]{2,1,0:T(8,128)(2,1)S(1)}, bf16[8,128,512]{2,1,0:T(8,128)(2,1)}, u32[]{:S(2)}) copy-start(bf16[8,128,512]{2,1,0:T(8,128)(2,1)} %reshape.180) | copy-start | bytes 3145732
  51.1 1.5 %copy-start.2 = (bf16[8,128,432]{1,2,0:T(8,128)(2,1)}, bf16[8,128,432]{1,2,0:T(8,128)(2,1)S(1)}, u32[]{:S(2)}) copy-start(bf16[8,128,432]{1,2,0:T(8,128)(2,1)S(1)} %convolution_convert_fusion) | copy-start | bytes 2654212
  51.5 1.7 %copy-start.1 = (bf16[8,128,432]{1,2,0:T(8,128)(2,1)}, bf16[8,128,432]{1,2,0:T(8,128)(2,1)S(1)}, u32[]{:S(2)}) copy-start(bf16[8,128,432]{1,2,0:T(8,128)(2,1)S(1)} %convolution_convert_fusion.1) | copy-start | bytes 2654212
  52.7 3.6 %collective-permute-start.4 = (bf16[4,432,256]{2,1,0:T(8,128)(2,1)}, bf16[4,432,256]{2,1,0:T(8,128)(2,1)}, u32[]{:S(2)}, u32[]{:S(2)}) collective-permute-start(bf16[4,432,256]{2,1,0:T(8,128)(2,1)} %fusion.21), channel_id=1, source_target_pairs={{0,1},{1,0},{2,3},{3,2},{4,5},{5,4},{6,7},{7,6},{8,9},{9,8},{10,11... | collective-permute-start | bytes 2654216 | tf_op jit(solution)/shard_map/ppermute | solution.py:119
  54.2 2.0 %copy-start.9 = (s32[4]{0:T(128)S(1)}, s32[4]{0:T(128)}, u32[]{:S(2)}) copy-start(s32[4]{0:T(128)} %copy-done.8) | copy-start | bytes 52
  54.5 17.2 %collective-permute-start.8 = (bf16[2,256,640]{2,1,0:T(8,128)(2,1)S(1)}, bf16[2,256,640]{2,1,0:T(8,128)(2,1)}, u32[]{:S(2)}, u32[]{:S(2)}) collective-permute-start(bf16[2,256,640]{2,1,0:T(8,128)(2,1)S(1)} %fusion.32), channel_id=1, source_target_pairs={{0,16},{8,24},{16,0},{24,8},{1,17},{9,25},{17,1},{25,9},{2,18},{10... | collective-permute-start | bytes 1966088 | tf_op jit(solution)/shard_map/ppermute | solution.py:194
  58.9 27.0 %all-to-all-start = ((bf16[4,432,256]{2,1,0:T(8,128)(2,1)}), bf16[4,432,256]{2,1,0:T(8,128)(2,1)}, u32[]{:S(2)}, u32[]{:S(2)}) async-start(bf16[4,432,256]{2,1,0:T(8,128)(2,1)} %fusion.4), calls=%async_computation | async-start | bytes 1769472 | tf_op jit(solution)/shard_map/all_to_all | solution.py:120
  63.1 11.4 %copy-start.12 = (s32[4]{0:T(128)S(1)}, s32[4]{0:T(128)}, u32[]{:S(2)}) copy-start(s32[4]{0:T(128)} %copy-done.11) | copy-start | bytes 52
  72.9 9.2 %collective-permute-start.9 = (bf16[256,640]{1,0:T(8,128)(2,1)S(1)}, bf16[256,640]{1,0:T(8,128)(2,1)S(1)}, u32[]{:S(2)}, u32[]{:S(2)}) collective-permute-start(bf16[256,640]{1,0:T(8,128)(2,1)S(1)} %fusion.45), channel_id=1, source_target_pairs={{0,8},{8,0},{16,24},{24,16},{1,9},{9,1},{17,25},{25,17},{2,10},{10... | collective-permute-start | bytes 983048 | tf_op jit(solution)/shard_map/ppermute | solution.py:194
  82.3 4.9 %copy-start.6 = (bf16[432,256]{1,0:T(8,128)(2,1)S(1)}, bf16[432,256]{1,0:T(8,128)(2,1)}, u32[]{:S(2)}) copy-start(bf16[432,256]{1,0:T(8,128)(2,1)} %copy-done.5) | copy-start | bytes 663556
  87.7 4.2 %collective-permute-start.5 = (bf16[192,128]{1,0:T(8,128)(2,1)S(1)}, bf16[192,128]{1,0:T(8,128)(2,1)S(1)}, u32[]{:S(2)}, u32[]{:S(2)}) collective-permute-start(bf16[192,128]{1,0:T(8,128)(2,1)S(1)} %get-tuple-element.56), channel_id=1, source_target_pairs={{0,8},{8,0},{16,24},{24,16},{1,9},{9,1},{17,25},{25,17},{2,10},{10... | collective-permute-start | bytes 147464 | tf_op jit(solution)/shard_map/ppermute | solution.py:51
  89.2 4.1 %collective-permute-start.6 = (bf16[192,128]{1,0:T(8,128)(2,1)S(1)}, bf16[192,128]{1,0:T(8,128)(2,1)S(1)}, u32[]{:S(2)}, u32[]{:S(2)}) collective-permute-start(bf16[192,128]{1,0:T(8,128)(2,1)S(1)} %get-tuple-element.55), channel_id=1, source_target_pairs={{0,16},{8,24},{16,0},{24,8},{1,17},{9,25},{17,1},{25,9},{2,18},{10... | collective-permute-start | bytes 147464 | tf_op jit(solution)/shard_map/ppermute | solution.py:51
  90.0 5.0 %collective-permute-start.7 = (bf16[192,128]{1,0:T(8,128)(2,1)S(1)}, bf16[192,128]{1,0:T(8,128)(2,1)S(1)}, u32[]{:S(2)}, u32[]{:S(2)}) collective-permute-start(bf16[192,128]{1,0:T(8,128)(2,1)S(1)} %get-tuple-element.54), channel_id=1, source_target_pairs={{0,24},{8,16},{16,8},{24,0},{1,25},{9,17},{17,9},{25,1},{2,26},{10... | collective-permute-start | bytes 147464 | tf_op jit(solution)/shard_map/ppermute | solution.py:51

commit v11 on v10

--- a/solution.py
+++ b/solution.py
@@ -117,8 +117,13 @@
     def reduce_blocks(part):
         keep, send = by_core(part, 0)
         pair_sum = (keep.astype(f32) + lax.ppermute(send, "tensor", sibling).astype(f32)).astype(bf16)
-        pieces = lax.all_to_all(pair_sum, "tensor", 0, 0, tiled=True, axis_index_groups=same_core)
-        return jnp.sum(pieces.astype(f32), axis=0)
+        chip = tensor_index // 2
+        total = lax.dynamic_index_in_dim(pair_sum, chip, 0, keepdims=False).astype(f32)
+        for k in range(1, half_count):
+            outgoing = lax.dynamic_index_in_dim(pair_sum, chip ^ k, 0, keepdims=False)
+            partners = [(t, ((t // 2) ^ k) * 2 + t % 2) for t in range(tensor_count)]
+            total = total + lax.ppermute(outgoing, "tensor", partners).astype(f32)
+        return total
 
     projected = jnp.einsum(
         "trc,tcn->rn", mine_tok, proj_mine, preferred_element_type=f32

time: 96.7 us -> 100 us (1.034)
  waiting for transfers between devices: 21.8 us -> 30.1 us
  other arithmetic: 13.3 us -> 8.49 us
    ppermute x0 -> x3, waiting for transfers between devices: none -> 10.6 us  [reduce_blocks(): total = total + lax.ppermute(outgoing, 'tensor', partners).astype(f32)]
    ppermute x0 -> x3, starting transfers between devices: none -> 4.39 us  [reduce_blocks(): total = total + lax.ppermute(outgoing, 'tensor', partners).astype(f32)]
    all_to_all x1 -> x0, starting transfers between devices: 4.2 us -> none  [reduce_blocks(): lax.all_to_all(pair_sum, 'tensor', 0, 0, tiled=True, axis_index_groups=sa...]
    convert_element_type x1, other arithmetic: 2.57 us -> 0.26 us  [reduce_blocks(): (keep.astype(f32) + lax.ppermute(send, 'tensor', sibling).astype(f32)).as...]
    all_to_all x1 -> x0, waiting for transfers between devices: 1.63 us -> none  [reduce_blocks(): lax.all_to_all(pair_sum, 'tensor', 0, 0, tiled=True, axis_index_groups=sa...]
    reduce_sum x1 -> x0, other arithmetic: 1.33 us -> none  [reduce_blocks(): return jnp.sum(pieces.astype(f32), axis=0)]
    add x2, other arithmetic: 1.29 us -> 0.17 us  [local(): keep + lax.ppermute(send.astype(bf16), 'dp', partners).astype(f32)]
    add x0 -> x1, other arithmetic: none -> 1.05 us  [reduce_blocks(): total = total + lax.ppermute(outgoing, 'tensor', partners).astype(f32)]
  transfers between devices with their start and end apart: 11 -> 13, of which waited for: 6 -> 7; matrix products, arithmetic and copies ran while one was open for 19% -> 15% of each run, Pallas kernels for 0% -> 0%
where the time goes in v11:
time: 100 us; the launch traced here: 99.6 us
  waiting for transfers between devices  30.1 us (30%)
  blocking collectives  21.5 us (22%)
  starting transfers between devices  15.6 us (16%)
  local copies, waits for them, and re-layouts  12.2 us (12%)
  matrix products  10.5 us (10%)
  other arithmetic  8.49 us (8%)
  between operations  1.13 us (1%)
    all_gather x1, blocking collectives, local(): lax.all_gather(own_both, 'tensor', axis=0, tiled=False, axis_index_groups...  21.5 us
    ppermute x2, waiting for transfers between devices, local(): lax.ppermute(send.astype(bf16), 'dp', partners).astype(f32)  15.1 us
    ppermute x3, waiting for transfers between devices, reduce_blocks(): total = total + lax.ppermute(outgoing, 'tensor', partners).astype(f32)  10.6 us
    ppermute x6, starting transfers between devices, exchange(): lax.ppermute(outgoing, 'dp', [(d, d ^ k) for d in range(dp_count)])  8.01 us
    ppermute x3, starting transfers between devices, reduce_blocks(): total = total + lax.ppermute(outgoing, 'tensor', partners).astype(f32)  4.39 us
    dot_general x5, matrix products, pick_rows(): return jnp.dot(one_hot, source, preferred_element_type=f32).astype(bf16)  4.37 us
    ppermute x2, starting transfers between devices, local(): lax.ppermute(send.astype(bf16), 'dp', partners).astype(f32)  3.14 us
    ppermute x6, waiting for transfers between devices, exchange(): lax.ppermute(outgoing, 'dp', [(d, d ^ k) for d in range(dp_count)])  2.89 us
  transfers between devices with their start and end apart: 13, of which 7 were waited for; matrix products, arithmetic and copies ran while one was open for 15% of the time, Pallas kernels for 0%

profile of v11, /device:TPU:0, one launch (start us, length us, event | category | flops | bytes accessed | tf_op | source)
XLA Modules:
  0.0 99.6 jit_solution(4108488576214891130)
XLA Ops:
  0.7 1.4 %fusion.57 = (s32[]{:T(128)}, s32[1,4]{1,0:T(1,128)S(1)}) fusion(s32[4,4]{1,0:T(4,128)} %param.9, s32[]{:T(128)S(6)} %select_n.137), kind=kLoop, calls=%fused_computation.159 | loop fusion | flops 3 | bytes 40 | tf_op jit(solution)/shard_map/reduce_sum | solution.py:213
  2.2 0.7 fusion.56
  2.9 0.8 select_reduce_fusion.3
  3.9 0.7 fusion.15
  4.6 1.6 %fusion.16 = bf16[768,128]{0,1:T(8,128)(2,1)S(1)} fusion(bf16[672,128]{1,0:T(8,128)(2,1)} %param.8, s32[768]{0:T(1024)S(1)} %min.38), kind=kOutput, calls=%fused_computation.38 | convolution fusion | flops 132734976 | bytes 371712 | tf_op jit(solution)/shard_map/dot_general | solution.py:56
  6.5 0.7 constant_dynamic-slice_fusion.7
  7.2 3.9 %collective-permute-start.2 = (bf16[192,256]{1,0:T(8,128)(2,1)}, bf16[192,256]{1,0:T(8,128)(2,1)}, u32[]{:S(2)}, u32[]{:S(2)}) collective-permute-start(bf16[192,256]{1,0:T(8,128)(2,1)} %get-tuple-element.51), channel_id=1, source_target_pairs={{0,24},{8,16},{16,8},{24,0},{1,25},{9,17},{17,9},{25,1},{2,26},{10... | collective-permute-start | bytes 294920 | tf_op jit(solution)/shard_map/ppermute | solution.py:51
  11.7 2.4 %constant_dynamic-slice_fusion.2 = (bf16[1024,4,128]{2,1,0:T(4,128)(2,1)S(1)}, bf16[1024,4,128]{2,1,0:T(4,128)(2,1)S(1)}) fusion(bf16[1024,4,1024]{2,1,0:T(4,128)(2,1)} %param.11, s32[]{:T(128)S(6)} %select_n.147, s32[]{:T(128)S(6)} %select_n.143), kind=kLoop, calls=%fused_computation.135 | loop fusion | bytes 4194312 | tf_op jit(solution)/shard_map/dynamic_slice | solution.py:80
  14.5 1.2 %reshape.182 = bf16[8,128,512]{2,1,0:T(8,128)(2,1)} reshape(bf16[1024,4,128]{2,1,0:T(4,128)(2,1)S(1)} %get-tuple-element.38) | data formatting | bytes 2097152 | tf_op jit(solution)/shard_map/reshape | solution.py:80
  15.8 1.1 %constant_dynamic-slice_fusion.1 = (bf16[128,1024]{1,0:T(8,128)(2,1)S(1)}, bf16[128,1024]{1,0:T(8,128)(2,1)S(1)}) fusion(bf16[1024,1024]{1,0:T(8,128)(2,1)} %param.13, s32[]{:T(128)S(6)} %select_n.147, s32[]{:T(128)S(6)} %select_n.143), kind=kLoop, calls=%fused_computation.134 | loop fusion | bytes 1048584 | tf_op jit(solution)/shard_map/dynamic_slice | solution.py:90
  17.4 0.8 copy.63
  18.2 0.8 dynamic_slice.111
  19.5 1.0 %pad_maximum_fusion.3 = bf16[4,192,256]{2,1,0:T(8,128)(2,1)S(1)} fusion(bf16[1,192,256]{2,1,0:T(8,128)(2,1)} %bitcast.10, bf16[1,192,256]{2,1,0:T(8,128)(2,1)} %bitcast.8, bf16[1,192,256]{2,1,0:T(8,128)(2,1)} %bitcast.6, bf16[1,192,256]{2,1,0:T(8,128)(2,1)S(1)} %get-tuple-element.50), kind=kLoop, calls=%fused_computation.83 | loop fusion | flops 589824 | bytes 786432 | tf_op jit(solution)/shard_map/stack | solution.py:52
  20.9 21.5 %all-gather = bf16[1728,256]{1,0:T(8,128)(2,1)S(1)} all-gather(bf16[432,256]{1,0:T(8,128)(2,1)S(1)} %fusion.11), channel_id=2, replica_groups={{0,2,4,6},{1,3,5,7},{8,10,12,14},{9,11,13,15},{16,18,20,22},{17,19,21,2..., dimensions={0}, use_global_device_ids=true | all-gather | bytes 1105920 | tf_op jit(solution)/shard_map/all_gather | solution.py:112
  43.4 1.5 %collective-permute-done.3 = bf16[4,432,256]{2,1,0:T(8,128)(2,1)S(1)} collective-permute-done((bf16[4,432,256]{2,1,0:T(8,128)(2,1)S(1)}, bf16[4,432,256]{2,1,0:T(8,128)(2,1)S(1)}, u32[]{:S(2)}, u32[]{:S(2)}) %collective-permute-start.3) | collective-permute-done | bytes 884768 | tf_op jit(solution)/shard_map/ppermute | solution.py:113
  51.1 1.6 %collective-permute-start.11 = (bf16[2,256,640]{2,1,0:T(8,128)(2,1)S(1)}, bf16[2,256,640]{2,1,0:T(8,128)(2,1)S(1)}, u32[]{:S(2)}, u32[]{:S(2)}) collective-permute-start(bf16[2,256,640]{2,1,0:T(8,128)(2,1)S(1)} %fusion.32), channel_id=1, source_target_pairs={{0,16},{8,24},{16,0},{24,8},{1,17},{9,25},{17,1},{25,9},{2,18},{10... | collective-permute-start | bytes 1966088 | tf_op jit(solution)/shard_map/ppermute | solution.py:199
  54.7 13.2 %collective-permute-done.11 = bf16[2,256,640]{2,1,0:T(8,128)(2,1)S(1)} collective-permute-done((bf16[2,256,640]{2,1,0:T(8,128)(2,1)S(1)}, bf16[2,256,640]{2,1,0:T(8,128)(2,1)S(1)}, u32[]{:S(2)}, u32[]{:S(2)}) %collective-permute-start.11) | collective-permute-done | bytes 655392 | tf_op jit(solution)/shard_map/ppermute | solution.py:199
  68.1 1.6 %collective-permute-start.12 = (bf16[256,640]{1,0:T(8,128)(2,1)S(1)}, bf16[256,640]{1,0:T(8,128)(2,1)S(1)}, u32[]{:S(2)}, u32[]{:S(2)}) collective-permute-start(bf16[256,640]{1,0:T(8,128)(2,1)S(1)} %fusion.47), channel_id=1, source_target_pairs={{0,8},{8,0},{16,24},{24,16},{1,9},{9,1},{17,25},{25,17},{2,10},{10... | collective-permute-start | bytes 983048 | tf_op jit(solution)/shard_map/ppermute | solution.py:199
  69.9 0.9 dynamic-slice_bitcast_fusion.4
  70.8 1.9 %collective-permute-start.6 = (bf16[432,256]{1,0:T(8,128)(2,1)}, bf16[432,256]{1,0:T(8,128)(2,1)S(1)}, u32[]{:S(2)}, u32[]{:S(2)}) collective-permute-start(bf16[432,256]{1,0:T(8,128)(2,1)} %get-tuple-element.46), channel_id=1, source_target_pairs={{0,4},{1,5},{2,6},{3,7},{4,0},{5,1},{6,2},{7,3},{8,12},{9,13},{10,... | collective-permute-start | bytes 663560 | tf_op jit(solution)/shard_map/ppermute | solution.py:125
  72.7 2.5 %collective-permute-start.7 = (bf16[432,256]{1,0:T(8,128)(2,1)}, bf16[432,256]{1,0:T(8,128)(2,1)}, u32[]{:S(2)}, u32[]{:S(2)}) collective-permute-start(bf16[432,256]{1,0:T(8,128)(2,1)} %get-tuple-element.45), channel_id=1, source_target_pairs={{0,6},{1,7},{2,4},{3,5},{4,2},{5,3},{6,0},{7,1},{8,14},{9,15},{10,... | collective-permute-start | bytes 663560 | tf_op jit(solution)/shard_map/ppermute | solution.py:125
  75.2 1.9 %collective-permute-done.12 = bf16[256,640]{1,0:T(8,128)(2,1)S(1)} collective-permute-done((bf16[256,640]{1,0:T(8,128)(2,1)S(1)}, bf16[256,640]{1,0:T(8,128)(2,1)S(1)}, u32[]{:S(2)}, u32[]{:S(2)}) %collective-permute-start.12) | collective-permute-done | bytes 327712 | tf_op jit(solution)/shard_map/ppermute | solution.py:199
  77.4 1.0 copy.58
  78.4 0.8 copy.59
  79.2 2.0 %collective-permute-done.5 = bf16[432,256]{1,0:T(8,128)(2,1)S(1)} collective-permute-done((bf16[432,256]{1,0:T(8,128)(2,1)}, bf16[432,256]{1,0:T(8,128)(2,1)S(1)}, u32[]{:S(2)}, u32[]{:S(2)}) %collective-permute-start.5) | collective-permute-done | bytes 221216 | tf_op jit(solution)/shard_map/ppermute | solution.py:125
  81.2 8.5 %collective-permute-done.6 = bf16[432,256]{1,0:T(8,128)(2,1)S(1)} collective-permute-done((bf16[432,256]{1,0:T(8,128)(2,1)}, bf16[432,256]{1,0:T(8,128)(2,1)S(1)}, u32[]{:S(2)}, u32[]{:S(2)}) %collective-permute-start.6) | collective-permute-done | bytes 221216 | tf_op jit(solution)/shard_map/ppermute | solution.py:125
  89.7 1.1 %fusion.35 = f32[432,256]{1,0:T(8,128)S(1)} fusion(bf16[432,256]{1,0:T(8,128)(2,1)} %collective-permute-done.7, bf16[432,256]{1,0:T(8,128)(2,1)S(1)} %collective-permute-done.6, bf16[432,256]{1,0:T(8,128)(2,1)S(1)} %collective-permute-done.5, bf16[4,432,256]{2,1,0:T(8,128)(2,1)S(1)} %fusion.4, s32[]{:T(128)S(6)} %select_n.151), kind=kLoop, calls=%fused_computation.78 | loop fusion | flops 774144 | bytes 1327108 | tf_op jit(solution)/shard_map/add | solution.py:125
  91.9 1.5 %collective-permute-start.9 = (bf16[192,128]{1,0:T(8,128)(2,1)S(1)}, bf16[192,128]{1,0:T(8,128)(2,1)S(1)}, u32[]{:S(2)}, u32[]{:S(2)}) collective-permute-start(bf16[192,128]{1,0:T(8,128)(2,1)S(1)} %get-tuple-element.58), channel_id=1, source_target_pairs={{0,16},{8,24},{16,0},{24,8},{1,17},{9,25},{17,1},{25,9},{2,18},{10... | collective-permute-start | bytes 147464 | tf_op jit(solution)/shard_map/ppermute | solution.py:51
  93.4 1.4 %collective-permute-start.10 = (bf16[192,128]{1,0:T(8,128)(2,1)S(1)}, bf16[192,128]{1,0:T(8,128)(2,1)S(1)}, u32[]{:S(2)}, u32[]{:S(2)}) collective-permute-start(bf16[192,128]{1,0:T(8,128)(2,1)S(1)} %get-tuple-element.57), channel_id=1, source_target_pairs={{0,24},{8,16},{16,8},{24,0},{1,25},{9,17},{17,9},{25,1},{2,26},{10... | collective-permute-start | bytes 147464 | tf_op jit(solution)/shard_map/ppermute | solution.py:51
  94.8 0.7 fusion.51
  96.0 2.4 %collective-permute-done.10 = bf16[192,128]{1,0:T(8,128)(2,1)S(1)} collective-permute-done((bf16[192,128]{1,0:T(8,128)(2,1)S(1)}, bf16[192,128]{1,0:T(8,128)(2,1)S(1)}, u32[]{:S(2)}, u32[]{:S(2)}) %collective-permute-start.10) | collective-permute-done | bytes 49184 | tf_op jit(solution)/shard_map/ppermute | solution.py:51
  98.4 1.2 %fusion.17 = bf16[672,128]{1,0:T(8,128)(2,1)} fusion(bf16[768,128]{1,0:T(8,128)(2,1)S(1)} %bitcast.202, s32[672]{0:T(1024)S(1)} %add_select_fusion), kind=kOutput, calls=%fused_computation.41 | convolution fusion | flops 132722688 | bytes 371328 | tf_op jit(solution)/shard_map/dot_general | solution.py:56
  (84 shorter events, 14.0 us)
Async XLA Ops:
  0.6 3.3 %copy-start = (bf16[672,128]{1,0:T(8,128)(2,1)S(1)}, bf16[672,128]{1,0:T(8,128)(2,1)}, u32[]{:S(2)}) copy-start(bf16[672,128]{1,0:T(8,128)(2,1)} %param.7) | copy-start | bytes 516100
  7.2 12.3 %collective-permute-start.2 = (bf16[192,256]{1,0:T(8,128)(2,1)}, bf16[192,256]{1,0:T(8,128)(2,1)}, u32[]{:S(2)}, u32[]{:S(2)}) collective-permute-start(bf16[192,256]{1,0:T(8,128)(2,1)} %get-tuple-element.51), channel_id=1, source_target_pairs={{0,24},{8,16},{16,8},{24,0},{1,25},{9,17},{17,9},{25,1},{2,26},{10... | collective-permute-start | bytes 294920 | tf_op jit(solution)/shard_map/ppermute | solution.py:51
  11.1 8.4 %collective-permute-start = (bf16[192,256]{1,0:T(8,128)(2,1)}, bf16[192,256]{1,0:T(8,128)(2,1)}, u32[]{:S(2)}, u32[]{:S(2)}) collective-permute-start(bf16[192,256]{1,0:T(8,128)(2,1)} %get-tuple-element.53), channel_id=1, source_target_pairs={{0,8},{8,0},{16,24},{24,16},{1,9},{9,1},{17,25},{25,17},{2,10},{10... | collective-permute-start | bytes 294920 | tf_op jit(solution)/shard_map/ppermute | solution.py:51
  11.6 7.9 %collective-permute-start.1 = (bf16[192,256]{1,0:T(8,128)(2,1)S(1)}, bf16[192,256]{1,0:T(8,128)(2,1)}, u32[]{:S(2)}, u32[]{:S(2)}) collective-permute-start(bf16[192,256]{1,0:T(8,128)(2,1)S(1)} %get-tuple-element.52), channel_id=1, source_target_pairs={{0,16},{8,24},{16,0},{24,8},{1,17},{9,25},{17,1},{25,9},{2,18},{10... | collective-permute-start | bytes 294920 | tf_op jit(solution)/shard_map/ppermute | solution.py:51
  42.5 2.4 %collective-permute-start.3 = (bf16[4,432,256]{2,1,0:T(8,128)(2,1)S(1)}, bf16[4,432,256]{2,1,0:T(8,128)(2,1)S(1)}, u32[]{:S(2)}, u32[]{:S(2)}) collective-permute-start(bf16[4,432,256]{2,1,0:T(8,128)(2,1)S(1)} %bitcast.185), channel_id=1, source_target_pairs={{0,1},{1,0},{2,3},{3,2},{4,5},{5,4},{6,7},{7,6},{8,9},{9,8},{10,11... | collective-permute-start | bytes 2654216 | tf_op jit(solution)/shard_map/ppermute | solution.py:113
  50.8 1.9 %copy-start.2 = (bf16[8,128,512]{2,1,0:T(8,128)(2,1)S(1)}, bf16[8,128,512]{2,1,0:T(8,128)(2,1)}, u32[]{:S(2)}) copy-start(bf16[8,128,512]{2,1,0:T(8,128)(2,1)} %reshape.182) | copy-start | bytes 3145732
  51.0 2.4 %copy-start.1 = (bf16[128,1024]{0,1:T(8,128)(2,1)S(1)}, bf16[128,1024]{0,1:T(8,128)(2,1)}, u32[]{:S(2)}) copy-start(bf16[128,1024]{0,1:T(8,128)(2,1)} %copy.63) | copy-start | bytes 786436
  51.1 16.8 %collective-permute-start.11 = (bf16[2,256,640]{2,1,0:T(8,128)(2,1)S(1)}, bf16[2,256,640]{2,1,0:T(8,128)(2,1)S(1)}, u32[]{:S(2)}, u32[]{:S(2)}) collective-permute-start(bf16[2,256,640]{2,1,0:T(8,128)(2,1)S(1)} %fusion.32), channel_id=1, source_target_pairs={{0,16},{8,24},{16,0},{24,8},{1,17},{9,25},{17,1},{25,9},{2,18},{10... | collective-permute-start | bytes 1966088 | tf_op jit(solution)/shard_map/ppermute | solution.py:199
  53.8 15.8 %collective-permute-start.4 = (bf16[4,432,256]{2,1,0:T(8,128)(2,1)S(1)}, bf16[4,432,256]{2,1,0:T(8,128)(2,1)S(1)}, u32[]{:S(2)}, u32[]{:S(2)}) collective-permute-start(bf16[4,432,256]{2,1,0:T(8,128)(2,1)S(1)} %fusion.21), channel_id=1, source_target_pairs={{0,1},{1,0},{2,3},{3,2},{4,5},{5,4},{6,7},{7,6},{8,9},{9,8},{10,11... | collective-permute-start | bytes 2654216 | tf_op jit(solution)/shard_map/ppermute | solution.py:119
  68.1 9.0 %collective-permute-start.12 = (bf16[256,640]{1,0:T(8,128)(2,1)S(1)}, bf16[256,640]{1,0:T(8,128)(2,1)S(1)}, u32[]{:S(2)}, u32[]{:S(2)}) collective-permute-start(bf16[256,640]{1,0:T(8,128)(2,1)S(1)} %fusion.47), channel_id=1, source_target_pairs={{0,8},{8,0},{16,24},{24,16},{1,9},{9,1},{17,25},{25,17},{2,10},{10... | collective-permute-start | bytes 983048 | tf_op jit(solution)/shard_map/ppermute | solution.py:199
  70.8 10.4 %collective-permute-start.5 = (bf16[432,256]{1,0:T(8,128)(2,1)}, bf16[432,256]{1,0:T(8,128)(2,1)S(1)}, u32[]{:S(2)}, u32[]{:S(2)}) collective-permute-start(bf16[432,256]{1,0:T(8,128)(2,1)} %get-tuple-element.44), channel_id=1, source_target_pairs={{0,2},{1,3},{2,0},{3,1},{4,6},{5,7},{6,4},{7,5},{8,10},{9,11},{10,... | collective-permute-start | bytes 663560 | tf_op jit(solution)/shard_map/ppermute | solution.py:125
  70.8 19.0 %collective-permute-start.6 = (bf16[432,256]{1,0:T(8,128)(2,1)}, bf16[432,256]{1,0:T(8,128)(2,1)S(1)}, u32[]{:S(2)}, u32[]{:S(2)}) collective-permute-start(bf16[432,256]{1,0:T(8,128)(2,1)} %get-tuple-element.46), channel_id=1, source_target_pairs={{0,4},{1,5},{2,6},{3,7},{4,0},{5,1},{6,2},{7,3},{8,12},{9,13},{10,... | collective-permute-start | bytes 663560 | tf_op jit(solution)/shard_map/ppermute | solution.py:125
  72.7 17.1 %collective-permute-start.7 = (bf16[432,256]{1,0:T(8,128)(2,1)}, bf16[432,256]{1,0:T(8,128)(2,1)}, u32[]{:S(2)}, u32[]{:S(2)}) collective-permute-start(bf16[432,256]{1,0:T(8,128)(2,1)} %get-tuple-element.45), channel_id=1, source_target_pairs={{0,6},{1,7},{2,4},{3,5},{4,2},{5,3},{6,0},{7,1},{8,14},{9,15},{10,... | collective-permute-start | bytes 663560 | tf_op jit(solution)/shard_map/ppermute | solution.py:125
  91.3 4.2 %collective-permute-start.8 = (bf16[192,128]{1,0:T(8,128)(2,1)S(1)}, bf16[192,128]{1,0:T(8,128)(2,1)S(1)}, u32[]{:S(2)}, u32[]{:S(2)}) collective-permute-start(bf16[192,128]{1,0:T(8,128)(2,1)S(1)} %get-tuple-element.59), channel_id=1, source_target_pairs={{0,8},{8,0},{16,24},{24,16},{1,9},{9,1},{17,25},{25,17},{2,10},{10... | collective-permute-start | bytes 147464 | tf_op jit(solution)/shard_map/ppermute | solution.py:51
  91.9 4.1 %collective-permute-start.9 = (bf16[192,128]{1,0:T(8,128)(2,1)S(1)}, bf16[192,128]{1,0:T(8,128)(2,1)S(1)}, u32[]{:S(2)}, u32[]{:S(2)}) collective-permute-start(bf16[192,128]{1,0:T(8,128)(2,1)S(1)} %get-tuple-element.58), channel_id=1, source_target_pairs={{0,16},{8,24},{16,0},{24,8},{1,17},{9,25},{17,1},{25,9},{2,18},{10... | collective-permute-start | bytes 147464 | tf_op jit(solution)/shard_map/ppermute | solution.py:51
  93.4 5.0 %collective-permute-start.10 = (bf16[192,128]{1,0:T(8,128)(2,1)S(1)}, bf16[192,128]{1,0:T(8,128)(2,1)S(1)}, u32[]{:S(2)}, u32[]{:S(2)}) collective-permute-start(bf16[192,128]{1,0:T(8,128)(2,1)S(1)} %get-tuple-element.57), channel_id=1, source_target_pairs={{0,24},{8,16},{16,8},{24,0},{1,25},{9,17},{17,9},{25,1},{2,26},{10... | collective-permute-start | bytes 147464 | tf_op jit(solution)/shard_map/ppermute | solution.py:51

commit v12 on v10

--- a/solution.py
+++ b/solution.py
@@ -90,12 +90,31 @@
     own_out = lax.dynamic_slice_in_dim(out_weight, own_start, col_width, 0).reshape(
         col_width, tensor_count, col_width
     )
-    weight_pack = (proj_mine, proj_other, out_mine, out_other, own_proj, own_out, head_gain)
-    recv_both, weight_pack = lax.optimization_barrier((recv_both, weight_pack))
-    proj_mine, proj_other, out_mine, out_other, own_proj, own_out, head_gain = weight_pack
-
     recv_len = jnp.sum(jnp.where(owners == dp_index, lengths, 0), axis=1)
     recv_start = exclusive_sum(recv_len)
+    back_src = jnp.minimum(recv_start[:, None] + places[None, :], owned_rows - 1)
+    back_pick = (
+        back_src.reshape(-1)[:, None] == jnp.arange(owned_rows, dtype=jnp.int32)[None, :]
+    ).astype(bf16)
+    load_ids = jnp.arange(load_rows, dtype=jnp.int32)
+    seq_of = jnp.sum((load_ids[:, None] >= my_starts[None, :]).astype(jnp.int32), axis=1) - 1
+    seq_pick = seq_of[:, None] == seq_ids[None, :]
+    owner_of = jnp.sum(jnp.where(seq_pick, my_owners[None, :], 0), axis=1)
+    start_of = jnp.sum(jnp.where(seq_pick, my_starts[None, :], 0), axis=1)
+    back_ids = (owner_of ^ dp_index) * MAXLEN + jnp.minimum(load_ids - start_of, MAXLEN - 1)
+    row_used = load_ids < jnp.sum(my_lengths)
+    final_ids = jnp.where(row_used, back_ids, -1)
+    final_pick = (
+        final_ids[:, None] == jnp.arange(dp_count * MAXLEN, dtype=jnp.int32)[None, :]
+    ).astype(bf16)
+    weight_pack = (
+        proj_mine, proj_other, out_mine, out_other, own_proj, own_out, head_gain, back_pick, final_pick
+    )
+    recv_both, weight_pack = lax.optimization_barrier((recv_both, weight_pack))
+    (
+        proj_mine, proj_other, out_mine, out_other, own_proj, own_out, head_gain, back_pick, final_pick
+    ) = weight_pack
+
     compact_ids = jnp.arange(owned_rows, dtype=jnp.int32)
     compact_slot = (
         jnp.sum((compact_ids[:, None] >= recv_start[None, :]).astype(jnp.int32), axis=1) - 1
@@ -114,9 +133,11 @@
     mine_tok, mine_cot = mine[..., :col_width], mine[..., col_width:]
     other_tok, other_cot = other[..., :col_width], other[..., col_width:]
 
-    def reduce_blocks(part):
+    def sibling_sum(part):
         keep, send = by_core(part, 0)
-        pair_sum = (keep.astype(f32) + lax.ppermute(send, "tensor", sibling).astype(f32)).astype(bf16)
+        return (keep.astype(f32) + lax.ppermute(send, "tensor", sibling).astype(f32)).astype(bf16)
+
+    def reduce_blocks(pair_sum):
         pieces = lax.all_to_all(pair_sum, "tensor", 0, 0, tiled=True, axis_index_groups=same_core)
         return jnp.sum(pieces.astype(f32), axis=0)
 
@@ -164,7 +185,9 @@
         owned_rows, 4 * col_width
     )
     grad_part = jnp.einsum("rn,tkn->trk", own_grad, own_proj, preferred_element_type=f32)
-    both_sum = reduce_blocks(jnp.concatenate([out_part, grad_part], axis=2).astype(bf16))
+    both_sum = reduce_blocks(
+        jnp.concatenate([sibling_sum(out_part.astype(bf16)), sibling_sum(grad_part.astype(bf16))], axis=2)
+    )
     out_sum = both_sum[:, :col_width]
     grad_sum = both_sum[:, col_width:]
     mixed_out = (own_tokens.astype(f32) + out_sum).astype(bf16)
@@ -195,18 +218,10 @@
     proj_grad = term_sum[:, : 4 * col_width].reshape(-1, 4, col_width)
     out_grad = term_sum[:, 4 * col_width :].T
 
-    back_src = jnp.minimum(recv_start[:, None] + places[None, :], owned_rows - 1)
-    back_send = pick_rows(back_src.reshape(-1), token_rows).reshape(dp_count, MAXLEN, col_width)
-    back_grads = exchange(back_send)
+    back_send = jnp.dot(back_pick, token_rows, preferred_element_type=f32).astype(bf16)
+    back_grads = exchange(back_send.reshape(dp_count, MAXLEN, col_width))
     back_grads = back_grads.reshape(dp_count * MAXLEN, col_width)
-    load_ids = jnp.arange(load_rows, dtype=jnp.int32)
-    seq_of = jnp.sum((load_ids[:, None] >= my_starts[None, :]).astype(jnp.int32), axis=1) - 1
-    seq_pick = seq_of[:, None] == seq_ids[None, :]
-    owner_of = jnp.sum(jnp.where(seq_pick, my_owners[None, :], 0), axis=1)
-    start_of = jnp.sum(jnp.where(seq_pick, my_starts[None, :], 0), axis=1)
-    back_ids = (owner_of ^ dp_index) * MAXLEN + jnp.minimum(load_ids - start_of, MAXLEN - 1)
-    row_used = load_ids < jnp.sum(my_lengths)
-    token_grad = pick_rows(jnp.where(row_used, back_ids, -1), back_grads)
+    token_grad = jnp.dot(final_pick, back_grads, preferred_element_type=f32).astype(bf16)
     return (mixed_out, token_grad, proj_grad, out_grad)
 
 

time: 96.7 us -> 101 us (1.044)
  other arithmetic: 13.3 us -> 15 us
  waiting for transfers between devices: 21.8 us -> 23.3 us
  local copies, waits for them, and re-layouts: 12.4 us -> 13.7 us
    ppermute x2, waiting for transfers between devices: 15.4 us -> 17.7 us  [local(): lax.ppermute(send.astype(bf16), 'dp', partners).astype(f32)]
    all_to_all x1, waiting for transfers between devices: 1.63 us -> 0.01 us  [reduce_blocks(): lax.all_to_all(pair_sum, 'tensor', 0, 0, tiled=True, axis_index_groups=sa...]
    dot_general x5 -> x3, matrix products: 4.36 us -> 2.74 us  [pick_rows(): return jnp.dot(one_hot, source, preferred_element_type=f32).astype(bf16)]
    dot_general x0 -> x2, matrix products: none -> 1.48 us  [the longest x1 1.11 us: local(): jnp.dot(final_pick, back_grads, preferred_element_type=f32).astype(bf16)]
    unnamed x30 -> x38, local copies, waits for them, and re-layouts: 2.64 us -> 3.88 us
    squeeze x1 -> x0, other arithmetic: 1.12 us -> none  [by_core(): lax.dynamic_index_in_dim(split, 1 - core, axis + 1, keepdims=False)]
    add x2, other arithmetic: 1.29 us -> 2.38 us  [local(): keep + lax.ppermute(send.astype(bf16), 'dp', partners).astype(f32)]
    concatenate x0 -> x1, other arithmetic: none -> 1.03 us  [local(): jnp.concatenate([sibling_sum(out_part.astype(bf16)), sibling_sum(grad_par...]
  transfers between devices with their start and end apart: 11 -> 12, of which waited for: 6 -> 6; matrix products, arithmetic and copies ran while one was open for 19% -> 21% of each run, Pallas kernels for 0% -> 0%
where the time goes in v12:
time: 101 us
  waiting for transfers between devices  23.3 us (23%)
  blocking collectives  21.3 us (21%)
  starting transfers between devices  15.8 us (16%)
  other arithmetic  15 us (15%)
  local copies, waits for them, and re-layouts  13.7 us (14%)
  matrix products  10.4 us (10%)
  between operations  1.24 us (1%)
    all_gather x1, blocking collectives, local(): lax.all_gather(own_both, 'tensor', axis=0, tiled=False, axis_index_groups...  21.3 us
    ppermute x2, waiting for transfers between devices, local(): lax.ppermute(send.astype(bf16), 'dp', partners).astype(f32)  17.7 us
    ppermute x6, starting transfers between devices, exchange(): lax.ppermute(outgoing, 'dp', [(d, d ^ k) for d in range(dp_count)])  8.02 us
    all_to_all x1, starting transfers between devices, reduce_blocks(): lax.all_to_all(pair_sum, 'tensor', 0, 0, tiled=True, axis_index_groups=sa...  4.22 us
    unnamed x38, local copies, waits for them, and re-layouts  3.88 us
    ppermute x6, waiting for transfers between devices, exchange(): lax.ppermute(outgoing, 'dp', [(d, d ^ k) for d in range(dp_count)])  3.85 us
    ppermute x2, starting transfers between devices, local(): lax.ppermute(send.astype(bf16), 'dp', partners).astype(f32)  3.14 us
    dot_general x3, matrix products, pick_rows(): return jnp.dot(one_hot, source, preferred_element_type=f32).astype(bf16)  2.74 us
  transfers between devices with their start and end apart: 12, of which 6 were waited for; matrix products, arithmetic and copies ran while one was open for 21% of the time, Pallas kernels for 0%

profile of v12, /device:TPU:0, one launch (start us, length us, event | category | flops | bytes accessed | tf_op | source)
XLA Modules:
  0.0 100.7 jit_solution(6194346205310291474)
XLA Ops:
  0.7 1.4 %fusion.48 = (s32[]{:T(128)}, s32[1,4]{1,0:T(1,128)S(1)}) fusion(s32[4,4]{1,0:T(4,128)} %param.9, s32[]{:T(128)S(6)} %select_n.123), kind=kLoop, calls=%fused_computation.149 | loop fusion | flops 3 | bytes 40 | tf_op jit(solution)/shard_map/reduce_sum | solution.py:105
  3.0 0.8 select_reduce_fusion.3
  4.7 1.6 %fusion.14 = bf16[768,128]{0,1:T(8,128)(2,1)S(1)} fusion(bf16[672,128]{1,0:T(8,128)(2,1)} %param.8, s32[768]{0:T(1024)S(1)} %min.38), kind=kOutput, calls=%fused_computation.32 | convolution fusion | flops 132734976 | bytes 371712 | tf_op jit(solution)/shard_map/dot_general | solution.py:56
  6.6 0.7 constant_dynamic-slice_fusion.7
  7.3 3.9 %collective-permute-start.2 = (bf16[192,256]{1,0:T(8,128)(2,1)}, bf16[192,256]{1,0:T(8,128)(2,1)}, u32[]{:S(2)}, u32[]{:S(2)}) collective-permute-start(bf16[192,256]{1,0:T(8,128)(2,1)} %get-tuple-element.52), channel_id=1, source_target_pairs={{0,24},{8,16},{16,8},{24,0},{1,25},{9,17},{17,9},{25,1},{2,26},{10... | collective-permute-start | bytes 294920 | tf_op jit(solution)/shard_map/ppermute | solution.py:51
  12.8 2.4 %constant_dynamic-slice_fusion.2 = (bf16[1024,4,128]{2,1,0:T(4,128)(2,1)S(1)}, bf16[1024,4,128]{2,1,0:T(4,128)(2,1)S(1)}) fusion(bf16[1024,4,1024]{2,1,0:T(4,128)(2,1)} %param.11, s32[]{:T(128)S(6)} %select_n.133, s32[]{:T(128)S(6)} %select_n.129), kind=kLoop, calls=%fused_computation.125 | loop fusion | bytes 4194312 | tf_op jit(solution)/shard_map/dynamic_slice | solution.py:80
  15.7 1.2 %reshape.183 = bf16[8,128,512]{2,1,0:T(8,128)(2,1)} reshape(bf16[1024,4,128]{2,1,0:T(4,128)(2,1)S(1)} %get-tuple-element.42) | data formatting | bytes 2097152 | tf_op jit(solution)/shard_map/reshape | solution.py:80
  16.9 1.1 %constant_dynamic-slice_fusion.1 = (bf16[128,1024]{1,0:T(8,128)(2,1)S(1)}, bf16[128,1024]{1,0:T(8,128)(2,1)S(1)}) fusion(bf16[1024,1024]{1,0:T(8,128)(2,1)} %param.13, s32[]{:T(128)S(6)} %select_n.133, s32[]{:T(128)S(6)} %select_n.129), kind=kLoop, calls=%fused_computation.124 | loop fusion | bytes 1048584 | tf_op jit(solution)/shard_map/dynamic_slice | solution.py:90
  18.4 0.8 copy.46
  20.0 1.2 %fusion.3 = bf16[672,768]{1,0:T(8,128)(2,1)} fusion(s32[672]{0:T(1024)S(1)} %add_select_fusion), kind=kLoop, calls=%fused_computation.7 | loop fusion | flops 1032192 | bytes 1034880 | tf_op jit(solution)/shard_map/convert_element_type | solution.py:109
  21.4 1.3 %dynamic_slice.104 = f32[128]{0:T(128)} dynamic-slice(f32[1024]{0:T(1024)} %param.12, s32[]{:T(128)S(6)} %select_n.129), dynamic_slice_sizes={128} | dynamic-slice | bytes 1028 | tf_op jit(solution)/shard_map/dynamic_slice | solution.py:86
  22.7 1.1 %fusion.4 = bf16[768,432]{1,0:T(8,128)(2,1)} fusion(s32[768]{0:T(1024)S(1)} %min.41), kind=kLoop, calls=%fused_computation.10 | loop fusion | flops 663552 | bytes 666624 | tf_op jit(solution)/shard_map/convert_element_type | solution.py:98
  24.0 1.0 %pad_maximum_fusion.4 = bf16[4,192,256]{2,1,0:T(8,128)(2,1)S(1)} fusion(bf16[1,192,256]{2,1,0:T(8,128)(2,1)} %bitcast.10, bf16[1,192,256]{2,1,0:T(8,128)(2,1)} %bitcast.8, bf16[1,192,256]{2,1,0:T(8,128)(2,1)} %bitcast.6, bf16[1,192,256]{2,1,0:T(8,128)(2,1)S(1)} %copy-done.8), kind=kLoop, calls=%fused_computation.76 | loop fusion | flops 589824 | bytes 786432 | tf_op jit(solution)/shard_map/stack | solution.py:52
  25.5 21.3 %all-gather = bf16[1728,256]{1,0:T(8,128)(2,1)S(1)} all-gather(bf16[432,256]{1,0:T(8,128)(2,1)S(1)} %fusion.10), channel_id=2, replica_groups={{0,2,4,6},{1,3,5,7},{8,10,12,14},{9,11,13,15},{16,18,20,22},{17,19,21,2..., dimensions={0}, use_global_device_ids=true | all-gather | bytes 1105920 | tf_op jit(solution)/shard_map/all_gather | solution.py:131
  47.5 1.7 %collective-permute-done.3 = bf16[4,432,256]{2,1,0:T(8,128)(2,1)S(1)} collective-permute-done((bf16[4,432,256]{2,1,0:T(8,128)(2,1)S(1)}, bf16[4,432,256]{2,1,0:T(8,128)(2,1)S(1)}, u32[]{:S(2)}, u32[]{:S(2)}) %collective-permute-start.3) | collective-permute-done | bytes 884768 | tf_op jit(solution)/shard_map/ppermute | solution.py:132
  57.7 1.6 %collective-permute-start.9 = (bf16[2,256,640]{2,1,0:T(8,128)(2,1)S(1)}, bf16[2,256,640]{2,1,0:T(8,128)(2,1)}, u32[]{:S(2)}, u32[]{:S(2)}) collective-permute-start(bf16[2,256,640]{2,1,0:T(8,128)(2,1)S(1)} %fusion.25), channel_id=1, source_target_pairs={{0,16},{8,24},{16,0},{24,8},{1,17},{9,25},{17,1},{25,9},{2,18},{10... | collective-permute-start | bytes 1966088 | tf_op jit(solution)/shard_map/ppermute | solution.py:217
  59.6 1.0 %pad_maximum_fusion.1 = bf16[4,432,256]{2,1,0:T(8,128)(2,1)} fusion(bf16[4,432,128]{2,1,0:T(8,128)(2,1)S(1)} %fusion.21, bf16[4,432,128]{2,1,0:T(8,128)(2,1)S(1)} %fusion.22), kind=kLoop, calls=%fused_computation.52 | loop fusion | flops 1769472 | bytes 1769472 | tf_op jit(solution)/shard_map/concatenate | solution.py:189
  60.6 4.2 %all-to-all-start = ((bf16[4,432,256]{2,1,0:T(8,128)(2,1)}), bf16[4,432,256]{2,1,0:T(8,128)(2,1)}, u32[]{:S(2)}, u32[]{:S(2)}) async-start(bf16[4,432,256]{2,1,0:T(8,128)(2,1)} %pad_maximum_fusion.1), calls=%async_computation | async-start | bytes 1769472 | tf_op jit(solution)/shard_map/all_to_all | solution.py:141
  64.8 10.0 %collective-permute-done.9 = bf16[2,256,640]{2,1,0:T(8,128)(2,1)} collective-permute-done((bf16[2,256,640]{2,1,0:T(8,128)(2,1)S(1)}, bf16[2,256,640]{2,1,0:T(8,128)(2,1)}, u32[]{:S(2)}, u32[]{:S(2)}) %collective-permute-start.9) | collective-permute-done | bytes 655392 | tf_op jit(solution)/shard_map/ppermute | solution.py:217
  74.9 1.2 %bitcast_add_fusion = f32[2,256,640]{2,1,0:T(8,128)S(1)} fusion(bf16[2,256,640]{2,1,0:T(8,128)(2,1)} %collective-permute-done.9, f32[2,2,256,640]{3,2,1,0:T(8,128)S(1)} %maximum_convert_fusion, s32[]{:T(128)S(6)} %select_n.143), kind=kLoop, calls=%fused_computation.24 | loop fusion | flops 655360 | bytes 3276804 | tf_op jit(solution)/shard_map/add | solution.py:217
  76.1 1.1 %copy-done.2 = f32[2,256,640]{2,1,0:T(8,128)} copy-done((f32[2,256,640]{2,1,0:T(8,128)}, f32[2,256,640]{2,1,0:T(8,128)S(1)}, u32[]{:S(2)}) %copy-start.2) | copy-done | bytes 1310744
  77.2 1.6 %collective-permute-start.10 = (bf16[256,640]{1,0:T(8,128)(2,1)S(1)}, bf16[256,640]{1,0:T(8,128)(2,1)S(1)}, u32[]{:S(2)}, u32[]{:S(2)}) collective-permute-start(bf16[256,640]{1,0:T(8,128)(2,1)S(1)} %fusion.38), channel_id=1, source_target_pairs={{0,8},{8,0},{16,24},{24,16},{1,9},{9,1},{17,25},{25,17},{2,10},{10... | collective-permute-start | bytes 983048 | tf_op jit(solution)/shard_map/ppermute | solution.py:217
  78.8 7.7 %collective-permute-done.10 = bf16[256,640]{1,0:T(8,128)(2,1)S(1)} collective-permute-done((bf16[256,640]{1,0:T(8,128)(2,1)S(1)}, bf16[256,640]{1,0:T(8,128)(2,1)S(1)}, u32[]{:S(2)}, u32[]{:S(2)}) %collective-permute-start.10) | collective-permute-done | bytes 327712 | tf_op jit(solution)/shard_map/ppermute | solution.py:217
  86.5 1.2 %bitcast_add_fusion.1 = f32[256,640]{1,0:T(8,128)S(1)} fusion(bf16[256,640]{1,0:T(8,128)(2,1)S(1)} %collective-permute-done.10, f32[2,256,640]{2,1,0:T(8,128)} %copy-done.2, s32[]{:T(128)S(6)} %select_n.145), kind=kLoop, calls=%fused_computation.64 | loop fusion | flops 327680 | bytes 1638404 | tf_op jit(solution)/shard_map/add | solution.py:217
  87.9 1.0 copy.56
  88.9 0.8 copy.57
  89.7 1.4 %convert_reduce_fusion = f32[432,256]{1,0:T(8,128)S(1)} fusion(bf16[4,432,256]{2,1,0:T(8,128)(2,1)} %all-to-all-done), kind=kLoop, calls=%fused_computation.8 | loop fusion | flops 774144 | bytes 1327104 | tf_op jit(solution)/shard_map/reduce_sum | solution.py:142
  91.5 1.6 %collective-permute-start.6 = (bf16[192,128]{1,0:T(8,128)(2,1)S(1)}, bf16[192,128]{1,0:T(8,128)(2,1)S(1)}, u32[]{:S(2)}, u32[]{:S(2)}) collective-permute-start(bf16[192,128]{1,0:T(8,128)(2,1)S(1)} %get-tuple-element.60), channel_id=1, source_target_pairs={{0,8},{8,0},{16,24},{24,16},{1,9},{9,1},{17,25},{25,17},{2,10},{10... | collective-permute-start | bytes 147464 | tf_op jit(solution)/shard_map/ppermute | solution.py:51
  93.1 1.5 %collective-permute-start.7 = (bf16[192,128]{1,0:T(8,128)(2,1)S(1)}, bf16[192,128]{1,0:T(8,128)(2,1)S(1)}, u32[]{:S(2)}, u32[]{:S(2)}) collective-permute-start(bf16[192,128]{1,0:T(8,128)(2,1)S(1)} %get-tuple-element.59), channel_id=1, source_target_pairs={{0,16},{8,24},{16,0},{24,8},{1,17},{9,25},{17,1},{25,9},{2,18},{10... | collective-permute-start | bytes 147464 | tf_op jit(solution)/shard_map/ppermute | solution.py:51
  96.0 1.5 %collective-permute-done.7 = bf16[192,128]{1,0:T(8,128)(2,1)S(1)} collective-permute-done((bf16[192,128]{1,0:T(8,128)(2,1)S(1)}, bf16[192,128]{1,0:T(8,128)(2,1)S(1)}, u32[]{:S(2)}, u32[]{:S(2)}) %collective-permute-start.7) | collective-permute-done | bytes 49184 | tf_op jit(solution)/shard_map/ppermute | solution.py:51
  97.5 2.1 %collective-permute-done.8 = bf16[192,128]{1,0:T(8,128)(2,1)S(1)} collective-permute-done((bf16[192,128]{1,0:T(8,128)(2,1)S(1)}, bf16[192,128]{1,0:T(8,128)(2,1)S(1)}, u32[]{:S(2)}, u32[]{:S(2)}) %collective-permute-start.8) | collective-permute-done | bytes 49184 | tf_op jit(solution)/shard_map/ppermute | solution.py:51
  99.6 1.1 %convolution_convert_fusion.3 = bf16[672,128]{1,0:T(8,128)(2,1)} fusion(bf16[672,768]{1,0:T(8,128)(2,1)S(1)} %copy-done.1, bf16[768,128]{1,0:T(8,128)(2,1)S(1)} %bitcast.193), kind=kOutput, calls=%fused_computation.36 | convolution fusion | flops 132206592 | bytes 1400832 | tf_op jit(solution)/shard_map/dot_general | solution.py:224
  (114 shorter events, 17.2 us)
Async XLA Ops:
  0.6 3.3 %copy-start = (bf16[672,128]{1,0:T(8,128)(2,1)S(1)}, bf16[672,128]{1,0:T(8,128)(2,1)}, u32[]{:S(2)}) copy-start(bf16[672,128]{1,0:T(8,128)(2,1)} %param.7) | copy-start | bytes 516100
  2.3 9.5 %copy-start.12 = (s32[4]{0:T(128)}, s32[4]{0:T(128)S(1)}, u32[]{:S(2)}) copy-start(s32[4]{0:T(128)S(1)} %subtract_bitcast_fusion) | copy-start | bytes 52
  3.0 3.4 %copy-start.15 = (s32[4]{0:T(128)}, s32[4]{0:T(128)S(1)}, u32[]{:S(2)}) copy-start(s32[4]{0:T(128)S(1)} %fusion.47) | copy-start | bytes 52
  7.3 16.7 %collective-permute-start.2 = (bf16[192,256]{1,0:T(8,128)(2,1)}, bf16[192,256]{1,0:T(8,128)(2,1)}, u32[]{:S(2)}, u32[]{:S(2)}) collective-permute-start(bf16[192,256]{1,0:T(8,128)(2,1)} %get-tuple-element.52), channel_id=1, source_target_pairs={{0,24},{8,16},{16,8},{24,0},{1,25},{9,17},{17,9},{25,1},{2,26},{10... | collective-permute-start | bytes 294920 | tf_op jit(solution)/shard_map/ppermute | solution.py:51
  11.2 12.8 %collective-permute-start = (bf16[192,256]{1,0:T(8,128)(2,1)}, bf16[192,256]{1,0:T(8,128)(2,1)}, u32[]{:S(2)}, u32[]{:S(2)}) collective-permute-start(bf16[192,256]{1,0:T(8,128)(2,1)} %get-tuple-element.54), channel_id=1, source_target_pairs={{0,8},{8,0},{16,24},{24,16},{1,9},{9,1},{17,25},{25,17},{2,10},{10... | collective-permute-start | bytes 294920 | tf_op jit(solution)/shard_map/ppermute | solution.py:51
  11.7 12.3 %collective-permute-start.1 = (bf16[192,256]{1,0:T(8,128)(2,1)S(1)}, bf16[192,256]{1,0:T(8,128)(2,1)}, u32[]{:S(2)}, u32[]{:S(2)}) collective-permute-start(bf16[192,256]{1,0:T(8,128)(2,1)S(1)} %get-tuple-element.53), channel_id=1, source_target_pairs={{0,16},{8,24},{16,0},{24,8},{1,17},{9,25},{17,1},{25,9},{2,18},{10... | collective-permute-start | bytes 294920 | tf_op jit(solution)/shard_map/ppermute | solution.py:51
  12.6 2.6 %copy-start.10 = (s32[4]{0:T(128)}, s32[4]{0:T(128)S(1)}, u32[]{:S(2)}) copy-start(s32[4]{0:T(128)S(1)} %bitcast_subtract_fusion) | copy-start | bytes 52
  16.9 2.3 %copy-start.9 = (s32[672]{0:T(1024)S(1)}, s32[672]{0:T(1024)}, u32[]{:S(2)}) copy-start(s32[672]{0:T(1024)} %convert_reduce_fusion.1) | copy-start | bytes 8068
  16.9 2.3 %copy-start.13 = (s32[4]{0:T(128)S(1)}, s32[4]{0:T(128)}, u32[]{:S(2)}) copy-start(s32[4]{0:T(128)} %copy-done.12) | copy-start | bytes 52
  16.9 2.3 %copy-start.16 = (s32[4]{0:T(128)S(1)}, s32[4]{0:T(128)}, u32[]{:S(2)}) copy-start(s32[4]{0:T(128)} %copy-done.15) | copy-start | bytes 52
  18.2 5.6 %copy-start.11 = (s32[4]{0:T(128)S(1)}, s32[4]{0:T(128)}, u32[]{:S(2)}) copy-start(s32[4]{0:T(128)} %copy-done.10) | copy-start | bytes 52
  21.2 2.9 %copy-start.8 = (bf16[1,192,256]{2,1,0:T(8,128)(2,1)S(1)}, bf16[1,192,256]{2,1,0:T(8,128)(2,1)}, u32[]{:S(2)}) copy-start(bf16[1,192,256]{2,1,0:T(8,128)(2,1)} %get-tuple-element.51) | copy-start | bytes 294916
  25.5 21.3 %copy-start.5 = (bf16[432,256]{1,0:T(8,128)(2,1)}, bf16[432,256]{1,0:T(8,128)(2,1)S(1)}, u32[]{:S(2)}) copy-start(bf16[432,256]{1,0:T(8,128)(2,1)S(1)} %fusion.10) | copy-start | bytes 663556
  46.8 2.4 %collective-permute-start.3 = (bf16[4,432,256]{2,1,0:T(8,128)(2,1)S(1)}, bf16[4,432,256]{2,1,0:T(8,128)(2,1)S(1)}, u32[]{:S(2)}, u32[]{:S(2)}) collective-permute-start(bf16[4,432,256]{2,1,0:T(8,128)(2,1)S(1)} %bitcast.177), channel_id=1, source_target_pairs={{0,1},{1,0},{2,3},{3,2},{4,5},{5,4},{6,7},{7,6},{8,9},{9,8},{10,11... | collective-permute-start | bytes 2654216 | tf_op jit(solution)/shard_map/ppermute | solution.py:132
  49.9 0.9 copy-start.7
  49.9 1.2 %copy-start.14 = (f32[128]{0:T(128)S(1)}, f32[128]{0:T(128)}, u32[]{:S(2)}) copy-start(f32[128]{0:T(128)} %dynamic_slice.104) | copy-start | bytes 1540
  53.9 1.2 %copy-start.4 = (bf16[8,128,512]{2,1,0:T(8,128)(2,1)S(1)}, bf16[8,128,512]{2,1,0:T(8,128)(2,1)}, u32[]{:S(2)}) copy-start(bf16[8,128,512]{2,1,0:T(8,128)(2,1)} %reshape.183) | copy-start | bytes 3145732
  54.8 4.6 %collective-permute-start.4 = (bf16[4,432,128]{2,1,0:T(8,128)(2,1)S(1)}, bf16[4,432,128]{2,1,0:T(8,128)(2,1)S(1)}, u32[]{:S(2)}, u32[]{:S(2)}) collective-permute-start(bf16[4,432,128]{2,1,0:T(8,128)(2,1)S(1)} %dynamic-slice_bitcast_fusion.3), channel_id=1, source_target_pairs={{0,1},{1,0},{2,3},{3,2},{4,5},{5,4},{6,7},{7,6},{8,9},{9,8},{10,11... | collective-permute-start | bytes 1327112 | tf_op jit(solution)/shard_map/ppermute | solution.py:138
  57.2 2.2 %collective-permute-start.5 = (bf16[4,432,128]{2,1,0:T(8,128)(2,1)S(1)}, bf16[4,432,128]{2,1,0:T(8,128)(2,1)S(1)}, u32[]{:S(2)}, u32[]{:S(2)}) collective-permute-start(bf16[4,432,128]{2,1,0:T(8,128)(2,1)S(1)} %dynamic-slice_bitcast_fusion.2), channel_id=1, source_target_pairs={{0,1},{1,0},{2,3},{3,2},{4,5},{5,4},{6,7},{7,6},{8,9},{9,8},{10,11... | collective-permute-start | bytes 1327112 | tf_op jit(solution)/shard_map/ppermute | solution.py:138
  57.7 17.2 %collective-permute-start.9 = (bf16[2,256,640]{2,1,0:T(8,128)(2,1)S(1)}, bf16[2,256,640]{2,1,0:T(8,128)(2,1)}, u32[]{:S(2)}, u32[]{:S(2)}) collective-permute-start(bf16[2,256,640]{2,1,0:T(8,128)(2,1)S(1)} %fusion.25), channel_id=1, source_target_pairs={{0,16},{8,24},{16,0},{24,8},{1,17},{9,25},{17,1},{25,9},{2,18},{10... | collective-permute-start | bytes 1966088 | tf_op jit(solution)/shard_map/ppermute | solution.py:217
  60.6 29.1 %all-to-all-start = ((bf16[4,432,256]{2,1,0:T(8,128)(2,1)}), bf16[4,432,256]{2,1,0:T(8,128)(2,1)}, u32[]{:S(2)}, u32[]{:S(2)}) async-start(bf16[4,432,256]{2,1,0:T(8,128)(2,1)} %pad_maximum_fusion.1), calls=%async_computation | async-start | bytes 1769472 | tf_op jit(solution)/shard_map/all_to_all | solution.py:141
  76.1 1.1 %copy-start.2 = (f32[2,256,640]{2,1,0:T(8,128)}, f32[2,256,640]{2,1,0:T(8,128)S(1)}, u32[]{:S(2)}) copy-start(f32[2,256,640]{2,1,0:T(8,128)S(1)} %bitcast_add_fusion) | copy-start | bytes 3932164
  77.2 9.2 %collective-permute-start.10 = (bf16[256,640]{1,0:T(8,128)(2,1)S(1)}, bf16[256,640]{1,0:T(8,128)(2,1)S(1)}, u32[]{:S(2)}, u32[]{:S(2)}) collective-permute-start(bf16[256,640]{1,0:T(8,128)(2,1)S(1)} %fusion.38), channel_id=1, source_target_pairs={{0,8},{8,0},{16,24},{24,16},{1,9},{9,1},{17,25},{25,17},{2,10},{10... | collective-permute-start | bytes 983048 | tf_op jit(solution)/shard_map/ppermute | solution.py:217
  87.7 3.4 %copy-start.3 = (bf16[768,432]{1,0:T(8,128)(2,1)S(1)}, bf16[768,432]{1,0:T(8,128)(2,1)}, u32[]{:S(2)}) copy-start(bf16[768,432]{1,0:T(8,128)(2,1)} %fusion.4) | copy-start | bytes 1990660
  87.7 3.4 %copy-start.6 = (bf16[432,256]{1,0:T(8,128)(2,1)S(1)}, bf16[432,256]{1,0:T(8,128)(2,1)}, u32[]{:S(2)}) copy-start(bf16[432,256]{1,0:T(8,128)(2,1)} %copy-done.5) | copy-start | bytes 663556
  89.7 9.9 %copy-start.1 = (bf16[672,768]{1,0:T(8,128)(2,1)S(1)}, bf16[672,768]{1,0:T(8,128)(2,1)}, u32[]{:S(2)}) copy-start(bf16[672,768]{1,0:T(8,128)(2,1)} %fusion.3) | copy-start | bytes 3096580
  91.5 4.5 %collective-permute-start.6 = (bf16[192,128]{1,0:T(8,128)(2,1)S(1)}, bf16[192,128]{1,0:T(8,128)(2,1)S(1)}, u32[]{:S(2)}, u32[]{:S(2)}) collective-permute-start(bf16[192,128]{1,0:T(8,128)(2,1)S(1)} %get-tuple-element.60), channel_id=1, source_target_pairs={{0,8},{8,0},{16,24},{24,16},{1,9},{9,1},{17,25},{25,17},{2,10},{10... | collective-permute-start | bytes 147464 | tf_op jit(solution)/shard_map/ppermute | solution.py:51
  93.1 4.4 %collective-permute-start.7 = (bf16[192,128]{1,0:T(8,128)(2,1)S(1)}, bf16[192,128]{1,0:T(8,128)(2,1)S(1)}, u32[]{:S(2)}, u32[]{:S(2)}) collective-permute-start(bf16[192,128]{1,0:T(8,128)(2,1)S(1)} %get-tuple-element.59), channel_id=1, source_target_pairs={{0,16},{8,24},{16,0},{24,8},{1,17},{9,25},{17,1},{25,9},{2,18},{10... | collective-permute-start | bytes 147464 | tf_op jit(solution)/shard_map/ppermute | solution.py:51
  94.6 5.0 %collective-permute-start.8 = (bf16[192,128]{1,0:T(8,128)(2,1)S(1)}, bf16[192,128]{1,0:T(8,128)(2,1)S(1)}, u32[]{:S(2)}, u32[]{:S(2)}) collective-permute-start(bf16[192,128]{1,0:T(8,128)(2,1)S(1)} %get-tuple-element.58), channel_id=1, source_target_pairs={{0,24},{8,16},{16,8},{24,0},{1,25},{9,17},{17,9},{25,1},{2,26},{10... | collective-permute-start | bytes 147464 | tf_op jit(solution)/shard_map/ppermute | solution.py:51

commit v13 on v10

--- a/solution.py
+++ b/solution.py
@@ -114,9 +114,11 @@
     mine_tok, mine_cot = mine[..., :col_width], mine[..., col_width:]
     other_tok, other_cot = other[..., :col_width], other[..., col_width:]
 
-    def reduce_blocks(part):
+    def sibling_sum(part):
         keep, send = by_core(part, 0)
-        pair_sum = (keep.astype(f32) + lax.ppermute(send, "tensor", sibling).astype(f32)).astype(bf16)
+        return (keep.astype(f32) + lax.ppermute(send, "tensor", sibling).astype(f32)).astype(bf16)
+
+    def reduce_blocks(pair_sum):
         pieces = lax.all_to_all(pair_sum, "tensor", 0, 0, tiled=True, axis_index_groups=same_core)
         return jnp.sum(pieces.astype(f32), axis=0)
 
@@ -164,7 +166,9 @@
         owned_rows, 4 * col_width
     )
     grad_part = jnp.einsum("rn,tkn->trk", own_grad, own_proj, preferred_element_type=f32)
-    both_sum = reduce_blocks(jnp.concatenate([out_part, grad_part], axis=2).astype(bf16))
+    both_sum = reduce_blocks(
+        jnp.concatenate([sibling_sum(out_part.astype(bf16)), sibling_sum(grad_part.astype(bf16))], axis=2)
+    )
     out_sum = both_sum[:, :col_width]
     grad_sum = both_sum[:, col_width:]
     mixed_out = (own_tokens.astype(f32) + out_sum).astype(bf16)

time: 96.7 us -> 95.3 us (0.986)
  other arithmetic: 13.3 us -> 11 us
    convert_element_type x2 -> x3, other arithmetic: 2.82 us -> 0.49 us  [the longest x1 0.25 us: local(): gated = (normed * gating).astype(bf16)]
    all_to_all x1, waiting for transfers between devices: 1.63 us -> 0.16 us  [reduce_blocks(): lax.all_to_all(pair_sum, 'tensor', 0, 0, tiled=True, axis_index_groups=sa...]
    ppermute x2, waiting for transfers between devices: 15.4 us -> 16.8 us  [local(): lax.ppermute(send.astype(bf16), 'dp', partners).astype(f32)]
    squeeze x1 -> x0, other arithmetic: 1.12 us -> none  [by_core(): lax.dynamic_index_in_dim(split, 1 - core, axis + 1, keepdims=False)]
    concatenate x0 -> x1, other arithmetic: none -> 1.07 us  [local(): jnp.concatenate([sibling_sum(out_part.astype(bf16)), sibling_sum(grad_par...]
    unnamed x30 -> x34, local copies, waits for them, and re-layouts: 2.64 us -> 2.8 us
  transfers between devices with their start and end apart: 11 -> 12, of which waited for: 6 -> 6; matrix products, arithmetic and copies ran while one was open for 19% -> 19% of each run, Pallas kernels for 0% -> 0%
where the time goes in v13:
time: 95.3 us; the launch traced here: 94.8 us
  waiting for transfers between devices  21.6 us (23%)
  blocking collectives  21.3 us (22%)
  starting transfers between devices  15.8 us (17%)
  local copies, waits for them, and re-layouts  13.3 us (14%)
  other arithmetic  11 us (12%)
  matrix products  10.5 us (11%)
  between operations  1.27 us (1%)
    all_gather x1, blocking collectives, local(): lax.all_gather(own_both, 'tensor', axis=0, tiled=False, axis_index_groups...  21.3 us
    ppermute x2, waiting for transfers between devices, local(): lax.ppermute(send.astype(bf16), 'dp', partners).astype(f32)  16.8 us
    ppermute x6, starting transfers between devices, exchange(): lax.ppermute(outgoing, 'dp', [(d, d ^ k) for d in range(dp_count)])  8.02 us
    dot_general x5, matrix products, pick_rows(): return jnp.dot(one_hot, source, preferred_element_type=f32).astype(bf16)  4.35 us
    all_to_all x1, starting transfers between devices, reduce_blocks(): lax.all_to_all(pair_sum, 'tensor', 0, 0, tiled=True, axis_index_groups=sa...  4.21 us
    ppermute x6, waiting for transfers between devices, exchange(): lax.ppermute(outgoing, 'dp', [(d, d ^ k) for d in range(dp_count)])  3.69 us
    ppermute x2, starting transfers between devices, local(): lax.ppermute(send.astype(bf16), 'dp', partners).astype(f32)  3.14 us
    unnamed x34, local copies, waits for them, and re-layouts  2.8 us
  transfers between devices with their start and end apart: 12, of which 6 were waited for; matrix products, arithmetic and copies ran while one was open for 19% of the time, Pallas kernels for 0%

profile of v13, /device:TPU:0, one launch (start us, length us, event | category | flops | bytes accessed | tf_op | source)
XLA Modules:
  0.0 94.8 jit_solution(1125770916450393728)
XLA Ops:
  0.7 1.4 %fusion.52 = (s32[]{:T(128)}, s32[1,4]{1,0:T(1,128)S(1)}) fusion(s32[4,4]{1,0:T(4,128)} %param.9, s32[]{:T(128)S(6)} %select_n.123), kind=kLoop, calls=%fused_computation.151 | loop fusion | flops 3 | bytes 40 | tf_op jit(solution)/shard_map/reduce_sum | solution.py:212
  2.3 0.7 fusion.51
  3.0 0.8 select_reduce_fusion.3
  4.0 0.7 fusion.14
  4.7 1.6 %fusion.15 = bf16[768,128]{0,1:T(8,128)(2,1)S(1)} fusion(bf16[672,128]{1,0:T(8,128)(2,1)} %param.8, s32[768]{0:T(1024)S(1)} %min.38), kind=kOutput, calls=%fused_computation.33 | convolution fusion | flops 132734976 | bytes 371712 | tf_op jit(solution)/shard_map/dot_general | solution.py:56
  6.6 0.8 constant_dynamic-slice_fusion.7
  7.3 3.9 %collective-permute-start.2 = (bf16[192,256]{1,0:T(8,128)(2,1)}, bf16[192,256]{1,0:T(8,128)(2,1)}, u32[]{:S(2)}, u32[]{:S(2)}) collective-permute-start(bf16[192,256]{1,0:T(8,128)(2,1)} %get-tuple-element.48), channel_id=1, source_target_pairs={{0,24},{8,16},{16,8},{24,0},{1,25},{9,17},{17,9},{25,1},{2,26},{10... | collective-permute-start | bytes 294920 | tf_op jit(solution)/shard_map/ppermute | solution.py:51
  11.8 2.4 %constant_dynamic-slice_fusion.2 = (bf16[1024,4,128]{2,1,0:T(4,128)(2,1)S(1)}, bf16[1024,4,128]{2,1,0:T(4,128)(2,1)S(1)}) fusion(bf16[1024,4,1024]{2,1,0:T(4,128)(2,1)} %param.11, s32[]{:T(128)S(6)} %select_n.133, s32[]{:T(128)S(6)} %select_n.129), kind=kLoop, calls=%fused_computation.127 | loop fusion | bytes 4194312 | tf_op jit(solution)/shard_map/dynamic_slice | solution.py:80
  14.7 1.2 %reshape.183 = bf16[8,128,512]{2,1,0:T(8,128)(2,1)} reshape(bf16[1024,4,128]{2,1,0:T(4,128)(2,1)S(1)} %get-tuple-element.38) | data formatting | bytes 2097152 | tf_op jit(solution)/shard_map/reshape | solution.py:80
  15.9 1.1 %constant_dynamic-slice_fusion.1 = (bf16[128,1024]{1,0:T(8,128)(2,1)S(1)}, bf16[128,1024]{1,0:T(8,128)(2,1)S(1)}) fusion(bf16[1024,1024]{1,0:T(8,128)(2,1)} %param.13, s32[]{:T(128)S(6)} %select_n.133, s32[]{:T(128)S(6)} %select_n.129), kind=kLoop, calls=%fused_computation.126 | loop fusion | bytes 1048584 | tf_op jit(solution)/shard_map/dynamic_slice | solution.py:90
  17.4 0.8 copy.46
  18.3 1.3 %dynamic_slice.104 = f32[128]{0:T(128)} dynamic-slice(f32[1024]{0:T(1024)} %param.12, s32[]{:T(128)S(6)} %select_n.129), dynamic_slice_sizes={128} | dynamic-slice | bytes 1028 | tf_op jit(solution)/shard_map/dynamic_slice | solution.py:86
  20.2 1.0 %pad_maximum_fusion.4 = bf16[4,192,256]{2,1,0:T(8,128)(2,1)S(1)} fusion(bf16[1,192,256]{2,1,0:T(8,128)(2,1)} %bitcast.10, bf16[1,192,256]{2,1,0:T(8,128)(2,1)} %bitcast.8, bf16[1,192,256]{2,1,0:T(8,128)(2,1)} %bitcast.6, bf16[1,192,256]{2,1,0:T(8,128)(2,1)S(1)} %copy-done.5), kind=kLoop, calls=%fused_computation.78 | loop fusion | flops 589824 | bytes 786432 | tf_op jit(solution)/shard_map/stack | solution.py:52
  21.7 21.3 %all-gather = bf16[1728,256]{1,0:T(8,128)(2,1)S(1)} all-gather(bf16[432,256]{1,0:T(8,128)(2,1)S(1)} %fusion.10), channel_id=2, replica_groups={{0,2,4,6},{1,3,5,7},{8,10,12,14},{9,11,13,15},{16,18,20,22},{17,19,21,2..., dimensions={0}, use_global_device_ids=true | all-gather | bytes 1105920 | tf_op jit(solution)/shard_map/all_gather | solution.py:112
  43.1 0.7 min.43
  44.5 0.9 collective-permute-done.3
  53.9 1.6 %collective-permute-start.9 = (bf16[2,256,640]{2,1,0:T(8,128)(2,1)S(1)}, bf16[2,256,640]{2,1,0:T(8,128)(2,1)}, u32[]{:S(2)}, u32[]{:S(2)}) collective-permute-start(bf16[2,256,640]{2,1,0:T(8,128)(2,1)S(1)} %fusion.29), channel_id=1, source_target_pairs={{0,16},{8,24},{16,0},{24,8},{1,17},{9,25},{17,1},{25,9},{2,18},{10... | collective-permute-start | bytes 1966088 | tf_op jit(solution)/shard_map/ppermute | solution.py:198
  55.8 1.1 %pad_maximum_fusion.1 = bf16[4,432,256]{2,1,0:T(8,128)(2,1)} fusion(bf16[4,432,128]{2,1,0:T(8,128)(2,1)S(1)} %fusion.24, bf16[4,432,128]{2,1,0:T(8,128)(2,1)S(1)} %fusion.25), kind=kLoop, calls=%fused_computation.53 | loop fusion | flops 1769472 | bytes 1769472 | tf_op jit(solution)/shard_map/concatenate | solution.py:170
  56.8 4.2 %all-to-all-start = ((bf16[4,432,256]{2,1,0:T(8,128)(2,1)}), bf16[4,432,256]{2,1,0:T(8,128)(2,1)}, u32[]{:S(2)}, u32[]{:S(2)}) async-start(bf16[4,432,256]{2,1,0:T(8,128)(2,1)} %pad_maximum_fusion.1), calls=%async_computation | async-start | bytes 1769472 | tf_op jit(solution)/shard_map/all_to_all | solution.py:122
  61.1 10.0 %collective-permute-done.9 = bf16[2,256,640]{2,1,0:T(8,128)(2,1)} collective-permute-done((bf16[2,256,640]{2,1,0:T(8,128)(2,1)S(1)}, bf16[2,256,640]{2,1,0:T(8,128)(2,1)}, u32[]{:S(2)}, u32[]{:S(2)}) %collective-permute-start.9) | collective-permute-done | bytes 655392 | tf_op jit(solution)/shard_map/ppermute | solution.py:198
  71.0 1.2 %bitcast_add_fusion = f32[2,256,640]{2,1,0:T(8,128)S(1)} fusion(bf16[2,256,640]{2,1,0:T(8,128)(2,1)} %collective-permute-done.9, f32[2,2,256,640]{3,2,1,0:T(8,128)S(1)} %maximum_convert_fusion, s32[]{:T(128)S(6)} %select_n.143), kind=kLoop, calls=%fused_computation.24 | loop fusion | flops 655360 | bytes 3276804 | tf_op jit(solution)/shard_map/add | solution.py:198
  72.3 1.6 %collective-permute-start.10 = (bf16[256,640]{1,0:T(8,128)(2,1)S(1)}, bf16[256,640]{1,0:T(8,128)(2,1)S(1)}, u32[]{:S(2)}, u32[]{:S(2)}) collective-permute-start(bf16[256,640]{1,0:T(8,128)(2,1)S(1)} %fusion.42), channel_id=1, source_target_pairs={{0,8},{8,0},{16,24},{24,16},{1,9},{9,1},{17,25},{25,17},{2,10},{10... | collective-permute-start | bytes 983048 | tf_op jit(solution)/shard_map/ppermute | solution.py:198
  74.0 0.7 add_select_fusion
  74.7 6.9 %collective-permute-done.10 = bf16[256,640]{1,0:T(8,128)(2,1)S(1)} collective-permute-done((bf16[256,640]{1,0:T(8,128)(2,1)S(1)}, bf16[256,640]{1,0:T(8,128)(2,1)S(1)}, u32[]{:S(2)}, u32[]{:S(2)}) %collective-permute-start.10) | collective-permute-done | bytes 327712 | tf_op jit(solution)/shard_map/ppermute | solution.py:198
  81.9 1.0 %copy.56 = f32[256,4,128]{2,1,0:T(4,128)} copy(f32[256,4,128]{0,2,1:T(8,128)S(1)} %bitcast.183) | data formatting | bytes 1048576
  82.9 0.8 copy.57
  83.8 1.3 %convert_reduce_fusion = f32[432,256]{1,0:T(8,128)S(1)} fusion(bf16[4,432,256]{2,1,0:T(8,128)(2,1)} %all-to-all-done), kind=kLoop, calls=%fused_computation.8 | loop fusion | flops 774144 | bytes 1327104 | tf_op jit(solution)/shard_map/reduce_sum | solution.py:123
  85.6 1.6 %collective-permute-start.6 = (bf16[192,128]{1,0:T(8,128)(2,1)S(1)}, bf16[192,128]{1,0:T(8,128)(2,1)S(1)}, u32[]{:S(2)}, u32[]{:S(2)}) collective-permute-start(bf16[192,128]{1,0:T(8,128)(2,1)S(1)} %get-tuple-element.56), channel_id=1, source_target_pairs={{0,8},{8,0},{16,24},{24,16},{1,9},{9,1},{17,25},{25,17},{2,10},{10... | collective-permute-start | bytes 147464 | tf_op jit(solution)/shard_map/ppermute | solution.py:51
  87.2 1.4 %collective-permute-start.7 = (bf16[192,128]{1,0:T(8,128)(2,1)S(1)}, bf16[192,128]{1,0:T(8,128)(2,1)S(1)}, u32[]{:S(2)}, u32[]{:S(2)}) collective-permute-start(bf16[192,128]{1,0:T(8,128)(2,1)S(1)} %get-tuple-element.55), channel_id=1, source_target_pairs={{0,16},{8,24},{16,0},{24,8},{1,17},{9,25},{17,1},{25,9},{2,18},{10... | collective-permute-start | bytes 147464 | tf_op jit(solution)/shard_map/ppermute | solution.py:51
  89.9 1.9 %collective-permute-done.7 = bf16[192,128]{1,0:T(8,128)(2,1)S(1)} collective-permute-done((bf16[192,128]{1,0:T(8,128)(2,1)S(1)}, bf16[192,128]{1,0:T(8,128)(2,1)S(1)}, u32[]{:S(2)}, u32[]{:S(2)}) %collective-permute-start.7) | collective-permute-done | bytes 49184 | tf_op jit(solution)/shard_map/ppermute | solution.py:51
  91.8 1.7 %collective-permute-done.8 = bf16[192,128]{1,0:T(8,128)(2,1)S(1)} collective-permute-done((bf16[192,128]{1,0:T(8,128)(2,1)S(1)}, bf16[192,128]{1,0:T(8,128)(2,1)S(1)}, u32[]{:S(2)}, u32[]{:S(2)}) %collective-permute-start.8) | collective-permute-done | bytes 49184 | tf_op jit(solution)/shard_map/ppermute | solution.py:51
  93.6 1.2 %fusion.16 = bf16[672,128]{1,0:T(8,128)(2,1)} fusion(bf16[768,128]{1,0:T(8,128)(2,1)S(1)} %bitcast.194, s32[672]{0:T(1024)S(1)} %add_select_fusion), kind=kOutput, calls=%fused_computation.36 | convolution fusion | flops 132722688 | bytes 371328 | tf_op jit(solution)/shard_map/dot_general | solution.py:56
  (108 shorter events, 14.7 us)
Async XLA Ops:
  0.6 3.4 %copy-start = (bf16[672,128]{1,0:T(8,128)(2,1)S(1)}, bf16[672,128]{1,0:T(8,128)(2,1)}, u32[]{:S(2)}) copy-start(bf16[672,128]{1,0:T(8,128)(2,1)} %param.7) | copy-start | bytes 516100
  2.3 1.5 %copy-start.8 = (s32[4]{0:T(128)}, s32[4]{0:T(128)S(1)}, u32[]{:S(2)}) copy-start(s32[4]{0:T(128)S(1)} %subtract_bitcast_fusion) | copy-start | bytes 52
  3.0 0.9 copy-start.13
  7.3 12.8 %collective-permute-start.2 = (bf16[192,256]{1,0:T(8,128)(2,1)}, bf16[192,256]{1,0:T(8,128)(2,1)}, u32[]{:S(2)}, u32[]{:S(2)}) collective-permute-start(bf16[192,256]{1,0:T(8,128)(2,1)} %get-tuple-element.48), channel_id=1, source_target_pairs={{0,24},{8,16},{16,8},{24,0},{1,25},{9,17},{17,9},{25,1},{2,26},{10... | collective-permute-start | bytes 294920 | tf_op jit(solution)/shard_map/ppermute | solution.py:51
  11.2 8.9 %collective-permute-start = (bf16[192,256]{1,0:T(8,128)(2,1)}, bf16[192,256]{1,0:T(8,128)(2,1)}, u32[]{:S(2)}, u32[]{:S(2)}) collective-permute-start(bf16[192,256]{1,0:T(8,128)(2,1)} %get-tuple-element.50), channel_id=1, source_target_pairs={{0,8},{8,0},{16,24},{24,16},{1,9},{9,1},{17,25},{25,17},{2,10},{10... | collective-permute-start | bytes 294920 | tf_op jit(solution)/shard_map/ppermute | solution.py:51
  11.8 8.4 %collective-permute-start.1 = (bf16[192,256]{1,0:T(8,128)(2,1)}, bf16[192,256]{1,0:T(8,128)(2,1)}, u32[]{:S(2)}, u32[]{:S(2)}) collective-permute-start(bf16[192,256]{1,0:T(8,128)(2,1)} %get-tuple-element.49), channel_id=1, source_target_pairs={{0,16},{8,24},{16,0},{24,8},{1,17},{9,25},{17,1},{25,9},{2,18},{10... | collective-permute-start | bytes 294920 | tf_op jit(solution)/shard_map/ppermute | solution.py:51
  17.2 3.0 %copy-start.5 = (bf16[1,192,256]{2,1,0:T(8,128)(2,1)S(1)}, bf16[1,192,256]{2,1,0:T(8,128)(2,1)}, u32[]{:S(2)}) copy-start(bf16[1,192,256]{2,1,0:T(8,128)(2,1)} %get-tuple-element.47) | copy-start | bytes 294916
  19.9 1.4 %copy-start.6 = (s32[4]{0:T(128)}, s32[4]{0:T(128)S(1)}, u32[]{:S(2)}) copy-start(s32[4]{0:T(128)S(1)} %bitcast_subtract_fusion) | copy-start | bytes 52
  20.1 23.6 %copy-start.9 = (s32[4]{0:T(128)S(1)}, s32[4]{0:T(128)}, u32[]{:S(2)}) copy-start(s32[4]{0:T(128)} %copy-done.8) | copy-start | bytes 52
  21.2 21.7 %copy-start.7 = (s32[4]{0:T(128)S(1)}, s32[4]{0:T(128)}, u32[]{:S(2)}) copy-start(s32[4]{0:T(128)} %copy-done.6) | copy-start | bytes 52
  21.6 21.3 %copy-start.3 = (bf16[432,256]{1,0:T(8,128)(2,1)}, bf16[432,256]{1,0:T(8,128)(2,1)S(1)}, u32[]{:S(2)}) copy-start(bf16[432,256]{1,0:T(8,128)(2,1)S(1)} %fusion.10) | copy-start | bytes 663556
  43.0 2.4 %collective-permute-start.3 = (bf16[4,432,256]{2,1,0:T(8,128)(2,1)S(1)}, bf16[4,432,256]{2,1,0:T(8,128)(2,1)S(1)}, u32[]{:S(2)}, u32[]{:S(2)}) collective-permute-start(bf16[4,432,256]{2,1,0:T(8,128)(2,1)S(1)} %bitcast.175), channel_id=1, source_target_pairs={{0,1},{1,0},{2,3},{3,2},{4,5},{5,4},{6,7},{7,6},{8,9},{9,8},{10,11... | collective-permute-start | bytes 2654216 | tf_op jit(solution)/shard_map/ppermute | solution.py:113
  46.1 0.9 copy-start.2
  46.1 1.2 %copy-start.12 = (f32[128]{0:T(128)S(1)}, f32[128]{0:T(128)}, u32[]{:S(2)}) copy-start(f32[128]{0:T(128)} %dynamic_slice.104) | copy-start | bytes 1540
  50.1 1.2 %copy-start.1 = (bf16[8,128,512]{2,1,0:T(8,128)(2,1)S(1)}, bf16[8,128,512]{2,1,0:T(8,128)(2,1)}, u32[]{:S(2)}) copy-start(bf16[8,128,512]{2,1,0:T(8,128)(2,1)} %reshape.183) | copy-start | bytes 3145732
  50.9 4.6 %collective-permute-start.4 = (bf16[4,432,128]{2,1,0:T(8,128)(2,1)S(1)}, bf16[4,432,128]{2,1,0:T(8,128)(2,1)S(1)}, u32[]{:S(2)}, u32[]{:S(2)}) collective-permute-start(bf16[4,432,128]{2,1,0:T(8,128)(2,1)S(1)} %dynamic-slice_bitcast_fusion.3), channel_id=1, source_target_pairs={{0,1},{1,0},{2,3},{3,2},{4,5},{5,4},{6,7},{7,6},{8,9},{9,8},{10,11... | collective-permute-start | bytes 1327112 | tf_op jit(solution)/shard_map/ppermute | solution.py:119
  53.4 2.2 %collective-permute-start.5 = (bf16[4,432,128]{2,1,0:T(8,128)(2,1)S(1)}, bf16[4,432,128]{2,1,0:T(8,128)(2,1)S(1)}, u32[]{:S(2)}, u32[]{:S(2)}) collective-permute-start(bf16[4,432,128]{2,1,0:T(8,128)(2,1)S(1)} %dynamic-slice_bitcast_fusion.2), channel_id=1, source_target_pairs={{0,1},{1,0},{2,3},{3,2},{4,5},{5,4},{6,7},{7,6},{8,9},{9,8},{10,11... | collective-permute-start | bytes 1327112 | tf_op jit(solution)/shard_map/ppermute | solution.py:119
  53.9 17.1 %collective-permute-start.9 = (bf16[2,256,640]{2,1,0:T(8,128)(2,1)S(1)}, bf16[2,256,640]{2,1,0:T(8,128)(2,1)}, u32[]{:S(2)}, u32[]{:S(2)}) collective-permute-start(bf16[2,256,640]{2,1,0:T(8,128)(2,1)S(1)} %fusion.29), channel_id=1, source_target_pairs={{0,16},{8,24},{16,0},{24,8},{1,17},{9,25},{17,1},{25,9},{2,18},{10... | collective-permute-start | bytes 1966088 | tf_op jit(solution)/shard_map/ppermute | solution.py:198
  56.8 27.0 %all-to-all-start = ((bf16[4,432,256]{2,1,0:T(8,128)(2,1)}), bf16[4,432,256]{2,1,0:T(8,128)(2,1)}, u32[]{:S(2)}, u32[]{:S(2)}) async-start(bf16[4,432,256]{2,1,0:T(8,128)(2,1)} %pad_maximum_fusion.1), calls=%async_computation | async-start | bytes 1769472 | tf_op jit(solution)/shard_map/all_to_all | solution.py:122
  61.1 12.8 %copy-start.10 = (s32[4]{0:T(128)S(1)}, s32[4]{0:T(128)}, u32[]{:S(2)}) copy-start(s32[4]{0:T(128)} %copy-done.8) | copy-start | bytes 52
  61.1 12.8 %copy-start.14 = (s32[4]{0:T(128)S(1)}, s32[4]{0:T(128)}, u32[]{:S(2)}) copy-start(s32[4]{0:T(128)} %copy-done.13) | copy-start | bytes 52
  72.3 9.2 %collective-permute-start.10 = (bf16[256,640]{1,0:T(8,128)(2,1)S(1)}, bf16[256,640]{1,0:T(8,128)(2,1)S(1)}, u32[]{:S(2)}, u32[]{:S(2)}) collective-permute-start(bf16[256,640]{1,0:T(8,128)(2,1)S(1)} %fusion.42), channel_id=1, source_target_pairs={{0,8},{8,0},{16,24},{24,16},{1,9},{9,1},{17,25},{25,17},{2,10},{10... | collective-permute-start | bytes 983048 | tf_op jit(solution)/shard_map/ppermute | solution.py:198
  81.7 3.5 %copy-start.4 = (bf16[432,256]{1,0:T(8,128)(2,1)S(1)}, bf16[432,256]{1,0:T(8,128)(2,1)}, u32[]{:S(2)}) copy-start(bf16[432,256]{1,0:T(8,128)(2,1)} %copy-done.3) | copy-start | bytes 663556
  81.7 3.5 %copy-start.11 = (s32[768]{0:T(1024)S(1)}, s32[768]{0:T(1024)}, u32[]{:S(2)}) copy-start(s32[768]{0:T(1024)} %min.43) | copy-start | bytes 9220
  85.6 4.2 %collective-permute-start.6 = (bf16[192,128]{1,0:T(8,128)(2,1)S(1)}, bf16[192,128]{1,0:T(8,128)(2,1)S(1)}, u32[]{:S(2)}, u32[]{:S(2)}) collective-permute-start(bf16[192,128]{1,0:T(8,128)(2,1)S(1)} %get-tuple-element.56), channel_id=1, source_target_pairs={{0,8},{8,0},{16,24},{24,16},{1,9},{9,1},{17,25},{25,17},{2,10},{10... | collective-permute-start | bytes 147464 | tf_op jit(solution)/shard_map/ppermute | solution.py:51
  87.2 4.6 %collective-permute-start.7 = (bf16[192,128]{1,0:T(8,128)(2,1)S(1)}, bf16[192,128]{1,0:T(8,128)(2,1)S(1)}, u32[]{:S(2)}, u32[]{:S(2)}) collective-permute-start(bf16[192,128]{1,0:T(8,128)(2,1)S(1)} %get-tuple-element.55), channel_id=1, source_target_pairs={{0,16},{8,24},{16,0},{24,8},{1,17},{9,25},{17,1},{25,9},{2,18},{10... | collective-permute-start | bytes 147464 | tf_op jit(solution)/shard_map/ppermute | solution.py:51
  88.6 5.0 %collective-permute-start.8 = (bf16[192,128]{1,0:T(8,128)(2,1)S(1)}, bf16[192,128]{1,0:T(8,128)(2,1)S(1)}, u32[]{:S(2)}, u32[]{:S(2)}) collective-permute-start(bf16[192,128]{1,0:T(8,128)(2,1)S(1)} %get-tuple-element.54), channel_id=1, source_target_pairs={{0,24},{8,16},{16,8},{24,0},{1,25},{9,17},{17,9},{25,1},{2,26},{10... | collective-permute-start | bytes 147464 | tf_op jit(solution)/shard_map/ppermute | solution.py:51

commit v14 on v13

--- a/solution.py
+++ b/solution.py
@@ -188,14 +188,12 @@
         jnp.einsum("trc,rd->tcd", other_cot, own_gated, preferred_element_type=f32),
     )
     terms = jnp.concatenate([proj_term, out_term], axis=1).astype(bf16)
-    bit_count = dp_count.bit_length() - 1
-    term_sum = terms.reshape((2,) * bit_count + (D // dp_count,) + terms.shape[1:]).astype(f32)
-    for level in range(bit_count - 1, -1, -1):
-        my_bit = (dp_index >> level) & 1
-        keep = lax.dynamic_index_in_dim(term_sum, my_bit, 0, keepdims=False)
-        send = lax.dynamic_index_in_dim(term_sum, 1 - my_bit, 0, keepdims=False)
-        partners = [(d, d ^ (1 << level)) for d in range(dp_count)]
-        term_sum = keep + lax.ppermute(send.astype(bf16), "dp", partners).astype(f32)
+    term_blocks = terms.reshape((dp_count, D // dp_count) + terms.shape[1:])
+    term_sum = lax.dynamic_index_in_dim(term_blocks, dp_index, 0, keepdims=False).astype(f32)
+    for k in range(1, dp_count):
+        outgoing = lax.dynamic_index_in_dim(term_blocks, dp_index ^ k, 0, keepdims=False)
+        partners = [(d, d ^ k) for d in range(dp_count)]
+        term_sum = term_sum + lax.ppermute(outgoing, "dp", partners).astype(f32)
     proj_grad = term_sum[:, : 4 * col_width].reshape(-1, 4, col_width)
     out_grad = term_sum[:, 4 * col_width :].T
 

time: 95.3 us -> 91.5 us (0.960)
  other arithmetic: 11 us -> 8.41 us
  waiting for transfers between devices: 21.6 us -> 20.4 us
    ppermute x2 -> x3, waiting for transfers between devices: 16.8 us -> 13.6 us  [local(): term_sum = term_sum + lax.ppermute(outgoing, 'dp', partners).astype(f32)]
    all_to_all x1, waiting for transfers between devices: 0.16 us -> 2.48 us  [reduce_blocks(): lax.all_to_all(pair_sum, 'tensor', 0, 0, tiled=True, axis_index_groups=sa...]
    reduce_sum x1, other arithmetic: 1.33 us -> 0.12 us  [reduce_blocks(): return jnp.sum(pieces.astype(f32), axis=0)]
    add x2 -> x1, other arithmetic: 1.29 us -> 0.15 us  [local(): term_sum = term_sum + lax.ppermute(outgoing, 'dp', partners).astype(f32)]
    unnamed x34 -> x24, local copies, waits for them, and re-layouts: 2.8 us -> 3.7 us
    ppermute x2 -> x3, starting transfers between devices: 3.14 us -> 3.55 us  [local(): term_sum = term_sum + lax.ppermute(outgoing, 'dp', partners).astype(f32)]
  transfers between devices with their start and end apart: 12 -> 13, of which waited for: 6 -> 8; matrix products, arithmetic and copies ran while one was open for 19% -> 17% of each run, Pallas kernels for 0% -> 0%
where the time goes in v14:
time: 91.5 us; the launch traced here: 91 us
  blocking collectives  21.3 us (23%)
  waiting for transfers between devices  20.4 us (22%)
  starting transfers between devices  15.7 us (17%)
  local copies, waits for them, and re-layouts  13.5 us (15%)
  matrix products  10.5 us (11%)
  other arithmetic  8.41 us (9%)
  between operations  1.18 us (1%)
    all_gather x1, blocking collectives, local(): lax.all_gather(own_both, 'tensor', axis=0, tiled=False, axis_index_groups...  21.3 us
    ppermute x3, waiting for transfers between devices, local(): term_sum = term_sum + lax.ppermute(outgoing, 'dp', partners).astype(f32)  13.6 us
    ppermute x6, starting transfers between devices, exchange(): lax.ppermute(outgoing, 'dp', [(d, d ^ k) for d in range(dp_count)])  8.02 us
    dot_general x5, matrix products, pick_rows(): return jnp.dot(one_hot, source, preferred_element_type=f32).astype(bf16)  4.36 us
    unnamed x24, local copies, waits for them, and re-layouts  3.7 us
    ppermute x3, starting transfers between devices, local(): term_sum = term_sum + lax.ppermute(outgoing, 'dp', partners).astype(f32)  3.55 us
    all_to_all x1, starting transfers between devices, reduce_blocks(): lax.all_to_all(pair_sum, 'tensor', 0, 0, tiled=True, axis_index_groups=sa...  3.5 us
    ppermute x6, waiting for transfers between devices, exchange(): lax.ppermute(outgoing, 'dp', [(d, d ^ k) for d in range(dp_count)])  2.89 us
  transfers between devices with their start and end apart: 13, of which 8 were waited for; matrix products, arithmetic and copies ran while one was open for 17% of the time, Pallas kernels for 0%

profile of v14, /device:TPU:0, one launch (start us, length us, event | category | flops | bytes accessed | tf_op | source)
XLA Modules:
  0.0 91.0 jit_solution(11420318767585600846)
XLA Ops:
  0.7 1.4 %fusion.60 = (s32[]{:T(128)}, s32[1,4]{1,0:T(1,128)S(1)}) fusion(s32[4,4]{1,0:T(4,128)} %param.9, s32[]{:T(128)S(6)} %select_n.114), kind=kLoop, calls=%fused_computation.163 | loop fusion | flops 3 | bytes 40 | tf_op jit(solution)/shard_map/reduce_sum | solution.py:210
  2.2 0.7 fusion.59
  2.9 0.8 select_reduce_fusion.3
  3.9 0.7 fusion.15
  4.7 1.6 %fusion.14 = bf16[768,128]{0,1:T(8,128)(2,1)S(1)} fusion(bf16[672,128]{1,0:T(8,128)(2,1)} %param.7, s32[768]{0:T(1024)S(1)} %min.38), kind=kOutput, calls=%fused_computation.37 | convolution fusion | flops 132734976 | bytes 371712 | tf_op jit(solution)/shard_map/dot_general | solution.py:56
  6.5 0.7 constant_dynamic-slice_fusion.7
  7.3 3.9 %collective-permute-start.2 = (bf16[192,256]{1,0:T(8,128)(2,1)}, bf16[192,256]{1,0:T(8,128)(2,1)}, u32[]{:S(2)}, u32[]{:S(2)}) collective-permute-start(bf16[192,256]{1,0:T(8,128)(2,1)} %get-tuple-element.51), channel_id=1, source_target_pairs={{0,24},{8,16},{16,8},{24,0},{1,25},{9,17},{17,9},{25,1},{2,26},{10... | collective-permute-start | bytes 294920 | tf_op jit(solution)/shard_map/ppermute | solution.py:51
  11.7 2.4 %constant_dynamic-slice_fusion.2 = (bf16[1024,4,128]{2,1,0:T(4,128)(2,1)S(1)}, bf16[1024,4,128]{2,1,0:T(4,128)(2,1)S(1)}) fusion(bf16[1024,4,1024]{2,1,0:T(4,128)(2,1)} %param.11, s32[]{:T(128)S(6)} %select_n.124, s32[]{:T(128)S(6)} %select_n.120), kind=kLoop, calls=%fused_computation.139 | loop fusion | bytes 4194312 | tf_op jit(solution)/shard_map/dynamic_slice | solution.py:80
  14.6 1.1 %constant_dynamic-slice_fusion.1 = (bf16[128,1024]{1,0:T(8,128)(2,1)S(1)}, bf16[128,1024]{1,0:T(8,128)(2,1)S(1)}) fusion(bf16[1024,1024]{1,0:T(8,128)(2,1)} %param.13, s32[]{:T(128)S(6)} %select_n.124, s32[]{:T(128)S(6)} %select_n.120), kind=kLoop, calls=%fused_computation.138 | loop fusion | bytes 1048584 | tf_op jit(solution)/shard_map/dynamic_slice | solution.py:90
  16.1 0.8 copy.46
  16.9 1.2 %reshape.183 = bf16[8,128,512]{2,1,0:T(8,128)(2,1)} reshape(bf16[1024,4,128]{2,1,0:T(4,128)(2,1)S(1)} %get-tuple-element.38) | data formatting | bytes 2097152 | tf_op jit(solution)/shard_map/reshape | solution.py:80
  18.1 0.8 copy.60
  18.9 1.3 %dynamic_slice.103 = f32[128]{0:T(128)} dynamic-slice(f32[1024]{0:T(1024)} %param.12, s32[]{:T(128)S(6)} %select_n.120), dynamic_slice_sizes={128} | dynamic-slice | bytes 1028 | tf_op jit(solution)/shard_map/dynamic_slice | solution.py:86
  20.8 1.0 %pad_maximum_fusion.4 = bf16[4,192,256]{2,1,0:T(8,128)(2,1)S(1)} fusion(bf16[1,192,256]{2,1,0:T(8,128)(2,1)} %bitcast.10, bf16[1,192,256]{2,1,0:T(8,128)(2,1)} %bitcast.8, bf16[1,192,256]{2,1,0:T(8,128)(2,1)} %bitcast.6, bf16[1,192,256]{2,1,0:T(8,128)(2,1)S(1)} %get-tuple-element.50), kind=kLoop, calls=%fused_computation.83 | loop fusion | flops 589824 | bytes 786432 | tf_op jit(solution)/shard_map/stack | solution.py:52
  22.2 21.3 %all-gather = bf16[1728,256]{1,0:T(8,128)(2,1)S(1)} all-gather(bf16[432,256]{1,0:T(8,128)(2,1)S(1)} %fusion.10), channel_id=2, replica_groups={{0,2,4,6},{1,3,5,7},{8,10,12,14},{9,11,13,15},{16,18,20,22},{17,19,21,2..., dimensions={0}, use_global_device_ids=true | all-gather | bytes 1105920 | tf_op jit(solution)/shard_map/all_gather | solution.py:112
  44.5 1.5 %collective-permute-done.3 = bf16[4,432,256]{2,1,0:T(8,128)(2,1)S(1)} collective-permute-done((bf16[4,432,256]{2,1,0:T(8,128)(2,1)S(1)}, bf16[4,432,256]{2,1,0:T(8,128)(2,1)S(1)}, u32[]{:S(2)}, u32[]{:S(2)}) %collective-permute-start.3) | collective-permute-done | bytes 884768 | tf_op jit(solution)/shard_map/ppermute | solution.py:113
  51.1 0.7 convolution_convert_fusion
  54.8 1.0 %pad_maximum_fusion.1 = bf16[4,432,256]{2,1,0:T(8,128)(2,1)} fusion(bf16[4,432,128]{2,1,0:T(8,128)(2,1)S(1)} %fusion.24, bf16[4,432,128]{2,1,0:T(8,128)(2,1)S(1)} %fusion.25), kind=kLoop, calls=%fused_computation.58 | loop fusion | flops 1769472 | bytes 1769472 | tf_op jit(solution)/shard_map/concatenate | solution.py:170
  55.8 3.5 %all-to-all-start = ((bf16[4,432,256]{2,1,0:T(8,128)(2,1)}), bf16[4,432,256]{2,1,0:T(8,128)(2,1)S(1)}, u32[]{:S(2)}, u32[]{:S(2)}) async-start(bf16[4,432,256]{2,1,0:T(8,128)(2,1)} %pad_maximum_fusion.1), calls=%async_computation | async-start | bytes 1769472 | tf_op jit(solution)/shard_map/all_to_all | solution.py:122
  59.6 2.5 %collective-permute-start.11 = (bf16[256,640]{1,0:T(8,128)(2,1)S(1)}, bf16[256,640]{1,0:T(8,128)(2,1)S(1)}, u32[]{:S(2)}, u32[]{:S(2)}) collective-permute-start(bf16[256,640]{1,0:T(8,128)(2,1)S(1)} %get-tuple-element.44), channel_id=1, source_target_pairs={{0,24},{8,16},{16,8},{24,0},{1,25},{9,17},{17,9},{25,1},{2,26},{10... | collective-permute-start | bytes 983048 | tf_op jit(solution)/shard_map/ppermute | solution.py:196
  63.2 0.6 add_select_fusion
  63.9 7.3 %collective-permute-done.11 = bf16[256,640]{1,0:T(8,128)(2,1)S(1)} collective-permute-done((bf16[256,640]{1,0:T(8,128)(2,1)S(1)}, bf16[256,640]{1,0:T(8,128)(2,1)S(1)}, u32[]{:S(2)}, u32[]{:S(2)}) %collective-permute-start.11) | collective-permute-done | bytes 327712 | tf_op jit(solution)/shard_map/ppermute | solution.py:196
  71.1 6.2 %collective-permute-done.10 = bf16[256,640]{1,0:T(8,128)(2,1)S(1)} collective-permute-done((bf16[256,640]{1,0:T(8,128)(2,1)S(1)}, bf16[256,640]{1,0:T(8,128)(2,1)S(1)}, u32[]{:S(2)}, u32[]{:S(2)}) %collective-permute-start.10) | collective-permute-done | bytes 327712 | tf_op jit(solution)/shard_map/ppermute | solution.py:196
  77.8 1.0 %copy.56 = f32[256,4,128]{2,1,0:T(4,128)} copy(f32[256,4,128]{0,2,1:T(8,128)S(1)} %bitcast.189) | data formatting | bytes 1048576
  78.9 0.8 copy.57
  79.6 2.5 %all-to-all-done = bf16[4,432,256]{2,1,0:T(8,128)(2,1)S(1)} async-done(((bf16[4,432,256]{2,1,0:T(8,128)(2,1)}), bf16[4,432,256]{2,1,0:T(8,128)(2,1)S(1)}, u32[]{:S(2)}, u32[]{:S(2)}) %all-to-all-start) | async-done | bytes 884768 | tf_op jit(solution)/shard_map/all_to_all | solution.py:122
  82.7 2.5 %collective-permute-start.8 = (bf16[192,128]{1,0:T(8,128)(2,1)S(1)}, bf16[192,128]{1,0:T(8,128)(2,1)S(1)}, u32[]{:S(2)}, u32[]{:S(2)}) collective-permute-start(bf16[192,128]{1,0:T(8,128)(2,1)S(1)} %get-tuple-element.57), channel_id=1, source_target_pairs={{0,24},{8,16},{16,8},{24,0},{1,25},{9,17},{17,9},{25,1},{2,26},{10... | collective-permute-start | bytes 147464 | tf_op jit(solution)/shard_map/ppermute | solution.py:51
  85.7 0.5 collective-permute-start.6
  86.2 0.7 fusion.54
  86.9 0.9 %collective-permute-done.8 = bf16[192,128]{1,0:T(8,128)(2,1)S(1)} collective-permute-done((bf16[192,128]{1,0:T(8,128)(2,1)S(1)}, bf16[192,128]{1,0:T(8,128)(2,1)S(1)}, u32[]{:S(2)}, u32[]{:S(2)}) %collective-permute-start.8) | collective-permute-done | bytes 49184 | tf_op jit(solution)/shard_map/ppermute | solution.py:51
  87.8 1.4 %collective-permute-done.7 = bf16[192,128]{1,0:T(8,128)(2,1)S(1)} collective-permute-done((bf16[192,128]{1,0:T(8,128)(2,1)S(1)}, bf16[192,128]{1,0:T(8,128)(2,1)S(1)}, u32[]{:S(2)}, u32[]{:S(2)}) %collective-permute-start.7) | collective-permute-done | bytes 49184 | tf_op jit(solution)/shard_map/ppermute | solution.py:51
  89.8 1.2 %fusion.16 = bf16[672,128]{1,0:T(8,128)(2,1)} fusion(bf16[768,128]{1,0:T(8,128)(2,1)S(1)} %bitcast.199, s32[672]{0:T(1024)S(1)} %add_select_fusion), kind=kOutput, calls=%fused_computation.41 | convolution fusion | flops 132722688 | bytes 371328 | tf_op jit(solution)/shard_map/dot_general | solution.py:56
  (97 shorter events, 15.1 us)
Async XLA Ops:
  0.6 3.3 %copy-start = (bf16[672,128]{1,0:T(8,128)(2,1)S(1)}, bf16[672,128]{1,0:T(8,128)(2,1)}, u32[]{:S(2)}) copy-start(bf16[672,128]{1,0:T(8,128)(2,1)} %param.8) | copy-start | bytes 516100
  2.2 1.5 %copy-start.4 = (s32[4]{0:T(128)}, s32[4]{0:T(128)S(1)}, u32[]{:S(2)}) copy-start(s32[4]{0:T(128)S(1)} %subtract_bitcast_fusion) | copy-start | bytes 52
  2.9 0.9 copy-start.8
  7.3 13.5 %collective-permute-start.2 = (bf16[192,256]{1,0:T(8,128)(2,1)}, bf16[192,256]{1,0:T(8,128)(2,1)}, u32[]{:S(2)}, u32[]{:S(2)}) collective-permute-start(bf16[192,256]{1,0:T(8,128)(2,1)} %get-tuple-element.51), channel_id=1, source_target_pairs={{0,24},{8,16},{16,8},{24,0},{1,25},{9,17},{17,9},{25,1},{2,26},{10... | collective-permute-start | bytes 294920 | tf_op jit(solution)/shard_map/ppermute | solution.py:51
  11.1 9.6 %collective-permute-start.1 = (bf16[192,256]{1,0:T(8,128)(2,1)}, bf16[192,256]{1,0:T(8,128)(2,1)}, u32[]{:S(2)}, u32[]{:S(2)}) collective-permute-start(bf16[192,256]{1,0:T(8,128)(2,1)} %get-tuple-element.52), channel_id=1, source_target_pairs={{0,16},{8,24},{16,0},{24,8},{1,17},{9,25},{17,1},{25,9},{2,18},{10... | collective-permute-start | bytes 294920 | tf_op jit(solution)/shard_map/ppermute | solution.py:51
  11.7 9.1 %collective-permute-start = (bf16[192,256]{1,0:T(8,128)(2,1)}, bf16[192,256]{1,0:T(8,128)(2,1)}, u32[]{:S(2)}, u32[]{:S(2)}) collective-permute-start(bf16[192,256]{1,0:T(8,128)(2,1)} %get-tuple-element.53), channel_id=1, source_target_pairs={{0,8},{8,0},{16,24},{24,16},{1,9},{9,1},{17,25},{25,17},{2,10},{10... | collective-permute-start | bytes 294920 | tf_op jit(solution)/shard_map/ppermute | solution.py:51
  20.7 23.0 %copy-start.5 = (s32[4]{0:T(128)S(1)}, s32[4]{0:T(128)}, u32[]{:S(2)}) copy-start(s32[4]{0:T(128)} %copy-done.4) | copy-start | bytes 52
  43.5 2.4 %collective-permute-start.3 = (bf16[4,432,256]{2,1,0:T(8,128)(2,1)S(1)}, bf16[4,432,256]{2,1,0:T(8,128)(2,1)S(1)}, u32[]{:S(2)}, u32[]{:S(2)}) collective-permute-start(bf16[4,432,256]{2,1,0:T(8,128)(2,1)S(1)} %bitcast.180), channel_id=1, source_target_pairs={{0,1},{1,0},{2,3},{3,2},{4,5},{5,4},{6,7},{7,6},{8,9},{9,8},{10,11... | collective-permute-start | bytes 2654216 | tf_op jit(solution)/shard_map/ppermute | solution.py:113
  46.6 0.9 copy-start.3
  46.6 1.2 %copy-start.7 = (f32[128]{0:T(128)S(1)}, f32[128]{0:T(128)}, u32[]{:S(2)}) copy-start(f32[128]{0:T(128)} %dynamic_slice.103) | copy-start | bytes 1540
  49.8 1.2 %copy-start.2 = (bf16[8,128,512]{2,1,0:T(8,128)(2,1)S(1)}, bf16[8,128,512]{2,1,0:T(8,128)(2,1)}, u32[]{:S(2)}) copy-start(bf16[8,128,512]{2,1,0:T(8,128)(2,1)} %reshape.183) | copy-start | bytes 3145732
  51.1 0.9 %copy-start.1 = (bf16[128,1024]{0,1:T(8,128)(2,1)S(1)}, bf16[128,1024]{0,1:T(8,128)(2,1)}, u32[]{:S(2)}) copy-start(bf16[128,1024]{0,1:T(8,128)(2,1)} %copy.60) | copy-start | bytes 786436
  51.8 2.7 %collective-permute-start.5 = (bf16[4,432,128]{2,1,0:T(8,128)(2,1)S(1)}, bf16[4,432,128]{2,1,0:T(8,128)(2,1)S(1)}, u32[]{:S(2)}, u32[]{:S(2)}) collective-permute-start(bf16[4,432,128]{2,1,0:T(8,128)(2,1)S(1)} %dynamic-slice_bitcast_fusion.2), channel_id=1, source_target_pairs={{0,1},{1,0},{2,3},{3,2},{4,5},{5,4},{6,7},{7,6},{8,9},{9,8},{10,11... | collective-permute-start | bytes 1327112 | tf_op jit(solution)/shard_map/ppermute | solution.py:119
  52.5 2.2 %collective-permute-start.4 = (bf16[4,432,128]{2,1,0:T(8,128)(2,1)S(1)}, bf16[4,432,128]{2,1,0:T(8,128)(2,1)S(1)}, u32[]{:S(2)}, u32[]{:S(2)}) collective-permute-start(bf16[4,432,128]{2,1,0:T(8,128)(2,1)S(1)} %dynamic-slice_bitcast_fusion.3), channel_id=1, source_target_pairs={{0,1},{1,0},{2,3},{3,2},{4,5},{5,4},{6,7},{7,6},{8,9},{9,8},{10,11... | collective-permute-start | bytes 1327112 | tf_op jit(solution)/shard_map/ppermute | solution.py:119
  55.8 26.3 %all-to-all-start = ((bf16[4,432,256]{2,1,0:T(8,128)(2,1)}), bf16[4,432,256]{2,1,0:T(8,128)(2,1)S(1)}, u32[]{:S(2)}, u32[]{:S(2)}) async-start(bf16[4,432,256]{2,1,0:T(8,128)(2,1)} %pad_maximum_fusion.1), calls=%async_computation | async-start | bytes 1769472 | tf_op jit(solution)/shard_map/all_to_all | solution.py:122
  59.4 3.8 %copy-start.6 = (s32[4]{0:T(128)S(1)}, s32[4]{0:T(128)}, u32[]{:S(2)}) copy-start(s32[4]{0:T(128)} %copy-done.4) | copy-start | bytes 52
  59.4 3.8 %copy-start.9 = (s32[4]{0:T(128)S(1)}, s32[4]{0:T(128)}, u32[]{:S(2)}) copy-start(s32[4]{0:T(128)} %copy-done.8) | copy-start | bytes 52
  59.6 11.6 %collective-permute-start.11 = (bf16[256,640]{1,0:T(8,128)(2,1)S(1)}, bf16[256,640]{1,0:T(8,128)(2,1)S(1)}, u32[]{:S(2)}, u32[]{:S(2)}) collective-permute-start(bf16[256,640]{1,0:T(8,128)(2,1)S(1)} %get-tuple-element.44), channel_id=1, source_target_pairs={{0,24},{8,16},{16,8},{24,0},{1,25},{9,17},{17,9},{25,1},{2,26},{10... | collective-permute-start | bytes 983048 | tf_op jit(solution)/shard_map/ppermute | solution.py:196
  62.1 15.2 %collective-permute-start.10 = (bf16[256,640]{1,0:T(8,128)(2,1)S(1)}, bf16[256,640]{1,0:T(8,128)(2,1)S(1)}, u32[]{:S(2)}, u32[]{:S(2)}) collective-permute-start(bf16[256,640]{1,0:T(8,128)(2,1)S(1)} %get-tuple-element.43), channel_id=1, source_target_pairs={{0,16},{8,24},{16,0},{24,8},{1,17},{9,25},{17,1},{25,9},{2,18},{10... | collective-permute-start | bytes 983048 | tf_op jit(solution)/shard_map/ppermute | solution.py:196
  62.6 14.8 %collective-permute-start.9 = (bf16[256,640]{1,0:T(8,128)(2,1)S(1)}, bf16[256,640]{1,0:T(8,128)(2,1)S(1)}, u32[]{:S(2)}, u32[]{:S(2)}) collective-permute-start(bf16[256,640]{1,0:T(8,128)(2,1)S(1)} %get-tuple-element.42), channel_id=1, source_target_pairs={{0,8},{8,0},{16,24},{24,16},{1,9},{9,1},{17,25},{25,17},{2,10},{10... | collective-permute-start | bytes 983048 | tf_op jit(solution)/shard_map/ppermute | solution.py:196
  82.7 5.2 %collective-permute-start.8 = (bf16[192,128]{1,0:T(8,128)(2,1)S(1)}, bf16[192,128]{1,0:T(8,128)(2,1)S(1)}, u32[]{:S(2)}, u32[]{:S(2)}) collective-permute-start(bf16[192,128]{1,0:T(8,128)(2,1)S(1)} %get-tuple-element.57), channel_id=1, source_target_pairs={{0,24},{8,16},{16,8},{24,0},{1,25},{9,17},{17,9},{25,1},{2,26},{10... | collective-permute-start | bytes 147464 | tf_op jit(solution)/shard_map/ppermute | solution.py:51
  85.2 4.1 %collective-permute-start.7 = (bf16[192,128]{1,0:T(8,128)(2,1)S(1)}, bf16[192,128]{1,0:T(8,128)(2,1)S(1)}, u32[]{:S(2)}, u32[]{:S(2)}) collective-permute-start(bf16[192,128]{1,0:T(8,128)(2,1)S(1)} %get-tuple-element.58), channel_id=1, source_target_pairs={{0,16},{8,24},{16,0},{24,8},{1,17},{9,25},{17,1},{25,9},{2,18},{10... | collective-permute-start | bytes 147464 | tf_op jit(solution)/shard_map/ppermute | solution.py:51
  85.7 4.1 %collective-permute-start.6 = (bf16[192,128]{1,0:T(8,128)(2,1)S(1)}, bf16[192,128]{1,0:T(8,128)(2,1)S(1)}, u32[]{:S(2)}, u32[]{:S(2)}) collective-permute-start(bf16[192,128]{1,0:T(8,128)(2,1)S(1)} %get-tuple-element.59), channel_id=1, source_target_pairs={{0,8},{8,0},{16,24},{24,16},{1,9},{9,1},{17,25},{25,17},{2,10},{10... | collective-permute-start | bytes 147464 | tf_op jit(solution)/shard_map/ppermute | solution.py:51

commit v15 on v14

--- a/solution.py
+++ b/solution.py
@@ -90,9 +90,9 @@
     own_out = lax.dynamic_slice_in_dim(out_weight, own_start, col_width, 0).reshape(
         col_width, tensor_count, col_width
     )
-    weight_pack = (proj_mine, proj_other, out_mine, out_other, own_proj, own_out, head_gain)
+    weight_pack = (proj_mine, proj_other, out_mine, out_other, head_gain)
     recv_both, weight_pack = lax.optimization_barrier((recv_both, weight_pack))
-    proj_mine, proj_other, out_mine, out_other, own_proj, own_out, head_gain = weight_pack
+    proj_mine, proj_other, out_mine, out_other, head_gain = weight_pack
 
     recv_len = jnp.sum(jnp.where(owners == dp_index, lengths, 0), axis=1)
     recv_start = exclusive_sum(recv_len)

time: 91.5 us -> 95.1 us (1.039)
  local copies, waits for them, and re-layouts: 13.5 us -> 16.9 us
  matrix products: 10.5 us -> 12.7 us
  waiting for transfers between devices: 20.4 us -> 19.1 us
  other arithmetic: 8.41 us -> 7.41 us
    ppermute x1, waiting for transfers between devices: 1.49 us -> 0.01 us  [local(): other = lax.ppermute(mine, 'tensor', sibling)]
    squeeze x3, local copies, waits for them, and re-layouts: 0.15 us -> 1.18 us  [by_core(): lax.dynamic_index_in_dim(split, 1 - core, axis + 1, keepdims=False)]
    another operation x2, other arithmetic: 1.07 us -> 0.08 us  [exchange(): return jnp.stack(pieces)]
    unnamed x24 -> x36, local copies, waits for them, and re-layouts: 3.7 us -> 4.67 us
  transfers between devices with their start and end apart: 13 -> 13, of which waited for: 8 -> 7; matrix products, arithmetic and copies ran while one was open for 17% -> 23% of each run, Pallas kernels for 0% -> 0%
where the time goes in v15:
time: 95.1 us; the launch traced here: 94.7 us
  blocking collectives  21.3 us (22%)
  waiting for transfers between devices  19.1 us (20%)
  local copies, waits for them, and re-layouts  16.9 us (18%)
  starting transfers between devices  16 us (17%)
  matrix products  12.7 us (13%)
  other arithmetic  7.41 us (8%)
  between operations  1.22 us (1%)
    all_gather x1, blocking collectives, local(): lax.all_gather(own_both, 'tensor', axis=0, tiled=False, axis_index_groups...  21.3 us
    ppermute x3, waiting for transfers between devices, local(): term_sum = term_sum + lax.ppermute(outgoing, 'dp', partners).astype(f32)  13.7 us
    ppermute x6, starting transfers between devices, exchange(): lax.ppermute(outgoing, 'dp', [(d, d ^ k) for d in range(dp_count)])  8.15 us
    unnamed x36, local copies, waits for them, and re-layouts  4.67 us
    dot_general x5, matrix products, pick_rows(): return jnp.dot(one_hot, source, preferred_element_type=f32).astype(bf16)  4.36 us
    ppermute x3, starting transfers between devices, local(): term_sum = term_sum + lax.ppermute(outgoing, 'dp', partners).astype(f32)  3.55 us
    all_to_all x1, starting transfers between devices, reduce_blocks(): lax.all_to_all(pair_sum, 'tensor', 0, 0, tiled=True, axis_index_groups=sa...  3.5 us
    ppermute x6, waiting for transfers between devices, exchange(): lax.ppermute(outgoing, 'dp', [(d, d ^ k) for d in range(dp_count)])  2.89 us
  transfers between devices with their start and end apart: 13, of which 7 were waited for; matrix products, arithmetic and copies ran while one was open for 23% of the time, Pallas kernels for 0%

profile of v15, /device:TPU:0, one launch (start us, length us, event | category | flops | bytes accessed | tf_op | source)
XLA Modules:
  0.0 94.7 jit_solution(12367096670428913042)
XLA Ops:
  0.7 1.4 %fusion.60 = (s32[]{:T(128)}, s32[1,4]{1,0:T(1,128)S(1)}) fusion(s32[4,4]{1,0:T(4,128)} %param.9, s32[]{:T(128)S(6)} %select_n.114), kind=kLoop, calls=%fused_computation.163 | loop fusion | flops 3 | bytes 40 | tf_op jit(solution)/shard_map/reduce_sum | solution.py:210
  2.2 0.7 fusion.59
  2.9 0.8 select_reduce_fusion.3
  3.9 0.7 fusion.15
  4.6 1.6 %fusion.14 = bf16[768,128]{0,1:T(8,128)(2,1)S(1)} fusion(bf16[672,128]{1,0:T(8,128)(2,1)} %param.7, s32[768]{0:T(1024)S(1)} %min.38), kind=kOutput, calls=%fused_computation.37 | convolution fusion | flops 132734976 | bytes 371712 | tf_op jit(solution)/shard_map/dot_general | solution.py:56
  6.5 4.0 %collective-permute-start.2 = (bf16[192,256]{1,0:T(8,128)(2,1)S(1)}, bf16[192,256]{1,0:T(8,128)(2,1)S(1)}, u32[]{:S(2)}, u32[]{:S(2)}) collective-permute-start(bf16[192,256]{1,0:T(8,128)(2,1)S(1)} %get-tuple-element.47), channel_id=1, source_target_pairs={{0,24},{8,16},{16,8},{24,0},{1,25},{9,17},{17,9},{25,1},{2,26},{10... | collective-permute-start | bytes 294920 | tf_op jit(solution)/shard_map/ppermute | solution.py:51
  11.2 2.4 %constant_dynamic-slice_fusion.6 = (bf16[1024,4,128]{2,1,0:T(4,128)(2,1)S(1)}, bf16[1024,4,128]{2,1,0:T(4,128)(2,1)S(1)}) fusion(bf16[1024,4,1024]{2,1,0:T(4,128)(2,1)} %param.11, s32[]{:T(128)S(6)} %select_n.120, s32[]{:T(128)S(6)} %select_n.124), kind=kLoop, calls=%fused_computation.143 | loop fusion | bytes 4194312 | tf_op jit(solution)/shard_map/dynamic_slice | solution.py:77
  13.6 1.2 %reshape_reshape.6 = bf16[4,2,128,512]{3,2,1,0:T(8,128)(2,1)} reshape(bf16[1024,4,128]{2,1,0:T(4,128)(2,1)S(1)} %get-tuple-element.34) | data formatting | bytes 2097152 | tf_op jit(solution)/shard_map/reshape;reshape | solution.py:68
  14.8 1.8 %constant_dynamic-slice_fusion.2 = (bf16[128,1024]{1,0:T(8,128)(2,1)}, bf16[128,1024]{1,0:T(8,128)(2,1)S(1)}) fusion(bf16[1024,1024]{1,0:T(8,128)(2,1)} %param.13, s32[]{:T(128)S(6)} %select_n.124, s32[]{:T(128)S(6)} %select_n.120), kind=kLoop, calls=%fused_computation.139 | loop fusion | bytes 1048584 | tf_op jit(solution)/shard_map/dynamic_slice | solution.py:90
  16.9 0.8 copy.45
  17.6 0.8 copy.46
  18.4 1.3 %dynamic_slice.101 = f32[128]{0:T(128)} dynamic-slice(f32[1024]{0:T(1024)} %param.12, s32[]{:T(128)S(6)} %select_n.120), dynamic_slice_sizes={128} | dynamic-slice | bytes 1028 | tf_op jit(solution)/shard_map/dynamic_slice | solution.py:86
  20.1 1.1 %dynamic-slice_bitcast_fusion = (bf16[4,128,512]{2,1,0:T(8,128)(2,1)}, bf16[4,128,512]{2,1,0:T(8,128)(2,1)}) fusion(bf16[4,2,128,512]{3,2,1,0:T(8,128)(2,1)S(1)} %copy-done.1, s32[]{:T(128)S(6)} %select_n.123, s32[]{:T(128)S(6)} %select_n.122), kind=kLoop, calls=%fused_computation.75 | loop fusion | bytes 2097160 | tf_op jit(solution)/shard_map/jit(dynamic_index_in_dim)/squeeze | solution.py:71
  21.7 21.3 %all-gather = bf16[1728,256]{1,0:T(8,128)(2,1)S(1)} all-gather(bf16[432,256]{1,0:T(8,128)(2,1)S(1)} %fusion.10), channel_id=2, replica_groups={{0,2,4,6},{1,3,5,7},{8,10,12,14},{9,11,13,15},{16,18,20,22},{17,19,21,2..., dimensions={0}, use_global_device_ids=true | all-gather | bytes 1105920 | tf_op jit(solution)/shard_map/all_gather | solution.py:112
  43.0 1.2 %reshape.187 = bf16[8,128,512]{2,1,0:T(8,128)(2,1)} reshape(bf16[1024,4,128]{2,1,0:T(4,128)(2,1)S(1)} %get-tuple-element.35) | data formatting | bytes 2097152 | tf_op jit(solution)/shard_map/reshape | solution.py:80
  44.3 1.8 %copy.60 = bf16[128,1024]{0,1:T(8,128)(2,1)} copy(bf16[128,1024]{1,0:T(8,128)(2,1)} %get-tuple-element.36) | data formatting | bytes 524288
  46.4 1.2 %convolution_bitcast_fusion.10 = f32[432,128]{1,0:T(8,128)S(1)} fusion(bf16[128,4,128]{2,0,1:T(8,128)(2,1)} %bitcast.195, bf16[4,432,256]{2,1,0:T(8,128)(2,1)S(1)} %bitcast.181), kind=kOutput, calls=%fused_computation.46 | convolution fusion | flops 56623104 | bytes 794624 | tf_op jit(solution)/shard_map/trc,dtc->rd/dot_general | solution.py:128
  55.8 1.0 %convolution_bitcast_fusion.5 = bf16[4,1,128,128]{3,2,0,1:T(8,128)(2,1)} fusion(bf16[432,128,1]{1,0,2:T(8,128)(2,1)S(1)} %get-tuple-element.43, bf16[4,432,256]{2,1,0:T(8,128)(2,1)S(1)} %bitcast.184), kind=kOutput, calls=%fused_computation.40 | convolution fusion | flops 56623104 | bytes 684032 | tf_op jit(solution)/shard_map/trc,rd->tcd/dot_general | solution.py:187
  56.9 1.0 %convolution_bitcast_fusion.4 = bf16[4,1,128,128]{3,2,0,1:T(8,128)(2,1)} fusion(bf16[432,128,1]{1,0,2:T(8,128)(2,1)S(1)} %get-tuple-element.43, bf16[4,432,256]{2,1,0:T(8,128)(2,1)S(1)} %collective-permute-done.3), kind=kOutput, calls=%fused_computation.39 | convolution fusion | flops 56623104 | bytes 684032 | tf_op jit(solution)/shard_map/trc,rd->tcd/dot_general | solution.py:188
  58.2 1.0 %pad_maximum_fusion.1 = bf16[4,432,256]{2,1,0:T(8,128)(2,1)} fusion(bf16[4,432,128]{2,1,0:T(8,128)(2,1)S(1)} %fusion.24, bf16[4,432,128]{2,1,0:T(8,128)(2,1)S(1)} %fusion.25), kind=kLoop, calls=%fused_computation.58 | loop fusion | flops 1769472 | bytes 1769472 | tf_op jit(solution)/shard_map/concatenate | solution.py:170
  59.3 3.5 %all-to-all-start = ((bf16[4,432,256]{2,1,0:T(8,128)(2,1)}), bf16[4,432,256]{2,1,0:T(8,128)(2,1)S(1)}, u32[]{:S(2)}, u32[]{:S(2)}) async-start(bf16[4,432,256]{2,1,0:T(8,128)(2,1)} %pad_maximum_fusion.1), calls=%async_computation | async-start | bytes 1769472 | tf_op jit(solution)/shard_map/all_to_all | solution.py:122
  63.0 2.5 %collective-permute-start.11 = (bf16[256,640]{1,0:T(8,128)(2,1)S(1)}, bf16[256,640]{1,0:T(8,128)(2,1)S(1)}, u32[]{:S(2)}, u32[]{:S(2)}) collective-permute-start(bf16[256,640]{1,0:T(8,128)(2,1)S(1)} %get-tuple-element.40), channel_id=1, source_target_pairs={{0,24},{8,16},{16,8},{24,0},{1,25},{9,17},{17,9},{25,1},{2,26},{10... | collective-permute-start | bytes 983048 | tf_op jit(solution)/shard_map/ppermute | solution.py:196
  67.3 7.2 %collective-permute-done.11 = bf16[256,640]{1,0:T(8,128)(2,1)S(1)} collective-permute-done((bf16[256,640]{1,0:T(8,128)(2,1)S(1)}, bf16[256,640]{1,0:T(8,128)(2,1)S(1)}, u32[]{:S(2)}, u32[]{:S(2)}) %collective-permute-start.11) | collective-permute-done | bytes 327712 | tf_op jit(solution)/shard_map/ppermute | solution.py:196
  74.6 6.4 %collective-permute-done.10 = bf16[256,640]{1,0:T(8,128)(2,1)S(1)} collective-permute-done((bf16[256,640]{1,0:T(8,128)(2,1)S(1)}, bf16[256,640]{1,0:T(8,128)(2,1)S(1)}, u32[]{:S(2)}, u32[]{:S(2)}) %collective-permute-start.10) | collective-permute-done | bytes 327712 | tf_op jit(solution)/shard_map/ppermute | solution.py:196
  81.5 1.0 %copy.56 = f32[256,4,128]{2,1,0:T(4,128)} copy(f32[256,4,128]{0,2,1:T(8,128)S(1)} %bitcast.189) | data formatting | bytes 1048576
  82.5 0.8 copy.57
  83.3 2.5 %all-to-all-done = bf16[4,432,256]{2,1,0:T(8,128)(2,1)S(1)} async-done(((bf16[4,432,256]{2,1,0:T(8,128)(2,1)}), bf16[4,432,256]{2,1,0:T(8,128)(2,1)S(1)}, u32[]{:S(2)}, u32[]{:S(2)}) %all-to-all-start) | async-done | bytes 884768 | tf_op jit(solution)/shard_map/all_to_all | solution.py:122
  86.3 2.5 %collective-permute-start.8 = (bf16[192,128]{1,0:T(8,128)(2,1)S(1)}, bf16[192,128]{1,0:T(8,128)(2,1)S(1)}, u32[]{:S(2)}, u32[]{:S(2)}) collective-permute-start(bf16[192,128]{1,0:T(8,128)(2,1)S(1)} %get-tuple-element.53), channel_id=1, source_target_pairs={{0,24},{8,16},{16,8},{24,0},{1,25},{9,17},{17,9},{25,1},{2,26},{10... | collective-permute-start | bytes 147464 | tf_op jit(solution)/shard_map/ppermute | solution.py:51
  89.9 0.7 fusion.54
  90.6 0.9 collective-permute-done.8
  91.5 1.4 %collective-permute-done.7 = bf16[192,128]{1,0:T(8,128)(2,1)S(1)} collective-permute-done((bf16[192,128]{1,0:T(8,128)(2,1)S(1)}, bf16[192,128]{1,0:T(8,128)(2,1)S(1)}, u32[]{:S(2)}, u32[]{:S(2)}) %collective-permute-start.7) | collective-permute-done | bytes 49184 | tf_op jit(solution)/shard_map/ppermute | solution.py:51
  93.5 1.2 %fusion.16 = bf16[672,128]{1,0:T(8,128)(2,1)} fusion(bf16[768,128]{1,0:T(8,128)(2,1)S(1)} %bitcast.199, s32[672]{0:T(1024)S(1)} %add_select_fusion), kind=kOutput, calls=%fused_computation.41 | convolution fusion | flops 132722688 | bytes 371328 | tf_op jit(solution)/shard_map/dot_general | solution.py:56
  (109 shorter events, 15.6 us)
Async XLA Ops:
  0.6 3.3 %copy-start = (bf16[672,128]{1,0:T(8,128)(2,1)S(1)}, bf16[672,128]{1,0:T(8,128)(2,1)}, u32[]{:S(2)}) copy-start(bf16[672,128]{1,0:T(8,128)(2,1)} %param.8) | copy-start | bytes 516100
  2.2 1.5 %copy-start.11 = (s32[4]{0:T(128)}, s32[4]{0:T(128)S(1)}, u32[]{:S(2)}) copy-start(s32[4]{0:T(128)S(1)} %subtract_bitcast_fusion) | copy-start | bytes 52
  2.9 0.9 copy-start.14
  6.5 14.7 %collective-permute-start.2 = (bf16[192,256]{1,0:T(8,128)(2,1)S(1)}, bf16[192,256]{1,0:T(8,128)(2,1)S(1)}, u32[]{:S(2)}, u32[]{:S(2)}) collective-permute-start(bf16[192,256]{1,0:T(8,128)(2,1)S(1)} %get-tuple-element.47), channel_id=1, source_target_pairs={{0,24},{8,16},{16,8},{24,0},{1,25},{9,17},{17,9},{25,1},{2,26},{10... | collective-permute-start | bytes 294920 | tf_op jit(solution)/shard_map/ppermute | solution.py:51
  10.5 10.7 %collective-permute-start.1 = (bf16[192,256]{1,0:T(8,128)(2,1)S(1)}, bf16[192,256]{1,0:T(8,128)(2,1)S(1)}, u32[]{:S(2)}, u32[]{:S(2)}) collective-permute-start(bf16[192,256]{1,0:T(8,128)(2,1)S(1)} %get-tuple-element.48), channel_id=1, source_target_pairs={{0,16},{8,24},{16,0},{24,8},{1,17},{9,25},{17,1},{25,9},{2,18},{10... | collective-permute-start | bytes 294920 | tf_op jit(solution)/shard_map/ppermute | solution.py:51
  11.0 10.2 %collective-permute-start = (bf16[192,256]{1,0:T(8,128)(2,1)S(1)}, bf16[192,256]{1,0:T(8,128)(2,1)S(1)}, u32[]{:S(2)}, u32[]{:S(2)}) collective-permute-start(bf16[192,256]{1,0:T(8,128)(2,1)S(1)} %get-tuple-element.49), channel_id=1, source_target_pairs={{0,8},{8,0},{16,24},{24,16},{1,9},{9,1},{17,25},{25,17},{2,10},{10... | collective-permute-start | bytes 294920 | tf_op jit(solution)/shard_map/ppermute | solution.py:51
  14.8 5.3 %copy-start.1 = (bf16[4,2,128,512]{3,2,1,0:T(8,128)(2,1)S(1)}, bf16[4,2,128,512]{3,2,1,0:T(8,128)(2,1)}, u32[]{:S(2)}) copy-start(bf16[4,2,128,512]{3,2,1,0:T(8,128)(2,1)} %reshape_reshape.6) | copy-start | bytes 3145732
  21.7 21.3 %copy-start.7 = (bf16[432,256]{1,0:T(8,128)(2,1)}, bf16[432,256]{1,0:T(8,128)(2,1)S(1)}, u32[]{:S(2)}) copy-start(bf16[432,256]{1,0:T(8,128)(2,1)S(1)} %fusion.10) | copy-start | bytes 663556
  21.7 24.6 %copy-start.12 = (s32[4]{0:T(128)S(1)}, s32[4]{0:T(128)}, u32[]{:S(2)}) copy-start(s32[4]{0:T(128)} %copy-done.11) | copy-start | bytes 52
  43.0 4.5 %copy-start.2 = (bf16[4,128,512]{2,1,0:T(8,128)(2,1)S(1)}, bf16[4,128,512]{2,1,0:T(8,128)(2,1)}, u32[]{:S(2)}) copy-start(bf16[4,128,512]{2,1,0:T(8,128)(2,1)} %get-tuple-element.11) | copy-start | bytes 1572868
  43.0 4.9 %collective-permute-start.3 = (bf16[4,432,256]{2,1,0:T(8,128)(2,1)S(1)}, bf16[4,432,256]{2,1,0:T(8,128)(2,1)S(1)}, u32[]{:S(2)}, u32[]{:S(2)}) collective-permute-start(bf16[4,432,256]{2,1,0:T(8,128)(2,1)S(1)} %bitcast.180), channel_id=1, source_target_pairs={{0,1},{1,0},{2,3},{3,2},{4,5},{5,4},{6,7},{7,6},{8,9},{9,8},{10,11... | collective-permute-start | bytes 2654216 | tf_op jit(solution)/shard_map/ppermute | solution.py:113
  44.3 3.7 %copy-start.3 = (bf16[4,128,512]{2,1,0:T(8,128)(2,1)S(1)}, bf16[4,128,512]{2,1,0:T(8,128)(2,1)}, u32[]{:S(2)}) copy-start(bf16[4,128,512]{2,1,0:T(8,128)(2,1)} %get-tuple-element.12) | copy-start | bytes 1572868
  48.6 0.9 copy-start.6
  48.6 1.2 %copy-start.13 = (f32[128]{0:T(128)S(1)}, f32[128]{0:T(128)}, u32[]{:S(2)}) copy-start(f32[128]{0:T(128)} %dynamic_slice.101) | copy-start | bytes 1540
  51.8 1.2 %copy-start.5 = (bf16[8,128,512]{2,1,0:T(8,128)(2,1)S(1)}, bf16[8,128,512]{2,1,0:T(8,128)(2,1)}, u32[]{:S(2)}) copy-start(bf16[8,128,512]{2,1,0:T(8,128)(2,1)} %reshape.187) | copy-start | bytes 3145732
  53.1 1.2 %copy-start.4 = (bf16[128,1024]{0,1:T(8,128)(2,1)S(1)}, bf16[128,1024]{0,1:T(8,128)(2,1)}, u32[]{:S(2)}) copy-start(bf16[128,1024]{0,1:T(8,128)(2,1)} %copy.60) | copy-start | bytes 786436
  53.8 4.2 %collective-permute-start.5 = (bf16[4,432,128]{2,1,0:T(8,128)(2,1)S(1)}, bf16[4,432,128]{2,1,0:T(8,128)(2,1)S(1)}, u32[]{:S(2)}, u32[]{:S(2)}) collective-permute-start(bf16[4,432,128]{2,1,0:T(8,128)(2,1)S(1)} %dynamic-slice_bitcast_fusion.2), channel_id=1, source_target_pairs={{0,1},{1,0},{2,3},{3,2},{4,5},{5,4},{6,7},{7,6},{8,9},{9,8},{10,11... | collective-permute-start | bytes 1327112 | tf_op jit(solution)/shard_map/ppermute | solution.py:119
  54.8 3.3 %collective-permute-start.4 = (bf16[4,432,128]{2,1,0:T(8,128)(2,1)S(1)}, bf16[4,432,128]{2,1,0:T(8,128)(2,1)S(1)}, u32[]{:S(2)}, u32[]{:S(2)}) collective-permute-start(bf16[4,432,128]{2,1,0:T(8,128)(2,1)S(1)} %dynamic-slice_bitcast_fusion.3), channel_id=1, source_target_pairs={{0,1},{1,0},{2,3},{3,2},{4,5},{5,4},{6,7},{7,6},{8,9},{9,8},{10,11... | collective-permute-start | bytes 1327112 | tf_op jit(solution)/shard_map/ppermute | solution.py:119
  58.2 4.6 %copy-start.9 = (bf16[4,1,128,128]{3,2,0,1:T(8,128)(2,1)S(1)}, bf16[4,1,128,128]{3,2,0,1:T(8,128)(2,1)}, u32[]{:S(2)}) copy-start(bf16[4,1,128,128]{3,2,0,1:T(8,128)(2,1)} %convolution_bitcast_fusion.5) | copy-start | bytes 393220
  58.2 4.6 %copy-start.10 = (bf16[4,1,128,128]{3,2,0,1:T(8,128)(2,1)S(1)}, bf16[4,1,128,128]{3,2,0,1:T(8,128)(2,1)}, u32[]{:S(2)}) copy-start(bf16[4,1,128,128]{3,2,0,1:T(8,128)(2,1)} %convolution_bitcast_fusion.4) | copy-start | bytes 393220
  59.3 26.5 %all-to-all-start = ((bf16[4,432,256]{2,1,0:T(8,128)(2,1)}), bf16[4,432,256]{2,1,0:T(8,128)(2,1)S(1)}, u32[]{:S(2)}, u32[]{:S(2)}) async-start(bf16[4,432,256]{2,1,0:T(8,128)(2,1)} %pad_maximum_fusion.1), calls=%async_computation | async-start | bytes 1769472 | tf_op jit(solution)/shard_map/all_to_all | solution.py:122
  62.8 3.8 %copy-start.15 = (s32[4]{0:T(128)S(1)}, s32[4]{0:T(128)}, u32[]{:S(2)}) copy-start(s32[4]{0:T(128)} %copy-done.14) | copy-start | bytes 52
  63.0 11.5 %collective-permute-start.11 = (bf16[256,640]{1,0:T(8,128)(2,1)S(1)}, bf16[256,640]{1,0:T(8,128)(2,1)S(1)}, u32[]{:S(2)}, u32[]{:S(2)}) collective-permute-start(bf16[256,640]{1,0:T(8,128)(2,1)S(1)} %get-tuple-element.40), channel_id=1, source_target_pairs={{0,24},{8,16},{16,8},{24,0},{1,25},{9,17},{17,9},{25,1},{2,26},{10... | collective-permute-start | bytes 983048 | tf_op jit(solution)/shard_map/ppermute | solution.py:196
  65.5 15.4 %collective-permute-start.10 = (bf16[256,640]{1,0:T(8,128)(2,1)S(1)}, bf16[256,640]{1,0:T(8,128)(2,1)S(1)}, u32[]{:S(2)}, u32[]{:S(2)}) collective-permute-start(bf16[256,640]{1,0:T(8,128)(2,1)S(1)} %get-tuple-element.39), channel_id=1, source_target_pairs={{0,16},{8,24},{16,0},{24,8},{1,17},{9,25},{17,1},{25,9},{2,18},{10... | collective-permute-start | bytes 983048 | tf_op jit(solution)/shard_map/ppermute | solution.py:196
  66.0 15.0 %collective-permute-start.9 = (bf16[256,640]{1,0:T(8,128)(2,1)S(1)}, bf16[256,640]{1,0:T(8,128)(2,1)S(1)}, u32[]{:S(2)}, u32[]{:S(2)}) collective-permute-start(bf16[256,640]{1,0:T(8,128)(2,1)S(1)} %get-tuple-element.38), channel_id=1, source_target_pairs={{0,8},{8,0},{16,24},{24,16},{1,9},{9,1},{17,25},{25,17},{2,10},{10... | collective-permute-start | bytes 983048 | tf_op jit(solution)/shard_map/ppermute | solution.py:196
  81.3 4.6 %copy-start.8 = (bf16[432,256]{1,0:T(8,128)(2,1)S(1)}, bf16[432,256]{1,0:T(8,128)(2,1)}, u32[]{:S(2)}) copy-start(bf16[432,256]{1,0:T(8,128)(2,1)} %copy-done.7) | copy-start | bytes 663556
  86.3 5.2 %collective-permute-start.8 = (bf16[192,128]{1,0:T(8,128)(2,1)S(1)}, bf16[192,128]{1,0:T(8,128)(2,1)S(1)}, u32[]{:S(2)}, u32[]{:S(2)}) collective-permute-start(bf16[192,128]{1,0:T(8,128)(2,1)S(1)} %get-tuple-element.53), channel_id=1, source_target_pairs={{0,24},{8,16},{16,8},{24,0},{1,25},{9,17},{17,9},{25,1},{2,26},{10... | collective-permute-start | bytes 147464 | tf_op jit(solution)/shard_map/ppermute | solution.py:51
  88.8 4.1 %collective-permute-start.7 = (bf16[192,128]{1,0:T(8,128)(2,1)S(1)}, bf16[192,128]{1,0:T(8,128)(2,1)S(1)}, u32[]{:S(2)}, u32[]{:S(2)}) collective-permute-start(bf16[192,128]{1,0:T(8,128)(2,1)S(1)} %get-tuple-element.54), channel_id=1, source_target_pairs={{0,16},{8,24},{16,0},{24,8},{1,17},{9,25},{17,1},{25,9},{2,18},{10... | collective-permute-start | bytes 147464 | tf_op jit(solution)/shard_map/ppermute | solution.py:51
  89.4 4.1 %collective-permute-start.6 = (bf16[192,128]{1,0:T(8,128)(2,1)S(1)}, bf16[192,128]{1,0:T(8,128)(2,1)S(1)}, u32[]{:S(2)}, u32[]{:S(2)}) collective-permute-start(bf16[192,128]{1,0:T(8,128)(2,1)S(1)} %get-tuple-element.55), channel_id=1, source_target_pairs={{0,8},{8,0},{16,24},{24,16},{1,9},{9,1},{17,25},{25,17},{2,10},{10... | collective-permute-start | bytes 147464 | tf_op jit(solution)/shard_map/ppermute | solution.py:51

commit v16 on v14

--- a/solution.py
+++ b/solution.py
@@ -43,12 +43,12 @@
     my_starts = exclusive_sum(my_lengths)
     sent_to = my_owners[None, :] == peer_ids[:, None]
     send_start = jnp.sum(jnp.where(sent_to, my_starts[None, :], 0), axis=1)
-    send_ids = jnp.minimum(send_start[:, None] + places[None, :], load_rows - 1)
+    xor_peers = dp_index ^ peer_ids
+    send_ids = jnp.minimum(jnp.take(send_start, xor_peers)[:, None] + places[None, :], load_rows - 1)
     def exchange(blocks):
-        pieces = [lax.dynamic_index_in_dim(blocks, dp_index, 0, keepdims=False)]
+        pieces = [blocks[0]]
         for k in range(1, dp_count):
-            outgoing = lax.dynamic_index_in_dim(blocks, dp_index ^ k, 0, keepdims=False)
-            pieces.append(lax.ppermute(outgoing, "dp", [(d, d ^ k) for d in range(dp_count)]))
+            pieces.append(lax.ppermute(blocks[k], "dp", [(d, d ^ k) for d in range(dp_count)]))
         return jnp.stack(pieces)
 
     def pick_rows(row_ids, source):
@@ -197,7 +197,9 @@
     proj_grad = term_sum[:, : 4 * col_width].reshape(-1, 4, col_width)
     out_grad = term_sum[:, 4 * col_width :].T
 
-    back_src = jnp.minimum(recv_start[:, None] + places[None, :], owned_rows - 1)
+    back_src = jnp.minimum(
+        jnp.take(recv_start, xor_peers)[:, None] + places[None, :], owned_rows - 1
+    )
     back_send = pick_rows(back_src.reshape(-1), token_rows).reshape(dp_count, MAXLEN, col_width)
     back_grads = exchange(back_send)
     back_grads = back_grads.reshape(dp_count * MAXLEN, col_width)

time: 91.5 us -> 92.4 us (level)
  other arithmetic: 8.41 us -> 9.39 us
    gather x0 -> x2, local copies, waits for them, and re-layouts: none -> 1.28 us  [the longest x1 0.65 us: local(): jnp.take(send_start, xor_peers)[:, None] + places[None, :]]
    unnamed x24 -> x14, local copies, waits for them, and re-layouts: 3.7 us -> 3.66 us
where the time goes in v16:
time: 92.4 us; the launch traced here: 91.9 us
  blocking collectives  21.3 us (23%)
  waiting for transfers between devices  20.4 us (22%)
  starting transfers between devices  15.7 us (17%)
  local copies, waits for them, and re-layouts  13.4 us (15%)
  matrix products  10.5 us (11%)
  other arithmetic  9.39 us (10%)
  between operations  1.12 us (1%)
    all_gather x1, blocking collectives, local(): lax.all_gather(own_both, 'tensor', axis=0, tiled=False, axis_index_groups...  21.3 us
    ppermute x3, waiting for transfers between devices, local(): term_sum = term_sum + lax.ppermute(outgoing, 'dp', partners).astype(f32)  13.5 us
    ppermute x6, starting transfers between devices, exchange(): lax.ppermute(blocks[k], 'dp', [(d, d ^ k) for d in range(dp_count)])  8.02 us
    dot_general x5, matrix products, pick_rows(): return jnp.dot(one_hot, source, preferred_element_type=f32).astype(bf16)  4.35 us
    unnamed x14, local copies, waits for them, and re-layouts  3.66 us
    ppermute x3, starting transfers between devices, local(): term_sum = term_sum + lax.ppermute(outgoing, 'dp', partners).astype(f32)  3.55 us
    all_to_all x1, starting transfers between devices, reduce_blocks(): lax.all_to_all(pair_sum, 'tensor', 0, 0, tiled=True, axis_index_groups=sa...  3.5 us
    ppermute x6, waiting for transfers between devices, exchange(): lax.ppermute(blocks[k], 'dp', [(d, d ^ k) for d in range(dp_count)])  2.89 us
  transfers between devices with their start and end apart: 13, of which 8 were waited for; matrix products, arithmetic and copies ran while one was open for 17% of the time, Pallas kernels for 0%

profile of v16, /device:TPU:0, one launch (start us, length us, event | category | flops | bytes accessed | tf_op | source)
XLA Modules:
  0.0 91.9 jit_solution(16037277355001318941)
XLA Ops:
  0.7 1.4 %fusion.64 = (s32[]{:T(128)}, s32[1,4]{1,0:T(1,128)S(1)}) fusion(s32[4,4]{1,0:T(4,128)} %param.11, s32[]{:T(128)S(6)} %select_n.111), kind=kLoop, calls=%fused_computation.173 | loop fusion | flops 3 | bytes 40 | tf_op jit(solution)/shard_map/reduce_sum | solution.py:212
  2.2 0.7 fusion.63
  2.9 0.8 select_reduce_fusion.3
  3.8 0.6 gather_fusion
  4.6 0.7 fusion.14
  5.3 1.6 %fusion.15 = bf16[768,128]{0,1:T(8,128)(2,1)S(1)} fusion(bf16[672,128]{1,0:T(8,128)(2,1)} %param.10, s32[768]{0:T(1024)S(1)} %min.38), kind=kOutput, calls=%fused_computation.40 | convolution fusion | flops 132734976 | bytes 371712 | tf_op jit(solution)/shard_map/dot_general | solution.py:56
  6.9 0.9 fusion.57
  7.8 3.9 %collective-permute-start.2 = (bf16[192,256]{0,1:T(8,128)(2,1)}, bf16[192,256]{0,1:T(8,128)(2,1)}, u32[]{:S(2)}, u32[]{:S(2)}) collective-permute-start(bf16[192,256]{0,1:T(8,128)(2,1)} %get-tuple-element.53), channel_id=1, source_target_pairs={{0,24},{8,16},{16,8},{24,0},{1,25},{9,17},{17,9},{25,1},{2,26},{10... | collective-permute-start | bytes 294920 | tf_op jit(solution)/shard_map/ppermute | solution.py:51
  13.2 2.4 %constant_dynamic-slice_fusion.1 = (bf16[1024,4,128]{2,1,0:T(4,128)(2,1)S(1)}, bf16[1024,4,128]{2,1,0:T(4,128)(2,1)S(1)}) fusion(bf16[1024,4,1024]{2,1,0:T(4,128)(2,1)} %param.13, s32[]{:T(128)S(6)} %select_n.118, s32[]{:T(128)S(6)} %select_n.114), kind=kLoop, calls=%fused_computation.145 | loop fusion | bytes 4194312 | tf_op jit(solution)/shard_map/dynamic_slice | solution.py:80
  16.0 1.1 %constant_dynamic-slice_fusion = (bf16[128,1024]{1,0:T(8,128)(2,1)S(1)}, bf16[128,1024]{1,0:T(8,128)(2,1)S(1)}) fusion(bf16[1024,1024]{1,0:T(8,128)(2,1)} %param.15, s32[]{:T(128)S(6)} %select_n.118, s32[]{:T(128)S(6)} %select_n.114), kind=kLoop, calls=%fused_computation.144 | loop fusion | bytes 1048584 | tf_op jit(solution)/shard_map/dynamic_slice | solution.py:90
  17.5 0.8 copy.45
  18.3 1.2 %reshape.193 = bf16[8,128,512]{2,1,0:T(8,128)(2,1)} reshape(bf16[1024,4,128]{2,1,0:T(4,128)(2,1)S(1)} %get-tuple-element.39) | data formatting | bytes 2097152 | tf_op jit(solution)/shard_map/reshape | solution.py:80
  19.5 0.8 copy.60
  20.4 0.8 dynamic_slice.73
  21.3 1.2 %pad_maximum_fusion.2 = bf16[4,192,256]{1,2,0:T(8,128)(2,1)S(1)} fusion(bf16[1,192,256]{1,2,0:T(8,128)(2,1)} %bitcast.7, bf16[1,192,256]{1,2,0:T(8,128)(2,1)} %bitcast.6, bf16[1,192,256]{1,2,0:T(8,128)(2,1)} %bitcast.5, bf16[1,192,256]{1,2,0:T(8,128)(2,1)S(1)} %copy-done.3), kind=kLoop, calls=%fused_computation.76 | loop fusion | flops 589824 | bytes 786432 | tf_op jit(solution)/shard_map/stack | solution.py:52
  23.1 21.3 %all-gather = bf16[1728,256]{1,0:T(8,128)(2,1)S(1)} all-gather(bf16[432,256]{1,0:T(8,128)(2,1)S(1)} %fusion.10), channel_id=2, replica_groups={{0,2,4,6},{1,3,5,7},{8,10,12,14},{9,11,13,15},{16,18,20,22},{17,19,21,2..., dimensions={0}, use_global_device_ids=true | all-gather | bytes 1105920 | tf_op jit(solution)/shard_map/all_gather | solution.py:112
  45.4 1.5 %collective-permute-done.3 = bf16[4,432,256]{2,1,0:T(8,128)(2,1)S(1)} collective-permute-done((bf16[4,432,256]{2,1,0:T(8,128)(2,1)S(1)}, bf16[4,432,256]{2,1,0:T(8,128)(2,1)S(1)}, u32[]{:S(2)}, u32[]{:S(2)}) %collective-permute-start.3) | collective-permute-done | bytes 884768 | tf_op jit(solution)/shard_map/ppermute | solution.py:113
  52.0 0.7 convolution_convert_fusion
  55.7 1.0 %pad_maximum_fusion.1 = bf16[4,432,256]{2,1,0:T(8,128)(2,1)} fusion(bf16[4,432,128]{2,1,0:T(8,128)(2,1)S(1)} %fusion.24, bf16[4,432,128]{2,1,0:T(8,128)(2,1)S(1)} %fusion.25), kind=kLoop, calls=%fused_computation.60 | loop fusion | flops 1769472 | bytes 1769472 | tf_op jit(solution)/shard_map/concatenate | solution.py:170
  56.7 3.5 %all-to-all-start = ((bf16[4,432,256]{2,1,0:T(8,128)(2,1)}), bf16[4,432,256]{2,1,0:T(8,128)(2,1)S(1)}, u32[]{:S(2)}, u32[]{:S(2)}) async-start(bf16[4,432,256]{2,1,0:T(8,128)(2,1)} %pad_maximum_fusion.1), calls=%async_computation | async-start | bytes 1769472 | tf_op jit(solution)/shard_map/all_to_all | solution.py:122
  60.4 2.5 %collective-permute-start.11 = (bf16[256,640]{1,0:T(8,128)(2,1)S(1)}, bf16[256,640]{1,0:T(8,128)(2,1)S(1)}, u32[]{:S(2)}, u32[]{:S(2)}) collective-permute-start(bf16[256,640]{1,0:T(8,128)(2,1)S(1)} %get-tuple-element.45), channel_id=1, source_target_pairs={{0,24},{8,16},{16,8},{24,0},{1,25},{9,17},{17,9},{25,1},{2,26},{10... | collective-permute-start | bytes 983048 | tf_op jit(solution)/shard_map/ppermute | solution.py:196
  64.1 0.7 add_select_fusion
  64.7 7.3 %collective-permute-done.11 = bf16[256,640]{1,0:T(8,128)(2,1)S(1)} collective-permute-done((bf16[256,640]{1,0:T(8,128)(2,1)S(1)}, bf16[256,640]{1,0:T(8,128)(2,1)S(1)}, u32[]{:S(2)}, u32[]{:S(2)}) %collective-permute-start.11) | collective-permute-done | bytes 327712 | tf_op jit(solution)/shard_map/ppermute | solution.py:196
  72.0 6.2 %collective-permute-done.10 = bf16[256,640]{1,0:T(8,128)(2,1)S(1)} collective-permute-done((bf16[256,640]{1,0:T(8,128)(2,1)S(1)}, bf16[256,640]{1,0:T(8,128)(2,1)S(1)}, u32[]{:S(2)}, u32[]{:S(2)}) %collective-permute-start.10) | collective-permute-done | bytes 327712 | tf_op jit(solution)/shard_map/ppermute | solution.py:196
  78.7 1.0 %copy.56 = f32[256,4,128]{2,1,0:T(4,128)} copy(f32[256,4,128]{0,2,1:T(8,128)S(1)} %bitcast.179) | data formatting | bytes 1048576
  79.7 0.8 copy.57
  80.5 2.5 %all-to-all-done = bf16[4,432,256]{2,1,0:T(8,128)(2,1)S(1)} async-done(((bf16[4,432,256]{2,1,0:T(8,128)(2,1)}), bf16[4,432,256]{2,1,0:T(8,128)(2,1)S(1)}, u32[]{:S(2)}, u32[]{:S(2)}) %all-to-all-start) | async-done | bytes 884768 | tf_op jit(solution)/shard_map/all_to_all | solution.py:122
  83.6 2.5 %collective-permute-start.8 = (bf16[192,128]{1,0:T(8,128)(2,1)S(1)}, bf16[192,128]{1,0:T(8,128)(2,1)S(1)}, u32[]{:S(2)}, u32[]{:S(2)}) collective-permute-start(bf16[192,128]{1,0:T(8,128)(2,1)S(1)} %get-tuple-element.58), channel_id=1, source_target_pairs={{0,24},{8,16},{16,8},{24,0},{1,25},{9,17},{17,9},{25,1},{2,26},{10... | collective-permute-start | bytes 147464 | tf_op jit(solution)/shard_map/ppermute | solution.py:51
  87.1 0.7 fusion.54
  87.8 0.9 %collective-permute-done.8 = bf16[192,128]{1,0:T(8,128)(2,1)S(1)} collective-permute-done((bf16[192,128]{1,0:T(8,128)(2,1)S(1)}, bf16[192,128]{1,0:T(8,128)(2,1)S(1)}, u32[]{:S(2)}, u32[]{:S(2)}) %collective-permute-start.8) | collective-permute-done | bytes 49184 | tf_op jit(solution)/shard_map/ppermute | solution.py:51
  88.7 1.4 %collective-permute-done.7 = bf16[192,128]{1,0:T(8,128)(2,1)S(1)} collective-permute-done((bf16[192,128]{1,0:T(8,128)(2,1)S(1)}, bf16[192,128]{1,0:T(8,128)(2,1)S(1)}, u32[]{:S(2)}, u32[]{:S(2)}) %collective-permute-start.7) | collective-permute-done | bytes 49184 | tf_op jit(solution)/shard_map/ppermute | solution.py:51
  90.7 1.2 %fusion.16 = bf16[672,128]{1,0:T(8,128)(2,1)} fusion(bf16[768,128]{1,0:T(8,128)(2,1)S(1)} %bitcast.187, s32[672]{0:T(1024)S(1)} %add_select_fusion), kind=kOutput, calls=%fused_computation.43 | convolution fusion | flops 132722688 | bytes 371328 | tf_op jit(solution)/shard_map/dot_general | solution.py:56
  (92 shorter events, 16.2 us)
Async XLA Ops:
  0.6 3.9 %copy-start = (bf16[672,128]{1,0:T(8,128)(2,1)S(1)}, bf16[672,128]{1,0:T(8,128)(2,1)}, u32[]{:S(2)}) copy-start(bf16[672,128]{1,0:T(8,128)(2,1)} %param.9) | copy-start | bytes 516100
  7.8 13.5 %collective-permute-start.2 = (bf16[192,256]{0,1:T(8,128)(2,1)}, bf16[192,256]{0,1:T(8,128)(2,1)}, u32[]{:S(2)}, u32[]{:S(2)}) collective-permute-start(bf16[192,256]{0,1:T(8,128)(2,1)} %get-tuple-element.53), channel_id=1, source_target_pairs={{0,24},{8,16},{16,8},{24,0},{1,25},{9,17},{17,9},{25,1},{2,26},{10... | collective-permute-start | bytes 294920 | tf_op jit(solution)/shard_map/ppermute | solution.py:51
  11.7 9.6 %collective-permute-start.1 = (bf16[192,256]{0,1:T(8,128)(2,1)}, bf16[192,256]{0,1:T(8,128)(2,1)}, u32[]{:S(2)}, u32[]{:S(2)}) collective-permute-start(bf16[192,256]{0,1:T(8,128)(2,1)} %get-tuple-element.54), channel_id=1, source_target_pairs={{0,16},{8,24},{16,0},{24,8},{1,17},{9,25},{17,1},{25,9},{2,18},{10... | collective-permute-start | bytes 294920 | tf_op jit(solution)/shard_map/ppermute | solution.py:51
  12.2 9.1 %collective-permute-start = (bf16[192,256]{0,1:T(8,128)(2,1)}, bf16[192,256]{0,1:T(8,128)(2,1)}, u32[]{:S(2)}, u32[]{:S(2)}) collective-permute-start(bf16[192,256]{0,1:T(8,128)(2,1)} %get-tuple-element.52), channel_id=1, source_target_pairs={{0,8},{8,0},{16,24},{24,16},{1,9},{9,1},{17,25},{25,17},{2,10},{10... | collective-permute-start | bytes 294920 | tf_op jit(solution)/shard_map/ppermute | solution.py:51
  19.5 1.8 %copy-start.3 = (bf16[1,192,256]{1,2,0:T(8,128)(2,1)S(1)}, bf16[1,192,256]{1,2,0:T(8,128)(2,1)}, u32[]{:S(2)}) copy-start(bf16[1,192,256]{1,2,0:T(8,128)(2,1)} %get-tuple-element.51) | copy-start | bytes 294916
  44.4 2.4 %collective-permute-start.3 = (bf16[4,432,256]{2,1,0:T(8,128)(2,1)S(1)}, bf16[4,432,256]{2,1,0:T(8,128)(2,1)S(1)}, u32[]{:S(2)}, u32[]{:S(2)}) collective-permute-start(bf16[4,432,256]{2,1,0:T(8,128)(2,1)S(1)} %bitcast.170), channel_id=1, source_target_pairs={{0,1},{1,0},{2,3},{3,2},{4,5},{5,4},{6,7},{7,6},{8,9},{9,8},{10,11... | collective-permute-start | bytes 2654216 | tf_op jit(solution)/shard_map/ppermute | solution.py:113
  47.5 0.9 copy-start.4
  50.7 1.2 %copy-start.2 = (bf16[8,128,512]{2,1,0:T(8,128)(2,1)S(1)}, bf16[8,128,512]{2,1,0:T(8,128)(2,1)}, u32[]{:S(2)}) copy-start(bf16[8,128,512]{2,1,0:T(8,128)(2,1)} %reshape.193) | copy-start | bytes 3145732
  52.0 0.9 %copy-start.1 = (bf16[128,1024]{0,1:T(8,128)(2,1)S(1)}, bf16[128,1024]{0,1:T(8,128)(2,1)}, u32[]{:S(2)}) copy-start(bf16[128,1024]{0,1:T(8,128)(2,1)} %copy.60) | copy-start | bytes 786436
  52.7 2.7 %collective-permute-start.5 = (bf16[4,432,128]{2,1,0:T(8,128)(2,1)S(1)}, bf16[4,432,128]{2,1,0:T(8,128)(2,1)S(1)}, u32[]{:S(2)}, u32[]{:S(2)}) collective-permute-start(bf16[4,432,128]{2,1,0:T(8,128)(2,1)S(1)} %dynamic-slice_bitcast_fusion.2), channel_id=1, source_target_pairs={{0,1},{1,0},{2,3},{3,2},{4,5},{5,4},{6,7},{7,6},{8,9},{9,8},{10,11... | collective-permute-start | bytes 1327112 | tf_op jit(solution)/shard_map/ppermute | solution.py:119
  53.3 2.2 %collective-permute-start.4 = (bf16[4,432,128]{2,1,0:T(8,128)(2,1)S(1)}, bf16[4,432,128]{2,1,0:T(8,128)(2,1)S(1)}, u32[]{:S(2)}, u32[]{:S(2)}) collective-permute-start(bf16[4,432,128]{2,1,0:T(8,128)(2,1)S(1)} %dynamic-slice_bitcast_fusion.3), channel_id=1, source_target_pairs={{0,1},{1,0},{2,3},{3,2},{4,5},{5,4},{6,7},{7,6},{8,9},{9,8},{10,11... | collective-permute-start | bytes 1327112 | tf_op jit(solution)/shard_map/ppermute | solution.py:119
  56.7 26.3 %all-to-all-start = ((bf16[4,432,256]{2,1,0:T(8,128)(2,1)}), bf16[4,432,256]{2,1,0:T(8,128)(2,1)S(1)}, u32[]{:S(2)}, u32[]{:S(2)}) async-start(bf16[4,432,256]{2,1,0:T(8,128)(2,1)} %pad_maximum_fusion.1), calls=%async_computation | async-start | bytes 1769472 | tf_op jit(solution)/shard_map/all_to_all | solution.py:122
  60.4 11.6 %collective-permute-start.11 = (bf16[256,640]{1,0:T(8,128)(2,1)S(1)}, bf16[256,640]{1,0:T(8,128)(2,1)S(1)}, u32[]{:S(2)}, u32[]{:S(2)}) collective-permute-start(bf16[256,640]{1,0:T(8,128)(2,1)S(1)} %get-tuple-element.45), channel_id=1, source_target_pairs={{0,24},{8,16},{16,8},{24,0},{1,25},{9,17},{17,9},{25,1},{2,26},{10... | collective-permute-start | bytes 983048 | tf_op jit(solution)/shard_map/ppermute | solution.py:196
  62.9 15.2 %collective-permute-start.10 = (bf16[256,640]{1,0:T(8,128)(2,1)S(1)}, bf16[256,640]{1,0:T(8,128)(2,1)S(1)}, u32[]{:S(2)}, u32[]{:S(2)}) collective-permute-start(bf16[256,640]{1,0:T(8,128)(2,1)S(1)} %get-tuple-element.44), channel_id=1, source_target_pairs={{0,16},{8,24},{16,0},{24,8},{1,17},{9,25},{17,1},{25,9},{2,18},{10... | collective-permute-start | bytes 983048 | tf_op jit(solution)/shard_map/ppermute | solution.py:196
  63.5 14.8 %collective-permute-start.9 = (bf16[256,640]{1,0:T(8,128)(2,1)S(1)}, bf16[256,640]{1,0:T(8,128)(2,1)S(1)}, u32[]{:S(2)}, u32[]{:S(2)}) collective-permute-start(bf16[256,640]{1,0:T(8,128)(2,1)S(1)} %get-tuple-element.43), channel_id=1, source_target_pairs={{0,8},{8,0},{16,24},{24,16},{1,9},{9,1},{17,25},{25,17},{2,10},{10... | collective-permute-start | bytes 983048 | tf_op jit(solution)/shard_map/ppermute | solution.py:196
  83.6 5.2 %collective-permute-start.8 = (bf16[192,128]{1,0:T(8,128)(2,1)S(1)}, bf16[192,128]{1,0:T(8,128)(2,1)S(1)}, u32[]{:S(2)}, u32[]{:S(2)}) collective-permute-start(bf16[192,128]{1,0:T(8,128)(2,1)S(1)} %get-tuple-element.58), channel_id=1, source_target_pairs={{0,24},{8,16},{16,8},{24,0},{1,25},{9,17},{17,9},{25,1},{2,26},{10... | collective-permute-start | bytes 147464 | tf_op jit(solution)/shard_map/ppermute | solution.py:51
  86.1 4.1 %collective-permute-start.7 = (bf16[192,128]{1,0:T(8,128)(2,1)S(1)}, bf16[192,128]{1,0:T(8,128)(2,1)S(1)}, u32[]{:S(2)}, u32[]{:S(2)}) collective-permute-start(bf16[192,128]{1,0:T(8,128)(2,1)S(1)} %get-tuple-element.59), channel_id=1, source_target_pairs={{0,16},{8,24},{16,0},{24,8},{1,17},{9,25},{17,1},{25,9},{2,18},{10... | collective-permute-start | bytes 147464 | tf_op jit(solution)/shard_map/ppermute | solution.py:51
  86.6 4.1 %collective-permute-start.6 = (bf16[192,128]{1,0:T(8,128)(2,1)S(1)}, bf16[192,128]{1,0:T(8,128)(2,1)S(1)}, u32[]{:S(2)}, u32[]{:S(2)}) collective-permute-start(bf16[192,128]{1,0:T(8,128)(2,1)S(1)} %get-tuple-element.60), channel_id=1, source_target_pairs={{0,8},{8,0},{16,24},{24,16},{1,9},{9,1},{17,25},{25,17},{2,10},{10... | collective-permute-start | bytes 147464 | tf_op jit(solution)/shard_map/ppermute | solution.py:51

commit v17 on v14

--- a/solution.py
+++ b/solution.py
@@ -117,6 +117,15 @@
     def sibling_sum(part):
         keep, send = by_core(part, 0)
         return (keep.astype(f32) + lax.ppermute(send, "tensor", sibling).astype(f32)).astype(bf16)
+
+    def reduce_by_permutes(pair_sum):
+        chip = tensor_index // 2
+        total = lax.dynamic_index_in_dim(pair_sum, chip, 0, keepdims=False).astype(f32)
+        for k in range(1, half_count):
+            outgoing = lax.dynamic_index_in_dim(pair_sum, chip ^ k, 0, keepdims=False)
+            partners = [(t, ((t // 2) ^ k) * 2 + t % 2) for t in range(tensor_count)]
+            total = total + lax.ppermute(outgoing, "tensor", partners).astype(f32)
+        return total
 
     def reduce_blocks(pair_sum):
         pieces = lax.all_to_all(pair_sum, "tensor", 0, 0, tiled=True, axis_index_groups=same_core)
@@ -166,11 +175,8 @@
         owned_rows, 4 * col_width
     )
     grad_part = jnp.einsum("rn,tkn->trk", own_grad, own_proj, preferred_element_type=f32)
-    both_sum = reduce_blocks(
-        jnp.concatenate([sibling_sum(out_part.astype(bf16)), sibling_sum(grad_part.astype(bf16))], axis=2)
-    )
-    out_sum = both_sum[:, :col_width]
-    grad_sum = both_sum[:, col_width:]
+    out_sum = reduce_by_permutes(sibling_sum(out_part.astype(bf16)))
+    grad_sum = reduce_blocks(sibling_sum(grad_part.astype(bf16)))
     mixed_out = (own_tokens.astype(f32) + out_sum).astype(bf16)
     token_rows = (own_cotan.astype(f32) + grad_sum).astype(bf16)
 

time: 91.5 us -> 93.7 us (1.024)
  waiting for transfers between devices: 20.4 us -> 15.3 us
  other arithmetic: 8.41 us -> 11.7 us
  starting transfers between devices: 15.7 us -> 18.7 us
    ppermute x0 -> x3, waiting for transfers between devices: none -> 5.01 us  [reduce_by_permutes(): total = total + lax.ppermute(outgoing, 'tensor', partners).astype(f32)]
    ppermute x3, waiting for transfers between devices: 13.6 us -> 9.45 us  [local(): term_sum = term_sum + lax.ppermute(outgoing, 'dp', partners).astype(f32)]
    ppermute x0 -> x3, starting transfers between devices: none -> 3.55 us  [reduce_by_permutes(): total = total + lax.ppermute(outgoing, 'tensor', partners).astype(f32)]
    ppermute x6, waiting for transfers between devices: 2.89 us -> 0.02 us  [exchange(): lax.ppermute(outgoing, 'dp', [(d, d ^ k) for d in range(dp_count)])]
    all_to_all x1, waiting for transfers between devices: 2.48 us -> 0.01 us  [reduce_blocks(): lax.all_to_all(pair_sum, 'tensor', 0, 0, tiled=True, axis_index_groups=sa...]
    convert_element_type x2, other arithmetic: 0.27 us -> 2.04 us  [sibling_sum(): (keep.astype(f32) + lax.ppermute(send, 'tensor', sibling).astype(f32)).as...]
    add x1, other arithmetic: 0.15 us -> 1.32 us  [local(): term_sum = term_sum + lax.ppermute(outgoing, 'dp', partners).astype(f32)]
    concatenate x1 -> x0, other arithmetic: 1.02 us -> none  [local(): jnp.concatenate([sibling_sum(out_part.astype(bf16)), sibling_sum(grad_par...]
  transfers between devices with their start and end apart: 13 -> 16, of which waited for: 8 -> 5; matrix products, arithmetic and copies ran while one was open for 17% -> 21% of each run, Pallas kernels for 0% -> 0%
where the time goes in v17:
time: 93.7 us; the launch traced here: 93.2 us
  blocking collectives  21.3 us (23%)
  starting transfers between devices  18.7 us (20%)
  waiting for transfers between devices  15.3 us (16%)
  local copies, waits for them, and re-layouts  14.3 us (15%)
  other arithmetic  11.7 us (12%)
  matrix products  10.5 us (11%)
  between operations  1.25 us (1%)
    all_gather x1, blocking collectives, local(): lax.all_gather(own_both, 'tensor', axis=0, tiled=False, axis_index_groups...  21.3 us
    ppermute x3, waiting for transfers between devices, local(): term_sum = term_sum + lax.ppermute(outgoing, 'dp', partners).astype(f32)  9.45 us
    ppermute x6, starting transfers between devices, exchange(): lax.ppermute(outgoing, 'dp', [(d, d ^ k) for d in range(dp_count)])  8.01 us
    ppermute x3, waiting for transfers between devices, reduce_by_permutes(): total = total + lax.ppermute(outgoing, 'tensor', partners).astype(f32)  5.01 us
    dot_general x5, matrix products, pick_rows(): return jnp.dot(one_hot, source, preferred_element_type=f32).astype(bf16)  4.36 us
    unnamed x32, local copies, waits for them, and re-layouts  3.69 us
    ppermute x3, starting transfers between devices, reduce_by_permutes(): total = total + lax.ppermute(outgoing, 'tensor', partners).astype(f32)  3.55 us
    ppermute x3, starting transfers between devices, local(): term_sum = term_sum + lax.ppermute(outgoing, 'dp', partners).astype(f32)  3.5 us
  transfers between devices with their start and end apart: 16, of which 5 were waited for; matrix products, arithmetic and copies ran while one was open for 21% of the time, Pallas kernels for 0%

profile of v17, /device:TPU:0, one launch (start us, length us, event | category | flops | bytes accessed | tf_op | source)
XLA Modules:
  0.0 93.2 jit_solution(2424107344932145837)
XLA Ops:
  1.4 1.4 %fusion.61 = (s32[]{:T(128)}, s32[1,4]{1,0:T(1,128)S(1)}) fusion(s32[4,4]{1,0:T(4,128)} %param.9, s32[]{:T(128)S(6)} %select_n.130), kind=kLoop, calls=%fused_computation.167 | loop fusion | flops 3 | bytes 40 | tf_op jit(solution)/shard_map/reduce_sum | solution.py:216
  3.0 0.8 select_reduce_fusion.3
  4.7 1.6 %fusion.14 = bf16[768,128]{0,1:T(8,128)(2,1)S(1)} fusion(bf16[672,128]{1,0:T(8,128)(2,1)} %param.7, s32[768]{0:T(1024)S(1)} %min.38), kind=kOutput, calls=%fused_computation.36 | convolution fusion | flops 132734976 | bytes 371712 | tf_op jit(solution)/shard_map/dot_general | solution.py:56
  7.3 3.9 %collective-permute-start.2 = (bf16[192,256]{1,0:T(8,128)(2,1)}, bf16[192,256]{1,0:T(8,128)(2,1)}, u32[]{:S(2)}, u32[]{:S(2)}) collective-permute-start(bf16[192,256]{1,0:T(8,128)(2,1)} %get-tuple-element.54), channel_id=1, source_target_pairs={{0,24},{8,16},{16,8},{24,0},{1,25},{9,17},{17,9},{25,1},{2,26},{10... | collective-permute-start | bytes 294920 | tf_op jit(solution)/shard_map/ppermute | solution.py:51
  12.8 1.3 %dynamic_slice.116 = f32[128]{0:T(128)} dynamic-slice(f32[1024]{0:T(1024)} %param.12, s32[]{:T(128)S(6)} %select_n.136), dynamic_slice_sizes={128} | dynamic-slice | bytes 1028 | tf_op jit(solution)/shard_map/dynamic_slice | solution.py:86
  14.1 1.1 %constant_dynamic-slice_fusion.1 = (bf16[128,1024]{1,0:T(8,128)(2,1)S(1)}, bf16[128,1024]{1,0:T(8,128)(2,1)S(1)}) fusion(bf16[1024,1024]{1,0:T(8,128)(2,1)} %param.13, s32[]{:T(128)S(6)} %select_n.140, s32[]{:T(128)S(6)} %select_n.136), kind=kLoop, calls=%fused_computation.138 | loop fusion | bytes 1048584 | tf_op jit(solution)/shard_map/dynamic_slice | solution.py:90
  15.2 0.9 copy.59
  16.3 0.8 copy.45
  17.2 2.4 %constant_dynamic-slice_fusion.2 = (bf16[1024,4,128]{2,1,0:T(4,128)(2,1)S(1)}, bf16[1024,4,128]{2,1,0:T(4,128)(2,1)S(1)}) fusion(bf16[1024,4,1024]{2,1,0:T(4,128)(2,1)} %param.11, s32[]{:T(128)S(6)} %select_n.140, s32[]{:T(128)S(6)} %select_n.136), kind=kLoop, calls=%fused_computation.139 | loop fusion | bytes 4194312 | tf_op jit(solution)/shard_map/dynamic_slice | solution.py:80
  19.7 1.2 %reshape.185 = bf16[8,128,512]{2,1,0:T(8,128)(2,1)} reshape(bf16[1024,4,128]{2,1,0:T(4,128)(2,1)S(1)} %get-tuple-element.38) | data formatting | bytes 2097152 | tf_op jit(solution)/shard_map/reshape | solution.py:80
  21.5 1.0 %pad_maximum_fusion.3 = bf16[4,192,256]{2,1,0:T(8,128)(2,1)S(1)} fusion(bf16[1,192,256]{2,1,0:T(8,128)(2,1)} %bitcast.10, bf16[1,192,256]{2,1,0:T(8,128)(2,1)} %bitcast.8, bf16[1,192,256]{2,1,0:T(8,128)(2,1)} %bitcast.6, bf16[1,192,256]{2,1,0:T(8,128)(2,1)S(1)} %get-tuple-element.53), kind=kLoop, calls=%fused_computation.82 | loop fusion | flops 589824 | bytes 786432 | tf_op jit(solution)/shard_map/stack | solution.py:52
  22.9 21.3 %all-gather = bf16[1728,256]{1,0:T(8,128)(2,1)S(1)} all-gather(bf16[432,256]{1,0:T(8,128)(2,1)S(1)} %fusion.10), channel_id=2, replica_groups={{0,2,4,6},{1,3,5,7},{8,10,12,14},{9,11,13,15},{16,18,20,22},{17,19,21,2..., dimensions={0}, use_global_device_ids=true | all-gather | bytes 1105920 | tf_op jit(solution)/shard_map/all_gather | solution.py:112
  45.9 0.8 collective-permute-done.3
  54.5 1.0 %fusion.48 = (bf16[256,640]{1,0:T(8,128)(2,1)}, bf16[256,640]{1,0:T(8,128)(2,1)}, bf16[256,640]{1,0:T(8,128)(2,1)}) fusion(s32[]{:T(128)S(6)} %select_n.132, bf16[4,256,512]{2,1,0:T(8,128)(2,1)S(1)} %bitcast.187, bf16[4,256,128]{2,1,0:T(8,128)(2,1)S(1)} %bitcast.196, s32[]{:T(128)S(6)} %select_n.133, s32[]{:T(128)S(6)} %select_n.134), kind=kLoop, calls=%fused_computation.96 | loop fusion | flops 1966080 | bytes 2293772 | tf_op jit(solution)/shard_map/jit(dynamic_index_in_dim)/squeeze | solution.py:200
  55.5 1.5 %collective-permute-start.12 = (bf16[256,640]{1,0:T(8,128)(2,1)}, bf16[256,640]{1,0:T(8,128)(2,1)}, u32[]{:S(2)}, u32[]{:S(2)}) collective-permute-start(bf16[256,640]{1,0:T(8,128)(2,1)} %get-tuple-element.42), channel_id=1, source_target_pairs={{0,8},{8,0},{16,24},{24,16},{1,9},{9,1},{17,25},{25,17},{2,10},{10... | collective-permute-start | bytes 983048 | tf_op jit(solution)/shard_map/ppermute | solution.py:202
  57.0 1.5 %collective-permute-start.13 = (bf16[256,640]{1,0:T(8,128)(2,1)}, bf16[256,640]{1,0:T(8,128)(2,1)}, u32[]{:S(2)}, u32[]{:S(2)}) collective-permute-start(bf16[256,640]{1,0:T(8,128)(2,1)} %get-tuple-element.43), channel_id=1, source_target_pairs={{0,16},{8,24},{16,0},{24,8},{1,17},{9,25},{17,1},{25,9},{2,18},{10... | collective-permute-start | bytes 983048 | tf_op jit(solution)/shard_map/ppermute | solution.py:202
  59.4 0.8 dynamic-slice_bitcast_fusion.3
  60.2 0.9 fusion.24
  61.1 3.5 %all-to-all-start = ((bf16[4,432,128]{2,1,0:T(8,128)(2,1)}), bf16[4,432,128]{2,1,0:T(8,128)(2,1)S(1)}, u32[]{:S(2)}, u32[]{:S(2)}) async-start(bf16[4,432,128]{2,1,0:T(8,128)(2,1)} %fusion.24), calls=%async_computation | async-start | bytes 884736 | tf_op jit(solution)/shard_map/all_to_all | solution.py:131
  64.6 1.8 %collective-permute-done.12 = bf16[256,640]{1,0:T(8,128)(2,1)} collective-permute-done((bf16[256,640]{1,0:T(8,128)(2,1)}, bf16[256,640]{1,0:T(8,128)(2,1)}, u32[]{:S(2)}, u32[]{:S(2)}) %collective-permute-start.12) | collective-permute-done | bytes 327712 | tf_op jit(solution)/shard_map/ppermute | solution.py:202
  66.3 7.7 %collective-permute-done.13 = bf16[256,640]{1,0:T(8,128)(2,1)} collective-permute-done((bf16[256,640]{1,0:T(8,128)(2,1)}, bf16[256,640]{1,0:T(8,128)(2,1)}, u32[]{:S(2)}, u32[]{:S(2)}) %collective-permute-start.13) | collective-permute-done | bytes 327712 | tf_op jit(solution)/shard_map/ppermute | solution.py:202
  74.0 1.3 %fusion.30 = f32[256,640]{1,0:T(8,128)S(1)} fusion(bf16[256,640]{1,0:T(8,128)(2,1)} %collective-permute-done.14, bf16[256,640]{1,0:T(8,128)(2,1)} %collective-permute-done.13, bf16[256,640]{1,0:T(8,128)(2,1)} %collective-permute-done.12, s32[]{:T(128)S(6)} %select_n.130, bf16[4,256,512]{2,1,0:T(8,128)(2,1)S(1)} %bitcast.188, ...), kind=kLoop, calls=%fused_computation.71 | loop fusion | flops 1802240 | bytes 2949124 | tf_op jit(solution)/shard_map/add | solution.py:202
  75.6 1.0 %copy.55 = f32[256,4,128]{2,1,0:T(4,128)} copy(f32[256,4,128]{0,2,1:T(8,128)S(1)} %bitcast.198) | data formatting | bytes 1048576
  77.4 1.1 %fusion.25 = bf16[4,432,128]{2,1,0:T(8,128)(2,1)S(1)} fusion(bf16[4,432,128]{2,1,0:T(8,128)(2,1)} %collective-permute-done.4, bf16[4,2,432,128]{3,2,1,0:T(8,128)(2,1)S(1)} %bitcast.195, s32[]{:T(128)S(6)} %select_n.138), kind=kLoop, calls=%fused_computation.60 | loop fusion | flops 884736 | bytes 1327108 | tf_op jit(solution)/shard_map/convert_element_type | solution.py:119
  78.6 2.3 %collective-permute-start.7 = (bf16[432,128]{1,0:T(8,128)(2,1)S(1)}, bf16[432,128]{1,0:T(8,128)(2,1)S(1)}, u32[]{:S(2)}, u32[]{:S(2)}) collective-permute-start(bf16[432,128]{1,0:T(8,128)(2,1)S(1)} %get-tuple-element.51), channel_id=1, source_target_pairs={{0,6},{1,7},{2,4},{3,5},{4,2},{5,3},{6,0},{7,1},{8,14},{9,15},{10,... | collective-permute-start | bytes 331784 | tf_op jit(solution)/shard_map/ppermute | solution.py:127
  80.9 1.2 %collective-permute-start.6 = (bf16[432,128]{1,0:T(8,128)(2,1)S(1)}, bf16[432,128]{1,0:T(8,128)(2,1)S(1)}, u32[]{:S(2)}, u32[]{:S(2)}) collective-permute-start(bf16[432,128]{1,0:T(8,128)(2,1)S(1)} %get-tuple-element.52), channel_id=1, source_target_pairs={{0,4},{1,5},{2,6},{3,7},{4,0},{5,1},{6,2},{7,3},{8,12},{9,13},{10,... | collective-permute-start | bytes 331784 | tf_op jit(solution)/shard_map/ppermute | solution.py:127
  82.7 1.6 %collective-permute-start.11 = (bf16[192,128]{1,0:T(8,128)(2,1)S(1)}, bf16[192,128]{1,0:T(8,128)(2,1)S(1)}, u32[]{:S(2)}, u32[]{:S(2)}) collective-permute-start(bf16[192,128]{1,0:T(8,128)(2,1)S(1)} %get-tuple-element.60), channel_id=1, source_target_pairs={{0,24},{8,16},{16,8},{24,0},{1,25},{9,17},{17,9},{25,1},{2,26},{10... | collective-permute-start | bytes 147464 | tf_op jit(solution)/shard_map/ppermute | solution.py:51
  84.2 1.2 %collective-permute-start.10 = (bf16[192,128]{1,0:T(8,128)(2,1)S(1)}, bf16[192,128]{1,0:T(8,128)(2,1)S(1)}, u32[]{:S(2)}, u32[]{:S(2)}) collective-permute-start(bf16[192,128]{1,0:T(8,128)(2,1)S(1)} %get-tuple-element.61), channel_id=1, source_target_pairs={{0,16},{8,24},{16,0},{24,8},{1,17},{9,25},{17,1},{25,9},{2,18},{10... | collective-permute-start | bytes 147464 | tf_op jit(solution)/shard_map/ppermute | solution.py:51
  85.4 0.8 collective-permute-start.9
  86.2 1.0 %collective-permute-done.7 = bf16[432,128]{1,0:T(8,128)(2,1)S(1)} collective-permute-done((bf16[432,128]{1,0:T(8,128)(2,1)S(1)}, bf16[432,128]{1,0:T(8,128)(2,1)S(1)}, u32[]{:S(2)}, u32[]{:S(2)}) %collective-permute-start.7) | collective-permute-done | bytes 110624 | tf_op jit(solution)/shard_map/ppermute | solution.py:127
  87.2 4.0 %collective-permute-done.6 = bf16[432,128]{1,0:T(8,128)(2,1)S(1)} collective-permute-done((bf16[432,128]{1,0:T(8,128)(2,1)S(1)}, bf16[432,128]{1,0:T(8,128)(2,1)S(1)}, u32[]{:S(2)}, u32[]{:S(2)}) %collective-permute-start.6) | collective-permute-done | bytes 110624 | tf_op jit(solution)/shard_map/ppermute | solution.py:127
  92.0 1.2 %fusion.16 = bf16[672,128]{1,0:T(8,128)(2,1)} fusion(bf16[768,128]{1,0:T(8,128)(2,1)S(1)} %bitcast.208, s32[672]{0:T(1024)S(1)} %add_select_fusion), kind=kOutput, calls=%fused_computation.40 | convolution fusion | flops 132722688 | bytes 371328 | tf_op jit(solution)/shard_map/dot_general | solution.py:56
  (111 shorter events, 17.9 us)
Async XLA Ops:
  0.6 3.4 %copy-start = (bf16[672,128]{1,0:T(8,128)(2,1)S(1)}, bf16[672,128]{1,0:T(8,128)(2,1)}, u32[]{:S(2)}) copy-start(bf16[672,128]{1,0:T(8,128)(2,1)} %param.8) | copy-start | bytes 516100
  1.4 2.4 %copy-start.12 = (s32[4]{0:T(128)}, s32[4]{0:T(128)S(1)}, u32[]{:S(2)}) copy-start(s32[4]{0:T(128)S(1)} %fusion.60) | copy-start | bytes 52
  3.0 0.9 copy-start.8
  7.3 14.2 %collective-permute-start.2 = (bf16[192,256]{1,0:T(8,128)(2,1)}, bf16[192,256]{1,0:T(8,128)(2,1)}, u32[]{:S(2)}, u32[]{:S(2)}) collective-permute-start(bf16[192,256]{1,0:T(8,128)(2,1)} %get-tuple-element.54), channel_id=1, source_target_pairs={{0,24},{8,16},{16,8},{24,0},{1,25},{9,17},{17,9},{25,1},{2,26},{10... | collective-permute-start | bytes 294920 | tf_op jit(solution)/shard_map/ppermute | solution.py:51
  11.2 10.3 %collective-permute-start.1 = (bf16[192,256]{1,0:T(8,128)(2,1)}, bf16[192,256]{1,0:T(8,128)(2,1)}, u32[]{:S(2)}, u32[]{:S(2)}) collective-permute-start(bf16[192,256]{1,0:T(8,128)(2,1)} %get-tuple-element.55), channel_id=1, source_target_pairs={{0,16},{8,24},{16,0},{24,8},{1,17},{9,25},{17,1},{25,9},{2,18},{10... | collective-permute-start | bytes 294920 | tf_op jit(solution)/shard_map/ppermute | solution.py:51
  11.7 9.8 %collective-permute-start = (bf16[192,256]{1,0:T(8,128)(2,1)}, bf16[192,256]{1,0:T(8,128)(2,1)}, u32[]{:S(2)}, u32[]{:S(2)}) collective-permute-start(bf16[192,256]{1,0:T(8,128)(2,1)} %get-tuple-element.56), channel_id=1, source_target_pairs={{0,8},{8,0},{16,24},{24,16},{1,9},{9,1},{17,25},{25,17},{2,10},{10... | collective-permute-start | bytes 294920 | tf_op jit(solution)/shard_map/ppermute | solution.py:51
  21.3 1.2 %copy-start.11 = (s32[432]{0:T(512)S(1)}, s32[432]{0:T(512)}, u32[]{:S(2)}) copy-start(s32[432]{0:T(512)} %add_subtract_fusion) | copy-start | bytes 5188
  21.4 22.9 %copy-start.9 = (s32[4]{0:T(128)S(1)}, s32[4]{0:T(128)}, u32[]{:S(2)}) copy-start(s32[4]{0:T(128)} %copy-done.8) | copy-start | bytes 52
  21.4 23.1 %copy-start.13 = (s32[4]{0:T(128)S(1)}, s32[4]{0:T(128)}, u32[]{:S(2)}) copy-start(s32[4]{0:T(128)} %copy-done.12) | copy-start | bytes 52
  22.9 21.3 %copy-start.6 = (bf16[432,256]{1,0:T(8,128)(2,1)}, bf16[432,256]{1,0:T(8,128)(2,1)S(1)}, u32[]{:S(2)}) copy-start(bf16[432,256]{1,0:T(8,128)(2,1)S(1)} %fusion.10) | copy-start | bytes 663556
  44.3 2.4 %collective-permute-start.3 = (bf16[4,432,256]{2,1,0:T(8,128)(2,1)S(1)}, bf16[4,432,256]{2,1,0:T(8,128)(2,1)S(1)}, u32[]{:S(2)}, u32[]{:S(2)}) collective-permute-start(bf16[4,432,256]{2,1,0:T(8,128)(2,1)S(1)} %bitcast.189), channel_id=1, source_target_pairs={{0,1},{1,0},{2,3},{3,2},{4,5},{5,4},{6,7},{7,6},{8,9},{9,8},{10,11... | collective-permute-start | bytes 2654216 | tf_op jit(solution)/shard_map/ppermute | solution.py:113
  46.7 4.2 %copy-start.1 = (bf16[4,432,256]{2,1,0:T(8,128)(2,1)}, bf16[4,432,256]{2,1,0:T(8,128)(2,1)S(1)}, u32[]{:S(2)}) copy-start(bf16[4,432,256]{2,1,0:T(8,128)(2,1)S(1)} %collective-permute-done.3) | copy-start | bytes 2654212
  47.3 0.9 copy-start.5
  47.4 1.2 %copy-start.10 = (f32[128]{0:T(128)S(1)}, f32[128]{0:T(128)}, u32[]{:S(2)}) copy-start(f32[128]{0:T(128)} %dynamic_slice.116) | copy-start | bytes 1540
  51.4 1.2 %copy-start.4 = (bf16[8,128,512]{2,1,0:T(8,128)(2,1)S(1)}, bf16[8,128,512]{2,1,0:T(8,128)(2,1)}, u32[]{:S(2)}) copy-start(bf16[8,128,512]{2,1,0:T(8,128)(2,1)} %reshape.185) | copy-start | bytes 3145732
  51.8 1.5 %copy-start.2 = (bf16[4,432,256]{2,1,0:T(8,128)(2,1)S(1)}, bf16[4,432,256]{2,1,0:T(8,128)(2,1)}, u32[]{:S(2)}) copy-start(bf16[4,432,256]{2,1,0:T(8,128)(2,1)} %copy-done.1) | copy-start | bytes 2654212
  54.2 4.8 %copy-start.3 = (bf16[128,1024]{0,1:T(8,128)(2,1)S(1)}, bf16[128,1024]{0,1:T(8,128)(2,1)}, u32[]{:S(2)}) copy-start(bf16[128,1024]{0,1:T(8,128)(2,1)} %copy.59) | copy-start | bytes 786436
  54.3 5.9 %collective-permute-start.8 = (bf16[4,432,128]{2,1,0:T(8,128)(2,1)S(1)}, bf16[4,432,128]{2,1,0:T(8,128)(2,1)S(1)}, u32[]{:S(2)}, u32[]{:S(2)}) collective-permute-start(bf16[4,432,128]{2,1,0:T(8,128)(2,1)S(1)} %dynamic-slice_bitcast_fusion.2), channel_id=1, source_target_pairs={{0,1},{1,0},{2,3},{3,2},{4,5},{5,4},{6,7},{7,6},{8,9},{9,8},{10,11... | collective-permute-start | bytes 1327112 | tf_op jit(solution)/shard_map/ppermute | solution.py:119
  55.5 10.9 %collective-permute-start.12 = (bf16[256,640]{1,0:T(8,128)(2,1)}, bf16[256,640]{1,0:T(8,128)(2,1)}, u32[]{:S(2)}, u32[]{:S(2)}) collective-permute-start(bf16[256,640]{1,0:T(8,128)(2,1)} %get-tuple-element.42), channel_id=1, source_target_pairs={{0,8},{8,0},{16,24},{24,16},{1,9},{9,1},{17,25},{25,17},{2,10},{10... | collective-permute-start | bytes 983048 | tf_op jit(solution)/shard_map/ppermute | solution.py:202
  57.0 17.0 %collective-permute-start.13 = (bf16[256,640]{1,0:T(8,128)(2,1)}, bf16[256,640]{1,0:T(8,128)(2,1)}, u32[]{:S(2)}, u32[]{:S(2)}) collective-permute-start(bf16[256,640]{1,0:T(8,128)(2,1)} %get-tuple-element.43), channel_id=1, source_target_pairs={{0,16},{8,24},{16,0},{24,8},{1,17},{9,25},{17,1},{25,9},{2,18},{10... | collective-permute-start | bytes 983048 | tf_op jit(solution)/shard_map/ppermute | solution.py:202
  58.5 15.5 %collective-permute-start.14 = (bf16[256,640]{1,0:T(8,128)(2,1)}, bf16[256,640]{1,0:T(8,128)(2,1)}, u32[]{:S(2)}, u32[]{:S(2)}) collective-permute-start(bf16[256,640]{1,0:T(8,128)(2,1)} %get-tuple-element.44), channel_id=1, source_target_pairs={{0,24},{8,16},{16,8},{24,0},{1,25},{9,17},{17,9},{25,1},{2,26},{10... | collective-permute-start | bytes 983048 | tf_op jit(solution)/shard_map/ppermute | solution.py:202
  60.2 17.2 %collective-permute-start.4 = (bf16[4,432,128]{2,1,0:T(8,128)(2,1)}, bf16[4,432,128]{2,1,0:T(8,128)(2,1)}, u32[]{:S(2)}, u32[]{:S(2)}) collective-permute-start(bf16[4,432,128]{2,1,0:T(8,128)(2,1)} %dynamic-slice_bitcast_fusion.3), channel_id=1, source_target_pairs={{0,1},{1,0},{2,3},{3,2},{4,5},{5,4},{6,7},{7,6},{8,9},{9,8},{10,11... | collective-permute-start | bytes 1327112 | tf_op jit(solution)/shard_map/ppermute | solution.py:119
  61.1 21.0 %all-to-all-start = ((bf16[4,432,128]{2,1,0:T(8,128)(2,1)}), bf16[4,432,128]{2,1,0:T(8,128)(2,1)S(1)}, u32[]{:S(2)}, u32[]{:S(2)}) async-start(bf16[4,432,128]{2,1,0:T(8,128)(2,1)} %fusion.24), calls=%async_computation | async-start | bytes 884736 | tf_op jit(solution)/shard_map/all_to_all | solution.py:131
  76.6 5.6 %copy-start.7 = (bf16[432,256]{1,0:T(8,128)(2,1)S(1)}, bf16[432,256]{1,0:T(8,128)(2,1)}, u32[]{:S(2)}) copy-start(bf16[432,256]{1,0:T(8,128)(2,1)} %copy-done.6) | copy-start | bytes 663556
  78.6 6.9 %collective-permute-start.5 = (bf16[432,128]{1,0:T(8,128)(2,1)S(1)}, bf16[432,128]{1,0:T(8,128)(2,1)S(1)}, u32[]{:S(2)}, u32[]{:S(2)}) collective-permute-start(bf16[432,128]{1,0:T(8,128)(2,1)S(1)} %get-tuple-element.50), channel_id=1, source_target_pairs={{0,2},{1,3},{2,0},{3,1},{4,6},{5,7},{6,4},{7,5},{8,10},{9,11},{10,... | collective-permute-start | bytes 331784 | tf_op jit(solution)/shard_map/ppermute | solution.py:127
  78.6 8.5 %collective-permute-start.7 = (bf16[432,128]{1,0:T(8,128)(2,1)S(1)}, bf16[432,128]{1,0:T(8,128)(2,1)S(1)}, u32[]{:S(2)}, u32[]{:S(2)}) collective-permute-start(bf16[432,128]{1,0:T(8,128)(2,1)S(1)} %get-tuple-element.51), channel_id=1, source_target_pairs={{0,6},{1,7},{2,4},{3,5},{4,2},{5,3},{6,0},{7,1},{8,14},{9,15},{10,... | collective-permute-start | bytes 331784 | tf_op jit(solution)/shard_map/ppermute | solution.py:127
  80.9 10.3 %collective-permute-start.6 = (bf16[432,128]{1,0:T(8,128)(2,1)S(1)}, bf16[432,128]{1,0:T(8,128)(2,1)S(1)}, u32[]{:S(2)}, u32[]{:S(2)}) collective-permute-start(bf16[432,128]{1,0:T(8,128)(2,1)S(1)} %get-tuple-element.52), channel_id=1, source_target_pairs={{0,4},{1,5},{2,6},{3,7},{4,0},{5,1},{6,2},{7,3},{8,12},{9,13},{10,... | collective-permute-start | bytes 331784 | tf_op jit(solution)/shard_map/ppermute | solution.py:127
  82.7 9.3 %collective-permute-start.11 = (bf16[192,128]{1,0:T(8,128)(2,1)S(1)}, bf16[192,128]{1,0:T(8,128)(2,1)S(1)}, u32[]{:S(2)}, u32[]{:S(2)}) collective-permute-start(bf16[192,128]{1,0:T(8,128)(2,1)S(1)} %get-tuple-element.60), channel_id=1, source_target_pairs={{0,24},{8,16},{16,8},{24,0},{1,25},{9,17},{17,9},{25,1},{2,26},{10... | collective-permute-start | bytes 147464 | tf_op jit(solution)/shard_map/ppermute | solution.py:51
  84.2 7.7 %collective-permute-start.10 = (bf16[192,128]{1,0:T(8,128)(2,1)S(1)}, bf16[192,128]{1,0:T(8,128)(2,1)S(1)}, u32[]{:S(2)}, u32[]{:S(2)}) collective-permute-start(bf16[192,128]{1,0:T(8,128)(2,1)S(1)} %get-tuple-element.61), channel_id=1, source_target_pairs={{0,16},{8,24},{16,0},{24,8},{1,17},{9,25},{17,1},{25,9},{2,18},{10... | collective-permute-start | bytes 147464 | tf_op jit(solution)/shard_map/ppermute | solution.py:51
  85.4 6.5 %collective-permute-start.9 = (bf16[192,128]{1,0:T(8,128)(2,1)S(1)}, bf16[192,128]{1,0:T(8,128)(2,1)S(1)}, u32[]{:S(2)}, u32[]{:S(2)}) collective-permute-start(bf16[192,128]{1,0:T(8,128)(2,1)S(1)} %get-tuple-element.62), channel_id=1, source_target_pairs={{0,8},{8,0},{16,24},{24,16},{1,9},{9,1},{17,25},{25,17},{2,10},{10... | collective-permute-start | bytes 147464 | tf_op jit(solution)/shard_map/ppermute | solution.py:51

commit v18 on v14

--- a/solution.py
+++ b/solution.py
@@ -56,9 +56,9 @@
         return jnp.dot(one_hot, source, preferred_element_type=f32).astype(bf16)
 
     flat_send = send_ids.reshape(-1)
-    send_both = jnp.concatenate(
-        [pick_rows(flat_send, tokens), pick_rows(flat_send, cotangent)], axis=1
-    ).reshape(dp_count, MAXLEN, 2 * col_width)
+    send_both = pick_rows(flat_send, jnp.concatenate([tokens, cotangent], axis=1)).reshape(
+        dp_count, MAXLEN, 2 * col_width
+    )
     recv_both = exchange(send_both)
 
     half_count = tensor_count // 2

time: 91.5 us -> 88 us (0.962)
  local copies, waits for them, and re-layouts: 13.5 us -> 10.9 us
    unnamed x24 -> x10, local copies, waits for them, and re-layouts: 3.7 us -> 2.49 us
    dot_general x5 -> x4, matrix products: 4.36 us -> 3.61 us  [pick_rows(): return jnp.dot(one_hot, source, preferred_element_type=f32).astype(bf16)]
  transfers between devices with their start and end apart: 13 -> 13, of which waited for: 8 -> 8; matrix products, arithmetic and copies ran while one was open for 17% -> 16% of each run, Pallas kernels for 0% -> 0%
where the time goes in v18:
time: 88 us; the launch traced here: 87.5 us
  blocking collectives  21.3 us (24%)
  waiting for transfers between devices  20.4 us (23%)
  starting transfers between devices  15.7 us (18%)
  local copies, waits for them, and re-layouts  10.9 us (12%)
  matrix products  9.75 us (11%)
  other arithmetic  8.31 us (9%)
  between operations  1.12 us (1%)
    all_gather x1, blocking collectives, local(): lax.all_gather(own_both, 'tensor', axis=0, tiled=False, axis_index_groups...  21.3 us
    ppermute x3, waiting for transfers between devices, local(): term_sum = term_sum + lax.ppermute(outgoing, 'dp', partners).astype(f32)  13.5 us
    ppermute x6, starting transfers between devices, exchange(): lax.ppermute(outgoing, 'dp', [(d, d ^ k) for d in range(dp_count)])  8.02 us
    dot_general x4, matrix products, pick_rows(): return jnp.dot(one_hot, source, preferred_element_type=f32).astype(bf16)  3.61 us
    ppermute x3, starting transfers between devices, local(): term_sum = term_sum + lax.ppermute(outgoing, 'dp', partners).astype(f32)  3.55 us
    all_to_all x1, starting transfers between devices, reduce_blocks(): lax.all_to_all(pair_sum, 'tensor', 0, 0, tiled=True, axis_index_groups=sa...  3.5 us
    ppermute x6, waiting for transfers between devices, exchange(): lax.ppermute(outgoing, 'dp', [(d, d ^ k) for d in range(dp_count)])  2.9 us
    unnamed x10, local copies, waits for them, and re-layouts  2.49 us
  transfers between devices with their start and end apart: 13, of which 8 were waited for; matrix products, arithmetic and copies ran while one was open for 16% of the time, Pallas kernels for 0%

profile of v18, /device:TPU:0, one launch (start us, length us, event | category | flops | bytes accessed | tf_op | source)
XLA Modules:
  0.0 87.5 jit_solution(11136137615955477125)
XLA Ops:
  0.6 1.3 %fusion.61 = (s32[]{:T(128)}, s32[1,4]{1,0:T(1,128)S(1)}) fusion(s32[4,4]{1,0:T(4,128)} %param.9, s32[]{:T(128)S(6)} %select_n.114), kind=kLoop, calls=%fused_computation.163 | loop fusion | flops 3 | bytes 40 | tf_op jit(solution)/shard_map/reduce_sum | solution.py:210
  2.2 0.7 fusion.59
  2.8 0.8 select_reduce_fusion.3
  3.8 1.6 %fusion.9 = bf16[768,256]{1,0:T(8,128)(2,1)S(1)} fusion(s32[768]{0:T(1024)S(1)} %min.38, bf16[672,128]{1,0:T(8,128)(2,1)} %param.8, bf16[672,128]{1,0:T(8,128)(2,1)} %param.7), kind=kOutput, calls=%fused_computation.28 | convolution fusion | flops 265641984 | bytes 740352 | tf_op jit(solution)/shard_map/dot_general | solution.py:56
  5.4 0.7 constant_dynamic-slice_fusion.7
  6.2 3.9 %collective-permute-start.2 = (bf16[192,256]{1,0:T(8,128)(2,1)}, bf16[192,256]{1,0:T(8,128)(2,1)}, u32[]{:S(2)}, u32[]{:S(2)}) collective-permute-start(bf16[192,256]{1,0:T(8,128)(2,1)} %get-tuple-element.51), channel_id=1, source_target_pairs={{0,24},{8,16},{16,8},{24,0},{1,25},{9,17},{17,9},{25,1},{2,26},{10... | collective-permute-start | bytes 294920 | tf_op jit(solution)/shard_map/ppermute | solution.py:51
  10.6 2.4 %constant_dynamic-slice_fusion.2 = (bf16[1024,4,128]{2,1,0:T(4,128)(2,1)S(1)}, bf16[1024,4,128]{2,1,0:T(4,128)(2,1)S(1)}) fusion(bf16[1024,4,1024]{2,1,0:T(4,128)(2,1)} %param.11, s32[]{:T(128)S(6)} %select_n.124, s32[]{:T(128)S(6)} %select_n.120), kind=kLoop, calls=%fused_computation.138 | loop fusion | bytes 4194312 | tf_op jit(solution)/shard_map/dynamic_slice | solution.py:80
  13.5 1.1 %constant_dynamic-slice_fusion.1 = (bf16[128,1024]{1,0:T(8,128)(2,1)S(1)}, bf16[128,1024]{1,0:T(8,128)(2,1)S(1)}) fusion(bf16[1024,1024]{1,0:T(8,128)(2,1)} %param.13, s32[]{:T(128)S(6)} %select_n.124, s32[]{:T(128)S(6)} %select_n.120), kind=kLoop, calls=%fused_computation.137 | loop fusion | bytes 1048584 | tf_op jit(solution)/shard_map/dynamic_slice | solution.py:90
  15.1 1.2 %reshape.183 = bf16[8,128,512]{2,1,0:T(8,128)(2,1)} reshape(bf16[1024,4,128]{2,1,0:T(4,128)(2,1)S(1)} %get-tuple-element.38) | data formatting | bytes 2097152 | tf_op jit(solution)/shard_map/reshape | solution.py:80
  16.6 0.8 dynamic_slice.103
  17.8 1.0 %pad_maximum_fusion.3 = bf16[4,192,256]{2,1,0:T(8,128)(2,1)S(1)} fusion(bf16[1,192,256]{2,1,0:T(8,128)(2,1)} %bitcast.10, bf16[1,192,256]{2,1,0:T(8,128)(2,1)} %bitcast.8, bf16[1,192,256]{2,1,0:T(8,128)(2,1)} %bitcast.6, bf16[1,192,256]{2,1,0:T(8,128)(2,1)S(1)} %get-tuple-element.50), kind=kLoop, calls=%fused_computation.79 | loop fusion | flops 589824 | bytes 786432 | tf_op jit(solution)/shard_map/stack | solution.py:52
  19.3 21.3 %all-gather = bf16[1728,256]{1,0:T(8,128)(2,1)S(1)} all-gather(bf16[432,256]{1,0:T(8,128)(2,1)S(1)} %fusion.10), channel_id=2, replica_groups={{0,2,4,6},{1,3,5,7},{8,10,12,14},{9,11,13,15},{16,18,20,22},{17,19,21,2..., dimensions={0}, use_global_device_ids=true | all-gather | bytes 1105920 | tf_op jit(solution)/shard_map/all_gather | solution.py:112
  41.5 1.5 %collective-permute-done.3 = bf16[4,432,256]{2,1,0:T(8,128)(2,1)S(1)} collective-permute-done((bf16[4,432,256]{2,1,0:T(8,128)(2,1)S(1)}, bf16[4,432,256]{2,1,0:T(8,128)(2,1)S(1)}, u32[]{:S(2)}, u32[]{:S(2)}) %collective-permute-start.3) | collective-permute-done | bytes 884768 | tf_op jit(solution)/shard_map/ppermute | solution.py:113
  47.6 0.7 convolution_convert_fusion
  51.3 1.0 %pad_maximum_fusion.1 = bf16[4,432,256]{2,1,0:T(8,128)(2,1)} fusion(bf16[4,432,128]{2,1,0:T(8,128)(2,1)S(1)} %fusion.21, bf16[4,432,128]{2,1,0:T(8,128)(2,1)S(1)} %fusion.22), kind=kLoop, calls=%fused_computation.55 | loop fusion | flops 1769472 | bytes 1769472 | tf_op jit(solution)/shard_map/concatenate | solution.py:170
  52.3 3.5 %all-to-all-start = ((bf16[4,432,256]{2,1,0:T(8,128)(2,1)}), bf16[4,432,256]{2,1,0:T(8,128)(2,1)S(1)}, u32[]{:S(2)}, u32[]{:S(2)}) async-start(bf16[4,432,256]{2,1,0:T(8,128)(2,1)} %pad_maximum_fusion.1), calls=%async_computation | async-start | bytes 1769472 | tf_op jit(solution)/shard_map/all_to_all | solution.py:122
  56.1 2.5 %collective-permute-start.11 = (bf16[256,640]{1,0:T(8,128)(2,1)S(1)}, bf16[256,640]{1,0:T(8,128)(2,1)S(1)}, u32[]{:S(2)}, u32[]{:S(2)}) collective-permute-start(bf16[256,640]{1,0:T(8,128)(2,1)S(1)} %get-tuple-element.44), channel_id=1, source_target_pairs={{0,24},{8,16},{16,8},{24,0},{1,25},{9,17},{17,9},{25,1},{2,26},{10... | collective-permute-start | bytes 983048 | tf_op jit(solution)/shard_map/ppermute | solution.py:196
  58.5 0.5 collective-permute-start.10
  59.1 0.6 collective-permute-start.9
  59.7 0.7 add_select_fusion
  60.4 7.3 %collective-permute-done.11 = bf16[256,640]{1,0:T(8,128)(2,1)S(1)} collective-permute-done((bf16[256,640]{1,0:T(8,128)(2,1)S(1)}, bf16[256,640]{1,0:T(8,128)(2,1)S(1)}, u32[]{:S(2)}, u32[]{:S(2)}) %collective-permute-start.11) | collective-permute-done | bytes 327712 | tf_op jit(solution)/shard_map/ppermute | solution.py:196
  67.6 6.2 %collective-permute-done.10 = bf16[256,640]{1,0:T(8,128)(2,1)S(1)} collective-permute-done((bf16[256,640]{1,0:T(8,128)(2,1)S(1)}, bf16[256,640]{1,0:T(8,128)(2,1)S(1)}, u32[]{:S(2)}, u32[]{:S(2)}) %collective-permute-start.10) | collective-permute-done | bytes 327712 | tf_op jit(solution)/shard_map/ppermute | solution.py:196
  74.3 1.0 %copy.53 = f32[256,4,128]{2,1,0:T(4,128)} copy(f32[256,4,128]{0,2,1:T(8,128)S(1)} %bitcast.187) | data formatting | bytes 1048576
  75.3 0.8 copy.54
  76.1 2.5 %all-to-all-done = bf16[4,432,256]{2,1,0:T(8,128)(2,1)S(1)} async-done(((bf16[4,432,256]{2,1,0:T(8,128)(2,1)}), bf16[4,432,256]{2,1,0:T(8,128)(2,1)S(1)}, u32[]{:S(2)}, u32[]{:S(2)}) %all-to-all-start) | async-done | bytes 884768 | tf_op jit(solution)/shard_map/all_to_all | solution.py:122
  79.2 2.5 %collective-permute-start.8 = (bf16[192,128]{1,0:T(8,128)(2,1)S(1)}, bf16[192,128]{1,0:T(8,128)(2,1)S(1)}, u32[]{:S(2)}, u32[]{:S(2)}) collective-permute-start(bf16[192,128]{1,0:T(8,128)(2,1)S(1)} %get-tuple-element.57), channel_id=1, source_target_pairs={{0,24},{8,16},{16,8},{24,0},{1,25},{9,17},{17,9},{25,1},{2,26},{10... | collective-permute-start | bytes 147464 | tf_op jit(solution)/shard_map/ppermute | solution.py:51
  82.2 0.5 collective-permute-start.6
  82.7 0.7 fusion.54
  83.4 0.9 %collective-permute-done.8 = bf16[192,128]{1,0:T(8,128)(2,1)S(1)} collective-permute-done((bf16[192,128]{1,0:T(8,128)(2,1)S(1)}, bf16[192,128]{1,0:T(8,128)(2,1)S(1)}, u32[]{:S(2)}, u32[]{:S(2)}) %collective-permute-start.8) | collective-permute-done | bytes 49184 | tf_op jit(solution)/shard_map/ppermute | solution.py:51
  84.3 1.4 %collective-permute-done.7 = bf16[192,128]{1,0:T(8,128)(2,1)S(1)} collective-permute-done((bf16[192,128]{1,0:T(8,128)(2,1)S(1)}, bf16[192,128]{1,0:T(8,128)(2,1)S(1)}, u32[]{:S(2)}, u32[]{:S(2)}) %collective-permute-start.7) | collective-permute-done | bytes 49184 | tf_op jit(solution)/shard_map/ppermute | solution.py:51
  85.8 0.5 collective-permute-done.6
  86.3 1.2 %fusion.13 = bf16[672,128]{1,0:T(8,128)(2,1)} fusion(bf16[768,128]{1,0:T(8,128)(2,1)S(1)} %bitcast.197, s32[672]{0:T(1024)S(1)} %add_select_fusion), kind=kOutput, calls=%fused_computation.38 | convolution fusion | flops 132722688 | bytes 371328 | tf_op jit(solution)/shard_map/dot_general | solution.py:56
  (80 shorter events, 13.1 us)
Async XLA Ops:
  6.2 11.6 %collective-permute-start.2 = (bf16[192,256]{1,0:T(8,128)(2,1)}, bf16[192,256]{1,0:T(8,128)(2,1)}, u32[]{:S(2)}, u32[]{:S(2)}) collective-permute-start(bf16[192,256]{1,0:T(8,128)(2,1)} %get-tuple-element.51), channel_id=1, source_target_pairs={{0,24},{8,16},{16,8},{24,0},{1,25},{9,17},{17,9},{25,1},{2,26},{10... | collective-permute-start | bytes 294920 | tf_op jit(solution)/shard_map/ppermute | solution.py:51
  10.1 7.7 %collective-permute-start.1 = (bf16[192,256]{1,0:T(8,128)(2,1)}, bf16[192,256]{1,0:T(8,128)(2,1)}, u32[]{:S(2)}, u32[]{:S(2)}) collective-permute-start(bf16[192,256]{1,0:T(8,128)(2,1)} %get-tuple-element.52), channel_id=1, source_target_pairs={{0,16},{8,24},{16,0},{24,8},{1,17},{9,25},{17,1},{25,9},{2,18},{10... | collective-permute-start | bytes 294920 | tf_op jit(solution)/shard_map/ppermute | solution.py:51
  10.6 7.2 %collective-permute-start = (bf16[192,256]{1,0:T(8,128)(2,1)}, bf16[192,256]{1,0:T(8,128)(2,1)}, u32[]{:S(2)}, u32[]{:S(2)}) collective-permute-start(bf16[192,256]{1,0:T(8,128)(2,1)} %get-tuple-element.53), channel_id=1, source_target_pairs={{0,8},{8,0},{16,24},{24,16},{1,9},{9,1},{17,25},{25,17},{2,10},{10... | collective-permute-start | bytes 294920 | tf_op jit(solution)/shard_map/ppermute | solution.py:51
  19.3 21.3 %copy-start.1 = (bf16[432,256]{1,0:T(8,128)(2,1)}, bf16[432,256]{1,0:T(8,128)(2,1)S(1)}, u32[]{:S(2)}) copy-start(bf16[432,256]{1,0:T(8,128)(2,1)S(1)} %fusion.10) | copy-start | bytes 663556
  40.6 2.4 %collective-permute-start.3 = (bf16[4,432,256]{2,1,0:T(8,128)(2,1)S(1)}, bf16[4,432,256]{2,1,0:T(8,128)(2,1)S(1)}, u32[]{:S(2)}, u32[]{:S(2)}) collective-permute-start(bf16[4,432,256]{2,1,0:T(8,128)(2,1)S(1)} %bitcast.178), channel_id=1, source_target_pairs={{0,1},{1,0},{2,3},{3,2},{4,5},{5,4},{6,7},{7,6},{8,9},{9,8},{10,11... | collective-permute-start | bytes 2654216 | tf_op jit(solution)/shard_map/ppermute | solution.py:113
  46.4 1.2 %copy-start = (bf16[8,128,512]{2,1,0:T(8,128)(2,1)S(1)}, bf16[8,128,512]{2,1,0:T(8,128)(2,1)}, u32[]{:S(2)}) copy-start(bf16[8,128,512]{2,1,0:T(8,128)(2,1)} %reshape.183) | copy-start | bytes 3145732
  48.4 2.7 %collective-permute-start.5 = (bf16[4,432,128]{2,1,0:T(8,128)(2,1)S(1)}, bf16[4,432,128]{2,1,0:T(8,128)(2,1)S(1)}, u32[]{:S(2)}, u32[]{:S(2)}) collective-permute-start(bf16[4,432,128]{2,1,0:T(8,128)(2,1)S(1)} %dynamic-slice_bitcast_fusion.2), channel_id=1, source_target_pairs={{0,1},{1,0},{2,3},{3,2},{4,5},{5,4},{6,7},{7,6},{8,9},{9,8},{10,11... | collective-permute-start | bytes 1327112 | tf_op jit(solution)/shard_map/ppermute | solution.py:119
  49.0 2.2 %collective-permute-start.4 = (bf16[4,432,128]{2,1,0:T(8,128)(2,1)S(1)}, bf16[4,432,128]{2,1,0:T(8,128)(2,1)S(1)}, u32[]{:S(2)}, u32[]{:S(2)}) collective-permute-start(bf16[4,432,128]{2,1,0:T(8,128)(2,1)S(1)} %dynamic-slice_bitcast_fusion.3), channel_id=1, source_target_pairs={{0,1},{1,0},{2,3},{3,2},{4,5},{5,4},{6,7},{7,6},{8,9},{9,8},{10,11... | collective-permute-start | bytes 1327112 | tf_op jit(solution)/shard_map/ppermute | solution.py:119
  52.3 26.3 %all-to-all-start = ((bf16[4,432,256]{2,1,0:T(8,128)(2,1)}), bf16[4,432,256]{2,1,0:T(8,128)(2,1)S(1)}, u32[]{:S(2)}, u32[]{:S(2)}) async-start(bf16[4,432,256]{2,1,0:T(8,128)(2,1)} %pad_maximum_fusion.1), calls=%async_computation | async-start | bytes 1769472 | tf_op jit(solution)/shard_map/all_to_all | solution.py:122
  56.1 11.6 %collective-permute-start.11 = (bf16[256,640]{1,0:T(8,128)(2,1)S(1)}, bf16[256,640]{1,0:T(8,128)(2,1)S(1)}, u32[]{:S(2)}, u32[]{:S(2)}) collective-permute-start(bf16[256,640]{1,0:T(8,128)(2,1)S(1)} %get-tuple-element.44), channel_id=1, source_target_pairs={{0,24},{8,16},{16,8},{24,0},{1,25},{9,17},{17,9},{25,1},{2,26},{10... | collective-permute-start | bytes 983048 | tf_op jit(solution)/shard_map/ppermute | solution.py:196
  58.5 15.2 %collective-permute-start.10 = (bf16[256,640]{1,0:T(8,128)(2,1)S(1)}, bf16[256,640]{1,0:T(8,128)(2,1)S(1)}, u32[]{:S(2)}, u32[]{:S(2)}) collective-permute-start(bf16[256,640]{1,0:T(8,128)(2,1)S(1)} %get-tuple-element.43), channel_id=1, source_target_pairs={{0,16},{8,24},{16,0},{24,8},{1,17},{9,25},{17,1},{25,9},{2,18},{10... | collective-permute-start | bytes 983048 | tf_op jit(solution)/shard_map/ppermute | solution.py:196
  59.1 14.8 %collective-permute-start.9 = (bf16[256,640]{1,0:T(8,128)(2,1)S(1)}, bf16[256,640]{1,0:T(8,128)(2,1)S(1)}, u32[]{:S(2)}, u32[]{:S(2)}) collective-permute-start(bf16[256,640]{1,0:T(8,128)(2,1)S(1)} %get-tuple-element.42), channel_id=1, source_target_pairs={{0,8},{8,0},{16,24},{24,16},{1,9},{9,1},{17,25},{25,17},{2,10},{10... | collective-permute-start | bytes 983048 | tf_op jit(solution)/shard_map/ppermute | solution.py:196
  74.1 4.6 %copy-start.2 = (bf16[432,256]{1,0:T(8,128)(2,1)S(1)}, bf16[432,256]{1,0:T(8,128)(2,1)}, u32[]{:S(2)}) copy-start(bf16[432,256]{1,0:T(8,128)(2,1)} %copy-done.1) | copy-start | bytes 663556
  79.2 5.2 %collective-permute-start.8 = (bf16[192,128]{1,0:T(8,128)(2,1)S(1)}, bf16[192,128]{1,0:T(8,128)(2,1)S(1)}, u32[]{:S(2)}, u32[]{:S(2)}) collective-permute-start(bf16[192,128]{1,0:T(8,128)(2,1)S(1)} %get-tuple-element.57), channel_id=1, source_target_pairs={{0,24},{8,16},{16,8},{24,0},{1,25},{9,17},{17,9},{25,1},{2,26},{10... | collective-permute-start | bytes 147464 | tf_op jit(solution)/shard_map/ppermute | solution.py:51
  81.7 4.1 %collective-permute-start.7 = (bf16[192,128]{1,0:T(8,128)(2,1)S(1)}, bf16[192,128]{1,0:T(8,128)(2,1)S(1)}, u32[]{:S(2)}, u32[]{:S(2)}) collective-permute-start(bf16[192,128]{1,0:T(8,128)(2,1)S(1)} %get-tuple-element.58), channel_id=1, source_target_pairs={{0,16},{8,24},{16,0},{24,8},{1,17},{9,25},{17,1},{25,9},{2,18},{10... | collective-permute-start | bytes 147464 | tf_op jit(solution)/shard_map/ppermute | solution.py:51
  82.2 4.1 %collective-permute-start.6 = (bf16[192,128]{1,0:T(8,128)(2,1)S(1)}, bf16[192,128]{1,0:T(8,128)(2,1)S(1)}, u32[]{:S(2)}, u32[]{:S(2)}) collective-permute-start(bf16[192,128]{1,0:T(8,128)(2,1)S(1)} %get-tuple-element.59), channel_id=1, source_target_pairs={{0,8},{8,0},{16,24},{24,16},{1,9},{9,1},{17,25},{25,17},{2,10},{10... | collective-permute-start | bytes 147464 | tf_op jit(solution)/shard_map/ppermute | solution.py:51

commit v19 on v18

--- a/solution.py
+++ b/solution.py
@@ -49,7 +49,17 @@
         for k in range(1, dp_count):
             outgoing = lax.dynamic_index_in_dim(blocks, dp_index ^ k, 0, keepdims=False)
             pieces.append(lax.ppermute(outgoing, "dp", [(d, d ^ k) for d in range(dp_count)]))
-        return jnp.stack(pieces)
+        return pieces
+
+    def pick_from_pieces(row_ids, pieces):
+        rows = pieces[0].shape[0]
+        total = None
+        for k, piece in enumerate(pieces):
+            span = k * rows + jnp.arange(rows, dtype=jnp.int32)
+            one_hot = (row_ids[:, None] == span[None, :]).astype(bf16)
+            term = jnp.dot(one_hot, piece, preferred_element_type=f32)
+            total = term if total is None else total + term
+        return total.astype(bf16)
 
     def pick_rows(row_ids, source):
         one_hot = (row_ids[:, None] == jnp.arange(source.shape[0], dtype=jnp.int32)[None, :]).astype(bf16)
@@ -103,7 +113,7 @@
     slot_pick = compact_slot[:, None] == peer_ids[None, :]
     compact_start = jnp.sum(jnp.where(slot_pick, recv_start[None, :], 0), axis=1)
     gather_ids = (compact_slot ^ dp_index) * MAXLEN + compact_ids - compact_start
-    own_both = pick_rows(gather_ids, recv_both.reshape(dp_count * MAXLEN, 2 * col_width))
+    own_both = pick_from_pieces(gather_ids, recv_both)
     own_tokens = own_both[:, :col_width]
     own_cotan = own_both[:, col_width:]
 
@@ -200,7 +210,6 @@
     back_src = jnp.minimum(recv_start[:, None] + places[None, :], owned_rows - 1)
     back_send = pick_rows(back_src.reshape(-1), token_rows).reshape(dp_count, MAXLEN, col_width)
     back_grads = exchange(back_send)
-    back_grads = back_grads.reshape(dp_count * MAXLEN, col_width)
     load_ids = jnp.arange(load_rows, dtype=jnp.int32)
     seq_of = jnp.sum((load_ids[:, None] >= my_starts[None, :]).astype(jnp.int32), axis=1) - 1
     seq_pick = seq_of[:, None] == seq_ids[None, :]
@@ -208,7 +217,7 @@
     start_of = jnp.sum(jnp.where(seq_pick, my_starts[None, :], 0), axis=1)
     back_ids = (owner_of ^ dp_index) * MAXLEN + jnp.minimum(load_ids - start_of, MAXLEN - 1)
     row_used = load_ids < jnp.sum(my_lengths)
-    token_grad = pick_rows(jnp.where(row_used, back_ids, -1), back_grads)
+    token_grad = pick_from_pieces(jnp.where(row_used, back_ids, -1), back_grads)
     return (mixed_out, token_grad, proj_grad, out_grad)
 
 

time: 88 us -> 94.4 us (1.073)
  matrix products: 9.75 us -> 13.8 us
  local copies, waits for them, and re-layouts: 10.9 us -> 13.3 us
  other arithmetic: 8.31 us -> 7.12 us
    dot_general x0 -> x8, matrix products: none -> 5.61 us  [pick_from_pieces(): term = jnp.dot(one_hot, piece, preferred_element_type=f32)]
    dot_general x4 -> x2, matrix products: 3.61 us -> 2.03 us  [pick_rows(): return jnp.dot(one_hot, source, preferred_element_type=f32).astype(bf16)]
    another operation x6 -> x4, other arithmetic: 1.69 us -> 0.62 us  [the longest x2 1.07 us: exchange(): return jnp.stack(pieces)]
    unnamed x10 -> x14, local copies, waits for them, and re-layouts: 2.49 us -> 2.95 us
  transfers between devices with their start and end apart: 13 -> 13, of which waited for: 8 -> 7; matrix products, arithmetic and copies ran while one was open for 16% -> 16% of each run, Pallas kernels for 0% -> 0%
where the time goes in v19:
time: 94.4 us; the launch traced here: 93.8 us
  blocking collectives  21.3 us (23%)
  waiting for transfers between devices  21.1 us (22%)
  starting transfers between devices  16 us (17%)
  matrix products  13.8 us (15%)
  local copies, waits for them, and re-layouts  13.3 us (14%)
  other arithmetic  7.12 us (8%)
  between operations  1.19 us (1%)
    all_gather x1, blocking collectives, local(): lax.all_gather(own_both, 'tensor', axis=0, tiled=False, axis_index_groups...  21.3 us
    ppermute x3, waiting for transfers between devices, local(): term_sum = term_sum + lax.ppermute(outgoing, 'dp', partners).astype(f32)  13.7 us
    ppermute x6, starting transfers between devices, exchange(): lax.ppermute(outgoing, 'dp', [(d, d ^ k) for d in range(dp_count)])  8.07 us
    dot_general x8, matrix products, pick_from_pieces(): term = jnp.dot(one_hot, piece, preferred_element_type=f32)  5.61 us
    all_to_all x1, starting transfers between devices, reduce_blocks(): lax.all_to_all(pair_sum, 'tensor', 0, 0, tiled=True, axis_index_groups=sa...  3.68 us
    ppermute x3, starting transfers between devices, local(): term_sum = term_sum + lax.ppermute(outgoing, 'dp', partners).astype(f32)  3.55 us
    ppermute x6, waiting for transfers between devices, exchange(): lax.ppermute(outgoing, 'dp', [(d, d ^ k) for d in range(dp_count)])  2.98 us
    unnamed x14, local copies, waits for them, and re-layouts  2.95 us
  transfers between devices with their start and end apart: 13, of which 7 were waited for; matrix products, arithmetic and copies ran while one was open for 16% of the time, Pallas kernels for 0%

profile of v19, /device:TPU:0, one launch (start us, length us, event | category | flops | bytes accessed | tf_op | source)
XLA Modules:
  0.0 93.8 jit_solution(1264372209372167888)
XLA Ops:
  0.6 1.3 %fusion.88 = (s32[]{:T(128)}, s32[1,4]{1,0:T(1,128)S(1)}) fusion(s32[4,4]{1,0:T(4,128)} %param.9, s32[]{:T(128)S(6)} %select_n.114), kind=kLoop, calls=%fused_computation.193 | loop fusion | flops 3 | bytes 40 | tf_op jit(solution)/shard_map/reduce_sum | solution.py:219
  2.1 0.7 fusion.86
  2.8 0.8 select_reduce_fusion.3
  3.8 1.6 %fusion.7 = bf16[768,256]{1,0:T(8,128)(2,1)S(1)} fusion(s32[768]{0:T(1024)S(1)} %min.38, bf16[672,128]{1,0:T(8,128)(2,1)} %param.8, bf16[672,128]{1,0:T(8,128)(2,1)} %param.7), kind=kOutput, calls=%fused_computation.24 | convolution fusion | flops 265641984 | bytes 740352 | tf_op jit(solution)/shard_map/dot_general | solution.py:66
  5.4 0.8 dynamic-slice_bitcast_fusion.4
  6.2 2.9 %collective-permute-start = (bf16[192,256]{1,0:T(8,128)(2,1)}, bf16[192,256]{1,0:T(8,128)(2,1)}, u32[]{:S(2)}, u32[]{:S(2)}) collective-permute-start(bf16[192,256]{1,0:T(8,128)(2,1)} %get-tuple-element.58), channel_id=1, source_target_pairs={{0,8},{8,0},{16,24},{24,16},{1,9},{9,1},{17,25},{25,17},{2,10},{10... | collective-permute-start | bytes 294920 | tf_op jit(solution)/shard_map/ppermute | solution.py:51
  9.1 1.5 %collective-permute-start.1 = (bf16[192,256]{1,0:T(8,128)(2,1)}, bf16[192,256]{1,0:T(8,128)(2,1)}, u32[]{:S(2)}, u32[]{:S(2)}) collective-permute-start(bf16[192,256]{1,0:T(8,128)(2,1)} %get-tuple-element.57), channel_id=1, source_target_pairs={{0,16},{8,24},{16,0},{24,8},{1,17},{9,25},{17,1},{25,9},{2,18},{10... | collective-permute-start | bytes 294920 | tf_op jit(solution)/shard_map/ppermute | solution.py:51
  10.7 2.4 %constant_dynamic-slice_fusion.1 = (bf16[1024,4,128]{2,1,0:T(4,128)(2,1)S(1)}, bf16[1024,4,128]{2,1,0:T(4,128)(2,1)S(1)}) fusion(bf16[1024,4,1024]{2,1,0:T(4,128)(2,1)} %param.11, s32[]{:T(128)S(6)} %select_n.124, s32[]{:T(128)S(6)} %select_n.120), kind=kLoop, calls=%fused_computation.166 | loop fusion | bytes 4194312 | tf_op jit(solution)/shard_map/dynamic_slice | solution.py:90
  13.5 1.8 %constant_dynamic-slice_fusion = (bf16[128,1024]{1,0:T(8,128)(2,1)}, bf16[128,1024]{1,0:T(8,128)(2,1)S(1)}) fusion(bf16[1024,1024]{1,0:T(8,128)(2,1)} %param.13, s32[]{:T(128)S(6)} %select_n.124, s32[]{:T(128)S(6)} %select_n.120), kind=kLoop, calls=%fused_computation.165 | loop fusion | bytes 1048584 | tf_op jit(solution)/shard_map/dynamic_slice | solution.py:100
  15.7 0.8 copy.42
  16.5 0.8 copy.43
  17.2 1.2 %reshape.189 = bf16[8,128,512]{2,1,0:T(8,128)(2,1)} reshape(bf16[1024,4,128]{2,1,0:T(4,128)(2,1)S(1)} %get-tuple-element.44) | data formatting | bytes 2097152 | tf_op jit(solution)/shard_map/reshape | solution.py:90
  18.6 0.8 dynamic_slice.103
  19.8 1.2 %fusion.36 = f32[432,256]{1,0:T(8,128)S(1)} fusion(bf16[192,256]{1,0:T(8,128)(2,1)} %collective-permute-done.2, s32[192]{0:T(256)S(1)} %iota_add_fusion, s32[432]{0:T(512)S(1)} %add_subtract_fusion), kind=kOutput, calls=%fused_computation.86 | convolution fusion | flops 42550272 | bytes 543168 | tf_op jit(solution)/shard_map/dot_general | solution.py:60
  21.0 1.2 %fusion.38 = f32[432,256]{1,0:T(8,128)S(1)} fusion(bf16[192,256]{1,0:T(8,128)(2,1)} %collective-permute-done.1, s32[192]{0:T(256)S(1)} %iota_add_fusion.1, s32[432]{0:T(512)S(1)} %add_subtract_fusion), kind=kOutput, calls=%fused_computation.88 | convolution fusion | flops 42550272 | bytes 543168 | tf_op jit(solution)/shard_map/dot_general | solution.py:60
  22.1 1.2 %fusion.40 = f32[432,256]{1,0:T(8,128)S(1)} fusion(bf16[192,256]{1,0:T(8,128)(2,1)} %collective-permute-done, s32[192]{0:T(256)S(1)} %iota_add_fusion.2, s32[432]{0:T(512)S(1)} %add_subtract_fusion), kind=kOutput, calls=%fused_computation.90 | convolution fusion | flops 42550272 | bytes 543168 | tf_op jit(solution)/shard_map/dot_general | solution.py:60
  23.6 21.3 %all-gather = bf16[1728,256]{1,0:T(8,128)(2,1)S(1)} all-gather(bf16[432,256]{1,0:T(8,128)(2,1)S(1)} %fusion.11), channel_id=2, replica_groups={{0,2,4,6},{1,3,5,7},{8,10,12,14},{9,11,13,15},{16,18,20,22},{17,19,21,2..., dimensions={0}, use_global_device_ids=true | all-gather | bytes 1105920 | tf_op jit(solution)/shard_map/all_gather | solution.py:122
  45.2 2.2 %collective-permute-done.3 = bf16[4,432,256]{2,1,0:T(8,128)(2,1)S(1)} collective-permute-done((bf16[4,432,256]{2,1,0:T(8,128)(2,1)S(1)}, bf16[4,432,256]{2,1,0:T(8,128)(2,1)S(1)}, u32[]{:S(2)}, u32[]{:S(2)}) %collective-permute-start.3) | collective-permute-done | bytes 884768 | tf_op jit(solution)/shard_map/ppermute | solution.py:123
  53.1 0.7 convolution_convert_fusion
  56.8 1.0 %pad_maximum_fusion.1 = bf16[4,432,256]{2,1,0:T(8,128)(2,1)} fusion(bf16[4,432,128]{2,1,0:T(8,128)(2,1)S(1)} %fusion.21, bf16[4,432,128]{2,1,0:T(8,128)(2,1)S(1)} %fusion.22), kind=kLoop, calls=%fused_computation.56 | loop fusion | flops 1769472 | bytes 1769472 | tf_op jit(solution)/shard_map/concatenate | solution.py:180
  57.8 3.7 %all-to-all-start = ((bf16[4,432,256]{2,1,0:T(8,128)(2,1)}), bf16[4,432,256]{2,1,0:T(8,128)(2,1)S(1)}, u32[]{:S(2)}, u32[]{:S(2)}) async-start(bf16[4,432,256]{2,1,0:T(8,128)(2,1)} %pad_maximum_fusion.1), calls=%async_computation | async-start | bytes 1769472 | tf_op jit(solution)/shard_map/all_to_all | solution.py:132
  61.7 2.5 %collective-permute-start.11 = (bf16[256,640]{1,0:T(8,128)(2,1)S(1)}, bf16[256,640]{1,0:T(8,128)(2,1)S(1)}, u32[]{:S(2)}, u32[]{:S(2)}) collective-permute-start(bf16[256,640]{1,0:T(8,128)(2,1)S(1)} %get-tuple-element.50), channel_id=1, source_target_pairs={{0,24},{8,16},{16,8},{24,0},{1,25},{9,17},{17,9},{25,1},{2,26},{10... | collective-permute-start | bytes 983048 | tf_op jit(solution)/shard_map/ppermute | solution.py:206
  65.9 7.4 %collective-permute-done.11 = bf16[256,640]{1,0:T(8,128)(2,1)S(1)} collective-permute-done((bf16[256,640]{1,0:T(8,128)(2,1)S(1)}, bf16[256,640]{1,0:T(8,128)(2,1)S(1)}, u32[]{:S(2)}, u32[]{:S(2)}) %collective-permute-start.11) | collective-permute-done | bytes 327712 | tf_op jit(solution)/shard_map/ppermute | solution.py:206
  73.3 6.2 %collective-permute-done.10 = bf16[256,640]{1,0:T(8,128)(2,1)S(1)} collective-permute-done((bf16[256,640]{1,0:T(8,128)(2,1)S(1)}, bf16[256,640]{1,0:T(8,128)(2,1)S(1)}, u32[]{:S(2)}, u32[]{:S(2)}) %collective-permute-start.10) | collective-permute-done | bytes 327712 | tf_op jit(solution)/shard_map/ppermute | solution.py:206
  80.0 1.0 %copy.53 = f32[256,4,128]{2,1,0:T(4,128)} copy(f32[256,4,128]{0,2,1:T(8,128)S(1)} %bitcast.189) | data formatting | bytes 1048576
  81.0 0.8 copy.54
  81.8 2.3 %all-to-all-done = bf16[4,432,256]{2,1,0:T(8,128)(2,1)S(1)} async-done(((bf16[4,432,256]{2,1,0:T(8,128)(2,1)}), bf16[4,432,256]{2,1,0:T(8,128)(2,1)S(1)}, u32[]{:S(2)}, u32[]{:S(2)}) %all-to-all-start) | async-done | bytes 884768 | tf_op jit(solution)/shard_map/all_to_all | solution.py:132
  84.2 0.7 fusion.71
  85.4 2.5 %collective-permute-start.8 = (bf16[192,128]{1,0:T(8,128)(2,1)S(1)}, bf16[192,128]{1,0:T(8,128)(2,1)S(1)}, u32[]{:S(2)}, u32[]{:S(2)}) collective-permute-start(bf16[192,128]{1,0:T(8,128)(2,1)S(1)} %get-tuple-element.63), channel_id=1, source_target_pairs={{0,24},{8,16},{16,8},{24,0},{1,25},{9,17},{17,9},{25,1},{2,26},{10... | collective-permute-start | bytes 147464 | tf_op jit(solution)/shard_map/ppermute | solution.py:51
  88.7 0.6 collective-permute-start.7
  89.3 2.7 %collective-permute-done.6 = bf16[192,128]{1,0:T(8,128)(2,1)S(1)} collective-permute-done((bf16[192,128]{1,0:T(8,128)(2,1)S(1)}, bf16[192,128]{1,0:T(8,128)(2,1)S(1)}, u32[]{:S(2)}, u32[]{:S(2)}) %collective-permute-start.6) | collective-permute-done | bytes 49184 | tf_op jit(solution)/shard_map/ppermute | solution.py:51
  92.9 1.0 %fusion.14 = bf16[672,128]{1,0:T(8,128)(2,1)} fusion(f32[672,128]{1,0:T(8,128)S(1)} %fusion.26, f32[672,128]{1,0:T(8,128)S(1)} %convolution_add_fusion.2, bf16[192,128]{1,0:T(8,128)(2,1)S(1)} %collective-permute-done.7, s32[192]{0:T(256)S(1)} %iota_add_fusion.1, s32[672]{0:T(1024)S(1)} %add_select_fusion), kind=kOutput, calls=%fused_computation.40 | convolution fusion | flops 33417216 | bytes 912768 | tf_op jit(solution)/shard_map/dot_general | solution.py:60
  (91 shorter events, 15.4 us)
Async XLA Ops:
  6.2 13.6 %collective-permute-start = (bf16[192,256]{1,0:T(8,128)(2,1)}, bf16[192,256]{1,0:T(8,128)(2,1)}, u32[]{:S(2)}, u32[]{:S(2)}) collective-permute-start(bf16[192,256]{1,0:T(8,128)(2,1)} %get-tuple-element.58), channel_id=1, source_target_pairs={{0,8},{8,0},{16,24},{24,16},{1,9},{9,1},{17,25},{25,17},{2,10},{10... | collective-permute-start | bytes 294920 | tf_op jit(solution)/shard_map/ppermute | solution.py:51
  9.1 10.7 %collective-permute-start.1 = (bf16[192,256]{1,0:T(8,128)(2,1)}, bf16[192,256]{1,0:T(8,128)(2,1)}, u32[]{:S(2)}, u32[]{:S(2)}) collective-permute-start(bf16[192,256]{1,0:T(8,128)(2,1)} %get-tuple-element.57), channel_id=1, source_target_pairs={{0,16},{8,24},{16,0},{24,8},{1,17},{9,25},{17,1},{25,9},{2,18},{10... | collective-permute-start | bytes 294920 | tf_op jit(solution)/shard_map/ppermute | solution.py:51
  10.6 9.2 %collective-permute-start.2 = (bf16[192,256]{1,0:T(8,128)(2,1)}, bf16[192,256]{1,0:T(8,128)(2,1)}, u32[]{:S(2)}, u32[]{:S(2)}) collective-permute-start(bf16[192,256]{1,0:T(8,128)(2,1)} %get-tuple-element.56), channel_id=1, source_target_pairs={{0,24},{8,16},{16,8},{24,0},{1,25},{9,17},{17,9},{25,1},{2,26},{10... | collective-permute-start | bytes 294920 | tf_op jit(solution)/shard_map/ppermute | solution.py:51
  15.6 2.8 %copy-start = (bf16[128,1024]{1,0:T(8,128)(2,1)S(1)}, bf16[128,1024]{1,0:T(8,128)(2,1)}, u32[]{:S(2)}) copy-start(bf16[128,1024]{1,0:T(8,128)(2,1)} %get-tuple-element.46) | copy-start | bytes 786436
  17.2 6.1 %copy-start.4 = (bf16[192,256]{1,0:T(8,128)(2,1)S(1)}, bf16[192,256]{1,0:T(8,128)(2,1)}, u32[]{:S(2)}) copy-start(bf16[192,256]{1,0:T(8,128)(2,1)} %get-tuple-element.15) | copy-start | bytes 294916
  44.9 2.4 %collective-permute-start.3 = (bf16[4,432,256]{2,1,0:T(8,128)(2,1)S(1)}, bf16[4,432,256]{2,1,0:T(8,128)(2,1)S(1)}, u32[]{:S(2)}, u32[]{:S(2)}) collective-permute-start(bf16[4,432,256]{2,1,0:T(8,128)(2,1)S(1)} %bitcast.180), channel_id=1, source_target_pairs={{0,1},{1,0},{2,3},{3,2},{4,5},{5,4},{6,7},{7,6},{8,9},{9,8},{10,11... | collective-permute-start | bytes 2654216 | tf_op jit(solution)/shard_map/ppermute | solution.py:123
  48.4 0.9 copy-start.2
  48.4 1.2 %copy-start.3 = (bf16[128,4,1,128]{3,0,2,1:T(8,128)(2,1)S(1)}, bf16[128,4,1,128]{3,0,2,1:T(8,128)(2,1)}, u32[]{:S(2)}) copy-start(bf16[128,4,1,128]{3,0,2,1:T(8,128)(2,1)} %copy.42) | copy-start | bytes 393220
  51.9 1.2 %copy-start.1 = (bf16[8,128,512]{2,1,0:T(8,128)(2,1)S(1)}, bf16[8,128,512]{2,1,0:T(8,128)(2,1)}, u32[]{:S(2)}) copy-start(bf16[8,128,512]{2,1,0:T(8,128)(2,1)} %reshape.189) | copy-start | bytes 3145732
  53.8 2.7 %collective-permute-start.5 = (bf16[4,432,128]{2,1,0:T(8,128)(2,1)S(1)}, bf16[4,432,128]{2,1,0:T(8,128)(2,1)S(1)}, u32[]{:S(2)}, u32[]{:S(2)}) collective-permute-start(bf16[4,432,128]{2,1,0:T(8,128)(2,1)S(1)} %dynamic-slice_bitcast_fusion.2), channel_id=1, source_target_pairs={{0,1},{1,0},{2,3},{3,2},{4,5},{5,4},{6,7},{7,6},{8,9},{9,8},{10,11... | collective-permute-start | bytes 1327112 | tf_op jit(solution)/shard_map/ppermute | solution.py:129
  54.5 2.2 %collective-permute-start.4 = (bf16[4,432,128]{2,1,0:T(8,128)(2,1)S(1)}, bf16[4,432,128]{2,1,0:T(8,128)(2,1)S(1)}, u32[]{:S(2)}, u32[]{:S(2)}) collective-permute-start(bf16[4,432,128]{2,1,0:T(8,128)(2,1)S(1)} %dynamic-slice_bitcast_fusion.3), channel_id=1, source_target_pairs={{0,1},{1,0},{2,3},{3,2},{4,5},{5,4},{6,7},{7,6},{8,9},{9,8},{10,11... | collective-permute-start | bytes 1327112 | tf_op jit(solution)/shard_map/ppermute | solution.py:129
  57.8 26.3 %all-to-all-start = ((bf16[4,432,256]{2,1,0:T(8,128)(2,1)}), bf16[4,432,256]{2,1,0:T(8,128)(2,1)S(1)}, u32[]{:S(2)}, u32[]{:S(2)}) async-start(bf16[4,432,256]{2,1,0:T(8,128)(2,1)} %pad_maximum_fusion.1), calls=%async_computation | async-start | bytes 1769472 | tf_op jit(solution)/shard_map/all_to_all | solution.py:132
  61.7 11.6 %collective-permute-start.11 = (bf16[256,640]{1,0:T(8,128)(2,1)S(1)}, bf16[256,640]{1,0:T(8,128)(2,1)S(1)}, u32[]{:S(2)}, u32[]{:S(2)}) collective-permute-start(bf16[256,640]{1,0:T(8,128)(2,1)S(1)} %get-tuple-element.50), channel_id=1, source_target_pairs={{0,24},{8,16},{16,8},{24,0},{1,25},{9,17},{17,9},{25,1},{2,26},{10... | collective-permute-start | bytes 983048 | tf_op jit(solution)/shard_map/ppermute | solution.py:206
  64.3 15.2 %collective-permute-start.10 = (bf16[256,640]{1,0:T(8,128)(2,1)S(1)}, bf16[256,640]{1,0:T(8,128)(2,1)S(1)}, u32[]{:S(2)}, u32[]{:S(2)}) collective-permute-start(bf16[256,640]{1,0:T(8,128)(2,1)S(1)} %get-tuple-element.49), channel_id=1, source_target_pairs={{0,16},{8,24},{16,0},{24,8},{1,17},{9,25},{17,1},{25,9},{2,18},{10... | collective-permute-start | bytes 983048 | tf_op jit(solution)/shard_map/ppermute | solution.py:206
  64.8 14.8 %collective-permute-start.9 = (bf16[256,640]{1,0:T(8,128)(2,1)S(1)}, bf16[256,640]{1,0:T(8,128)(2,1)S(1)}, u32[]{:S(2)}, u32[]{:S(2)}) collective-permute-start(bf16[256,640]{1,0:T(8,128)(2,1)S(1)} %get-tuple-element.48), channel_id=1, source_target_pairs={{0,8},{8,0},{16,24},{24,16},{1,9},{9,1},{17,25},{25,17},{2,10},{10... | collective-permute-start | bytes 983048 | tf_op jit(solution)/shard_map/ppermute | solution.py:206
  85.4 6.9 %collective-permute-start.8 = (bf16[192,128]{1,0:T(8,128)(2,1)S(1)}, bf16[192,128]{1,0:T(8,128)(2,1)S(1)}, u32[]{:S(2)}, u32[]{:S(2)}) collective-permute-start(bf16[192,128]{1,0:T(8,128)(2,1)S(1)} %get-tuple-element.63), channel_id=1, source_target_pairs={{0,24},{8,16},{16,8},{24,0},{1,25},{9,17},{17,9},{25,1},{2,26},{10... | collective-permute-start | bytes 147464 | tf_op jit(solution)/shard_map/ppermute | solution.py:51
  87.9 4.1 %collective-permute-start.6 = (bf16[192,128]{1,0:T(8,128)(2,1)S(1)}, bf16[192,128]{1,0:T(8,128)(2,1)S(1)}, u32[]{:S(2)}, u32[]{:S(2)}) collective-permute-start(bf16[192,128]{1,0:T(8,128)(2,1)S(1)} %get-tuple-element.64), channel_id=1, source_target_pairs={{0,8},{8,0},{16,24},{24,16},{1,9},{9,1},{17,25},{25,17},{2,10},{10... | collective-permute-start | bytes 147464 | tf_op jit(solution)/shard_map/ppermute | solution.py:51
  88.7 4.2 %collective-permute-start.7 = (bf16[192,128]{1,0:T(8,128)(2,1)S(1)}, bf16[192,128]{1,0:T(8,128)(2,1)S(1)}, u32[]{:S(2)}, u32[]{:S(2)}) collective-permute-start(bf16[192,128]{1,0:T(8,128)(2,1)S(1)} %get-tuple-element.62), channel_id=1, source_target_pairs={{0,16},{8,24},{16,0},{24,8},{1,17},{9,25},{17,1},{25,9},{2,18},{10... | collective-permute-start | bytes 147464 | tf_op jit(solution)/shard_map/ppermute | solution.py:51

commit v20 on v18

--- a/solution.py
+++ b/solution.py
@@ -90,9 +90,9 @@
     own_out = lax.dynamic_slice_in_dim(out_weight, own_start, col_width, 0).reshape(
         col_width, tensor_count, col_width
     )
-    weight_pack = (proj_mine, proj_other, out_mine, out_other, own_proj, own_out, head_gain)
+    weight_pack = (proj_mine, proj_other, out_mine, out_other, own_proj, own_out)
     recv_both, weight_pack = lax.optimization_barrier((recv_both, weight_pack))
-    proj_mine, proj_other, out_mine, out_other, own_proj, own_out, head_gain = weight_pack
+    proj_mine, proj_other, out_mine, out_other, own_proj, own_out = weight_pack
 
     recv_len = jnp.sum(jnp.where(owners == dp_index, lengths, 0), axis=1)
     recv_start = exclusive_sum(recv_len)

time: 88 us -> 87.2 us (level)
  no operation moved by 1% of the time
where the time goes in v20:
time: 87.2 us; the launch traced here: 86.8 us
  blocking collectives  21.3 us (24%)
  waiting for transfers between devices  19.7 us (23%)
  starting transfers between devices  15.7 us (18%)
  local copies, waits for them, and re-layouts  10.9 us (12%)
  matrix products  9.74 us (11%)
  other arithmetic  8.31 us (10%)
  between operations  1.13 us (1%)
    all_gather x1, blocking collectives, local(): lax.all_gather(own_both, 'tensor', axis=0, tiled=False, axis_index_groups...  21.3 us
    ppermute x3, waiting for transfers between devices, local(): term_sum = term_sum + lax.ppermute(outgoing, 'dp', partners).astype(f32)  13.5 us
    ppermute x6, starting transfers between devices, exchange(): lax.ppermute(outgoing, 'dp', [(d, d ^ k) for d in range(dp_count)])  8.02 us
    dot_general x4, matrix products, pick_rows(): return jnp.dot(one_hot, source, preferred_element_type=f32).astype(bf16)  3.61 us
    ppermute x3, starting transfers between devices, local(): term_sum = term_sum + lax.ppermute(outgoing, 'dp', partners).astype(f32)  3.55 us
    all_to_all x1, starting transfers between devices, reduce_blocks(): lax.all_to_all(pair_sum, 'tensor', 0, 0, tiled=True, axis_index_groups=sa...  3.5 us
    ppermute x6, waiting for transfers between devices, exchange(): lax.ppermute(outgoing, 'dp', [(d, d ^ k) for d in range(dp_count)])  2.88 us
    all_to_all x1, waiting for transfers between devices, reduce_blocks(): lax.all_to_all(pair_sum, 'tensor', 0, 0, tiled=True, axis_index_groups=sa...  2.51 us
  transfers between devices with their start and end apart: 13, of which 8 were waited for; matrix products, arithmetic and copies ran while one was open for 16% of the time, Pallas kernels for 0%

profile of v20, /device:TPU:0, one launch (start us, length us, event | category | flops | bytes accessed | tf_op | source)
XLA Modules:
  0.0 86.8 jit_solution(6854885596108043747)
XLA Ops:
  0.6 1.3 %fusion.61 = (s32[]{:T(128)}, s32[1,4]{1,0:T(1,128)S(1)}) fusion(s32[4,4]{1,0:T(4,128)} %param.9, s32[]{:T(128)S(6)} %select_n.114), kind=kLoop, calls=%fused_computation.163 | loop fusion | flops 3 | bytes 40 | tf_op jit(solution)/shard_map/reduce_sum | solution.py:210
  2.2 0.7 fusion.59
  2.8 0.8 select_reduce_fusion.3
  3.8 1.6 %fusion.9 = bf16[768,256]{1,0:T(8,128)(2,1)S(1)} fusion(s32[768]{0:T(1024)S(1)} %min.38, bf16[672,128]{1,0:T(8,128)(2,1)} %param.8, bf16[672,128]{1,0:T(8,128)(2,1)} %param.7), kind=kOutput, calls=%fused_computation.28 | convolution fusion | flops 265641984 | bytes 740352 | tf_op jit(solution)/shard_map/dot_general | solution.py:56
  5.4 0.7 constant_dynamic-slice_fusion.7
  6.2 3.9 %collective-permute-start.2 = (bf16[192,256]{1,0:T(8,128)(2,1)}, bf16[192,256]{1,0:T(8,128)(2,1)}, u32[]{:S(2)}, u32[]{:S(2)}) collective-permute-start(bf16[192,256]{1,0:T(8,128)(2,1)} %get-tuple-element.49), channel_id=1, source_target_pairs={{0,24},{8,16},{16,8},{24,0},{1,25},{9,17},{17,9},{25,1},{2,26},{10... | collective-permute-start | bytes 294920 | tf_op jit(solution)/shard_map/ppermute | solution.py:51
  10.6 2.4 %constant_dynamic-slice_fusion.2 = (bf16[1024,4,128]{2,1,0:T(4,128)(2,1)S(1)}, bf16[1024,4,128]{2,1,0:T(4,128)(2,1)S(1)}) fusion(bf16[1024,4,1024]{2,1,0:T(4,128)(2,1)} %param.11, s32[]{:T(128)S(6)} %select_n.124, s32[]{:T(128)S(6)} %select_n.120), kind=kLoop, calls=%fused_computation.138 | loop fusion | bytes 4194312 | tf_op jit(solution)/shard_map/dynamic_slice | solution.py:80
  13.5 1.1 %constant_dynamic-slice_fusion.1 = (bf16[128,1024]{1,0:T(8,128)(2,1)S(1)}, bf16[128,1024]{1,0:T(8,128)(2,1)S(1)}) fusion(bf16[1024,1024]{1,0:T(8,128)(2,1)} %param.13, s32[]{:T(128)S(6)} %select_n.124, s32[]{:T(128)S(6)} %select_n.120), kind=kLoop, calls=%fused_computation.137 | loop fusion | bytes 1048584 | tf_op jit(solution)/shard_map/dynamic_slice | solution.py:90
  15.1 1.2 %reshape.183 = bf16[8,128,512]{2,1,0:T(8,128)(2,1)} reshape(bf16[1024,4,128]{2,1,0:T(4,128)(2,1)S(1)} %get-tuple-element.36) | data formatting | bytes 2097152 | tf_op jit(solution)/shard_map/reshape | solution.py:80
  17.1 1.0 %pad_maximum_fusion.3 = bf16[4,192,256]{2,1,0:T(8,128)(2,1)S(1)} fusion(bf16[1,192,256]{2,1,0:T(8,128)(2,1)} %bitcast.10, bf16[1,192,256]{2,1,0:T(8,128)(2,1)} %bitcast.8, bf16[1,192,256]{2,1,0:T(8,128)(2,1)} %bitcast.6, bf16[1,192,256]{2,1,0:T(8,128)(2,1)S(1)} %get-tuple-element.48), kind=kLoop, calls=%fused_computation.79 | loop fusion | flops 589824 | bytes 786432 | tf_op jit(solution)/shard_map/stack | solution.py:52
  18.5 21.3 %all-gather = bf16[1728,256]{1,0:T(8,128)(2,1)S(1)} all-gather(bf16[432,256]{1,0:T(8,128)(2,1)S(1)} %fusion.10), channel_id=2, replica_groups={{0,2,4,6},{1,3,5,7},{8,10,12,14},{9,11,13,15},{16,18,20,22},{17,19,21,2..., dimensions={0}, use_global_device_ids=true | all-gather | bytes 1105920 | tf_op jit(solution)/shard_map/all_gather | solution.py:112
  39.9 0.8 dynamic_slice.103
  41.5 0.7 collective-permute-done.3
  46.9 0.7 convolution_convert_fusion
  50.5 1.0 %pad_maximum_fusion.1 = bf16[4,432,256]{2,1,0:T(8,128)(2,1)} fusion(bf16[4,432,128]{2,1,0:T(8,128)(2,1)S(1)} %fusion.21, bf16[4,432,128]{2,1,0:T(8,128)(2,1)S(1)} %fusion.22), kind=kLoop, calls=%fused_computation.55 | loop fusion | flops 1769472 | bytes 1769472 | tf_op jit(solution)/shard_map/concatenate | solution.py:170
  51.6 3.5 %all-to-all-start = ((bf16[4,432,256]{2,1,0:T(8,128)(2,1)}), bf16[4,432,256]{2,1,0:T(8,128)(2,1)S(1)}, u32[]{:S(2)}, u32[]{:S(2)}) async-start(bf16[4,432,256]{2,1,0:T(8,128)(2,1)} %pad_maximum_fusion.1), calls=%async_computation | async-start | bytes 1769472 | tf_op jit(solution)/shard_map/all_to_all | solution.py:122
  55.3 2.5 %collective-permute-start.11 = (bf16[256,640]{1,0:T(8,128)(2,1)S(1)}, bf16[256,640]{1,0:T(8,128)(2,1)S(1)}, u32[]{:S(2)}, u32[]{:S(2)}) collective-permute-start(bf16[256,640]{1,0:T(8,128)(2,1)S(1)} %get-tuple-element.42), channel_id=1, source_target_pairs={{0,24},{8,16},{16,8},{24,0},{1,25},{9,17},{17,9},{25,1},{2,26},{10... | collective-permute-start | bytes 983048 | tf_op jit(solution)/shard_map/ppermute | solution.py:196
  58.3 0.6 collective-permute-start.9
  58.9 0.7 add_select_fusion
  59.6 7.3 %collective-permute-done.11 = bf16[256,640]{1,0:T(8,128)(2,1)S(1)} collective-permute-done((bf16[256,640]{1,0:T(8,128)(2,1)S(1)}, bf16[256,640]{1,0:T(8,128)(2,1)S(1)}, u32[]{:S(2)}, u32[]{:S(2)}) %collective-permute-start.11) | collective-permute-done | bytes 327712 | tf_op jit(solution)/shard_map/ppermute | solution.py:196
  66.9 6.2 %collective-permute-done.10 = bf16[256,640]{1,0:T(8,128)(2,1)S(1)} collective-permute-done((bf16[256,640]{1,0:T(8,128)(2,1)S(1)}, bf16[256,640]{1,0:T(8,128)(2,1)S(1)}, u32[]{:S(2)}, u32[]{:S(2)}) %collective-permute-start.10) | collective-permute-done | bytes 327712 | tf_op jit(solution)/shard_map/ppermute | solution.py:196
  73.6 1.0 %copy.53 = f32[256,4,128]{2,1,0:T(4,128)} copy(f32[256,4,128]{0,2,1:T(8,128)S(1)} %bitcast.187) | data formatting | bytes 1048576
  74.6 0.8 copy.54
  75.3 2.5 %all-to-all-done = bf16[4,432,256]{2,1,0:T(8,128)(2,1)S(1)} async-done(((bf16[4,432,256]{2,1,0:T(8,128)(2,1)}), bf16[4,432,256]{2,1,0:T(8,128)(2,1)S(1)}, u32[]{:S(2)}, u32[]{:S(2)}) %all-to-all-start) | async-done | bytes 884768 | tf_op jit(solution)/shard_map/all_to_all | solution.py:122
  78.4 2.5 %collective-permute-start.8 = (bf16[192,128]{1,0:T(8,128)(2,1)S(1)}, bf16[192,128]{1,0:T(8,128)(2,1)S(1)}, u32[]{:S(2)}, u32[]{:S(2)}) collective-permute-start(bf16[192,128]{1,0:T(8,128)(2,1)S(1)} %get-tuple-element.55), channel_id=1, source_target_pairs={{0,24},{8,16},{16,8},{24,0},{1,25},{9,17},{17,9},{25,1},{2,26},{10... | collective-permute-start | bytes 147464 | tf_op jit(solution)/shard_map/ppermute | solution.py:51
  80.9 0.5 collective-permute-start.7
  81.5 0.5 collective-permute-start.6
  82.0 0.7 fusion.54
  82.7 0.9 %collective-permute-done.8 = bf16[192,128]{1,0:T(8,128)(2,1)S(1)} collective-permute-done((bf16[192,128]{1,0:T(8,128)(2,1)S(1)}, bf16[192,128]{1,0:T(8,128)(2,1)S(1)}, u32[]{:S(2)}, u32[]{:S(2)}) %collective-permute-start.8) | collective-permute-done | bytes 49184 | tf_op jit(solution)/shard_map/ppermute | solution.py:51
  83.6 1.4 %collective-permute-done.7 = bf16[192,128]{1,0:T(8,128)(2,1)S(1)} collective-permute-done((bf16[192,128]{1,0:T(8,128)(2,1)S(1)}, bf16[192,128]{1,0:T(8,128)(2,1)S(1)}, u32[]{:S(2)}, u32[]{:S(2)}) %collective-permute-start.7) | collective-permute-done | bytes 49184 | tf_op jit(solution)/shard_map/ppermute | solution.py:51
  85.0 0.5 collective-permute-done.6
  85.6 1.2 %fusion.13 = bf16[672,128]{1,0:T(8,128)(2,1)} fusion(bf16[768,128]{1,0:T(8,128)(2,1)S(1)} %bitcast.197, s32[672]{0:T(1024)S(1)} %add_select_fusion), kind=kOutput, calls=%fused_computation.38 | convolution fusion | flops 132722688 | bytes 371328 | tf_op jit(solution)/shard_map/dot_general | solution.py:56
  (80 shorter events, 13.0 us)
Async XLA Ops:
  6.2 10.9 %collective-permute-start.2 = (bf16[192,256]{1,0:T(8,128)(2,1)}, bf16[192,256]{1,0:T(8,128)(2,1)}, u32[]{:S(2)}, u32[]{:S(2)}) collective-permute-start(bf16[192,256]{1,0:T(8,128)(2,1)} %get-tuple-element.49), channel_id=1, source_target_pairs={{0,24},{8,16},{16,8},{24,0},{1,25},{9,17},{17,9},{25,1},{2,26},{10... | collective-permute-start | bytes 294920 | tf_op jit(solution)/shard_map/ppermute | solution.py:51
  10.1 7.0 %collective-permute-start.1 = (bf16[192,256]{1,0:T(8,128)(2,1)}, bf16[192,256]{1,0:T(8,128)(2,1)}, u32[]{:S(2)}, u32[]{:S(2)}) collective-permute-start(bf16[192,256]{1,0:T(8,128)(2,1)} %get-tuple-element.50), channel_id=1, source_target_pairs={{0,16},{8,24},{16,0},{24,8},{1,17},{9,25},{17,1},{25,9},{2,18},{10... | collective-permute-start | bytes 294920 | tf_op jit(solution)/shard_map/ppermute | solution.py:51
  10.6 6.5 %collective-permute-start = (bf16[192,256]{1,0:T(8,128)(2,1)}, bf16[192,256]{1,0:T(8,128)(2,1)}, u32[]{:S(2)}, u32[]{:S(2)}) collective-permute-start(bf16[192,256]{1,0:T(8,128)(2,1)} %get-tuple-element.51), channel_id=1, source_target_pairs={{0,8},{8,0},{16,24},{24,16},{1,9},{9,1},{17,25},{25,17},{2,10},{10... | collective-permute-start | bytes 294920 | tf_op jit(solution)/shard_map/ppermute | solution.py:51
  18.5 21.4 %copy-start.1 = (bf16[432,256]{1,0:T(8,128)(2,1)}, bf16[432,256]{1,0:T(8,128)(2,1)S(1)}, u32[]{:S(2)}) copy-start(bf16[432,256]{1,0:T(8,128)(2,1)S(1)} %fusion.10) | copy-start | bytes 663556
  39.8 2.4 %collective-permute-start.3 = (bf16[4,432,256]{2,1,0:T(8,128)(2,1)S(1)}, bf16[4,432,256]{2,1,0:T(8,128)(2,1)S(1)}, u32[]{:S(2)}, u32[]{:S(2)}) collective-permute-start(bf16[4,432,256]{2,1,0:T(8,128)(2,1)S(1)} %bitcast.178), channel_id=1, source_target_pairs={{0,1},{1,0},{2,3},{3,2},{4,5},{5,4},{6,7},{7,6},{8,9},{9,8},{10,11... | collective-permute-start | bytes 2654216 | tf_op jit(solution)/shard_map/ppermute | solution.py:113
  45.6 1.2 %copy-start = (bf16[8,128,512]{2,1,0:T(8,128)(2,1)S(1)}, bf16[8,128,512]{2,1,0:T(8,128)(2,1)}, u32[]{:S(2)}) copy-start(bf16[8,128,512]{2,1,0:T(8,128)(2,1)} %reshape.183) | copy-start | bytes 3145732
  47.6 2.7 %collective-permute-start.5 = (bf16[4,432,128]{2,1,0:T(8,128)(2,1)S(1)}, bf16[4,432,128]{2,1,0:T(8,128)(2,1)S(1)}, u32[]{:S(2)}, u32[]{:S(2)}) collective-permute-start(bf16[4,432,128]{2,1,0:T(8,128)(2,1)S(1)} %dynamic-slice_bitcast_fusion.2), channel_id=1, source_target_pairs={{0,1},{1,0},{2,3},{3,2},{4,5},{5,4},{6,7},{7,6},{8,9},{9,8},{10,11... | collective-permute-start | bytes 1327112 | tf_op jit(solution)/shard_map/ppermute | solution.py:119
  48.2 2.2 %collective-permute-start.4 = (bf16[4,432,128]{2,1,0:T(8,128)(2,1)S(1)}, bf16[4,432,128]{2,1,0:T(8,128)(2,1)S(1)}, u32[]{:S(2)}, u32[]{:S(2)}) collective-permute-start(bf16[4,432,128]{2,1,0:T(8,128)(2,1)S(1)} %dynamic-slice_bitcast_fusion.3), channel_id=1, source_target_pairs={{0,1},{1,0},{2,3},{3,2},{4,5},{5,4},{6,7},{7,6},{8,9},{9,8},{10,11... | collective-permute-start | bytes 1327112 | tf_op jit(solution)/shard_map/ppermute | solution.py:119
  51.6 26.3 %all-to-all-start = ((bf16[4,432,256]{2,1,0:T(8,128)(2,1)}), bf16[4,432,256]{2,1,0:T(8,128)(2,1)S(1)}, u32[]{:S(2)}, u32[]{:S(2)}) async-start(bf16[4,432,256]{2,1,0:T(8,128)(2,1)} %pad_maximum_fusion.1), calls=%async_computation | async-start | bytes 1769472 | tf_op jit(solution)/shard_map/all_to_all | solution.py:122
  55.3 11.6 %collective-permute-start.11 = (bf16[256,640]{1,0:T(8,128)(2,1)S(1)}, bf16[256,640]{1,0:T(8,128)(2,1)S(1)}, u32[]{:S(2)}, u32[]{:S(2)}) collective-permute-start(bf16[256,640]{1,0:T(8,128)(2,1)S(1)} %get-tuple-element.42), channel_id=1, source_target_pairs={{0,24},{8,16},{16,8},{24,0},{1,25},{9,17},{17,9},{25,1},{2,26},{10... | collective-permute-start | bytes 983048 | tf_op jit(solution)/shard_map/ppermute | solution.py:196
  57.8 15.3 %collective-permute-start.10 = (bf16[256,640]{1,0:T(8,128)(2,1)S(1)}, bf16[256,640]{1,0:T(8,128)(2,1)S(1)}, u32[]{:S(2)}, u32[]{:S(2)}) collective-permute-start(bf16[256,640]{1,0:T(8,128)(2,1)S(1)} %get-tuple-element.41), channel_id=1, source_target_pairs={{0,16},{8,24},{16,0},{24,8},{1,17},{9,25},{17,1},{25,9},{2,18},{10... | collective-permute-start | bytes 983048 | tf_op jit(solution)/shard_map/ppermute | solution.py:196
  58.3 14.8 %collective-permute-start.9 = (bf16[256,640]{1,0:T(8,128)(2,1)S(1)}, bf16[256,640]{1,0:T(8,128)(2,1)S(1)}, u32[]{:S(2)}, u32[]{:S(2)}) collective-permute-start(bf16[256,640]{1,0:T(8,128)(2,1)S(1)} %get-tuple-element.40), channel_id=1, source_target_pairs={{0,8},{8,0},{16,24},{24,16},{1,9},{9,1},{17,25},{25,17},{2,10},{10... | collective-permute-start | bytes 983048 | tf_op jit(solution)/shard_map/ppermute | solution.py:196
  73.3 4.6 %copy-start.2 = (bf16[432,256]{1,0:T(8,128)(2,1)S(1)}, bf16[432,256]{1,0:T(8,128)(2,1)}, u32[]{:S(2)}) copy-start(bf16[432,256]{1,0:T(8,128)(2,1)} %copy-done.1) | copy-start | bytes 663556
  78.4 5.2 %collective-permute-start.8 = (bf16[192,128]{1,0:T(8,128)(2,1)S(1)}, bf16[192,128]{1,0:T(8,128)(2,1)S(1)}, u32[]{:S(2)}, u32[]{:S(2)}) collective-permute-start(bf16[192,128]{1,0:T(8,128)(2,1)S(1)} %get-tuple-element.55), channel_id=1, source_target_pairs={{0,24},{8,16},{16,8},{24,0},{1,25},{9,17},{17,9},{25,1},{2,26},{10... | collective-permute-start | bytes 147464 | tf_op jit(solution)/shard_map/ppermute | solution.py:51
  80.9 4.1 %collective-permute-start.7 = (bf16[192,128]{1,0:T(8,128)(2,1)S(1)}, bf16[192,128]{1,0:T(8,128)(2,1)S(1)}, u32[]{:S(2)}, u32[]{:S(2)}) collective-permute-start(bf16[192,128]{1,0:T(8,128)(2,1)S(1)} %get-tuple-element.56), channel_id=1, source_target_pairs={{0,16},{8,24},{16,0},{24,8},{1,17},{9,25},{17,1},{25,9},{2,18},{10... | collective-permute-start | bytes 147464 | tf_op jit(solution)/shard_map/ppermute | solution.py:51
  81.5 4.1 %collective-permute-start.6 = (bf16[192,128]{1,0:T(8,128)(2,1)S(1)}, bf16[192,128]{1,0:T(8,128)(2,1)S(1)}, u32[]{:S(2)}, u32[]{:S(2)}) collective-permute-start(bf16[192,128]{1,0:T(8,128)(2,1)S(1)} %get-tuple-element.57), channel_id=1, source_target_pairs={{0,8},{8,0},{16,24},{24,16},{1,9},{9,1},{17,25},{25,17},{2,10},{10... | collective-permute-start | bytes 147464 | tf_op jit(solution)/shard_map/ppermute | solution.py:51
